TPU v7x, 32 devices: a whole 2x2x4 slice. The times are simulated.
32 devices in a mesh: groups: 2 (over y), row: 4 (over x, core), col: 4 (over z).
Axes of the slice: x: 2, y: 2, z: 4, core: 2. Of those that a mesh axis runs over, the one named last changes fastest.
Arguments:
- latent_in: bfloat16 [48, 16, 32, 640], P('groups', 'row', 'col'), parts along dimension 0, may hold values from -6 to 6
- cached_mid: bfloat16 [48, 16, 32, 640], P('groups', 'row', 'col'), parts along dimension 0, may hold values from -5 to 5
- cached_out: bfloat16 [48, 16, 32, 640], P('groups', 'row', 'col'), parts along dimension 0, may hold values from -6 to 6
- edit_tiles: int32 [48, 16], P('groups'), parts along dimension 0, may hold values from -1 to 31, as said below
- norm1_mean: float32 [48, 32], P('groups'), parts along dimension 0, may hold values from -2 to 2
- norm1_rstd: float32 [48, 32], P('groups'), parts along dimension 0, may hold values from 0.6 to 1.8
- norm1_gain: float32 [640], replicated, may hold values from 0.1 to 1.9
- norm1_shift: float32 [640], replicated, may hold values from -2 to 2
- conv1_weight: bfloat16 [3, 3, 640, 640], P(None, None, 'row'), may hold values from -0.078125 to 0.078125
- conv1_bias: float32 [640], replicated, may hold values from -2 to 2
- step_embed: float32 [48, 640], P('groups'), parts along dimension 0, may hold values from -3 to 3
- norm2_mean: float32 [48, 32], P('groups'), parts along dimension 0, may hold values from -1.5 to 1.5
- norm2_rstd: float32 [48, 32], P('groups'), parts along dimension 0, may hold values from 0.8 to 2.5
- norm2_gain: float32 [640], replicated, may hold values from 0.1 to 1.9
- norm2_shift: float32 [640], replicated, may hold values from -2 to 2
- conv2_weight: bfloat16 [3, 3, 640, 640], P(None, None, 'row'), may hold values from -0.078125 to 0.078125
- conv2_bias: float32 [640], replicated, may hold values from -2 to 2
Outputs:
- latent_out: bfloat16 [48, 16, 32, 640], P('groups', 'row', 'col'), parts along dimension 0
There are 2 independent parts, one for each index of `groups`. A program takes and returns all parts, laid end to end along the dimension named above; an argument that names none is the same for every part. Nothing has to cross between parts.
Inputs may be any that keep to these rules, and one draw needn't show every extreme that they name: `edit_tiles`: each request lists, in increasing order, the tile numbers of one rectangle exactly 2 tile rows tall and 4 to 7 tile columns wide, then -1 to the end of the row.
All inputs are finite; a program needn't handle non-finite values.
Results may differ from a plain program's by a relative error of at most 0.0042.
Values may be sent and summed in bfloat16 or wider, within the bound.
No kernel may reach another device: no remote copies, remote signals or barrier semaphores. Data moves between devices by JAX's collectives and lax.ppermute only.
A program may use at most 128 MiB of HBM per device.

v0:
```python
import jax
import jax.numpy as jnp
from jax import lax
from jax.sharding import PartitionSpec as P

TILE = 4


def padded_2(block, sides, width):
    for axis, dim in sides:
        count = lax.axis_size(axis)
        forward = [(i, i + 1) for i in range(count - 1)]
        backward = [(target, source) for source, target in forward]
        low = lax.ppermute(
            lax.slice_in_dim(block, block.shape[dim] - width, None, axis=dim), axis, forward
        )
        high = lax.ppermute(lax.slice_in_dim(block, 0, width, axis=dim), axis, backward)
        block = jnp.concatenate([low, block, high], axis=dim)
    return block


def border_mask(tile_row, tile_col, rows_total, cols_total):
    offsets = jnp.arange(TILE + 2, dtype=jnp.int32) - 1
    cell_rows = tile_row[:, None] * TILE + offsets[None, :]
    cell_cols = tile_col[:, None] * TILE + offsets[None, :]
    row_inside = (cell_rows >= 0) & (cell_rows < rows_total * TILE)
    col_inside = (cell_cols >= 0) & (cell_cols < cols_total * TILE)
    return (row_inside[:, :, None] & col_inside[:, None, :]).astype(jnp.float32)


def lookup(tables, request):
    onehot = (request[:, None] == jnp.arange(tables.shape[0], dtype=jnp.int32)[None, :]).astype(
        jnp.float32
    )
    return jnp.dot(onehot, tables, precision=lax.Precision.HIGHEST)


def conv_apply(activation, whole_kernel):
    tile_count = activation.shape[0]
    width_in = activation.shape[3]
    windows = [
        activation[:, tap_row : tap_row + TILE, tap_col : tap_col + TILE, :]
        for tap_row in range(3)
        for tap_col in range(3)
    ]
    unfolded = jnp.concatenate(windows, axis=3).reshape(tile_count * TILE * TILE, 9 * width_in)
    return jnp.dot(unfolded, whole_kernel, preferred_element_type=jnp.float32)


def body(
    latent_in,
    cached_mid,
    cached_out,
    edit_tiles,
    norm1_mean,
    norm1_rstd,
    norm1_gain,
    norm1_shift,
    conv1_weight,
    conv1_bias,
    step_embed,
    norm2_mean,
    norm2_rstd,
    norm2_gain,
    norm2_shift,
    conv2_weight,
    conv2_bias,
):
    requests, rows_dev, cols_dev, channels = latent_in.shape
    tiles_down = rows_dev // TILE
    tiles_across = cols_dev // TILE
    row_devices = lax.axis_size("row")
    rows_total = tiles_down * row_devices
    cols_total = tiles_across * lax.axis_size("col")
    groups_total = norm1_mean.shape[1]
    per_group = channels // groups_total
    first_whole = lax.all_gather(conv1_weight, "row", axis=2, tiled=True).reshape(
        9 * channels, channels
    )
    second_whole = lax.all_gather(conv2_weight, "row", axis=2, tiled=True).reshape(
        9 * channels, channels
    )
    tables = jnp.concatenate([norm1_mean, norm1_rstd, norm2_mean, norm2_rstd, step_embed], axis=1)
    edge_index = jnp.arange(TILE + 2, dtype=jnp.int32)
    edge_line = (edge_index == 0) | (edge_index == TILE + 1)
    margin_mask = (edge_line[:, None] | edge_line[None, :])[None, :, :, None]

    def expand(values, column):
        return jnp.repeat(
            values[:, column * groups_total : (column + 1) * groups_total], per_group, axis=1
        )[:, None, None, :]

    stacked = jnp.stack([latent_in, cached_mid])
    padded = padded_2(stacked, (("row", 2), ("col", 3)), 1)
    columns = []
    for tile_across in range(tiles_across):
        tile_cells = [
            padded[:, :, 0 : TILE + 2, TILE * tile_across : TILE * tile_across + TILE + 2]
        ]
        columns.append(jnp.stack(tile_cells))
    patches = jnp.transpose(jnp.stack(columns), (3, 0, 1, 2, 4, 5, 6))
    own_rows = lax.axis_index("row") * tiles_down + jnp.arange(tiles_down, dtype=jnp.int32)
    own_cols = lax.axis_index("col") * tiles_across + jnp.arange(tiles_across, dtype=jnp.int32)
    tile_numbers = own_rows[None, :] * cols_total + own_cols[:, None]
    edited = jnp.any(edit_tiles[:, None, None, :] == tile_numbers[None, :, :, None], axis=-1)
    grid_shape = edited.shape
    request_grid = jnp.broadcast_to(
        jnp.arange(requests, dtype=jnp.int32)[:, None, None], grid_shape
    )
    row_grid = jnp.broadcast_to(own_rows[None, None, :], grid_shape)
    col_grid = jnp.broadcast_to(own_cols[None, :, None], grid_shape)
    flattened = patches.reshape((-1,) + patches.shape[3:])
    inputs = flattened[:, 0].astype(jnp.float32)
    margins = flattened[:, 1].astype(jnp.float32)
    border = border_mask(row_grid.reshape(-1), col_grid.reshape(-1), rows_total, cols_total)[
        ..., None
    ]
    looked = lookup(tables, request_grid.reshape(-1))
    embedding = looked[:, 4 * groups_total :][:, None, None, :]
    first_act = (
        jax.nn.silu((inputs - expand(looked, 0)) * expand(looked, 1) * norm1_gain + norm1_shift)
        * border
    ).astype(jnp.bfloat16)
    first_sum = conv_apply(first_act, first_whole)
    fresh_mid = first_sum.reshape(-1, TILE, TILE, channels) + conv1_bias + embedding
    padded_mid = jnp.pad(fresh_mid, ((0, 0), (1, 1), (1, 1), (0, 0)))
    middle = jnp.where(margin_mask, margins, padded_mid)
    second_act = (
        jax.nn.silu((middle - expand(looked, 2)) * expand(looked, 3) * norm2_gain + norm2_shift)
        * border
    ).astype(jnp.bfloat16)
    second_sum = conv_apply(second_act, second_whole)
    renewed = (
        second_sum.reshape(-1, TILE, TILE, channels)
        + conv2_bias
        + inputs[:, 1 : 1 + TILE, 1 : 1 + TILE]
    ).astype(jnp.bfloat16)
    results = renewed.reshape(requests, tiles_across, tiles_down, TILE, TILE, channels)
    renewed_cells = jnp.transpose(results, (0, 2, 3, 1, 4, 5)).reshape(
        requests, rows_dev, cols_dev, channels
    )
    cell_mask = jnp.repeat(jnp.repeat(jnp.transpose(edited, (0, 2, 1)), TILE, axis=1), TILE, axis=2)
    return jnp.where(cell_mask[..., None], renewed_cells, cached_out)


def solution(mesh):
    placed = (
        P("groups", "row", "col", None),
        P("groups", "row", "col", None),
        P("groups", "row", "col", None),
        P("groups", None),
        P("groups", None),
        P("groups", None),
        P(),
        P(),
        P(None, None, "row", None),
        P(),
        P("groups", None),
        P("groups", None),
        P("groups", None),
        P(),
        P(),
        P(None, None, "row", None),
        P(),
    )
    return jax.shard_map(
        body, mesh=mesh, in_specs=placed, out_specs=P("groups", "row", "col", None), check_vma=False
    )
```

profile of v0, /device:TPU:1, one launch (start us, length us, event | category | flops | bytes accessed | tf_op | source)
XLA Modules:
  0.0 142.8 jit_solution(16553166397954714331)
XLA Ops:
  6.5 0.7 all-gather.3.cloned.1.call-update
  7.4 2.1 %copy_bitcast_fusion = (bf16[1,24,4,8,640]{4,1,3,2,0:T(8,128)(2,1)S(1)}, bf16[1,24,4,8,640]{4,1,3,2,0:T(8,128)(2,1)S(1)}) fusion(bf16[24,4,8,640]{3,2,1,0:T(8,128)(2,1)} %param.18, bf16[24,4,8,640]{3,2,1,0:T(8,128)(2,1)} %param.17), kind=kLoop, calls=%fused_computation.42 | loop fusion | bytes 3932160 | tf_op jit(solution)/shard_map/stack | solution.py:93
  9.5 1.0 pad_maximum_fusion.9
  10.6 4.5 %collective-permute-start = (bf16[2,24,1,8,640]{4,1,3,2,0:T(8,128)(2,1)}, bf16[2,24,1,8,640]{4,1,3,2,0:T(8,128)(2,1)S(1)}, u32[]{:S(2)}, u32[]{:S(2)}) collective-permute-start(bf16[2,24,1,8,640]{4,1,3,2,0:T(8,128)(2,1)} %get-tuple-element.9), channel_id=1, source_target_pairs={{0,4},{4,8},{8,12},{1,5},{5,9},{9,13},{2,6},{6,10},{10,14},{3,7},{... | collective-permute-start | bytes 1474568 | tf_op jit(solution)/shard_map/ppermute | solution.py:14
  15.1 1.9 %collective-permute-start.1 = (bf16[2,24,1,8,640]{4,1,3,2,0:T(8,128)(2,1)}, bf16[2,24,1,8,640]{4,1,3,2,0:T(8,128)(2,1)S(1)}, u32[]{:S(2)}, u32[]{:S(2)}) collective-permute-start(bf16[2,24,1,8,640]{4,1,3,2,0:T(8,128)(2,1)} %get-tuple-element.10), channel_id=1, source_target_pairs={{4,0},{8,4},{12,8},{5,1},{9,5},{13,9},{6,2},{10,6},{14,10},{7,3},{... | collective-permute-start | bytes 1474568 | tf_op jit(solution)/shard_map/ppermute | solution.py:17
  17.2 0.7 broadcast_or_fusion
  17.8 0.7 fusion.10
  19.0 0.7 fusion.13
  19.7 2.5 %collective-permute-done = bf16[2,24,1,8,640]{4,1,3,2,0:T(8,128)(2,1)S(1)} collective-permute-done((bf16[2,24,1,8,640]{4,1,3,2,0:T(8,128)(2,1)}, bf16[2,24,1,8,640]{4,1,3,2,0:T(8,128)(2,1)S(1)}, u32[]{:S(2)}, u32[]{:S(2)}) %collective-permute-start) | collective-permute-done | bytes 491552 | tf_op jit(solution)/shard_map/ppermute | solution.py:14
  22.2 9.7 %collective-permute-done.1 = bf16[2,24,1,8,640]{4,1,3,2,0:T(8,128)(2,1)S(1)} collective-permute-done((bf16[2,24,1,8,640]{4,1,3,2,0:T(8,128)(2,1)}, bf16[2,24,1,8,640]{4,1,3,2,0:T(8,128)(2,1)S(1)}, u32[]{:S(2)}, u32[]{:S(2)}) %collective-permute-start.1) | collective-permute-done | bytes 491552 | tf_op jit(solution)/shard_map/ppermute | solution.py:17
  31.9 1.0 pad_maximum_fusion.13
  32.9 4.1 %collective-permute-start.2 = (bf16[2,24,6,1,640]{4,1,3,2,0:T(8,128)(2,1)}, bf16[2,24,6,1,640]{4,1,3,2,0:T(8,128)(2,1)}, u32[]{:S(2)}, u32[]{:S(2)}) collective-permute-start(bf16[2,24,6,1,640]{4,1,3,2,0:T(8,128)(2,1)} %get-tuple-element.7), channel_id=1, source_target_pairs={{0,1},{1,2},{2,3},{4,5},{5,6},{6,7},{8,9},{9,10},{10,11},{12,13},{... | collective-permute-start | bytes 1105928 | tf_op jit(solution)/shard_map/ppermute | solution.py:14
  37.1 1.3 collective-permute-start.3
  38.4 0.7 compare_reduce_fusion
  39.1 0.8 sub.25
  39.9 1.8 %copy.52 = f32[48,640]{1,0:T(8,128)} copy(f32[48,640]{0,1:T(8,128)} %sub.25) | data formatting | bytes 245760 | tf_op jit(solution)/shard_map/sub | solution.py:121
  41.6 0.8 copy.53
  42.5 0.8 mul.82
  43.2 1.8 %copy.54 = f32[48,640]{1,0:T(8,128)} copy(f32[48,640]{0,1:T(8,128)} %mul.82) | data formatting | bytes 245760 | tf_op jit(solution)/shard_map/mul | solution.py:121
  45.1 0.8 sub.29
  45.9 1.8 %copy.56 = f32[48,640]{1,0:T(8,128)} copy(f32[48,640]{0,1:T(8,128)} %sub.29) | data formatting | bytes 245760 | tf_op jit(solution)/shard_map/sub | solution.py:129
  47.8 0.8 mul.93
  48.5 1.1 copy.58
  49.6 0.7 broadcast_in_dim.28
  50.4 0.7 and_convert_fusion
  51.1 2.5 %fusion.6 = (bf16[1,1,2,24,6,6,640]{6,3,5,4,2,1,0:T(8,128)(2,1)S(1)}, bf16[1,1,2,24,6,6,640]{6,3,5,4,2,1,0:T(8,128)(2,1)S(1)}) fusion(bf16[2,24,6,1,640]{4,1,3,2,0:T(8,128)(2,1)} %collective-permute-done.2, bf16[2,24,1,8,640]{4,1,3,2,0:T(8,128)(2,1)S(1)} %collective-permute-done.1, bf16[2,24,1,8,640]{4,1,3,2,0:T(8,128)(2,1)S(1)} %collective-permute-done, ...), kind=kLoop, calls=%fused_computation.17 | loop fusion | flops 8847360 | bytes 8110080 | tf_op jit(solution)/shard_map/stack;stack | solution.py:101
  53.7 2.5 %maximum_bitcast_fusion = bf16[24,2,1,2,6,6,640]{6,0,5,4,3,2,1:T(8,128)(2,1)} fusion(bf16[1,1,2,24,6,6,640]{6,3,5,4,2,1,0:T(8,128)(2,1)S(1)} %get-tuple-element.6, bf16[1,1,2,24,6,6,640]{6,3,5,4,2,1,0:T(8,128)(2,1)S(1)} %get-tuple-element.5), kind=kLoop, calls=%fused_computation | loop fusion | flops 2211840 | bytes 8847360 | tf_op jit(solution)/shard_map/transpose | solution.py:101
  56.2 8.9 %copy.50 = bf16[24,2,1,2,6,6,640]{6,1,0,5,4,3,2:T(2,128)(2,1)} copy(bf16[24,2,1,2,6,6,640]{6,0,5,4,3,2,1:T(8,128)(2,1)} %maximum_bitcast_fusion) | data formatting | bytes 8847360 | tf_op jit(solution)/shard_map/transpose | solution.py:101
  65.1 10.1 %reshape.189 = bf16[48,2,6,6,640]{4,0,3,2,1:T(8,128)(2,1)} reshape(bf16[24,2,1,2,6,6,640]{6,1,0,5,4,3,2:T(2,128)(2,1)} %copy.50) | data formatting | bytes 8847360 | tf_op jit(solution)/shard_map/reshape | solution.py:112
  75.2 3.2 %multiply_convert_fusion.1 = bf16[48,6,6,640]{3,0,2,1:T(8,128)(2,1)S(1)} fusion(f32[48,6,6]{0,2,1:T(8,128)S(1)} %and_convert_fusion, f32[640]{0:T(1024)S(1)} %copy-done.12, f32[640]{0:T(1024)S(1)} %copy-done.13, f32[48,640]{1,0:T(8,128)S(1)} %copy-done.4, f32[48,640]{1,0:T(8,128)S(1)} %copy-done.3, bf16[48,2,6,6,640]{4,0,3,2,1:T(8,128)(2,1)} %reshape.189), kind=kLoop, calls=%fused_computation.7 | loop fusion | flops 12165120 | bytes 4681472 | tf_op jit(solution)/shard_map/convert_element_type | solution.py:123
  79.9 3.9 %copy-done.5 = bf16[48,4,4,5760]{3,0,2,1:T(8,128)(2,1)} copy-done((bf16[48,4,4,5760]{3,0,2,1:T(8,128)(2,1)}, bf16[48,4,4,5760]{3,0,2,1:T(8,128)(2,1)S(1)}, u32[]{:S(2)}) %copy-start.5) | copy-done | bytes 8847384
  83.8 2.5 %fusion.4 = f32[48,6,6,640]{3,0,2,1:T(8,128)} fusion(bf16[48,2,6,6,640]{4,0,3,2,1:T(8,128)(2,1)S(1)} %bitcast.56), kind=kLoop, calls=%fused_computation.9 | loop fusion | flops 1105920 | bytes 6635520 | tf_op jit(solution)/shard_map/convert_element_type | solution.py:113
  86.3 12.1 %add_add_fusion = f32[48,4,4,640]{3,0,2,1:T(8,128)S(1)} fusion(bf16[48,4,4,5760]{3,0,2,1:T(8,128)(2,1)} %copy-done.5, bf16[5760,640,1,1]{1,0,3,2:T(8,128)(2,1)} %bitcast.62, f32[48,640]{1,0:T(8,128)S(1)} %slice-done.4, f32[640]{0:T(1024)S(1)} %copy-done.17), kind=kOutput, calls=%fused_computation.23 | convolution fusion | flops 5663293440 | bytes 18311680 | tf_op jit(solution)/shard_map/dot_general | solution.py:47
  98.5 2.3 %multiply_convert_fusion = bf16[48,6,6,640]{3,0,2,1:T(8,128)(2,1)S(1)} fusion(f32[48,4,4,640]{3,0,2,1:T(8,128)S(1)} %add_add_fusion, bf16[48,2,6,6,640]{4,0,3,2,1:T(8,128)(2,1)S(1)} %bitcast.58, f32[640]{0:T(1024)S(1)} %copy-done.14, f32[640]{0:T(1024)S(1)} %copy-done.15, f32[48,640]{1,0:T(8,128)S(1)} %copy.58, f32[48,640]{1,0:T(8,128)S(1)} %copy-done.2, ...), kind=kLoop, calls=%fused_computation.6 | loop fusion | flops 13271040 | bytes 6647588 | tf_op jit(solution)/shard_map/convert_element_type | solution.py:131
  100.9 1.1 slice_dynamic-update-slice_fusion.8
  102.0 1.1 slice_dynamic-update-slice_fusion.7
  103.0 1.1 slice_dynamic-update-slice_fusion.6
  104.1 1.1 slice_dynamic-update-slice_fusion.5
  105.2 1.2 slice_dynamic-update-slice_fusion.4
  106.4 1.1 slice_dynamic-update-slice_fusion.3
  107.5 1.1 slice_dynamic-update-slice_fusion.2
  108.6 1.1 slice_dynamic-update-slice_fusion.1
  109.7 1.1 slice_dynamic-update-slice_fusion
  110.8 10.7 %all-gather.5.cloned.1.call-done = bf16[3,3,640,640]{3,2,1,0:T(8,128)(2,1)} async-done(((bf16[3,3,160,640]{3,2,1,0:T(8,128)(2,1)}), bf16[3,3,640,640]{3,2,1,0:T(8,128)(2,1)}) %all-gather.5.cloned.1.call-update) | async-done | bytes 7372816 | tf_op jit(solution)/shard_map/all_gather | solution.py:80
  121.5 12.1 %fusion.7 = bf16[48,4,4,640]{3,0,2,1:T(8,128)(2,1)S(1)} fusion(f32[48,6,6,640]{3,0,2,1:T(8,128)} %fusion.4, bf16[48,4,4,5760]{3,0,2,1:T(8,128)(2,1)} %slice_dynamic-update-slice_fusion, bf16[5760,640,1,1]{1,0,3,2:T(8,128)(2,1)} %bitcast.61, f32[640]{0:T(1024)S(1)} %copy-done.18), kind=kOutput, calls=%fused_computation.22 | convolution fusion | flops 5663784960 | bytes 19171840 | tf_op jit(solution)/shard_map/dot_general | solution.py:47
  133.6 0.4 reshape.192
  134.0 0.4 copy.59
  134.8 1.1 broadcast_select_fusion
  (83 shorter events, 2.9 us)
Async XLA Ops:
  6.5 79.8 %all-gather.3.cloned.1.call-start = ((), (), s32[]{:S(2)}) async-start(), calls=%async_computation | async-start | bytes 9216000 | tf_op jit(solution)/shard_map/all_gather | solution.py:77
  7.3 11.3 %copy-start.6 = (f32[24,640]{1,0:T(8,128)S(1)}, f32[24,640]{1,0:T(8,128)}, u32[]{:S(2)}) copy-start(f32[24,640]{1,0:T(8,128)} %param.27) | copy-start | bytes 184324
  7.3 11.3 %copy-start.7 = (f32[24,32]{1,0:T(8,128)S(1)}, f32[24,32]{1,0:T(8,128)}, u32[]{:S(2)}) copy-start(f32[24,32]{1,0:T(8,128)} %param.21) | copy-start | bytes 9220
  7.3 11.3 %copy-start.8 = (f32[24,32]{1,0:T(8,128)S(1)}, f32[24,32]{1,0:T(8,128)}, u32[]{:S(2)}) copy-start(f32[24,32]{1,0:T(8,128)} %param.22) | copy-start | bytes 9220
  7.3 11.3 %copy-start.9 = (f32[24,32]{1,0:T(8,128)S(1)}, f32[24,32]{1,0:T(8,128)}, u32[]{:S(2)}) copy-start(f32[24,32]{1,0:T(8,128)} %param.28) | copy-start | bytes 9220
  7.3 11.3 %copy-start.10 = (f32[24,32]{1,0:T(8,128)S(1)}, f32[24,32]{1,0:T(8,128)}, u32[]{:S(2)}) copy-start(f32[24,32]{1,0:T(8,128)} %param.29) | copy-start | bytes 9220
  7.3 114.2 %all-gather.5.cloned.1.call-start = ((), (), s32[]{:S(2)}) async-start(), calls=%async_computation.1 | async-start | bytes 9216000 | tf_op jit(solution)/shard_map/all_gather | solution.py:80
  9.5 28.8 %copy-start.11 = (s32[24,16]{0,1:T(8,128)S(1)}, s32[24,16]{0,1:T(8,128)}, u32[]{:S(2)}) copy-start(s32[24,16]{0,1:T(8,128)} %param.20) | copy-start | bytes 4612
  10.6 11.6 %collective-permute-start = (bf16[2,24,1,8,640]{4,1,3,2,0:T(8,128)(2,1)}, bf16[2,24,1,8,640]{4,1,3,2,0:T(8,128)(2,1)S(1)}, u32[]{:S(2)}, u32[]{:S(2)}) collective-permute-start(bf16[2,24,1,8,640]{4,1,3,2,0:T(8,128)(2,1)} %get-tuple-element.9), channel_id=1, source_target_pairs={{0,4},{4,8},{8,12},{1,5},{5,9},{9,13},{2,6},{6,10},{10,14},{3,7},{... | collective-permute-start | bytes 1474568 | tf_op jit(solution)/shard_map/ppermute | solution.py:14
  15.1 16.9 %collective-permute-start.1 = (bf16[2,24,1,8,640]{4,1,3,2,0:T(8,128)(2,1)}, bf16[2,24,1,8,640]{4,1,3,2,0:T(8,128)(2,1)S(1)}, u32[]{:S(2)}, u32[]{:S(2)}) collective-permute-start(bf16[2,24,1,8,640]{4,1,3,2,0:T(8,128)(2,1)} %get-tuple-element.10), channel_id=1, source_target_pairs={{4,0},{8,4},{12,8},{5,1},{9,5},{13,9},{6,2},{10,6},{14,10},{7,3},{... | collective-permute-start | bytes 1474568 | tf_op jit(solution)/shard_map/ppermute | solution.py:17
  19.0 28.6 %copy-start.1 = (f32[48,768]{1,0:T(8,128)}, f32[48,768]{1,0:T(8,128)S(1)}, u32[]{:S(2)}) copy-start(f32[48,768]{1,0:T(8,128)S(1)} %fusion.8) | copy-start | bytes 442372
  32.9 18.2 %collective-permute-start.2 = (bf16[2,24,6,1,640]{4,1,3,2,0:T(8,128)(2,1)}, bf16[2,24,6,1,640]{4,1,3,2,0:T(8,128)(2,1)}, u32[]{:S(2)}, u32[]{:S(2)}) collective-permute-start(bf16[2,24,6,1,640]{4,1,3,2,0:T(8,128)(2,1)} %get-tuple-element.7), channel_id=1, source_target_pairs={{0,1},{1,2},{2,3},{4,5},{5,6},{6,7},{8,9},{9,10},{10,11},{12,13},{... | collective-permute-start | bytes 1105928 | tf_op jit(solution)/shard_map/ppermute | solution.py:14
  37.1 14.1 %collective-permute-start.3 = (bf16[2,24,6,1,640]{4,1,3,2,0:T(8,128)(2,1)}, bf16[2,24,6,1,640]{4,1,3,2,0:T(8,128)(2,1)}, u32[]{:S(2)}, u32[]{:S(2)}) collective-permute-start(bf16[2,24,6,1,640]{4,1,3,2,0:T(8,128)(2,1)} %get-tuple-element.8), channel_id=1, source_target_pairs={{1,0},{2,1},{3,2},{5,4},{6,5},{7,6},{9,8},{10,9},{11,10},{13,12},{... | collective-permute-start | bytes 1105928 | tf_op jit(solution)/shard_map/ppermute | solution.py:17
  65.1 10.1 %copy-start.3 = (f32[48,640]{1,0:T(8,128)S(1)}, f32[48,640]{1,0:T(8,128)}, u32[]{:S(2)}) copy-start(f32[48,640]{1,0:T(8,128)} %copy.52) | copy-start | bytes 368644
  65.1 10.1 %copy-start.4 = (f32[48,640]{1,0:T(8,128)S(1)}, f32[48,640]{1,0:T(8,128)}, u32[]{:S(2)}) copy-start(f32[48,640]{1,0:T(8,128)} %copy.54) | copy-start | bytes 368644
  65.1 10.1 %copy-start.12 = (f32[640]{0:T(1024)S(1)}, f32[640]{0:T(1024)}, u32[]{:S(2)}) copy-start(f32[640]{0:T(1024)} %param.24) | copy-start | bytes 7684
  65.1 10.1 %copy-start.13 = (f32[640]{0:T(1024)S(1)}, f32[640]{0:T(1024)}, u32[]{:S(2)}) copy-start(f32[640]{0:T(1024)} %param.23) | copy-start | bytes 7684
  78.6 5.1 %slice-start = ((s8[4423680]{0:T(1024)(128)(4,1)}), s8[4194304]{0:T(1024)(128)(4,1)S(1)}, s32[]{:S(2)}) async-start(s8[4423680]{0:T(1024)(128)(4,1)} %bitcast.55), calls=%async_computation.2 | async-start | bytes 8388608
  79.2 4.6 %slice-start.1 = ((s8[4423680]{0:T(1024)(128)(4,1)}), s8[229376]{0:T(1024)(128)(4,1)S(1)}, s32[]{:S(2)}) async-start(s8[4423680]{0:T(1024)(128)(4,1)} %bitcast.55), calls=%async_computation.3 | async-start | bytes 458752
  79.7 6.6 %slice-start.4 = ((f32[48,768]{1,0:T(8,128)}), f32[48,640]{1,0:T(8,128)S(1)}, s32[]{:S(2)}) async-start(f32[48,768]{1,0:T(8,128)} %copy-done.1), calls=%async_computation.6 | async-start | bytes 245760 | tf_op jit(solution)/shard_map/slice | solution.py:119
  79.7 6.6 %copy-start.17 = (f32[640]{0:T(1024)S(1)}, f32[640]{0:T(1024)}, u32[]{:S(2)}) copy-start(f32[640]{0:T(1024)} %param.26) | copy-start | bytes 7684
  79.9 3.9 %copy-start.5 = (bf16[48,4,4,5760]{3,0,2,1:T(8,128)(2,1)}, bf16[48,4,4,5760]{3,0,2,1:T(8,128)(2,1)S(1)}, u32[]{:S(2)}) copy-start(bf16[48,4,4,5760]{3,0,2,1:T(8,128)(2,1)S(1)} %slice_dynamic-update-slice_fusion.9) | copy-start | bytes 26542084
  83.8 14.7 %slice-start.2 = ((s8[4423680]{0:T(1024)(128)(4,1)}), s8[229376]{0:T(1024)(128)(4,1)S(1)}, s32[]{:S(2)}) async-start(s8[4423680]{0:T(1024)(128)(4,1)} %bitcast.57), calls=%async_computation.4 | async-start | bytes 458752
  86.3 12.2 %slice-start.3 = ((s8[4423680]{0:T(1024)(128)(4,1)}), s8[4194304]{0:T(1024)(128)(4,1)S(1)}, s32[]{:S(2)}) async-start(s8[4423680]{0:T(1024)(128)(4,1)} %bitcast.57), calls=%async_computation.5 | async-start | bytes 8388608
  86.3 12.2 %copy-start.2 = (f32[48,640]{1,0:T(8,128)S(1)}, f32[48,640]{1,0:T(8,128)}, u32[]{:S(2)}) copy-start(f32[48,640]{1,0:T(8,128)} %copy.56) | copy-start | bytes 368644
  86.3 12.2 %copy-start.14 = (f32[640]{0:T(1024)S(1)}, f32[640]{0:T(1024)}, u32[]{:S(2)}) copy-start(f32[640]{0:T(1024)} %param.31) | copy-start | bytes 7684
  86.3 12.2 %copy-start.15 = (f32[640]{0:T(1024)S(1)}, f32[640]{0:T(1024)}, u32[]{:S(2)}) copy-start(f32[640]{0:T(1024)} %param.30) | copy-start | bytes 7684
  86.3 12.2 %copy-start.16 = (pred[6,6]{1,0:T(8,128)(4,1)S(1)}, pred[6,6]{1,0:T(8,128)(4,1)}, u32[]{:S(2)}) copy-start(pred[6,6]{1,0:T(8,128)(4,1)} %broadcast_or_fusion) | copy-start | bytes 112
  106.4 15.2 %copy-start.18 = (f32[640]{0:T(1024)S(1)}, f32[640]{0:T(1024)}, u32[]{:S(2)}) copy-start(f32[640]{0:T(1024)} %param.33) | copy-start | bytes 7684
  133.6 1.2 copy-start
Sparse Core Ops, SparseCore 0:
  8.9 58.1 all-gather.2
  68.7 52.8 all-gather.4
where the time goes:
time: 144 us; the launch traced here: 143 us
  local copies, waits for them, and re-layouts  49.9 us (35%)
  matrix products  24.4 us (17%)
  waiting for transfers between devices  23.7 us (16%)
  other arithmetic  18.9 us (13%)
  between operations  13.9 us (10%)
  starting transfers between devices  11.8 us (8%)
    dot_general x2, matrix products, conv_apply(): return jnp.dot(unfolded, whole_kernel, preferred_element_type=jnp.float32)  24.2 us
    unnamed x62, local copies, waits for them, and re-layouts  14.2 us
    all_gather x1, waiting for transfers between devices, body(): lax.all_gather(conv2_weight, 'row', axis=2, tiled=True)  10.7 us
    reshape x1, local copies, waits for them, and re-layouts, body(): flattened = patches.reshape((-1,) + patches.shape[3:])  10.1 us
    ppermute x2, waiting for transfers between devices, padded_2(): lax.ppermute(lax.slice_in_dim(block, 0, width, axis=dim), axis, backward)  9.75 us
    transpose x1, local copies, waits for them, and re-layouts, body(): patches = jnp.transpose(jnp.stack(columns), (3, 0, 1, 2, 4, 5, 6))  8.92 us
    ppermute x2, starting transfers between devices, padded_2(): lax.ppermute(lax.slice_in_dim(block, block.shape[dim] - width, None, axis...  8.61 us
    ppermute x2, starting transfers between devices, padded_2(): lax.ppermute(lax.slice_in_dim(block, 0, width, axis=dim), axis, backward)  3.2 us
  transfers between devices with their start and end apart: 6, of which 3 were waited for; matrix products, arithmetic and copies ran while one was open for 52% of the time, Pallas kernels for 0%

commit v1 on v0

v1 whole, which is shorter than its diff:
```python
import jax
import jax.numpy as jnp
from jax import lax
from jax.sharding import PartitionSpec as P

TILE = 4


def padded_2(block, sides, width):
    for axis, dim in sides:
        count = lax.axis_size(axis)
        forward = [(i, i + 1) for i in range(count - 1)]
        backward = [(target, source) for source, target in forward]
        low = lax.ppermute(
            lax.slice_in_dim(block, block.shape[dim] - width, None, axis=dim), axis, forward
        )
        high = lax.ppermute(lax.slice_in_dim(block, 0, width, axis=dim), axis, backward)
        block = jnp.concatenate([low, block, high], axis=dim)
    return block


def gather_shards(shard, axis):
    count = lax.axis_size(axis)
    chips = count // 2
    me = lax.axis_index(axis)
    chip = me // 2
    core = me % 2
    mate_pairs = [(i, i ^ 1) for i in range(count)]
    pieces = [(shard, me), (lax.ppermute(shard, axis, mate_pairs), me + 1 - 2 * core)]
    for step in range(1, chips):
        pairs = [(((i // 2 + step) % chips) * 2 + i % 2, i) for i in range(count)]
        fetched = lax.ppermute(shard, axis, pairs)
        far_chip = (chip + step) % chips
        pieces.append((fetched, far_chip * 2 + core))
        pieces.append((lax.ppermute(fetched, axis, mate_pairs), far_chip * 2 + 1 - core))
    depth = shard.shape[2]
    whole = jnp.zeros(shard.shape[:2] + (depth * count,) + shard.shape[3:], shard.dtype)
    zero = jnp.zeros((), jnp.int32)
    for piece, source in pieces:
        whole = lax.dynamic_update_slice(
            whole, piece, (zero, zero, (source * depth).astype(jnp.int32), zero)
        )
    return whole


def conv_valid(activation, kernel):
    return lax.conv_general_dilated(
        activation,
        kernel,
        window_strides=(1, 1),
        padding="VALID",
        dimension_numbers=("NHWC", "HWIO", "NHWC"),
        preferred_element_type=jnp.float32,
    )


def body(
    latent_in,
    cached_mid,
    cached_out,
    edit_tiles,
    norm1_mean,
    norm1_rstd,
    norm1_gain,
    norm1_shift,
    conv1_weight,
    conv1_bias,
    step_embed,
    norm2_mean,
    norm2_rstd,
    norm2_gain,
    norm2_shift,
    conv2_weight,
    conv2_bias,
):
    requests, rows_dev, cols_dev, channels = latent_in.shape
    tiles_down = rows_dev // TILE
    tiles_across = cols_dev // TILE
    rows_total = rows_dev * lax.axis_size("row")
    cols_total = cols_dev * lax.axis_size("col")
    tile_cols_total = tiles_across * lax.axis_size("col")
    groups_total = norm1_mean.shape[1]
    per_group = channels // groups_total

    first_whole = gather_shards(conv1_weight, "row")
    second_whole = gather_shards(conv2_weight, "row")

    def expand(values):
        return jnp.repeat(values, per_group, axis=1)[:, None, None, :]

    stacked = jnp.stack([latent_in, cached_mid])
    padded = padded_2(stacked, (("row", 2), ("col", 3)), 1)
    inputs_pad = padded[0].astype(jnp.float32)
    margins_pad = padded[1].astype(jnp.float32)

    row_start = lax.axis_index("row") * rows_dev - 1
    col_start = lax.axis_index("col") * cols_dev - 1
    cell_rows = row_start + jnp.arange(rows_dev + 2, dtype=jnp.int32)
    cell_cols = col_start + jnp.arange(cols_dev + 2, dtype=jnp.int32)
    inside = ((cell_rows >= 0) & (cell_rows < rows_total))[:, None] & (
        (cell_cols >= 0) & (cell_cols < cols_total)
    )[None, :]
    inside = inside.astype(jnp.float32)[None, :, :, None]

    first_act = (
        jax.nn.silu(
            (inputs_pad - expand(norm1_mean)) * expand(norm1_rstd) * norm1_gain + norm1_shift
        )
        * inside
    ).astype(jnp.bfloat16)
    fresh_mid = (
        conv_valid(first_act, first_whole) + conv1_bias + step_embed[:, None, None, :]
    )

    windows = []
    masks = []
    for tile_down in range(tiles_down):
        for tile_across in range(tiles_across):
            r0 = tile_down * TILE
            c0 = tile_across * TILE
            margin = margins_pad[:, r0 : r0 + TILE + 2, c0 : c0 + TILE + 2]
            own = fresh_mid[:, r0 : r0 + TILE, c0 : c0 + TILE]
            windows.append(lax.dynamic_update_slice(margin, own, (0, 1, 1, 0)))
            masks.append(inside[:, r0 : r0 + TILE + 2, c0 : c0 + TILE + 2])
    middle = jnp.stack(windows, axis=1)
    border = jnp.stack(masks, axis=1)
    middle = middle.reshape((-1,) + middle.shape[2:])
    second_mean = expand(norm2_mean)[:, None]
    second_rstd = expand(norm2_rstd)[:, None]
    second_act = (
        jax.nn.silu(
            (middle.reshape((requests, -1) + middle.shape[1:]) - second_mean) * second_rstd
            * norm2_gain
            + norm2_shift
        )
        * border
    ).astype(jnp.bfloat16)
    second_act = second_act.reshape((-1,) + second_act.shape[2:])
    second_sum = conv_valid(second_act, second_whole)
    second_sum = second_sum.reshape(requests, tiles_down, tiles_across, TILE, TILE, channels)
    second_sum = jnp.transpose(second_sum, (0, 1, 3, 2, 4, 5)).reshape(
        requests, rows_dev, cols_dev, channels
    )
    renewed = (
        second_sum + conv2_bias + inputs_pad[:, 1 : 1 + rows_dev, 1 : 1 + cols_dev]
    ).astype(jnp.bfloat16)

    own_rows = lax.axis_index("row") * tiles_down + jnp.arange(tiles_down, dtype=jnp.int32)
    own_cols = lax.axis_index("col") * tiles_across + jnp.arange(tiles_across, dtype=jnp.int32)
    tile_numbers = own_rows[:, None] * tile_cols_total + own_cols[None, :]
    edited = jnp.any(edit_tiles[:, None, None, :] == tile_numbers[None, :, :, None], axis=-1)
    cell_mask = jnp.repeat(jnp.repeat(edited, TILE, axis=1), TILE, axis=2)
    return jnp.where(cell_mask[..., None], renewed, cached_out)


def solution(mesh):
    placed = (
        P("groups", "row", "col", None),
        P("groups", "row", "col", None),
        P("groups", "row", "col", None),
        P("groups", None),
        P("groups", None),
        P("groups", None),
        P(),
        P(),
        P(None, None, "row", None),
        P(),
        P("groups", None),
        P("groups", None),
        P("groups", None),
        P(),
        P(),
        P(None, None, "row", None),
        P(),
    )
    return jax.shard_map(
        body, mesh=mesh, in_specs=placed, out_specs=P("groups", "row", "col", None), check_vma=False
    )
```

time: 144 us -> 147 us (1.021)
  waiting for transfers between devices: 23.7 us -> 52.1 us
  between operations: 13.9 us -> 0.47 us
  other arithmetic: 18.9 us -> 8.9 us
  local copies, waits for them, and re-layouts: 49.9 us -> 44.4 us
  starting transfers between devices: 11.8 us -> 14.6 us
  matrix products: 24.4 us -> 25.9 us
    ppermute x2, waiting for transfers between devices: 2.52 us -> 42.7 us  [padded_2(): lax.ppermute(lax.slice_in_dim(block, block.shape[dim] - width, None, axis...]
    conv_general_dilated x0 -> x2, matrix products: none -> 25.9 us  [conv_valid(): lax.conv_general_dilated(activation, kernel, window_strides=(1, 1), paddi...]
    dot_general x3 -> x0, matrix products: 24.4 us -> none  [the longest x2 24.2 us: conv_apply(): return jnp.dot(unfolded, whole_kernel, preferred_element_type=jnp.float32)]
    another operation x0 -> x6, local copies, waits for them, and re-layouts: none -> 16.7 us  [the longest x3 12.2 us: body(): middle = jnp.stack(windows, axis=1)]
    dynamic_update_slice x0 -> x9, local copies, waits for them, and re-layouts: none -> 16 us  [the longest x8 15.9 us: gather_shards(): lax.dynamic_update_slice(whole, piece, (zero, zero, (source * depth).asty...]
    unnamed x62 -> x36, local copies, waits for them, and re-layouts: 14.2 us -> 1.89 us
    all_gather x2 -> x0, waiting for transfers between devices: 10.7 us -> none  [the longest x1 10.7 us: body(): lax.all_gather(conv2_weight, 'row', axis=2, tiled=True)]
    transpose x2 -> x1, local copies, waits for them, and re-layouts: 9.31 us -> 0.17 us  [body(): jnp.transpose(second_sum, (0, 1, 3, 2, 4, 5))]
  transfers between devices with their start and end apart: 6 -> 10, of which waited for: 3 -> 3; matrix products, arithmetic and copies ran while one was open for 52% -> 40% of each run, Pallas kernels for 0% -> 0%
where the time goes in v1:
time: 147 us; the launch traced here: 146 us
  waiting for transfers between devices  52.1 us (35%)
  local copies, waits for them, and re-layouts  44.4 us (30%)
  matrix products  25.9 us (18%)
  starting transfers between devices  14.6 us (10%)
  other arithmetic  8.9 us (6%)
    ppermute x2, waiting for transfers between devices, padded_2(): lax.ppermute(lax.slice_in_dim(block, block.shape[dim] - width, None, axis...  42.7 us
    conv_general_dilated x2, matrix products, conv_valid(): lax.conv_general_dilated(activation, kernel, window_strides=(1, 1), paddi...  25.9 us
    dynamic_update_slice x8, local copies, waits for them, and re-layouts, gather_shards(): lax.dynamic_update_slice(whole, piece, (zero, zero, (source * depth).asty...  15.9 us
    another operation x3, local copies, waits for them, and re-layouts, body(): middle = jnp.stack(windows, axis=1)  12.2 us
    ppermute x2, waiting for transfers between devices, gather_shards(): fetched = lax.ppermute(shard, axis, pairs)  8.47 us
    ppermute x2, starting transfers between devices, padded_2(): lax.ppermute(lax.slice_in_dim(block, block.shape[dim] - width, None, axis...  6.43 us
    another operation x2, local copies, waits for them, and re-layouts  4.41 us
    ppermute x2, starting transfers between devices, padded_2(): lax.ppermute(lax.slice_in_dim(block, 0, width, axis=dim), axis, backward)  3.71 us
  transfers between devices with their start and end apart: 10, of which 3 were waited for; matrix products, arithmetic and copies ran while one was open for 40% of the time, Pallas kernels for 0%

profile of v1, /device:TPU:1, one launch (start us, length us, event | category | flops | bytes accessed | tf_op | source)
XLA Modules:
  0.0 146.4 jit_solution(7808620288326431966)
XLA Ops:
  0.1 2.7 %collective-permute-start.5 = (bf16[3,3,160,640]{3,2,1,0:T(8,128)(2,1)}, bf16[3,3,160,640]{3,2,1,0:T(8,128)(2,1)}, u32[]{:S(2)}, u32[]{:S(2)}) collective-permute-start(bf16[3,3,160,640]{3,2,1,0:T(8,128)(2,1)} %param.25), channel_id=1, source_target_pairs={{8,0},{12,4},{0,8},{4,12},{9,1},{13,5},{1,9},{5,13},{10,2},{14,6},... | collective-permute-start | bytes 5529608 | tf_op jit(solution)/shard_map/ppermute | solution.py:32
  2.7 2.1 %copy_bitcast_fusion = (bf16[1,24,4,8,640]{4,1,3,2,0:T(8,128)(2,1)S(1)}, bf16[1,24,4,8,640]{4,1,3,2,0:T(8,128)(2,1)S(1)}) fusion(bf16[24,4,8,640]{3,2,1,0:T(8,128)(2,1)} %param.18, bf16[24,4,8,640]{3,2,1,0:T(8,128)(2,1)} %param.17), kind=kLoop, calls=%fused_computation.26 | loop fusion | bytes 3932160 | tf_op jit(solution)/shard_map/stack | solution.py:91
  4.9 0.9 pad_maximum_fusion.3
  5.8 1.9 %collective-permute-start = (bf16[2,24,1,8,640]{4,1,3,2,0:T(8,128)(2,1)}, bf16[2,24,1,8,640]{4,1,3,2,0:T(8,128)(2,1)S(1)}, u32[]{:S(2)}, u32[]{:S(2)}) collective-permute-start(bf16[2,24,1,8,640]{4,1,3,2,0:T(8,128)(2,1)} %get-tuple-element.13), channel_id=1, source_target_pairs={{0,4},{4,8},{8,12},{1,5},{5,9},{9,13},{2,6},{6,10},{10,14},{3,7},{... | collective-permute-start | bytes 1474568 | tf_op jit(solution)/shard_map/ppermute | solution.py:14
  7.7 2.4 %collective-permute-start.1 = (bf16[2,24,1,8,640]{4,1,3,2,0:T(8,128)(2,1)S(1)}, bf16[2,24,1,8,640]{4,1,3,2,0:T(8,128)(2,1)S(1)}, u32[]{:S(2)}, u32[]{:S(2)}) collective-permute-start(bf16[2,24,1,8,640]{4,1,3,2,0:T(8,128)(2,1)S(1)} %get-tuple-element.14), channel_id=1, source_target_pairs={{4,0},{8,4},{12,8},{5,1},{9,5},{13,9},{6,2},{10,6},{14,10},{7,3},{... | collective-permute-start | bytes 1474568 | tf_op jit(solution)/shard_map/ppermute | solution.py:17
  10.5 42.7 %collective-permute-done = bf16[2,24,1,8,640]{4,1,3,2,0:T(8,128)(2,1)S(1)} collective-permute-done((bf16[2,24,1,8,640]{4,1,3,2,0:T(8,128)(2,1)}, bf16[2,24,1,8,640]{4,1,3,2,0:T(8,128)(2,1)S(1)}, u32[]{:S(2)}, u32[]{:S(2)}) %collective-permute-start) | collective-permute-done | bytes 491552 | tf_op jit(solution)/shard_map/ppermute | solution.py:14
  53.2 0.9 collective-permute-done.1
  54.1 0.9 pad_maximum_fusion.7
  55.0 4.5 %collective-permute-start.2 = (bf16[2,24,6,1,640]{4,1,3,2,0:T(8,128)(2,1)S(1)}, bf16[2,24,6,1,640]{4,1,3,2,0:T(8,128)(2,1)}, u32[]{:S(2)}, u32[]{:S(2)}) collective-permute-start(bf16[2,24,6,1,640]{4,1,3,2,0:T(8,128)(2,1)S(1)} %get-tuple-element.9), channel_id=1, source_target_pairs={{0,1},{1,2},{2,3},{4,5},{5,6},{6,7},{8,9},{9,10},{10,11},{12,13},{... | collective-permute-start | bytes 1105928 | tf_op jit(solution)/shard_map/ppermute | solution.py:14
  59.5 3.7 %broadcast.157.clone.1 = bf16[3,3,640,640]{3,2,1,0:T(8,128)(2,1)} broadcast(bf16[]{:T(256)} %constant.68.clone.1), dimensions={} | broadcast | bytes 7372802 | tf_op jit(solution)/shard_map/broadcast.13
  63.2 1.4 constant_dynamic-update-slice_fusion.7
  64.7 1.3 collective-permute-start.3
  66.0 0.6 compare_reduce_fusion
  66.6 0.2 broadcast_in_dim.21
  66.8 0.8 mul.115
  67.6 0.2 broadcast_in_dim.20
  67.8 0.8 sub.44
  68.7 0.1 copy.43
  68.8 0.2 broadcast_in_dim.45
  69.0 0.2 mul.131
  69.3 0.1 mul.133
  69.3 0.9 broadcast_in_dim.44
  70.2 0.2 sub.52
  70.6 0.7 broadcast.157.clone
  71.3 1.8 %constant_dynamic-update-slice_fusion.3 = bf16[3,3,640,640]{3,2,1,0:T(8,128)(2,1)S(1)} fusion(bf16[3,3,640,640]{3,2,1,0:T(8,128)(2,1)S(1)} %broadcast.157.clone, bf16[3,3,160,640]{3,2,1,0:T(8,128)(2,1)} %param.32, s32[]{:T(128)S(6)} %select_n.40), kind=kLoop, calls=%fused_computation.43 | loop fusion | bytes 3686404 | tf_op jit(solution)/shard_map/dynamic_update_slice | solution.py:40
  73.1 0.6 collective-permute-start.6
  73.7 3.0 %pad_maximum_fusion.1 = bf16[2,24,6,10,640]{4,1,3,2,0:T(8,128)(2,1)S(1)} fusion(bf16[2,24,6,1,640]{4,1,3,2,0:T(8,128)(2,1)} %collective-permute-done.3, bf16[2,24,1,8,640]{4,1,3,2,0:T(8,128)(2,1)S(1)} %collective-permute-done.1, bf16[1,24,4,8,640]{4,1,3,2,0:T(8,128)(2,1)S(1)} %get-tuple-element.17, bf16[1,24,4,8,640]{4,1,3,2,0:T(8,128)(2,1)S(1)} %get-tuple-element.18, ...), kind=kLoop, calls=%fused_computation.2 | loop fusion | flops 9216000 | bytes 7372800 | tf_op jit(solution)/shard_map/concatenate | solution.py:18
  76.7 2.4 %fusion.4 = (f32[24,6,10,640]{3,0,2,1:T(8,128)S(1)}, f32[24,6,10,640]{3,0,2,1:T(8,128)}) fusion(bf16[2,24,6,10,640]{4,1,3,2,0:T(8,128)(2,1)S(1)} %pad_maximum_fusion.1), kind=kLoop, calls=%fused_computation.14 | loop fusion | flops 1843200 | bytes 11059200 | tf_op jit(solution)/shard_map/convert_element_type | solution.py:94
  79.1 0.3 slice_bitcast_fusion.1
  79.3 8.5 %collective-permute-done.8 = bf16[3,3,160,640]{3,2,1,0:T(8,128)(2,1)} collective-permute-done((bf16[3,3,160,640]{3,2,1,0:T(8,128)(2,1)}, bf16[3,3,160,640]{3,2,1,0:T(8,128)(2,1)}, u32[]{:S(2)}, u32[]{:S(2)}) %collective-permute-start.8) | collective-permute-done | bytes 1843232 | tf_op jit(solution)/shard_map/ppermute | solution.py:32
  87.8 1.1 collective-permute-start.9
  88.9 2.9 %constant_dynamic-update-slice_fusion.6 = bf16[3,3,640,640]{3,2,1,0:T(8,128)(2,1)} fusion(bf16[3,3,640,640]{3,2,1,0:T(8,128)(2,1)} %constant_dynamic-update-slice_fusion.7, bf16[3,3,160,640]{3,2,1,0:T(8,128)(2,1)} %collective-permute-done.4, s32[]{:T(128)S(6)} %select_n.42), kind=kLoop, calls=%fused_computation.46 | loop fusion | bytes 3686404 | tf_op jit(solution)/shard_map/dynamic_update_slice | solution.py:40
  91.9 2.9 %constant_dynamic-update-slice_fusion.5 = bf16[3,3,640,640]{3,2,1,0:T(8,128)(2,1)} fusion(bf16[3,3,640,640]{3,2,1,0:T(8,128)(2,1)} %constant_dynamic-update-slice_fusion.6, bf16[3,3,160,640]{3,2,1,0:T(8,128)(2,1)} %collective-permute-done.5, s32[]{:T(128)S(6)} %select_n.45), kind=kLoop, calls=%fused_computation.45 | loop fusion | bytes 3686404 | tf_op jit(solution)/shard_map/dynamic_update_slice | solution.py:40
  94.8 1.8 %constant_dynamic-update-slice_fusion.2 = bf16[3,3,640,640]{3,2,1,0:T(8,128)(2,1)S(1)} fusion(bf16[3,3,640,640]{3,2,1,0:T(8,128)(2,1)S(1)} %constant_dynamic-update-slice_fusion.3, bf16[3,3,160,640]{3,2,1,0:T(8,128)(2,1)} %collective-permute-done.7, s32[]{:T(128)S(6)} %select_n.42), kind=kLoop, calls=%fused_computation.42 | loop fusion | bytes 3686404 | tf_op jit(solution)/shard_map/dynamic_update_slice | solution.py:40
  96.7 1.9 %constant_dynamic-update-slice_fusion.1 = bf16[3,3,640,640]{3,2,1,0:T(8,128)(2,1)S(1)} fusion(bf16[3,3,640,640]{3,2,1,0:T(8,128)(2,1)S(1)} %constant_dynamic-update-slice_fusion.2, bf16[3,3,160,640]{3,2,1,0:T(8,128)(2,1)} %collective-permute-done.8, s32[]{:T(128)S(6)} %select_n.45), kind=kLoop, calls=%fused_computation.41 | loop fusion | bytes 3686404 | tf_op jit(solution)/shard_map/dynamic_update_slice | solution.py:40
  98.6 1.6 %constant_dynamic-update-slice_fusion.4 = bf16[3,3,640,640]{3,2,1,0:T(8,128)(2,1)} fusion(bf16[3,3,640,640]{3,2,1,0:T(8,128)(2,1)} %constant_dynamic-update-slice_fusion.5, bf16[3,3,160,640]{3,2,1,0:T(8,128)(2,1)S(1)} %collective-permute-done.6, s32[]{:T(128)S(6)} %select_n.46), kind=kLoop, calls=%fused_computation.44 | loop fusion | bytes 3686404 | tf_op jit(solution)/shard_map/dynamic_update_slice | solution.py:40
  100.3 12.6 %add_add_fusion = f32[24,4,8,640]{3,0,2,1:T(8,128)S(1)} fusion(bf16[3,3,640,640]{3,2,1,0:T(8,128)(2,1)} %constant_dynamic-update-slice_fusion.4, f32[6,10]{1,0:T(8,128)S(1)} %and_convert_fusion.1, f32[640]{0:T(1024)S(1)} %copy-done.13, f32[640]{0:T(1024)S(1)} %copy-done.14, f32[24,640]{1,0:T(8,128)S(1)} %copy-done.4, f32[24,640]{1,0:T(8,128)S(1)} %copy-done.5, ...), kind=kOutput, calls=%fused_computation.9 | convolution fusion | flops 5673431040 | bytes 11382784 | tf_op jit(solution)/shard_map/conv_general_dilated | solution.py:47
  112.9 0.1 fusion.13
  113.0 0.3 pad_maximum_fusion
  113.3 5.8 %copy.42 = f32[24,2,6,6,640]{4,1,0,3,2:T(2,128)} copy(f32[24,2,6,6,640]{4,0,3,2,1:T(8,128)S(1)} %pad_maximum_fusion) | data formatting | bytes 8847360 | tf_op jit(solution)/shard_map/stack | solution.py:125
  119.1 6.2 %stack.41 = f32[48,6,6,640]{3,0,2,1:T(8,128)} reshape(f32[24,2,6,6,640]{4,1,0,3,2:T(2,128)} %copy.42) | data formatting | bytes 8847360 | tf_op jit(solution)/shard_map/stack | solution.py:125
  125.3 1.4 constant_dynamic-update-slice_fusion
  126.7 13.3 %fusion = f32[48,4,4,640]{3,0,2,1:T(8,128)} fusion(bf16[3,3,640,640]{3,2,1,0:T(8,128)(2,1)} %constant_dynamic-update-slice_fusion, f32[48,6,6,640]{3,0,2,1:T(8,128)} %stack.41, f32[48,6,6]{0,2,1:T(8,128)S(1)} %copy.43, f32[640]{0:T(1024)S(1)} %copy-done.16, f32[640]{0:T(1024)S(1)} %copy-done.17, f32[48,640]{1,0:T(8,128)S(1)} %mul.133, f32[48,640]{1,0:T(8,128)S(1)} %sub.54), kind=kOutput, calls=%fused_computation.6 | convolution fusion | flops 5673369600 | bytes 14020352 | tf_op jit(solution)/shard_map/conv_general_dilated | solution.py:47
  140.0 2.6 %reshape.128 = f32[24,1,2,4,4,640]{5,2,0,4,3,1:T(2,128)S(1)} reshape(f32[48,4,4,640]{3,0,2,1:T(8,128)} %fusion) | data formatting | bytes 3932160 | tf_op jit(solution)/shard_map/reshape | solution.py:140
  142.6 0.2 copy.44
  142.8 1.8 %copy-done = f32[24,6,10,640]{3,0,2,1:T(8,128)S(1)} copy-done((f32[24,6,10,640]{3,0,2,1:T(8,128)S(1)}, f32[24,6,10,640]{3,0,2,1:T(8,128)}, u32[]{:S(2)}) %copy-start) | copy-done | bytes 3686424
  144.6 0.8 fusion.11
  145.4 1.1 copy.46
  (57 shorter events, 0.7 us)
Async XLA Ops:
  0.0 88.9 %collective-permute-start.4 = (bf16[3,3,160,640]{3,2,1,0:T(8,128)(2,1)}, bf16[3,3,160,640]{3,2,1,0:T(8,128)(2,1)}, u32[]{:S(2)}, u32[]{:S(2)}) collective-permute-start(bf16[3,3,160,640]{3,2,1,0:T(8,128)(2,1)} %param.25), channel_id=1, source_target_pairs={{0,4},{4,0},{8,12},{12,8},{1,5},{5,1},{9,13},{13,9},{2,6},{6,2},{1... | collective-permute-start | bytes 5529608 | tf_op jit(solution)/shard_map/ppermute | solution.py:29
  0.1 73.1 %collective-permute-start.5 = (bf16[3,3,160,640]{3,2,1,0:T(8,128)(2,1)}, bf16[3,3,160,640]{3,2,1,0:T(8,128)(2,1)}, u32[]{:S(2)}, u32[]{:S(2)}) collective-permute-start(bf16[3,3,160,640]{3,2,1,0:T(8,128)(2,1)} %param.25), channel_id=1, source_target_pairs={{8,0},{12,4},{0,8},{4,12},{9,1},{13,5},{1,9},{5,13},{10,2},{14,6},... | collective-permute-start | bytes 5529608 | tf_op jit(solution)/shard_map/ppermute | solution.py:32
  5.8 47.4 %collective-permute-start = (bf16[2,24,1,8,640]{4,1,3,2,0:T(8,128)(2,1)}, bf16[2,24,1,8,640]{4,1,3,2,0:T(8,128)(2,1)S(1)}, u32[]{:S(2)}, u32[]{:S(2)}) collective-permute-start(bf16[2,24,1,8,640]{4,1,3,2,0:T(8,128)(2,1)} %get-tuple-element.13), channel_id=1, source_target_pairs={{0,4},{4,8},{8,12},{1,5},{5,9},{9,13},{2,6},{6,10},{10,14},{3,7},{... | collective-permute-start | bytes 1474568 | tf_op jit(solution)/shard_map/ppermute | solution.py:14
  7.7 46.4 %collective-permute-start.1 = (bf16[2,24,1,8,640]{4,1,3,2,0:T(8,128)(2,1)S(1)}, bf16[2,24,1,8,640]{4,1,3,2,0:T(8,128)(2,1)S(1)}, u32[]{:S(2)}, u32[]{:S(2)}) collective-permute-start(bf16[2,24,1,8,640]{4,1,3,2,0:T(8,128)(2,1)S(1)} %get-tuple-element.14), channel_id=1, source_target_pairs={{4,0},{8,4},{12,8},{5,1},{9,5},{13,9},{6,2},{10,6},{14,10},{7,3},{... | collective-permute-start | bytes 1474568 | tf_op jit(solution)/shard_map/ppermute | solution.py:17
  10.1 77.7 %collective-permute-start.8 = (bf16[3,3,160,640]{3,2,1,0:T(8,128)(2,1)}, bf16[3,3,160,640]{3,2,1,0:T(8,128)(2,1)}, u32[]{:S(2)}, u32[]{:S(2)}) collective-permute-start(bf16[3,3,160,640]{3,2,1,0:T(8,128)(2,1)} %param.32), channel_id=1, source_target_pairs={{8,0},{12,4},{0,8},{4,12},{9,1},{13,5},{1,9},{5,13},{10,2},{14,6},... | collective-permute-start | bytes 5529608 | tf_op jit(solution)/shard_map/ppermute | solution.py:32
  55.0 8.2 %copy-start.2 = (bf16[3,3,160,640]{3,2,1,0:T(8,128)(2,1)S(1)}, bf16[3,3,160,640]{3,2,1,0:T(8,128)(2,1)}, u32[]{:S(2)}) copy-start(bf16[3,3,160,640]{3,2,1,0:T(8,128)(2,1)} %param.25) | copy-start | bytes 5529604
  55.0 11.6 %collective-permute-start.2 = (bf16[2,24,6,1,640]{4,1,3,2,0:T(8,128)(2,1)S(1)}, bf16[2,24,6,1,640]{4,1,3,2,0:T(8,128)(2,1)}, u32[]{:S(2)}, u32[]{:S(2)}) collective-permute-start(bf16[2,24,6,1,640]{4,1,3,2,0:T(8,128)(2,1)S(1)} %get-tuple-element.9), channel_id=1, source_target_pairs={{0,1},{1,2},{2,3},{4,5},{5,6},{6,7},{8,9},{9,10},{10,11},{12,13},{... | collective-permute-start | bytes 1105928 | tf_op jit(solution)/shard_map/ppermute | solution.py:14
  63.2 2.7 %copy-start.9 = (s32[24,16]{0,1:T(8,128)S(1)}, s32[24,16]{0,1:T(8,128)}, u32[]{:S(2)}) copy-start(s32[24,16]{0,1:T(8,128)} %param.20) | copy-start | bytes 4612
  63.2 3.4 %copy-start.6 = (f32[24,32]{1,0:T(8,128)S(1)}, f32[24,32]{1,0:T(8,128)}, u32[]{:S(2)}) copy-start(f32[24,32]{1,0:T(8,128)} %param.22) | copy-start | bytes 9220
  63.2 4.4 %copy-start.7 = (f32[24,32]{1,0:T(8,128)S(1)}, f32[24,32]{1,0:T(8,128)}, u32[]{:S(2)}) copy-start(f32[24,32]{1,0:T(8,128)} %param.21) | copy-start | bytes 9220
  63.2 5.6 %copy-start.8 = (f32[24,32]{1,0:T(8,128)S(1)}, f32[24,32]{1,0:T(8,128)}, u32[]{:S(2)}) copy-start(f32[24,32]{1,0:T(8,128)} %param.29) | copy-start | bytes 9220
  64.7 9.1 %collective-permute-start.3 = (bf16[2,24,6,1,640]{4,1,3,2,0:T(8,128)(2,1)}, bf16[2,24,6,1,640]{4,1,3,2,0:T(8,128)(2,1)}, u32[]{:S(2)}, u32[]{:S(2)}) collective-permute-start(bf16[2,24,6,1,640]{4,1,3,2,0:T(8,128)(2,1)} %get-tuple-element.10), channel_id=1, source_target_pairs={{1,0},{2,1},{3,2},{5,4},{6,5},{7,6},{9,8},{10,9},{11,10},{13,12},{... | collective-permute-start | bytes 1105928 | tf_op jit(solution)/shard_map/ppermute | solution.py:17
  66.5 28.3 %collective-permute-start.7 = (bf16[3,3,160,640]{3,2,1,0:T(8,128)(2,1)}, bf16[3,3,160,640]{3,2,1,0:T(8,128)(2,1)}, u32[]{:S(2)}, u32[]{:S(2)}) collective-permute-start(bf16[3,3,160,640]{3,2,1,0:T(8,128)(2,1)} %param.32), channel_id=1, source_target_pairs={{0,4},{4,0},{8,12},{12,8},{1,5},{5,1},{9,13},{13,9},{2,6},{6,2},{1... | collective-permute-start | bytes 5529608 | tf_op jit(solution)/shard_map/ppermute | solution.py:29
  73.1 25.5 %collective-permute-start.6 = (bf16[3,3,160,640]{3,2,1,0:T(8,128)(2,1)}, bf16[3,3,160,640]{3,2,1,0:T(8,128)(2,1)S(1)}, u32[]{:S(2)}, u32[]{:S(2)}) collective-permute-start(bf16[3,3,160,640]{3,2,1,0:T(8,128)(2,1)} %collective-permute-done.5), channel_id=1, source_target_pairs={{0,4},{4,0},{8,12},{12,8},{1,5},{5,1},{9,13},{13,9},{2,6},{6,2},{1... | collective-permute-start | bytes 5529608 | tf_op jit(solution)/shard_map/ppermute | solution.py:35
  87.8 37.5 %collective-permute-start.9 = (bf16[3,3,160,640]{3,2,1,0:T(8,128)(2,1)}, bf16[3,3,160,640]{3,2,1,0:T(8,128)(2,1)S(1)}, u32[]{:S(2)}, u32[]{:S(2)}) collective-permute-start(bf16[3,3,160,640]{3,2,1,0:T(8,128)(2,1)} %collective-permute-done.8), channel_id=1, source_target_pairs={{0,4},{4,0},{8,12},{12,8},{1,5},{5,1},{9,13},{13,9},{2,6},{6,2},{1... | collective-permute-start | bytes 5529608 | tf_op jit(solution)/shard_map/ppermute | solution.py:35
  96.7 3.6 %copy-start.4 = (f32[24,640]{1,0:T(8,128)S(1)}, f32[24,640]{1,0:T(8,128)}, u32[]{:S(2)}) copy-start(f32[24,640]{1,0:T(8,128)} %mul.115) | copy-start | bytes 184324
  96.7 3.6 %copy-start.5 = (f32[24,640]{1,0:T(8,128)S(1)}, f32[24,640]{1,0:T(8,128)}, u32[]{:S(2)}) copy-start(f32[24,640]{1,0:T(8,128)} %sub.44) | copy-start | bytes 184324
  96.7 3.6 %copy-start.12 = (f32[24,640]{1,0:T(8,128)S(1)}, f32[24,640]{1,0:T(8,128)}, u32[]{:S(2)}) copy-start(f32[24,640]{1,0:T(8,128)} %param.27) | copy-start | bytes 184324
  96.7 3.6 %copy-start.13 = (f32[640]{0:T(1024)S(1)}, f32[640]{0:T(1024)}, u32[]{:S(2)}) copy-start(f32[640]{0:T(1024)} %param.24) | copy-start | bytes 7684
  96.7 3.6 %copy-start.14 = (f32[640]{0:T(1024)S(1)}, f32[640]{0:T(1024)}, u32[]{:S(2)}) copy-start(f32[640]{0:T(1024)} %param.23) | copy-start | bytes 7684
  96.7 3.6 %copy-start.15 = (f32[640]{0:T(1024)S(1)}, f32[640]{0:T(1024)}, u32[]{:S(2)}) copy-start(f32[640]{0:T(1024)} %param.26) | copy-start | bytes 7684
  98.6 14.3 %copy-start.1 = (bf16[3,3,640,640]{3,2,1,0:T(8,128)(2,1)}, bf16[3,3,640,640]{3,2,1,0:T(8,128)(2,1)S(1)}, u32[]{:S(2)}) copy-start(bf16[3,3,640,640]{3,2,1,0:T(8,128)(2,1)S(1)} %constant_dynamic-update-slice_fusion.1) | copy-start | bytes 22118404
  125.3 1.4 copy-start.16
  125.3 1.4 copy-start.17
  140.0 2.8 %copy-start.11 = (pred[24,2]{0,1:T(4,128)(4,1)S(1)}, pred[24,2]{0,1:T(4,128)(4,1)}, u32[]{:S(2)}) copy-start(pred[24,2]{0,1:T(4,128)(4,1)} %compare_reduce_fusion) | copy-start | bytes 148
  140.0 2.8 %copy-start.3 = (bf16[24,4,8,640]{3,2,1,0:T(8,128)(2,1)S(1)}, bf16[24,4,8,640]{3,2,1,0:T(8,128)(2,1)}, u32[]{:S(2)}) copy-start(bf16[24,4,8,640]{3,2,1,0:T(8,128)(2,1)} %param.19) | copy-start | bytes 2949124
  140.0 2.8 %copy-start.10 = (f32[640]{0:T(1024)S(1)}, f32[640]{0:T(1024)}, u32[]{:S(2)}) copy-start(f32[640]{0:T(1024)} %param.33) | copy-start | bytes 7684
  142.6 2.0 %copy-start = (f32[24,6,10,640]{3,0,2,1:T(8,128)S(1)}, f32[24,6,10,640]{3,0,2,1:T(8,128)}, u32[]{:S(2)}) copy-start(f32[24,6,10,640]{3,0,2,1:T(8,128)} %get-tuple-element.8) | copy-start | bytes 11059204

commit v2 on v1

--- a/solution.py
+++ b/solution.py
@@ -19,28 +19,48 @@
     return block
 
 
-def gather_shards(shard, axis):
-    count = lax.axis_size(axis)
+def gather_shards(shard):
+    count = lax.axis_size("row")
     chips = count // 2
-    me = lax.axis_index(axis)
+    plane = lax.axis_size("groups") * lax.axis_size("col")
+    spot = lax.axis_index("groups") * lax.axis_size("col") + lax.axis_index("col")
+    mate_pairs = [(i, i ^ 1) for i in range(count)]
+    piece = lax.dynamic_slice_in_dim(shard.reshape(plane, -1), spot, 1, axis=0)
+    local = [shard, lax.ppermute(shard, "row", mate_pairs)]
+    remote = []
+    for step in range(1, chips):
+        pairs = [(((i // 2 + step) % chips) * 2 + i % 2, i) for i in range(count)]
+        fetched = lax.ppermute(piece, "row", pairs)
+        rebuilt = lax.all_gather(fetched, ("groups", "col"), axis=0, tiled=True)
+        rebuilt = rebuilt.reshape(shard.shape)
+        remote += [rebuilt, lax.ppermute(rebuilt, "row", mate_pairs)]
+    return jnp.concatenate(local, axis=2), jnp.concatenate(remote, axis=2)
+
+
+def relative_order(channels):
+    count = lax.axis_size("row")
+    chips = count // 2
+    depth = channels // count
+    me = lax.axis_index("row")
     chip = me // 2
     core = me % 2
-    mate_pairs = [(i, i ^ 1) for i in range(count)]
-    pieces = [(shard, me), (lax.ppermute(shard, axis, mate_pairs), me + 1 - 2 * core)]
-    for step in range(1, chips):
-        pairs = [(((i // 2 + step) % chips) * 2 + i % 2, i) for i in range(count)]
-        fetched = lax.ppermute(shard, axis, pairs)
-        far_chip = (chip + step) % chips
-        pieces.append((fetched, far_chip * 2 + core))
-        pieces.append((lax.ppermute(fetched, axis, mate_pairs), far_chip * 2 + 1 - core))
-    depth = shard.shape[2]
-    whole = jnp.zeros(shard.shape[:2] + (depth * count,) + shard.shape[3:], shard.dtype)
-    zero = jnp.zeros((), jnp.int32)
-    for piece, source in pieces:
-        whole = lax.dynamic_update_slice(
-            whole, piece, (zero, zero, (source * depth).astype(jnp.int32), zero)
-        )
-    return whole
+    position = jnp.arange(channels, dtype=jnp.int32)
+    block = position // depth
+    source = 2 * ((chip + block // 2) % chips) + jnp.where(block % 2 == 0, core, 1 - core)
+    return source * depth + position % depth
+
+
+def conv_relative(activation, kernels, order):
+    local_kernel, remote_kernel = kernels
+    split = local_kernel.shape[2]
+    natural = jnp.arange(activation.shape[-1], dtype=jnp.int32)[:, None]
+    total = None
+    for kernel, picks in ((local_kernel, order[:split]), (remote_kernel, order[split:])):
+        chooser = (natural == picks[None, :]).astype(activation.dtype)
+        part = jnp.dot(activation, chooser, preferred_element_type=jnp.float32)
+        part = conv_valid(part.astype(activation.dtype), kernel)
+        total = part if total is None else total + part
+    return total
 
 
 def conv_valid(activation, kernel):
@@ -82,8 +102,9 @@
     groups_total = norm1_mean.shape[1]
     per_group = channels // groups_total
 
-    first_whole = gather_shards(conv1_weight, "row")
-    second_whole = gather_shards(conv2_weight, "row")
+    first_whole = gather_shards(conv1_weight)
+    second_whole = gather_shards(conv2_weight)
+    order = relative_order(channels)
 
     def expand(values):
         return jnp.repeat(values, per_group, axis=1)[:, None, None, :]
@@ -109,7 +130,7 @@
         * inside
     ).astype(jnp.bfloat16)
     fresh_mid = (
-        conv_valid(first_act, first_whole) + conv1_bias + step_embed[:, None, None, :]
+        conv_relative(first_act, first_whole, order) + conv1_bias + step_embed[:, None, None, :]
     )
 
     windows = []
@@ -136,7 +157,7 @@
         * border
     ).astype(jnp.bfloat16)
     second_act = second_act.reshape((-1,) + second_act.shape[2:])
-    second_sum = conv_valid(second_act, second_whole)
+    second_sum = conv_relative(second_act, second_whole, order)
     second_sum = second_sum.reshape(requests, tiles_down, tiles_across, TILE, TILE, channels)
     second_sum = jnp.transpose(second_sum, (0, 1, 3, 2, 4, 5)).reshape(
         requests, rows_dev, cols_dev, channels

time: 147 us -> 305 us (2.07); the launches traced: 146 us -> 299 us
  other arithmetic: 8.9 us -> 93 us
  waiting for transfers between devices: 52.1 us -> 74.8 us
  matrix products: 25.9 us -> 47.2 us
  between operations: 0.47 us -> 14.1 us
  starting transfers between devices: 14.6 us -> 20.4 us
  local copies, waits for them, and re-layouts: 44.4 us -> 49.6 us
    all_gather x0 -> x2, other arithmetic: none -> 81 us  [gather_shards(): rebuilt = lax.all_gather(fetched, ('groups', 'col'), axis=0, tiled=True)]
    all_gather x0 -> x2, waiting for transfers between devices: none -> 45.1 us  [gather_shards(): rebuilt = lax.all_gather(fetched, ('groups', 'col'), axis=0, tiled=True)]
    ppermute x2, waiting for transfers between devices: 42.7 us -> 7.25 us  [padded_2(): lax.ppermute(lax.slice_in_dim(block, block.shape[dim] - width, None, axis...]
    conv_general_dilated x2 -> x4, matrix products: 25.9 us -> 47.2 us  [conv_valid(): lax.conv_general_dilated(activation, kernel, window_strides=(1, 1), paddi...]
    reshape x0 -> x4, local copies, waits for them, and re-layouts: none -> 18.4 us  [the longest x2 11.2 us: gather_shards(): rebuilt = rebuilt.reshape(shard.shape)]
    dynamic_update_slice x8 -> x0, local copies, waits for them, and re-layouts: 15.9 us -> none  [gather_shards(): lax.dynamic_update_slice(whole, piece, (zero, zero, (source * depth).asty...]
    ppermute x2, waiting for transfers between devices: 0.91 us -> 7.62 us  [padded_2(): lax.ppermute(lax.slice_in_dim(block, 0, width, axis=dim), axis, backward)]
    ppermute x6, waiting for transfers between devices: 8.48 us -> 14.8 us  [the longest x2 14.7 us: gather_shards(): fetched = lax.ppermute(piece, 'row', pairs)]
  transfers between devices with their start and end apart: 10 -> 12, of which waited for: 3 -> 5; matrix products, arithmetic and copies ran while one was open for 40% -> 55% of each run, Pallas kernels for 0% -> 0%
where the time goes in v2:
time: 305 us; the launch traced here: 299 us
  other arithmetic  93 us (30%)
  waiting for transfers between devices  74.8 us (25%)
  local copies, waits for them, and re-layouts  49.6 us (16%)
  matrix products  47.2 us (15%)
  starting transfers between devices  20.4 us (7%)
  between operations  14.1 us (5%)
    all_gather x2, other arithmetic, gather_shards(): rebuilt = lax.all_gather(fetched, ('groups', 'col'), axis=0, tiled=True)  81 us
    conv_general_dilated x4, matrix products, conv_valid(): lax.conv_general_dilated(activation, kernel, window_strides=(1, 1), paddi...  47.2 us
    all_gather x2, waiting for transfers between devices, gather_shards(): rebuilt = lax.all_gather(fetched, ('groups', 'col'), axis=0, tiled=True)  45.1 us
    ppermute x2, waiting for transfers between devices, gather_shards(): fetched = lax.ppermute(piece, 'row', pairs)  14.7 us
    another operation x3, local copies, waits for them, and re-layouts, body(): middle = jnp.stack(windows, axis=1)  13.4 us
    reshape x2, local copies, waits for them, and re-layouts, gather_shards(): rebuilt = rebuilt.reshape(shard.shape)  11.2 us
    ppermute x2, starting transfers between devices, padded_2(): lax.ppermute(lax.slice_in_dim(block, block.shape[dim] - width, None, axis...  8.63 us
    ppermute x2, waiting for transfers between devices, padded_2(): lax.ppermute(lax.slice_in_dim(block, 0, width, axis=dim), axis, backward)  7.62 us
  transfers between devices with their start and end apart: 12, of which 5 were waited for; matrix products, arithmetic and copies ran while one was open for 55% of the time, Pallas kernels for 0%

profile of v2, /device:TPU:1, one launch (start us, length us, event | category | flops | bytes accessed | tf_op | source)
XLA Modules:
  0.0 299.1 jit_solution(12361333874709283882)
XLA Ops:
  6.5 3.6 %reshape.142 = bf16[8,115200]{1,0:T(8,128)(2,1)S(1)} reshape(bf16[3,3,160,640]{3,2,1,0:T(8,128)(2,1)} %param.25) | data formatting | bytes 3686400 | tf_op jit(solution)/shard_map/reshape | solution.py:28
  10.2 1.3 constant_dynamic-slice_fusion.1
  11.4 2.0 collective-permute-start.5
  13.4 3.6 %reshape.144 = bf16[8,115200]{1,0:T(8,128)(2,1)S(1)} reshape(bf16[3,3,160,640]{3,2,1,0:T(8,128)(2,1)} %param.32) | data formatting | bytes 3686400 | tf_op jit(solution)/shard_map/reshape | solution.py:28
  17.0 6.9 %collective-permute-done.5 = bf16[1,115200]{1,0:T(2,128)(2,1)S(1)} collective-permute-done((bf16[1,115200]{1,0:T(2,128)(2,1)}, bf16[1,115200]{1,0:T(2,128)(2,1)S(1)}, u32[]{:S(2)}, u32[]{:S(2)}) %collective-permute-start.5) | collective-permute-done | bytes 230432 | tf_op jit(solution)/shard_map/ppermute | solution.py:33
  23.9 0.8 copy-done.6
  24.8 0.5 constant_dynamic-slice_fusion
  25.3 1.2 collective-permute-start.8
  26.5 1.8 collective-permute-start.4
  28.4 7.9 %collective-permute-done.8 = bf16[1,115200]{1,0:T(2,128)(2,1)S(1)} collective-permute-done((bf16[1,115200]{1,0:T(2,128)(2,1)S(1)}, bf16[1,115200]{1,0:T(2,128)(2,1)S(1)}, u32[]{:S(2)}, u32[]{:S(2)}) %collective-permute-start.8) | collective-permute-done | bytes 230432 | tf_op jit(solution)/shard_map/ppermute | solution.py:33
  36.2 0.8 copy-done.5
  37.0 1.9 copy_bitcast_fusion
  38.9 0.9 pad_maximum_fusion.3
  39.8 5.1 %collective-permute-start = (bf16[2,24,1,8,640]{4,1,3,2,0:T(8,128)(2,1)}, bf16[2,24,1,8,640]{4,1,3,2,0:T(8,128)(2,1)S(1)}, u32[]{:S(2)}, u32[]{:S(2)}) collective-permute-start(bf16[2,24,1,8,640]{4,1,3,2,0:T(8,128)(2,1)} %get-tuple-element.13), channel_id=1, source_target_pairs={{0,4},{4,8},{8,12},{1,5},{5,9},{9,13},{2,6},{6,10},{10,14},{3,7},{... | collective-permute-start | bytes 1474568 | tf_op jit(solution)/shard_map/ppermute | solution.py:14
  44.9 2.1 collective-permute-start.1
  47.2 0.7 and_convert_fusion.1
  47.9 45.1 %all-gather.5.cloned.1.call-done = bf16[8,1,115200]{2,1,0:T(2,128)(2,1)} async-done(((bf16[1,1,115200]{2,1,0:T(2,128)(2,1)}), bf16[8,1,115200]{2,1,0:T(2,128)(2,1)}) %all-gather.5.cloned.1.call-update) | async-done | bytes 1843216 | tf_op jit(solution)/shard_map/all_gather | solution.py:34
  93.0 40.4 %reduce.1 = bf16[8,115200]{1,0:T(8,128)(2,1)} reduce(bf16[8,1,115200]{2,1,0:T(2,128)(2,1)} %all-gather.5.cloned.1.call-done, bf16[]{:T(256)} %constant.99), dimensions={1}, to_apply=%all-gather.reduce_sub_computation | reduce | bytes 3686402 | tf_op jit(solution)/shard_map/all_gather | solution.py:34
  133.4 5.6 %reshape.143 = bf16[3,3,160,640]{3,2,1,0:T(8,128)(2,1)} reshape(bf16[8,115200]{1,0:T(8,128)(2,1)} %reduce.1) | data formatting | bytes 3686400 | tf_op jit(solution)/shard_map/reshape | solution.py:35
  139.0 1.7 collective-permute-start.6
  140.7 1.0 pad_maximum_fusion.7
  141.7 3.6 %collective-permute-start.2 = (bf16[2,24,6,1,640]{4,1,3,2,0:T(8,128)(2,1)}, bf16[2,24,6,1,640]{4,1,3,2,0:T(8,128)(2,1)}, u32[]{:S(2)}, u32[]{:S(2)}) collective-permute-start(bf16[2,24,6,1,640]{4,1,3,2,0:T(8,128)(2,1)} %get-tuple-element.9), channel_id=1, source_target_pairs={{0,1},{1,2},{2,3},{4,5},{5,6},{6,7},{8,9},{9,10},{10,11},{12,13},{... | collective-permute-start | bytes 1105928 | tf_op jit(solution)/shard_map/ppermute | solution.py:14
  145.2 1.7 collective-permute-start.3
  146.9 0.6 add_add_fusion.1
  147.7 0.8 mul.101
  148.7 0.8 sub.50
  150.2 0.9 broadcast_in_dim.60
  151.5 0.8 compare_reduce_fusion
  152.3 7.2 %collective-permute-done.2 = bf16[2,24,6,1,640]{4,1,3,2,0:T(8,128)(2,1)} collective-permute-done((bf16[2,24,6,1,640]{4,1,3,2,0:T(8,128)(2,1)}, bf16[2,24,6,1,640]{4,1,3,2,0:T(8,128)(2,1)}, u32[]{:S(2)}, u32[]{:S(2)}) %collective-permute-start.2) | collective-permute-done | bytes 368672 | tf_op jit(solution)/shard_map/ppermute | solution.py:14
  159.6 7.6 %collective-permute-done.3 = bf16[2,24,6,1,640]{4,1,3,2,0:T(8,128)(2,1)} collective-permute-done((bf16[2,24,6,1,640]{4,1,3,2,0:T(8,128)(2,1)}, bf16[2,24,6,1,640]{4,1,3,2,0:T(8,128)(2,1)}, u32[]{:S(2)}, u32[]{:S(2)}) %collective-permute-start.3) | collective-permute-done | bytes 368672 | tf_op jit(solution)/shard_map/ppermute | solution.py:17
  167.2 2.8 pad_maximum_fusion.1
  170.0 2.6 fusion.18
  172.9 1.7 slice_bitcast_fusion.1
  174.7 40.6 %reduce.2 = bf16[8,115200]{1,0:T(8,128)(2,1)} reduce(bf16[8,1,115200]{2,1,0:T(2,128)(2,1)} %all-gather.7.cloned.1.call-done, bf16[]{:T(256)} %constant.99), dimensions={1}, to_apply=%all-gather.1.reduce_sub_computation | reduce | bytes 3686402 | tf_op jit(solution)/shard_map/all_gather | solution.py:34
  215.3 5.6 %reshape.145 = bf16[3,3,160,640]{3,2,1,0:T(8,128)(2,1)} reshape(bf16[8,115200]{1,0:T(8,128)(2,1)} %reduce.2) | data formatting | bytes 3686400 | tf_op jit(solution)/shard_map/reshape | solution.py:35
  220.8 1.1 collective-permute-start.9
  222.0 11.8 %fusion.4 = f32[24,4,8,640]{3,0,2,1:T(8,128)} fusion(bf16[3,3,160,640]{3,2,1,0:T(8,128)(2,1)} %collective-permute-done.6, bf16[3,3,160,640]{3,2,1,0:T(8,128)(2,1)} %reshape.143, s32[320]{0:T(512)S(1)} %get-tuple-element.16, f32[6,10]{1,0:T(8,128)S(1)} %copy-done.12, f32[640]{0:T(1024)S(1)} %copy-done.15, f32[640]{0:T(1024)S(1)} %copy-done.16, ...), kind=kOutput, calls=%fused_computation.7 | convolution fusion | flops 3439155200 | bytes 7625200 | tf_op jit(solution)/shard_map/conv_general_dilated | solution.py:67
  233.8 10.6 %add_add_fusion = f32[24,4,8,640]{3,0,2,1:T(8,128)} fusion(f32[24,4,8,640]{3,0,2,1:T(8,128)} %fusion.4, bf16[3,3,160,640]{3,2,1,0:T(8,128)(2,1)} %collective-permute-done.4, bf16[3,3,160,640]{3,2,1,0:T(8,128)(2,1)} %param.25, f32[24,640]{1,0:T(8,128)S(1)} %copy-done.14, f32[640]{0:T(1024)S(1)} %copy-done.17, s32[320]{0:T(512)S(1)} %get-tuple-element.15, ...), kind=kOutput, calls=%fused_computation.24 | convolution fusion | flops 3440629760 | bytes 9655280 | tf_op jit(solution)/shard_map/conv_general_dilated | solution.py:67
  244.4 2.6 fusion.26
  247.0 1.9 pad_maximum_fusion
  248.9 5.5 %copy.52 = f32[24,2,6,6,640]{4,1,0,3,2:T(2,128)} copy(f32[24,2,6,6,640]{4,0,3,2,1:T(8,128)S(1)} %pad_maximum_fusion) | data formatting | bytes 8847360 | tf_op jit(solution)/shard_map/stack | solution.py:146
  254.4 6.2 %stack.41 = f32[48,6,6,640]{3,0,2,1:T(8,128)} reshape(f32[24,2,6,6,640]{4,1,0,3,2:T(2,128)} %copy.52) | data formatting | bytes 8847360 | tf_op jit(solution)/shard_map/stack | solution.py:146
  260.7 12.4 %fusion.12 = f32[48,4,4,640]{3,0,2,1:T(8,128)} fusion(bf16[3,3,160,640]{3,2,1,0:T(8,128)(2,1)} %collective-permute-done.9, bf16[3,3,160,640]{3,2,1,0:T(8,128)(2,1)} %reshape.145, s32[320]{0:T(512)S(1)} %get-tuple-element.16, f32[48,6,6,640]{3,0,2,1:T(8,128)} %stack.41, f32[48,6,6]{0,2,1:T(8,128)S(1)} %copy.53, f32[640]{0:T(1024)S(1)} %copy-done.18, ...), kind=kOutput, calls=%fused_computation.15 | convolution fusion | flops 3558133760 | bytes 10335232 | tf_op jit(solution)/shard_map/conv_general_dilated | solution.py:67
  273.1 12.4 %fusion.21 = f32[48,4,4,640]{3,0,2,1:T(8,128)} fusion(f32[48,4,4,640]{3,0,2,1:T(8,128)} %fusion.12, bf16[3,3,160,640]{3,2,1,0:T(8,128)(2,1)} %collective-permute-done.7, bf16[3,3,160,640]{3,2,1,0:T(8,128)(2,1)S(1)} %copy-done.2, s32[320]{0:T(512)S(1)} %get-tuple-element.15, f32[48,6,6,640]{3,0,2,1:T(8,128)} %stack.41, f32[48,6,6]{0,2,1:T(8,128)S(1)} %copy.53, ...), kind=kOutput, calls=%fused_computation.31 | convolution fusion | flops 3558625280 | bytes 12301312 | tf_op jit(solution)/shard_map/conv_general_dilated | solution.py:67
  285.5 2.5 reshape.146
  288.2 1.8 copy-done.1
  290.1 0.8 fusion.24
  290.8 1.1 copy.56
  (69 shorter events, 2.4 us)
Async XLA Ops:
  6.5 86.5 %all-gather.5.cloned.1.call-start = ((), (), s32[]{:S(2)}) async-start(), calls=%async_computation | async-start | bytes 4147200 | tf_op jit(solution)/shard_map/all_gather | solution.py:34
  10.1 26.9 %copy-start.4 = (bf16[24,4,8,640]{3,2,1,0:T(8,128)(2,1)S(1)}, bf16[24,4,8,640]{3,2,1,0:T(8,128)(2,1)}, u32[]{:S(2)}) copy-start(bf16[24,4,8,640]{3,2,1,0:T(8,128)(2,1)} %param.18) | copy-start | bytes 2949124
  11.4 12.5 %collective-permute-start.5 = (bf16[1,115200]{1,0:T(2,128)(2,1)}, bf16[1,115200]{1,0:T(2,128)(2,1)S(1)}, u32[]{:S(2)}, u32[]{:S(2)}) collective-permute-start(bf16[1,115200]{1,0:T(2,128)(2,1)} %constant_dynamic-slice_fusion.1), channel_id=1, source_target_pairs={{8,0},{12,4},{0,8},{4,12},{9,1},{13,5},{1,9},{5,13},{10,2},{14,6},... | collective-permute-start | bytes 691208 | tf_op jit(solution)/shard_map/ppermute | solution.py:33
  23.9 0.8 copy-start.6
  24.8 149.9 %all-gather.7.cloned.1.call-start = ((), (), s32[]{:S(2)}) async-start(), calls=%async_computation.1 | async-start | bytes 4147200 | tf_op jit(solution)/shard_map/all_gather | solution.py:34
  25.3 10.9 %collective-permute-start.8 = (bf16[1,115200]{1,0:T(2,128)(2,1)S(1)}, bf16[1,115200]{1,0:T(2,128)(2,1)S(1)}, u32[]{:S(2)}, u32[]{:S(2)}) collective-permute-start(bf16[1,115200]{1,0:T(2,128)(2,1)S(1)} %constant_dynamic-slice_fusion), channel_id=1, source_target_pairs={{8,0},{12,4},{0,8},{4,12},{9,1},{13,5},{1,9},{5,13},{10,2},{14,6},... | collective-permute-start | bytes 691208 | tf_op jit(solution)/shard_map/ppermute | solution.py:33
  26.5 207.3 %collective-permute-start.4 = (bf16[3,3,160,640]{3,2,1,0:T(8,128)(2,1)}, bf16[3,3,160,640]{3,2,1,0:T(8,128)(2,1)}, u32[]{:S(2)}, u32[]{:S(2)}) collective-permute-start(bf16[3,3,160,640]{3,2,1,0:T(8,128)(2,1)} %param.25), channel_id=1, source_target_pairs={{0,4},{4,0},{8,12},{12,8},{1,5},{5,1},{9,13},{13,9},{2,6},{6,2},{1... | collective-permute-start | bytes 5529608 | tf_op jit(solution)/shard_map/ppermute | solution.py:29
  28.4 244.7 %collective-permute-start.7 = (bf16[3,3,160,640]{3,2,1,0:T(8,128)(2,1)}, bf16[3,3,160,640]{3,2,1,0:T(8,128)(2,1)}, u32[]{:S(2)}, u32[]{:S(2)}) collective-permute-start(bf16[3,3,160,640]{3,2,1,0:T(8,128)(2,1)} %param.32), channel_id=1, source_target_pairs={{0,4},{4,0},{8,12},{12,8},{1,5},{5,1},{9,13},{13,9},{2,6},{6,2},{1... | collective-permute-start | bytes 5529608 | tf_op jit(solution)/shard_map/ppermute | solution.py:29
  36.2 0.8 copy-start.5
  39.8 100.9 %collective-permute-start = (bf16[2,24,1,8,640]{4,1,3,2,0:T(8,128)(2,1)}, bf16[2,24,1,8,640]{4,1,3,2,0:T(8,128)(2,1)S(1)}, u32[]{:S(2)}, u32[]{:S(2)}) collective-permute-start(bf16[2,24,1,8,640]{4,1,3,2,0:T(8,128)(2,1)} %get-tuple-element.13), channel_id=1, source_target_pairs={{0,4},{4,8},{8,12},{1,5},{5,9},{9,13},{2,6},{6,10},{10,14},{3,7},{... | collective-permute-start | bytes 1474568 | tf_op jit(solution)/shard_map/ppermute | solution.py:14
  44.9 95.8 %collective-permute-start.1 = (bf16[2,24,1,8,640]{4,1,3,2,0:T(8,128)(2,1)S(1)}, bf16[2,24,1,8,640]{4,1,3,2,0:T(8,128)(2,1)S(1)}, u32[]{:S(2)}, u32[]{:S(2)}) collective-permute-start(bf16[2,24,1,8,640]{4,1,3,2,0:T(8,128)(2,1)S(1)} %get-tuple-element.14), channel_id=1, source_target_pairs={{4,0},{8,4},{12,8},{5,1},{9,5},{13,9},{6,2},{10,6},{14,10},{7,3},{... | collective-permute-start | bytes 1474568 | tf_op jit(solution)/shard_map/ppermute | solution.py:17
  133.4 14.1 %copy-start.9 = (f32[24,32]{1,0:T(8,128)S(1)}, f32[24,32]{1,0:T(8,128)}, u32[]{:S(2)}) copy-start(f32[24,32]{1,0:T(8,128)} %param.22) | copy-start | bytes 9220
  133.4 15.1 %copy-start.10 = (f32[24,32]{1,0:T(8,128)S(1)}, f32[24,32]{1,0:T(8,128)}, u32[]{:S(2)}) copy-start(f32[24,32]{1,0:T(8,128)} %param.21) | copy-start | bytes 9220
  139.0 10.7 %copy-start.11 = (f32[24,32]{1,0:T(8,128)S(1)}, f32[24,32]{1,0:T(8,128)}, u32[]{:S(2)}) copy-start(f32[24,32]{1,0:T(8,128)} %param.29) | copy-start | bytes 9220
  139.0 83.0 %collective-permute-start.6 = (bf16[3,3,160,640]{3,2,1,0:T(8,128)(2,1)}, bf16[3,3,160,640]{3,2,1,0:T(8,128)(2,1)}, u32[]{:S(2)}, u32[]{:S(2)}) collective-permute-start(bf16[3,3,160,640]{3,2,1,0:T(8,128)(2,1)} %reshape.143), channel_id=1, source_target_pairs={{0,4},{4,0},{8,12},{12,8},{1,5},{5,1},{9,13},{13,9},{2,6},{6,2},{1... | collective-permute-start | bytes 5529608 | tf_op jit(solution)/shard_map/ppermute | solution.py:36
  141.7 17.9 %collective-permute-start.2 = (bf16[2,24,6,1,640]{4,1,3,2,0:T(8,128)(2,1)}, bf16[2,24,6,1,640]{4,1,3,2,0:T(8,128)(2,1)}, u32[]{:S(2)}, u32[]{:S(2)}) collective-permute-start(bf16[2,24,6,1,640]{4,1,3,2,0:T(8,128)(2,1)} %get-tuple-element.9), channel_id=1, source_target_pairs={{0,1},{1,2},{2,3},{4,5},{5,6},{6,7},{8,9},{9,10},{10,11},{12,13},{... | collective-permute-start | bytes 1105928 | tf_op jit(solution)/shard_map/ppermute | solution.py:14
  145.2 22.0 %collective-permute-start.3 = (bf16[2,24,6,1,640]{4,1,3,2,0:T(8,128)(2,1)}, bf16[2,24,6,1,640]{4,1,3,2,0:T(8,128)(2,1)}, u32[]{:S(2)}, u32[]{:S(2)}) collective-permute-start(bf16[2,24,6,1,640]{4,1,3,2,0:T(8,128)(2,1)} %get-tuple-element.10), channel_id=1, source_target_pairs={{1,0},{2,1},{3,2},{5,4},{6,5},{7,6},{9,8},{10,9},{11,10},{13,12},{... | collective-permute-start | bytes 1105928 | tf_op jit(solution)/shard_map/ppermute | solution.py:17
  170.0 3.0 copy-start
  174.6 47.4 %copy-start.7 = (f32[24,640]{1,0:T(8,128)S(1)}, f32[24,640]{1,0:T(8,128)}, u32[]{:S(2)}) copy-start(f32[24,640]{1,0:T(8,128)} %mul.101) | copy-start | bytes 184324
  174.6 47.4 %copy-start.8 = (f32[24,640]{1,0:T(8,128)S(1)}, f32[24,640]{1,0:T(8,128)}, u32[]{:S(2)}) copy-start(f32[24,640]{1,0:T(8,128)} %sub.50) | copy-start | bytes 184324
  174.6 47.4 %copy-start.12 = (f32[6,10]{1,0:T(8,128)S(1)}, f32[6,10]{1,0:T(8,128)}, u32[]{:S(2)}) copy-start(f32[6,10]{1,0:T(8,128)} %and_convert_fusion.1) | copy-start | bytes 724
  174.6 47.4 %copy-start.15 = (f32[640]{0:T(1024)S(1)}, f32[640]{0:T(1024)}, u32[]{:S(2)}) copy-start(f32[640]{0:T(1024)} %param.24) | copy-start | bytes 7684
  174.6 47.4 %copy-start.16 = (f32[640]{0:T(1024)S(1)}, f32[640]{0:T(1024)}, u32[]{:S(2)}) copy-start(f32[640]{0:T(1024)} %param.23) | copy-start | bytes 7684
  220.8 39.8 %collective-permute-start.9 = (bf16[3,3,160,640]{3,2,1,0:T(8,128)(2,1)}, bf16[3,3,160,640]{3,2,1,0:T(8,128)(2,1)}, u32[]{:S(2)}, u32[]{:S(2)}) collective-permute-start(bf16[3,3,160,640]{3,2,1,0:T(8,128)(2,1)} %reshape.145), channel_id=1, source_target_pairs={{0,4},{4,0},{8,12},{12,8},{1,5},{5,1},{9,13},{13,9},{2,6},{6,2},{1... | collective-permute-start | bytes 5529608 | tf_op jit(solution)/shard_map/ppermute | solution.py:36
  222.0 11.8 %copy-start.14 = (f32[24,640]{1,0:T(8,128)S(1)}, f32[24,640]{1,0:T(8,128)}, u32[]{:S(2)}) copy-start(f32[24,640]{1,0:T(8,128)} %param.27) | copy-start | bytes 184324
  222.0 11.8 %copy-start.17 = (f32[640]{0:T(1024)S(1)}, f32[640]{0:T(1024)}, u32[]{:S(2)}) copy-start(f32[640]{0:T(1024)} %param.26) | copy-start | bytes 7684
  254.4 6.2 %copy-start.18 = (f32[640]{0:T(1024)S(1)}, f32[640]{0:T(1024)}, u32[]{:S(2)}) copy-start(f32[640]{0:T(1024)} %param.31) | copy-start | bytes 7684
  254.4 6.2 %copy-start.19 = (f32[640]{0:T(1024)S(1)}, f32[640]{0:T(1024)}, u32[]{:S(2)}) copy-start(f32[640]{0:T(1024)} %param.30) | copy-start | bytes 7684
  260.6 12.4 %copy-start.2 = (bf16[3,3,160,640]{3,2,1,0:T(8,128)(2,1)S(1)}, bf16[3,3,160,640]{3,2,1,0:T(8,128)(2,1)}, u32[]{:S(2)}) copy-start(bf16[3,3,160,640]{3,2,1,0:T(8,128)(2,1)} %param.32) | copy-start | bytes 5529604
  285.4 2.8 copy-start.3
  285.5 2.8 copy-start.13
  288.0 2.0 copy-start.1
Sparse Core Ops, SparseCore 0:
  24.9 68.0 all-gather.4
  95.1 70.7 all-gather.6

commit v3 on v2

--- a/solution.py
+++ b/solution.py
@@ -19,22 +19,38 @@
     return block
 
 
+def quarter_index():
+    return 2 * (lax.axis_index("groups") % 2) + lax.axis_index("col") % 2
+
+
 def gather_shards(shard):
     count = lax.axis_size("row")
     chips = count // 2
-    plane = lax.axis_size("groups") * lax.axis_size("col")
-    spot = lax.axis_index("groups") * lax.axis_size("col") + lax.axis_index("col")
+    y_pairs = [(i, i ^ 1) for i in range(lax.axis_size("groups"))]
+    z_pairs = [(i, i ^ 1) for i in range(lax.axis_size("col"))]
     mate_pairs = [(i, i ^ 1) for i in range(count)]
-    piece = lax.dynamic_slice_in_dim(shard.reshape(plane, -1), spot, 1, axis=0)
-    local = [shard, lax.ppermute(shard, "row", mate_pairs)]
-    remote = []
+    depth = shard.shape[2]
+    channels = shard.shape[3]
+    lanes = ((channels // 2 + 127) // 128) * 128
+    quarters = shard.reshape(shard.shape[:2] + (4, depth // 4, channels))
+    mine = lax.dynamic_index_in_dim(quarters, quarter_index(), axis=2, keepdims=False)
+    held = [shard, lax.ppermute(shard, "row", mate_pairs)]
     for step in range(1, chips):
         pairs = [(((i // 2 + step) % chips) * 2 + i % 2, i) for i in range(count)]
-        fetched = lax.ppermute(piece, "row", pairs)
-        rebuilt = lax.all_gather(fetched, ("groups", "col"), axis=0, tiled=True)
-        rebuilt = rebuilt.reshape(shard.shape)
-        remote += [rebuilt, lax.ppermute(rebuilt, "row", mate_pairs)]
-    return jnp.concatenate(local, axis=2), jnp.concatenate(remote, axis=2)
+        fetched = lax.ppermute(mine, "row", pairs)
+        from_z = lax.ppermute(fetched, "col", z_pairs)
+        from_y = lax.ppermute(fetched, "groups", y_pairs)
+        diagonal = jnp.concatenate(
+            [
+                lax.ppermute(from_z[..., :lanes], "groups", y_pairs),
+                lax.ppermute(from_y[..., lanes:], "col", z_pairs),
+            ],
+            axis=3,
+        )
+        parts = [fetched, from_z, from_y, diagonal]
+        relayed = [lax.ppermute(part, "row", mate_pairs) for part in parts]
+        held += [jnp.concatenate(parts, axis=2), jnp.concatenate(relayed, axis=2)]
+    return jnp.concatenate(held, axis=2)
 
 
 def relative_order(channels):
@@ -46,21 +62,18 @@
     core = me % 2
     position = jnp.arange(channels, dtype=jnp.int32)
     block = position // depth
+    within = position % depth
     source = 2 * ((chip + block // 2) % chips) + jnp.where(block % 2 == 0, core, 1 - core)
-    return source * depth + position % depth
-
-
-def conv_relative(activation, kernels, order):
-    local_kernel, remote_kernel = kernels
-    split = local_kernel.shape[2]
+    quarter = depth // 4
+    shuffled = (quarter_index() ^ (within // quarter)) * quarter + within % quarter
+    return source * depth + jnp.where(block >= 2, shuffled, within)
+
+
+def conv_relative(activation, kernel, order):
     natural = jnp.arange(activation.shape[-1], dtype=jnp.int32)[:, None]
-    total = None
-    for kernel, picks in ((local_kernel, order[:split]), (remote_kernel, order[split:])):
-        chooser = (natural == picks[None, :]).astype(activation.dtype)
-        part = jnp.dot(activation, chooser, preferred_element_type=jnp.float32)
-        part = conv_valid(part.astype(activation.dtype), kernel)
-        total = part if total is None else total + part
-    return total
+    chooser = (natural == order[None, :]).astype(activation.dtype)
+    moved = jnp.dot(activation, chooser, preferred_element_type=jnp.float32)
+    return conv_valid(moved.astype(activation.dtype), kernel)
 
 
 def conv_valid(activation, kernel):

time: 305 us -> 158 us (0.52); the launches traced: 299 us -> 157 us
  other arithmetic: 93 us -> 12.1 us
  waiting for transfers between devices: 74.8 us -> 22.9 us
  local copies, waits for them, and re-layouts: 49.6 us -> 65.7 us
  between operations: 14.1 us -> 0.38 us
  matrix products: 47.2 us -> 34.3 us
    all_gather x2 -> x0, other arithmetic: 81 us -> none  [gather_shards(): rebuilt = lax.all_gather(fetched, ('groups', 'col'), axis=0, tiled=True)]
    all_gather x2 -> x0, waiting for transfers between devices: 45.1 us -> none  [gather_shards(): rebuilt = lax.all_gather(fetched, ('groups', 'col'), axis=0, tiled=True)]
    unnamed x40 -> x68, local copies, waits for them, and re-layouts: 3.88 us -> 31.7 us
    reshape x4 -> x0, local copies, waits for them, and re-layouts: 18.4 us -> none  [the longest x2 11.2 us: gather_shards(): rebuilt = rebuilt.reshape(shard.shape)]
    conv_general_dilated x4 -> x2, matrix products: 47.2 us -> 34.3 us  [conv_valid(): lax.conv_general_dilated(activation, kernel, window_strides=(1, 1), paddi...]
    ppermute x2, waiting for transfers between devices: 7.62 us -> 3.53 us  [padded_2(): lax.ppermute(lax.slice_in_dim(block, 0, width, axis=dim), axis, backward)]
    squeeze x0 -> x2, local copies, waits for them, and re-layouts: none -> 3.84 us  [gather_shards(): lax.dynamic_index_in_dim(quarters, quarter_index(), axis=2, keepdims=False)]
    ppermute x6 -> x20, starting transfers between devices: 7.87 us -> 11.7 us  [the longest x2 2.66 us: gather_shards(): fetched = lax.ppermute(mine, 'row', pairs)]
  transfers between devices with their start and end apart: 12 -> 24, of which waited for: 5 -> 8; matrix products, arithmetic and copies ran while one was open for 55% -> 54% of each run, Pallas kernels for 0% -> 0%
where the time goes in v3:
time: 158 us; the launch traced here: 157 us
  local copies, waits for them, and re-layouts  65.7 us (42%)
  matrix products  34.3 us (22%)
  waiting for transfers between devices  22.9 us (14%)
  starting transfers between devices  21.9 us (14%)
  other arithmetic  12.1 us (8%)
    conv_general_dilated x2, matrix products, conv_valid(): lax.conv_general_dilated(activation, kernel, window_strides=(1, 1), paddi...  34.3 us
    unnamed x68, local copies, waits for them, and re-layouts  31.7 us
    another operation x3, local copies, waits for them, and re-layouts, body(): middle = jnp.stack(windows, axis=1)  13.5 us
    ppermute x2, waiting for transfers between devices, gather_shards(): from_z = lax.ppermute(fetched, 'col', z_pairs)  9.89 us
    ppermute x2, starting transfers between devices, padded_2(): lax.ppermute(lax.slice_in_dim(block, block.shape[dim] - width, None, axis...  6.5 us
    ppermute x2, waiting for transfers between devices, padded_2(): lax.ppermute(lax.slice_in_dim(block, block.shape[dim] - width, None, axis...  5.24 us
    squeeze x2, local copies, waits for them, and re-layouts, gather_shards(): lax.dynamic_index_in_dim(quarters, quarter_index(), axis=2, keepdims=False)  3.84 us
    ppermute x2, starting transfers between devices, padded_2(): lax.ppermute(lax.slice_in_dim(block, 0, width, axis=dim), axis, backward)  3.71 us
  transfers between devices with their start and end apart: 24, of which 8 were waited for; matrix products, arithmetic and copies ran while one was open for 54% of the time, Pallas kernels for 0%

profile of v3, /device:TPU:1, one launch (start us, length us, event | category | flops | bytes accessed | tf_op | source)
XLA Modules:
  0.0 157.3 jit_solution(16570407860677546842)
XLA Ops:
  0.1 2.0 %dynamic-slice_bitcast_fusion.1 = bf16[3,3,40,640]{3,2,1,0:T(8,128)(2,1)} fusion(bf16[3,3,4,40,640]{4,3,2,1,0:T(8,128)(2,1)} %bitcast.74, s32[]{:T(128)S(6)} %select_n.129), kind=kLoop, calls=%fused_computation.35 | loop fusion | bytes 921604 | tf_op jit(solution)/shard_map/jit(dynamic_index_in_dim)/squeeze | solution.py:36
  2.1 2.7 %collective-permute-start.5 = (bf16[3,3,40,640]{3,2,1,0:T(8,128)(2,1)}, bf16[3,3,40,640]{3,2,1,0:T(8,128)(2,1)}, u32[]{:S(2)}, u32[]{:S(2)}) collective-permute-start(bf16[3,3,40,640]{3,2,1,0:T(8,128)(2,1)} %dynamic-slice_bitcast_fusion.1), channel_id=1, source_target_pairs={{8,0},{12,4},{0,8},{4,12},{9,1},{13,5},{1,9},{5,13},{10,2},{14,6},... | collective-permute-start | bytes 1382408 | tf_op jit(solution)/shard_map/ppermute | solution.py:40
  4.7 2.1 %copy_bitcast_fusion = (bf16[1,24,4,8,640]{4,1,3,2,0:T(8,128)(2,1)S(1)}, bf16[1,24,4,8,640]{4,1,3,2,0:T(8,128)(2,1)S(1)}) fusion(bf16[24,4,8,640]{3,2,1,0:T(8,128)(2,1)} %param.18, bf16[24,4,8,640]{3,2,1,0:T(8,128)(2,1)} %param.17), kind=kLoop, calls=%fused_computation.26 | loop fusion | bytes 3932160 | tf_op jit(solution)/shard_map/stack | solution.py:125
  6.9 0.9 pad_maximum_fusion.3
  7.8 2.0 %collective-permute-start = (bf16[2,24,1,8,640]{4,1,3,2,0:T(8,128)(2,1)}, bf16[2,24,1,8,640]{4,1,3,2,0:T(8,128)(2,1)S(1)}, u32[]{:S(2)}, u32[]{:S(2)}) collective-permute-start(bf16[2,24,1,8,640]{4,1,3,2,0:T(8,128)(2,1)} %get-tuple-element.13), channel_id=1, source_target_pairs={{0,4},{4,8},{8,12},{1,5},{5,9},{9,13},{2,6},{6,10},{10,14},{3,7},{... | collective-permute-start | bytes 1474568 | tf_op jit(solution)/shard_map/ppermute | solution.py:14
  9.8 2.4 %collective-permute-start.1 = (bf16[2,24,1,8,640]{4,1,3,2,0:T(8,128)(2,1)S(1)}, bf16[2,24,1,8,640]{4,1,3,2,0:T(8,128)(2,1)S(1)}, u32[]{:S(2)}, u32[]{:S(2)}) collective-permute-start(bf16[2,24,1,8,640]{4,1,3,2,0:T(8,128)(2,1)S(1)} %get-tuple-element.14), channel_id=1, source_target_pairs={{4,0},{8,4},{12,8},{5,1},{9,5},{13,9},{6,2},{10,6},{14,10},{7,3},{... | collective-permute-start | bytes 1474568 | tf_op jit(solution)/shard_map/ppermute | solution.py:17
  12.2 1.9 %dynamic-slice_bitcast_fusion = bf16[3,3,40,640]{3,2,1,0:T(8,128)(2,1)} fusion(bf16[3,3,4,40,640]{4,3,2,1,0:T(8,128)(2,1)} %bitcast.18, s32[]{:T(128)S(6)} %select_n.129), kind=kLoop, calls=%fused_computation.34 | loop fusion | bytes 921604 | tf_op jit(solution)/shard_map/jit(dynamic_index_in_dim)/squeeze | solution.py:36
  14.1 1.4 constant_dynamic-update-slice_fusion.10
  15.5 3.0 %constant_dynamic-update-slice_fusion.21 = bf16[3,3,640,640]{3,2,1,0:T(8,128)(2,1)} fusion(bf16[3,3,160,640]{3,2,1,0:T(8,128)(2,1)} %param.32), kind=kLoop, calls=%fused_computation.61 | loop fusion | bytes 3686400
  19.3 5.2 %collective-permute-done = bf16[2,24,1,8,640]{4,1,3,2,0:T(8,128)(2,1)S(1)} collective-permute-done((bf16[2,24,1,8,640]{4,1,3,2,0:T(8,128)(2,1)}, bf16[2,24,1,8,640]{4,1,3,2,0:T(8,128)(2,1)S(1)}, u32[]{:S(2)}, u32[]{:S(2)}) %collective-permute-start) | collective-permute-done | bytes 491552 | tf_op jit(solution)/shard_map/ppermute | solution.py:14
  25.2 1.0 pad_maximum_fusion.9
  26.3 4.5 %collective-permute-start.2 = (bf16[2,24,6,1,640]{4,1,3,2,0:T(8,128)(2,1)}, bf16[2,24,6,1,640]{4,1,3,2,0:T(8,128)(2,1)}, u32[]{:S(2)}, u32[]{:S(2)}) collective-permute-start(bf16[2,24,6,1,640]{4,1,3,2,0:T(8,128)(2,1)} %get-tuple-element.9), channel_id=1, source_target_pairs={{0,1},{1,2},{2,3},{4,5},{5,6},{6,7},{8,9},{9,10},{10,11},{12,13},{... | collective-permute-start | bytes 1105928 | tf_op jit(solution)/shard_map/ppermute | solution.py:14
  30.7 1.3 collective-permute-start.3
  32.3 0.8 mul.117
  33.3 0.8 sub.56
  36.7 2.1 %collective-permute-start.6 = (bf16[3,3,40,640]{3,2,1,0:T(8,128)(2,1)}, bf16[3,3,40,640]{3,2,1,0:T(8,128)(2,1)S(1)}, u32[]{:S(2)}, u32[]{:S(2)}) collective-permute-start(bf16[3,3,40,640]{3,2,1,0:T(8,128)(2,1)} %collective-permute-done.5), channel_id=1, source_target_pairs={{0,1},{1,0},{2,3},{3,2},{4,5},{5,4},{6,7},{7,6},{8,9},{9,8},{10,11... | collective-permute-start | bytes 1382408 | tf_op jit(solution)/shard_map/ppermute | solution.py:41
  38.8 1.2 collective-permute-start.7
  40.1 2.9 %collective-permute-done.3 = bf16[2,24,6,1,640]{4,1,3,2,0:T(8,128)(2,1)} collective-permute-done((bf16[2,24,6,1,640]{4,1,3,2,0:T(8,128)(2,1)}, bf16[2,24,6,1,640]{4,1,3,2,0:T(8,128)(2,1)}, u32[]{:S(2)}, u32[]{:S(2)}) %collective-permute-start.3) | collective-permute-done | bytes 368672 | tf_op jit(solution)/shard_map/ppermute | solution.py:17
  43.0 1.2 collective-permute-start.17
  44.2 3.0 %pad_maximum_fusion.1 = bf16[2,24,6,10,640]{4,1,3,2,0:T(8,128)(2,1)S(1)} fusion(bf16[2,24,6,1,640]{4,1,3,2,0:T(8,128)(2,1)} %collective-permute-done.3, bf16[2,24,1,8,640]{4,1,3,2,0:T(8,128)(2,1)S(1)} %collective-permute-done.1, bf16[1,24,4,8,640]{4,1,3,2,0:T(8,128)(2,1)S(1)} %get-tuple-element.17, bf16[1,24,4,8,640]{4,1,3,2,0:T(8,128)(2,1)S(1)} %get-tuple-element.18, ...), kind=kLoop, calls=%fused_computation.2 | loop fusion | flops 9216000 | bytes 7372800 | tf_op jit(solution)/shard_map/concatenate | solution.py:18
  47.2 2.6 %fusion.5 = (f32[24,6,10,640]{3,0,2,1:T(8,128)S(1)}, f32[24,6,10,640]{3,0,2,1:T(8,128)}) fusion(bf16[2,24,6,10,640]{4,1,3,2,0:T(8,128)(2,1)S(1)} %pad_maximum_fusion.1), kind=kLoop, calls=%fused_computation.15 | loop fusion | flops 1843200 | bytes 11059200 | tf_op jit(solution)/shard_map/convert_element_type | solution.py:128
  50.2 2.8 %collective-permute-done.6 = bf16[3,3,40,640]{3,2,1,0:T(8,128)(2,1)S(1)} collective-permute-done((bf16[3,3,40,640]{3,2,1,0:T(8,128)(2,1)}, bf16[3,3,40,640]{3,2,1,0:T(8,128)(2,1)S(1)}, u32[]{:S(2)}, u32[]{:S(2)}) %collective-permute-start.6) | collective-permute-done | bytes 460832 | tf_op jit(solution)/shard_map/ppermute | solution.py:41
  53.0 1.3 collective-permute-start.8
  54.4 7.1 %collective-permute-done.16 = bf16[3,3,40,640]{3,2,1,0:T(8,128)(2,1)S(1)} collective-permute-done((bf16[3,3,40,640]{3,2,1,0:T(8,128)(2,1)}, bf16[3,3,40,640]{3,2,1,0:T(8,128)(2,1)S(1)}, u32[]{:S(2)}, u32[]{:S(2)}) %collective-permute-start.16) | collective-permute-done | bytes 460832 | tf_op jit(solution)/shard_map/ppermute | solution.py:41
  61.6 1.3 collective-permute-start.18
  62.9 0.9 slice.79
  63.9 1.7 %slice_bitcast_fusion.1 = (f32[24,1,6,6,640]{4,0,3,2,1:T(8,128)S(1)}, f32[24,1,6,6,640]{4,0,3,2,1:T(8,128)}) fusion(f32[24,6,10,640]{3,0,2,1:T(8,128)S(1)} %get-tuple-element.7), kind=kLoop, calls=%fused_computation.5 | loop fusion | bytes 8847360 | tf_op jit(solution)/shard_map/stack | solution.py:159
  65.6 1.5 collective-permute-done.8
  67.2 1.1 collective-permute-done.19
  68.3 1.7 %collective-permute-done.18 = bf16[3,3,40,384]{3,2,1,0:T(8,128)(2,1)S(1)} collective-permute-done((bf16[3,3,40,384]{3,2,1,0:T(8,128)(2,1)S(1)}, bf16[3,3,40,384]{3,2,1,0:T(8,128)(2,1)S(1)}, u32[]{:S(2)}, u32[]{:S(2)}) %collective-permute-start.18) | collective-permute-done | bytes 276512 | tf_op jit(solution)/shard_map/ppermute | solution.py:45
  71.3 3.0 %constant_dynamic-update-slice_fusion.9 = bf16[3,3,640,640]{3,2,1,0:T(8,128)(2,1)} fusion(bf16[3,3,640,640]{3,2,1,0:T(8,128)(2,1)} %constant_dynamic-update-slice_fusion.10, bf16[3,3,160,640]{3,2,1,0:T(8,128)(2,1)} %collective-permute-done.4), kind=kLoop, calls=%fused_computation.49 | loop fusion | bytes 3686400
  74.3 1.9 %constant_dynamic-update-slice_fusion.8 = bf16[3,3,640,640]{3,2,1,0:T(8,128)(2,1)} fusion(bf16[3,3,640,640]{3,2,1,0:T(8,128)(2,1)} %constant_dynamic-update-slice_fusion.9, bf16[3,3,40,640]{3,2,1,0:T(8,128)(2,1)} %collective-permute-done.5), kind=kLoop, calls=%fused_computation.48 | loop fusion | bytes 921600
  83.7 15.2 %add_add_fusion = f32[24,4,8,640]{3,0,2,1:T(8,128)} fusion(bf16[3,3,640,640]{3,2,1,0:T(8,128)(2,1)} %constant_dynamic-update-slice_fusion, f32[24,640]{1,0:T(8,128)} %param.27, f32[640]{0:T(1024)S(1)} %copy-done.19, f32[6,10]{1,0:T(8,128)S(1)} %and_convert_fusion.1, f32[640]{0:T(1024)S(1)} %copy-done.20, f32[640]{0:T(1024)S(1)} %copy-done.21, ...), kind=kOutput, calls=%fused_computation.11 | convolution fusion | flops 6854410240 | bytes 11376880 | tf_op jit(solution)/shard_map/conv_general_dilated | solution.py:80
  98.8 2.6 %fusion.16 = (f32[24,1,6,6,640]{4,0,3,2,1:T(8,128)S(1)}, f32[24,1,6,6,640]{4,0,3,2,1:T(8,128)}) fusion(f32[24,1,6,6,640]{4,0,3,2,1:T(8,128)S(1)} %get-tuple-element.5, f32[24,4,8,640]{3,0,2,1:T(8,128)} %add_add_fusion, f32[24,1,6,6,640]{4,0,3,2,1:T(8,128)} %get-tuple-element.6), kind=kLoop, calls=%fused_computation.25 | loop fusion | bytes 3932160 | tf_op jit(solution)/shard_map/dynamic_update_slice | solution.py:157
  101.4 2.1 %pad_maximum_fusion = f32[24,2,6,6,640]{4,0,3,2,1:T(8,128)S(1)} fusion(f32[24,1,6,6,640]{4,0,3,2,1:T(8,128)} %get-tuple-element.12, f32[24,1,6,6,640]{4,0,3,2,1:T(8,128)S(1)} %get-tuple-element.11), kind=kLoop, calls=%fused_computation | loop fusion | flops 1105920 | bytes 8847360 | tf_op jit(solution)/shard_map/stack | solution.py:159
  103.6 5.5 %copy.49 = f32[24,2,6,6,640]{4,1,0,3,2:T(2,128)} copy(f32[24,2,6,6,640]{4,0,3,2,1:T(8,128)S(1)} %pad_maximum_fusion) | data formatting | bytes 8847360 | tf_op jit(solution)/shard_map/stack | solution.py:159
  109.1 6.2 %stack.41 = f32[48,6,6,640]{3,0,2,1:T(8,128)} reshape(f32[24,2,6,6,640]{4,1,0,3,2:T(2,128)} %copy.49) | data formatting | bytes 8847360 | tf_op jit(solution)/shard_map/stack | solution.py:159
  115.3 2.9 %constant_dynamic-update-slice_fusion.20 = bf16[3,3,640,640]{3,2,1,0:T(8,128)(2,1)} fusion(bf16[3,3,640,640]{3,2,1,0:T(8,128)(2,1)} %constant_dynamic-update-slice_fusion.21, bf16[3,3,160,640]{3,2,1,0:T(8,128)(2,1)} %collective-permute-done.14), kind=kLoop, calls=%fused_computation.60 | loop fusion | bytes 3686400
  118.2 1.9 %constant_dynamic-update-slice_fusion.19 = bf16[3,3,640,640]{3,2,1,0:T(8,128)(2,1)} fusion(bf16[3,3,640,640]{3,2,1,0:T(8,128)(2,1)} %constant_dynamic-update-slice_fusion.20, bf16[3,3,40,640]{3,2,1,0:T(8,128)(2,1)} %collective-permute-done.15), kind=kLoop, calls=%fused_computation.59 | loop fusion | bytes 921600
  120.9 1.9 %constant_dynamic-update-slice_fusion.17 = bf16[3,3,640,640]{3,2,1,0:T(8,128)(2,1)} fusion(bf16[3,3,640,640]{3,2,1,0:T(8,128)(2,1)} %constant_dynamic-update-slice_fusion.18, bf16[3,3,40,640]{3,2,1,0:T(8,128)(2,1)} %collective-permute-done.17), kind=kLoop, calls=%fused_computation.57 | loop fusion | bytes 921600
  124.3 1.9 %constant_dynamic-update-slice_fusion.14 = bf16[3,3,640,640]{3,2,1,0:T(8,128)(2,1)} fusion(bf16[3,3,640,640]{3,2,1,0:T(8,128)(2,1)} %constant_dynamic-update-slice_fusion.15, bf16[3,3,40,640]{3,2,1,0:T(8,128)(2,1)} %collective-permute-done.20), kind=kLoop, calls=%fused_computation.54 | loop fusion | bytes 921600
  126.1 1.9 %constant_dynamic-update-slice_fusion.13 = bf16[3,3,640,640]{3,2,1,0:T(8,128)(2,1)} fusion(bf16[3,3,640,640]{3,2,1,0:T(8,128)(2,1)} %constant_dynamic-update-slice_fusion.14, bf16[3,3,40,640]{3,2,1,0:T(8,128)(2,1)} %collective-permute-done.21), kind=kLoop, calls=%fused_computation.53 | loop fusion | bytes 921600
  128.0 1.8 %constant_dynamic-update-slice_fusion.12 = bf16[3,3,640,640]{3,2,1,0:T(8,128)(2,1)} fusion(bf16[3,3,640,640]{3,2,1,0:T(8,128)(2,1)} %constant_dynamic-update-slice_fusion.13, bf16[3,3,40,640]{3,2,1,0:T(8,128)(2,1)} %collective-permute-done.22), kind=kLoop, calls=%fused_computation.52 | loop fusion | bytes 921600
  129.8 1.8 %constant_dynamic-update-slice_fusion.11 = bf16[3,3,640,640]{3,2,1,0:T(8,128)(2,1)} fusion(bf16[3,3,640,640]{3,2,1,0:T(8,128)(2,1)} %constant_dynamic-update-slice_fusion.12, bf16[3,3,40,640]{3,2,1,0:T(8,128)(2,1)} %collective-permute-done.23), kind=kLoop, calls=%fused_computation.51 | loop fusion | bytes 921600 | tf_op jit(solution)/shard_map/concatenate | solution.py:53
  131.7 19.2 %fusion = f32[48,4,4,640]{3,0,2,1:T(8,128)} fusion(bf16[3,3,640,640]{3,2,1,0:T(8,128)(2,1)} %constant_dynamic-update-slice_fusion.11, f32[48,6,6,640]{3,0,2,1:T(8,128)} %stack.41, f32[48,6,6]{0,2,1:T(8,128)S(1)} %copy-done.9, f32[640]{0:T(1024)S(1)} %copy-done.22, f32[640]{0:T(1024)S(1)} %copy-done.23, f32[48,640]{1,0:T(8,128)S(1)} %mul.133, ...), kind=kOutput, calls=%fused_computation.6 | convolution fusion | flops 7090462720 | bytes 14022912 | tf_op jit(solution)/shard_map/conv_general_dilated | solution.py:80
  150.8 2.5 %reshape.214 = f32[24,1,2,4,4,640]{5,2,0,4,3,1:T(2,128)S(1)} reshape(f32[48,4,4,640]{3,0,2,1:T(8,128)} %fusion) | data formatting | bytes 3932160 | tf_op jit(solution)/shard_map/reshape | solution.py:174
  153.6 1.8 %copy-done.1 = f32[24,6,10,640]{3,0,2,1:T(8,128)S(1)} copy-done((f32[24,6,10,640]{3,0,2,1:T(8,128)S(1)}, f32[24,6,10,640]{3,0,2,1:T(8,128)}, u32[]{:S(2)}) %copy-start.1) | copy-done | bytes 3686424
  156.2 1.1 copy.54
  (118 shorter events, 17.3 us)
Async XLA Ops:
  0.0 70.8 %collective-permute-start.4 = (bf16[3,3,160,640]{3,2,1,0:T(8,128)(2,1)}, bf16[3,3,160,640]{3,2,1,0:T(8,128)(2,1)}, u32[]{:S(2)}, u32[]{:S(2)}) collective-permute-start(bf16[3,3,160,640]{3,2,1,0:T(8,128)(2,1)} %param.25), channel_id=1, source_target_pairs={{0,4},{4,0},{8,12},{12,8},{1,5},{5,1},{9,13},{13,9},{2,6},{6,2},{1... | collective-permute-start | bytes 5529608 | tf_op jit(solution)/shard_map/ppermute | solution.py:37
  0.1 14.0 %copy-start.2 = (bf16[3,3,160,640]{3,2,1,0:T(8,128)(2,1)S(1)}, bf16[3,3,160,640]{3,2,1,0:T(8,128)(2,1)}, u32[]{:S(2)}) copy-start(bf16[3,3,160,640]{3,2,1,0:T(8,128)(2,1)} %param.25) | copy-start | bytes 5529604
  2.1 34.6 %collective-permute-start.5 = (bf16[3,3,40,640]{3,2,1,0:T(8,128)(2,1)}, bf16[3,3,40,640]{3,2,1,0:T(8,128)(2,1)}, u32[]{:S(2)}, u32[]{:S(2)}) collective-permute-start(bf16[3,3,40,640]{3,2,1,0:T(8,128)(2,1)} %dynamic-slice_bitcast_fusion.1), channel_id=1, source_target_pairs={{8,0},{12,4},{0,8},{4,12},{9,1},{13,5},{1,9},{5,13},{10,2},{14,6},... | collective-permute-start | bytes 1382408 | tf_op jit(solution)/shard_map/ppermute | solution.py:40
  7.7 10.8 %copy-start.14 = (s32[24,16]{0,1:T(8,128)S(1)}, s32[24,16]{0,1:T(8,128)}, u32[]{:S(2)}) copy-start(s32[24,16]{0,1:T(8,128)} %param.20) | copy-start | bytes 4612
  7.8 16.8 %collective-permute-start = (bf16[2,24,1,8,640]{4,1,3,2,0:T(8,128)(2,1)}, bf16[2,24,1,8,640]{4,1,3,2,0:T(8,128)(2,1)S(1)}, u32[]{:S(2)}, u32[]{:S(2)}) collective-permute-start(bf16[2,24,1,8,640]{4,1,3,2,0:T(8,128)(2,1)} %get-tuple-element.13), channel_id=1, source_target_pairs={{0,4},{4,8},{8,12},{1,5},{5,9},{9,13},{2,6},{6,10},{10,14},{3,7},{... | collective-permute-start | bytes 1474568 | tf_op jit(solution)/shard_map/ppermute | solution.py:14
  9.8 15.4 %collective-permute-start.1 = (bf16[2,24,1,8,640]{4,1,3,2,0:T(8,128)(2,1)S(1)}, bf16[2,24,1,8,640]{4,1,3,2,0:T(8,128)(2,1)S(1)}, u32[]{:S(2)}, u32[]{:S(2)}) collective-permute-start(bf16[2,24,1,8,640]{4,1,3,2,0:T(8,128)(2,1)S(1)} %get-tuple-element.14), channel_id=1, source_target_pairs={{4,0},{8,4},{12,8},{5,1},{9,5},{13,9},{6,2},{10,6},{14,10},{7,3},{... | collective-permute-start | bytes 1474568 | tf_op jit(solution)/shard_map/ppermute | solution.py:17
  14.1 24.7 %collective-permute-start.15 = (bf16[3,3,40,640]{3,2,1,0:T(8,128)(2,1)}, bf16[3,3,40,640]{3,2,1,0:T(8,128)(2,1)}, u32[]{:S(2)}, u32[]{:S(2)}) collective-permute-start(bf16[3,3,40,640]{3,2,1,0:T(8,128)(2,1)} %dynamic-slice_bitcast_fusion), channel_id=1, source_target_pairs={{8,0},{12,4},{0,8},{4,12},{9,1},{13,5},{1,9},{5,13},{10,2},{14,6},... | collective-permute-start | bytes 1382408 | tf_op jit(solution)/shard_map/ppermute | solution.py:40
  15.5 16.6 %copy-start.10 = (f32[24,32]{1,0:T(8,128)S(1)}, f32[24,32]{1,0:T(8,128)}, u32[]{:S(2)}) copy-start(f32[24,32]{1,0:T(8,128)} %param.22) | copy-start | bytes 9220
  15.5 17.6 %copy-start.11 = (f32[24,32]{1,0:T(8,128)S(1)}, f32[24,32]{1,0:T(8,128)}, u32[]{:S(2)}) copy-start(f32[24,32]{1,0:T(8,128)} %param.21) | copy-start | bytes 9220
  15.5 19.4 %copy-start.12 = (f32[24,32]{1,0:T(8,128)S(1)}, f32[24,32]{1,0:T(8,128)}, u32[]{:S(2)}) copy-start(f32[24,32]{1,0:T(8,128)} %param.29) | copy-start | bytes 9220
  18.5 16.9 %copy-start.13 = (f32[24,32]{1,0:T(8,128)S(1)}, f32[24,32]{1,0:T(8,128)}, u32[]{:S(2)}) copy-start(f32[24,32]{1,0:T(8,128)} %param.28) | copy-start | bytes 9220
  19.2 12.9 %copy-start.16 = (pred[10]{0:T(512)(128)(4,1)}, pred[10]{0:T(512)(128)(4,1)S(1)}, u32[]{:S(2)}) copy-start(pred[10]{0:T(512)(128)(4,1)S(1)} %compare_and_fusion) | copy-start | bytes 34
  26.3 13.8 %collective-permute-start.2 = (bf16[2,24,6,1,640]{4,1,3,2,0:T(8,128)(2,1)}, bf16[2,24,6,1,640]{4,1,3,2,0:T(8,128)(2,1)}, u32[]{:S(2)}, u32[]{:S(2)}) collective-permute-start(bf16[2,24,6,1,640]{4,1,3,2,0:T(8,128)(2,1)} %get-tuple-element.9), channel_id=1, source_target_pairs={{0,1},{1,2},{2,3},{4,5},{5,6},{6,7},{8,9},{9,10},{10,11},{12,13},{... | collective-permute-start | bytes 1105928 | tf_op jit(solution)/shard_map/ppermute | solution.py:14
  30.7 12.2 %collective-permute-start.3 = (bf16[2,24,6,1,640]{4,1,3,2,0:T(8,128)(2,1)}, bf16[2,24,6,1,640]{4,1,3,2,0:T(8,128)(2,1)}, u32[]{:S(2)}, u32[]{:S(2)}) collective-permute-start(bf16[2,24,6,1,640]{4,1,3,2,0:T(8,128)(2,1)} %get-tuple-element.10), channel_id=1, source_target_pairs={{1,0},{2,1},{3,2},{5,4},{6,5},{7,6},{9,8},{10,9},{11,10},{13,12},{... | collective-permute-start | bytes 1105928 | tf_op jit(solution)/shard_map/ppermute | solution.py:17
  32.1 4.6 %copy-start.17 = (pred[10]{0:T(512)(128)(4,1)S(1)}, pred[10]{0:T(512)(128)(4,1)}, u32[]{:S(2)}) copy-start(pred[10]{0:T(512)(128)(4,1)} %copy-done.16) | copy-start | bytes 34
  36.7 16.3 %collective-permute-start.6 = (bf16[3,3,40,640]{3,2,1,0:T(8,128)(2,1)}, bf16[3,3,40,640]{3,2,1,0:T(8,128)(2,1)S(1)}, u32[]{:S(2)}, u32[]{:S(2)}) collective-permute-start(bf16[3,3,40,640]{3,2,1,0:T(8,128)(2,1)} %collective-permute-done.5), channel_id=1, source_target_pairs={{0,1},{1,0},{2,3},{3,2},{4,5},{5,4},{6,7},{7,6},{8,9},{9,8},{10,11... | collective-permute-start | bytes 1382408 | tf_op jit(solution)/shard_map/ppermute | solution.py:41
  38.8 15.5 %collective-permute-start.7 = (bf16[3,3,40,640]{3,2,1,0:T(8,128)(2,1)}, bf16[3,3,40,640]{3,2,1,0:T(8,128)(2,1)S(1)}, u32[]{:S(2)}, u32[]{:S(2)}) collective-permute-start(bf16[3,3,40,640]{3,2,1,0:T(8,128)(2,1)} %collective-permute-done.5), channel_id=1, source_target_pairs={{0,16},{16,0},{1,17},{17,1},{2,18},{18,2},{3,19},{19,3},{4,20},{20... | collective-permute-start | bytes 1382408 | tf_op jit(solution)/shard_map/ppermute | solution.py:42
  40.0 21.5 %collective-permute-start.16 = (bf16[3,3,40,640]{3,2,1,0:T(8,128)(2,1)}, bf16[3,3,40,640]{3,2,1,0:T(8,128)(2,1)S(1)}, u32[]{:S(2)}, u32[]{:S(2)}) collective-permute-start(bf16[3,3,40,640]{3,2,1,0:T(8,128)(2,1)} %collective-permute-done.15), channel_id=1, source_target_pairs={{0,1},{1,0},{2,3},{3,2},{4,5},{5,4},{6,7},{7,6},{8,9},{9,8},{10,11... | collective-permute-start | bytes 1382408 | tf_op jit(solution)/shard_map/ppermute | solution.py:41
  43.0 19.9 %collective-permute-start.17 = (bf16[3,3,40,640]{3,2,1,0:T(8,128)(2,1)}, bf16[3,3,40,640]{3,2,1,0:T(8,128)(2,1)}, u32[]{:S(2)}, u32[]{:S(2)}) collective-permute-start(bf16[3,3,40,640]{3,2,1,0:T(8,128)(2,1)} %collective-permute-done.15), channel_id=1, source_target_pairs={{0,16},{16,0},{1,17},{17,1},{2,18},{18,2},{3,19},{19,3},{4,20},{20... | collective-permute-start | bytes 1382408 | tf_op jit(solution)/shard_map/ppermute | solution.py:42
  47.2 3.0 %copy-start = (bf16[2,24,6,10,640]{4,1,3,2,0:T(8,128)(2,1)}, bf16[2,24,6,10,640]{4,1,3,2,0:T(8,128)(2,1)S(1)}, u32[]{:S(2)}) copy-start(bf16[2,24,6,10,640]{4,1,3,2,0:T(8,128)(2,1)S(1)} %pad_maximum_fusion.1) | copy-start | bytes 11059204
  53.0 14.1 %collective-permute-start.8 = (bf16[3,3,40,384]{3,2,1,0:T(8,128)(2,1)S(1)}, bf16[3,3,40,384]{3,2,1,0:T(8,128)(2,1)S(1)}, u32[]{:S(2)}, u32[]{:S(2)}) collective-permute-start(bf16[3,3,40,384]{3,2,1,0:T(8,128)(2,1)S(1)} %slice.71), channel_id=1, source_target_pairs={{0,16},{16,0},{1,17},{17,1},{2,18},{18,2},{3,19},{19,3},{4,20},{20... | collective-permute-start | bytes 829448 | tf_op jit(solution)/shard_map/ppermute | solution.py:45
  54.3 11.3 %collective-permute-start.9 = (bf16[3,3,40,256]{3,2,1,0:T(8,128)(2,1)S(1)}, bf16[3,3,40,256]{3,2,1,0:T(8,128)(2,1)S(1)}, u32[]{:S(2)}, u32[]{:S(2)}) collective-permute-start(bf16[3,3,40,256]{3,2,1,0:T(8,128)(2,1)S(1)} %slice.72), channel_id=1, source_target_pairs={{0,1},{1,0},{2,3},{3,2},{4,5},{5,4},{6,7},{7,6},{8,9},{9,8},{10,11... | collective-permute-start | bytes 552968 | tf_op jit(solution)/shard_map/ppermute | solution.py:46
  61.6 8.4 %collective-permute-start.18 = (bf16[3,3,40,384]{3,2,1,0:T(8,128)(2,1)S(1)}, bf16[3,3,40,384]{3,2,1,0:T(8,128)(2,1)S(1)}, u32[]{:S(2)}, u32[]{:S(2)}) collective-permute-start(bf16[3,3,40,384]{3,2,1,0:T(8,128)(2,1)S(1)} %slice.78), channel_id=1, source_target_pairs={{0,16},{16,0},{1,17},{17,1},{2,18},{18,2},{3,19},{19,3},{4,20},{20... | collective-permute-start | bytes 829448 | tf_op jit(solution)/shard_map/ppermute | solution.py:45
  63.8 4.5 %collective-permute-start.19 = (bf16[3,3,40,256]{3,2,1,0:T(8,128)(2,1)S(1)}, bf16[3,3,40,256]{3,2,1,0:T(8,128)(2,1)S(1)}, u32[]{:S(2)}, u32[]{:S(2)}) collective-permute-start(bf16[3,3,40,256]{3,2,1,0:T(8,128)(2,1)S(1)} %slice.79), channel_id=1, source_target_pairs={{0,1},{1,0},{2,3},{3,2},{4,5},{5,4},{6,7},{7,6},{8,9},{9,8},{10,11... | collective-permute-start | bytes 552968 | tf_op jit(solution)/shard_map/ppermute | solution.py:46
  65.6 49.7 %collective-permute-start.14 = (bf16[3,3,160,640]{3,2,1,0:T(8,128)(2,1)}, bf16[3,3,160,640]{3,2,1,0:T(8,128)(2,1)}, u32[]{:S(2)}, u32[]{:S(2)}) collective-permute-start(bf16[3,3,160,640]{3,2,1,0:T(8,128)(2,1)} %param.32), channel_id=1, source_target_pairs={{0,4},{4,0},{8,12},{12,8},{1,5},{5,1},{9,13},{13,9},{2,6},{6,2},{1... | collective-permute-start | bytes 5529608 | tf_op jit(solution)/shard_map/ppermute | solution.py:37
  67.1 12.2 %collective-permute-start.10 = (bf16[3,3,40,640]{3,2,1,0:T(8,128)(2,1)}, bf16[3,3,40,640]{3,2,1,0:T(8,128)(2,1)S(1)}, u32[]{:S(2)}, u32[]{:S(2)}) collective-permute-start(bf16[3,3,40,640]{3,2,1,0:T(8,128)(2,1)} %collective-permute-done.5), channel_id=1, source_target_pairs={{0,4},{4,0},{8,12},{12,8},{1,5},{5,1},{9,13},{13,9},{2,6},{6,2},{1... | collective-permute-start | bytes 1382408 | tf_op jit(solution)/shard_map/ppermute | solution.py:51
  68.3 11.9 %copy-start.4 = (bf16[3,3,40,256]{3,2,1,0:T(8,128)(2,1)}, bf16[3,3,40,256]{3,2,1,0:T(8,128)(2,1)S(1)}, u32[]{:S(2)}) copy-start(bf16[3,3,40,256]{3,2,1,0:T(8,128)(2,1)S(1)} %collective-permute-done.19) | copy-start | bytes 552964
  68.3 11.9 %collective-permute-start.11 = (bf16[3,3,40,640]{3,2,1,0:T(8,128)(2,1)S(1)}, bf16[3,3,40,640]{3,2,1,0:T(8,128)(2,1)S(1)}, u32[]{:S(2)}, u32[]{:S(2)}) collective-permute-start(bf16[3,3,40,640]{3,2,1,0:T(8,128)(2,1)S(1)} %collective-permute-done.6), channel_id=1, source_target_pairs={{0,4},{4,0},{8,12},{12,8},{1,5},{5,1},{9,13},{13,9},{2,6},{6,2},{1... | collective-permute-start | bytes 1382408 | tf_op jit(solution)/shard_map/ppermute | solution.py:51
  69.9 11.6 %collective-permute-start.12 = (bf16[3,3,40,640]{3,2,1,0:T(8,128)(2,1)S(1)}, bf16[3,3,40,640]{3,2,1,0:T(8,128)(2,1)S(1)}, u32[]{:S(2)}, u32[]{:S(2)}) collective-permute-start(bf16[3,3,40,640]{3,2,1,0:T(8,128)(2,1)S(1)} %collective-permute-done.7), channel_id=1, source_target_pairs={{0,4},{4,0},{8,12},{12,8},{1,5},{5,1},{9,13},{13,9},{2,6},{6,2},{1... | collective-permute-start | bytes 1382408 | tf_op jit(solution)/shard_map/ppermute | solution.py:51
  70.8 11.6 %collective-permute-start.13 = (bf16[3,3,40,640]{3,2,1,0:T(8,128)(2,1)S(1)}, bf16[3,3,40,640]{3,2,1,0:T(8,128)(2,1)S(1)}, u32[]{:S(2)}, u32[]{:S(2)}) collective-permute-start(bf16[3,3,40,640]{3,2,1,0:T(8,128)(2,1)S(1)} %pad_maximum_fusion.4), channel_id=1, source_target_pairs={{0,4},{4,0},{8,12},{12,8},{1,5},{5,1},{9,13},{13,9},{2,6},{6,2},{1... | collective-permute-start | bytes 1382408 | tf_op jit(solution)/shard_map/ppermute | solution.py:51
  74.3 9.4 %copy-start.7 = (f32[24,640]{1,0:T(8,128)S(1)}, f32[24,640]{1,0:T(8,128)}, u32[]{:S(2)}) copy-start(f32[24,640]{1,0:T(8,128)} %mul.117) | copy-start | bytes 184324
  74.3 9.4 %copy-start.8 = (f32[24,640]{1,0:T(8,128)S(1)}, f32[24,640]{1,0:T(8,128)}, u32[]{:S(2)}) copy-start(f32[24,640]{1,0:T(8,128)} %sub.56) | copy-start | bytes 184324
  74.3 9.4 %copy-start.19 = (f32[640]{0:T(1024)S(1)}, f32[640]{0:T(1024)}, u32[]{:S(2)}) copy-start(f32[640]{0:T(1024)} %param.26) | copy-start | bytes 7684
  74.3 9.4 %copy-start.20 = (f32[640]{0:T(1024)S(1)}, f32[640]{0:T(1024)}, u32[]{:S(2)}) copy-start(f32[640]{0:T(1024)} %param.24) | copy-start | bytes 7684
  74.3 9.4 %copy-start.21 = (f32[640]{0:T(1024)S(1)}, f32[640]{0:T(1024)}, u32[]{:S(2)}) copy-start(f32[640]{0:T(1024)} %param.23) | copy-start | bytes 7684
  79.3 44.9 %collective-permute-start.20 = (bf16[3,3,40,640]{3,2,1,0:T(8,128)(2,1)}, bf16[3,3,40,640]{3,2,1,0:T(8,128)(2,1)}, u32[]{:S(2)}, u32[]{:S(2)}) collective-permute-start(bf16[3,3,40,640]{3,2,1,0:T(8,128)(2,1)} %collective-permute-done.15), channel_id=1, source_target_pairs={{0,4},{4,0},{8,12},{12,8},{1,5},{5,1},{9,13},{13,9},{2,6},{6,2},{1... | collective-permute-start | bytes 1382408 | tf_op jit(solution)/shard_map/ppermute | solution.py:51
  80.2 46.0 %collective-permute-start.21 = (bf16[3,3,40,640]{3,2,1,0:T(8,128)(2,1)S(1)}, bf16[3,3,40,640]{3,2,1,0:T(8,128)(2,1)}, u32[]{:S(2)}, u32[]{:S(2)}) collective-permute-start(bf16[3,3,40,640]{3,2,1,0:T(8,128)(2,1)S(1)} %collective-permute-done.16), channel_id=1, source_target_pairs={{0,4},{4,0},{8,12},{12,8},{1,5},{5,1},{9,13},{13,9},{2,6},{6,2},{1... | collective-permute-start | bytes 1382408 | tf_op jit(solution)/shard_map/ppermute | solution.py:51
  81.5 46.5 %collective-permute-start.22 = (bf16[3,3,40,640]{3,2,1,0:T(8,128)(2,1)}, bf16[3,3,40,640]{3,2,1,0:T(8,128)(2,1)}, u32[]{:S(2)}, u32[]{:S(2)}) collective-permute-start(bf16[3,3,40,640]{3,2,1,0:T(8,128)(2,1)} %collective-permute-done.17), channel_id=1, source_target_pairs={{0,4},{4,0},{8,12},{12,8},{1,5},{5,1},{9,13},{13,9},{2,6},{6,2},{1... | collective-permute-start | bytes 1382408 | tf_op jit(solution)/shard_map/ppermute | solution.py:51
  82.3 47.5 %collective-permute-start.23 = (bf16[3,3,40,640]{3,2,1,0:T(8,128)(2,1)}, bf16[3,3,40,640]{3,2,1,0:T(8,128)(2,1)}, u32[]{:S(2)}, u32[]{:S(2)}) collective-permute-start(bf16[3,3,40,640]{3,2,1,0:T(8,128)(2,1)} %pad_maximum_fusion.5), channel_id=1, source_target_pairs={{0,4},{4,0},{8,12},{12,8},{1,5},{5,1},{9,13},{13,9},{2,6},{6,2},{1... | collective-permute-start | bytes 1382408 | tf_op jit(solution)/shard_map/ppermute | solution.py:51
  115.3 8.3 %copy-start.5 = (bf16[3,3,40,256]{3,2,1,0:T(8,128)(2,1)S(1)}, bf16[3,3,40,256]{3,2,1,0:T(8,128)(2,1)}, u32[]{:S(2)}) copy-start(bf16[3,3,40,256]{3,2,1,0:T(8,128)(2,1)} %copy-done.4) | copy-start | bytes 552964
  118.2 13.4 %copy-start.6 = (f32[48,640]{1,0:T(8,128)S(1)}, f32[48,640]{1,0:T(8,128)}, u32[]{:S(2)}) copy-start(f32[48,640]{1,0:T(8,128)} %sub.68) | copy-start | bytes 368644
  118.2 13.4 %copy-start.9 = (f32[48,6,6]{0,2,1:T(8,128)S(1)}, f32[48,6,6]{0,2,1:T(8,128)}, u32[]{:S(2)}) copy-start(f32[48,6,6]{0,2,1:T(8,128)} %copy.50) | copy-start | bytes 20740
  118.2 13.4 %copy-start.22 = (f32[640]{0:T(1024)S(1)}, f32[640]{0:T(1024)}, u32[]{:S(2)}) copy-start(f32[640]{0:T(1024)} %param.31) | copy-start | bytes 7684
  118.2 13.4 %copy-start.23 = (f32[640]{0:T(1024)S(1)}, f32[640]{0:T(1024)}, u32[]{:S(2)}) copy-start(f32[640]{0:T(1024)} %param.30) | copy-start | bytes 7684
  150.8 2.8 %copy-start.18 = (pred[24,2]{0,1:T(4,128)(4,1)S(1)}, pred[24,2]{0,1:T(4,128)(4,1)}, u32[]{:S(2)}) copy-start(pred[24,2]{0,1:T(4,128)(4,1)} %compare_reduce_fusion) | copy-start | bytes 148
  150.8 2.8 %copy-start.3 = (bf16[24,4,8,640]{3,2,1,0:T(8,128)(2,1)S(1)}, bf16[24,4,8,640]{3,2,1,0:T(8,128)(2,1)}, u32[]{:S(2)}) copy-start(bf16[24,4,8,640]{3,2,1,0:T(8,128)(2,1)} %param.19) | copy-start | bytes 2949124
  150.8 2.8 %copy-start.15 = (f32[640]{0:T(1024)S(1)}, f32[640]{0:T(1024)}, u32[]{:S(2)}) copy-start(f32[640]{0:T(1024)} %param.33) | copy-start | bytes 7684
  153.4 2.0 %copy-start.1 = (f32[24,6,10,640]{3,0,2,1:T(8,128)S(1)}, f32[24,6,10,640]{3,0,2,1:T(8,128)}, u32[]{:S(2)}) copy-start(f32[24,6,10,640]{3,0,2,1:T(8,128)} %get-tuple-element.8) | copy-start | bytes 11059204

commit v4 on v3

--- a/solution.py
+++ b/solution.py
@@ -19,38 +19,27 @@
     return block
 
 
-def quarter_index():
-    return 2 * (lax.axis_index("groups") % 2) + lax.axis_index("col") % 2
-
-
-def gather_shards(shard):
+def gather_weights(kernels):
     count = lax.axis_size("row")
     chips = count // 2
     y_pairs = [(i, i ^ 1) for i in range(lax.axis_size("groups"))]
-    z_pairs = [(i, i ^ 1) for i in range(lax.axis_size("col"))]
     mate_pairs = [(i, i ^ 1) for i in range(count)]
-    depth = shard.shape[2]
-    channels = shard.shape[3]
-    lanes = ((channels // 2 + 127) // 128) * 128
-    quarters = shard.reshape(shard.shape[:2] + (4, depth // 4, channels))
-    mine = lax.dynamic_index_in_dim(quarters, quarter_index(), axis=2, keepdims=False)
-    held = [shard, lax.ppermute(shard, "row", mate_pairs)]
-    for step in range(1, chips):
-        pairs = [(((i // 2 + step) % chips) * 2 + i % 2, i) for i in range(count)]
-        fetched = lax.ppermute(mine, "row", pairs)
-        from_z = lax.ppermute(fetched, "col", z_pairs)
-        from_y = lax.ppermute(fetched, "groups", y_pairs)
-        diagonal = jnp.concatenate(
-            [
-                lax.ppermute(from_z[..., :lanes], "groups", y_pairs),
-                lax.ppermute(from_y[..., lanes:], "col", z_pairs),
-            ],
-            axis=3,
-        )
-        parts = [fetched, from_z, from_y, diagonal]
-        relayed = [lax.ppermute(part, "row", mate_pairs) for part in parts]
-        held += [jnp.concatenate(parts, axis=2), jnp.concatenate(relayed, axis=2)]
-    return jnp.concatenate(held, axis=2)
+    parity = lax.axis_index("groups") % 2
+    mates = lax.ppermute(jnp.stack(kernels), "row", mate_pairs)
+    wholes = []
+    for index, shard in enumerate(kernels):
+        depth = shard.shape[2]
+        halves = shard.reshape(shard.shape[:2] + (2, depth // 2) + shard.shape[3:])
+        mine = lax.dynamic_index_in_dim(halves, parity, axis=2, keepdims=False)
+        held = [shard, mates[index]]
+        for step in range(1, chips):
+            pairs = [(((i // 2 + step) % chips) * 2 + i % 2, i) for i in range(count)]
+            fetched = lax.ppermute(mine, "row", pairs)
+            other = lax.ppermute(fetched, "groups", y_pairs)
+            remote = jnp.concatenate([fetched, other], axis=2)
+            held += [remote, lax.ppermute(remote, "row", mate_pairs)]
+        wholes.append(jnp.concatenate(held, axis=2))
+    return wholes
 
 
 def relative_order(channels):
@@ -64,8 +53,9 @@
     block = position // depth
     within = position % depth
     source = 2 * ((chip + block // 2) % chips) + jnp.where(block % 2 == 0, core, 1 - core)
-    quarter = depth // 4
-    shuffled = (quarter_index() ^ (within // quarter)) * quarter + within % quarter
+    half = depth // 2
+    parity = lax.axis_index("groups") % 2
+    shuffled = (parity ^ (within // half)) * half + within % half
     return source * depth + jnp.where(block >= 2, shuffled, within)
 
 
@@ -115,8 +105,7 @@
     groups_total = norm1_mean.shape[1]
     per_group = channels // groups_total
 
-    first_whole = gather_shards(conv1_weight)
-    second_whole = gather_shards(conv2_weight)
+    first_whole, second_whole = gather_weights([conv1_weight, conv2_weight])
     order = relative_order(channels)
 
     def expand(values):
@@ -146,28 +135,25 @@
         conv_relative(first_act, first_whole, order) + conv1_bias + step_embed[:, None, None, :]
     )
 
+    fresh_pad = jnp.pad(fresh_mid, ((0, 0), (1, 1), (1, 1), (0, 0)))
+    edge = jnp.arange(TILE + 2, dtype=jnp.int32)
+    interior = ((edge >= 1) & (edge <= TILE))[:, None] & ((edge >= 1) & (edge <= TILE))[None, :]
+    interior = interior[None, :, :, None]
     windows = []
     masks = []
     for tile_down in range(tiles_down):
         for tile_across in range(tiles_across):
             r0 = tile_down * TILE
             c0 = tile_across * TILE
-            margin = margins_pad[:, r0 : r0 + TILE + 2, c0 : c0 + TILE + 2]
-            own = fresh_mid[:, r0 : r0 + TILE, c0 : c0 + TILE]
-            windows.append(lax.dynamic_update_slice(margin, own, (0, 1, 1, 0)))
-            masks.append(inside[:, r0 : r0 + TILE + 2, c0 : c0 + TILE + 2])
+            cut = (slice(None), slice(r0, r0 + TILE + 2), slice(c0, c0 + TILE + 2))
+            windows.append(jnp.where(interior, fresh_pad[cut], margins_pad[cut]))
+            masks.append(inside[cut])
     middle = jnp.stack(windows, axis=1)
     border = jnp.stack(masks, axis=1)
-    middle = middle.reshape((-1,) + middle.shape[2:])
     second_mean = expand(norm2_mean)[:, None]
     second_rstd = expand(norm2_rstd)[:, None]
     second_act = (
-        jax.nn.silu(
-            (middle.reshape((requests, -1) + middle.shape[1:]) - second_mean) * second_rstd
-            * norm2_gain
-            + norm2_shift
-        )
-        * border
+        jax.nn.silu((middle - second_mean) * second_rstd * norm2_gain + norm2_shift) * border
     ).astype(jnp.bfloat16)
     second_act = second_act.reshape((-1,) + second_act.shape[2:])
     second_sum = conv_relative(second_act, second_whole, order)

time: 158 us -> 154 us (0.975)
  other arithmetic: 12.1 us -> 21.6 us
  local copies, waits for them, and re-layouts: 65.7 us -> 58.3 us
  starting transfers between devices: 21.9 us -> 18.1 us
    unnamed x68 -> x61, local copies, waits for them, and re-layouts: 31.7 us -> 18.5 us
    ppermute x20 -> x7, waiting for transfers between devices: 14.2 us -> 19.4 us  [the longest x2 12.8 us: gather_weights(): other = lax.ppermute(fetched, 'groups', y_pairs)]
    ppermute x2, waiting for transfers between devices: 5.24 us -> 0.01 us  [padded_2(): lax.ppermute(lax.slice_in_dim(block, block.shape[dim] - width, None, axis...]
    another operation x0 -> x1, other arithmetic: none -> 4.46 us  [gather_weights(): mates = lax.ppermute(jnp.stack(kernels), 'row', mate_pairs)]
    broadcast_in_dim x4, local copies, waits for them, and re-layouts: 0.62 us -> 5.06 us  [expand(): return jnp.repeat(values, per_group, axis=1)[:, None, None, :]]
    dynamic_update_slice x1 -> x0, local copies, waits for them, and re-layouts: 2.61 us -> none  [body(): windows.append(lax.dynamic_update_slice(margin, own, (0, 1, 1, 0)))]
    ppermute x20 -> x7, starting transfers between devices: 11.7 us -> 9.07 us  [the longest x2 4.12 us: gather_weights(): held += [remote, lax.ppermute(remote, 'row', mate_pairs)]]
    mul x5, local copies, waits for them, and re-layouts: 1.1 us -> 3.59 us  [the longest x3 3.46 us: body(): (middle - second_mean) * second_rstd * norm2_gain + norm2_shift]
  transfers between devices with their start and end apart: 24 -> 11, of which waited for: 8 -> 3; matrix products, arithmetic and copies ran while one was open for 54% -> 53% of each run, Pallas kernels for 0% -> 0%
where the time goes in v4:
time: 154 us; the launch traced here: 153 us
  local copies, waits for them, and re-layouts  58.3 us (38%)
  matrix products  33.1 us (21%)
  other arithmetic  21.6 us (14%)
  waiting for transfers between devices  21.5 us (14%)
  starting transfers between devices  18.1 us (12%)
    conv_general_dilated x2, matrix products, conv_valid(): lax.conv_general_dilated(activation, kernel, window_strides=(1, 1), paddi...  33.1 us
    unnamed x61, local copies, waits for them, and re-layouts  18.5 us
    ppermute x2, waiting for transfers between devices, gather_weights(): other = lax.ppermute(fetched, 'groups', y_pairs)  12.8 us
    another operation x2, local copies, waits for them, and re-layouts, body(): middle = jnp.stack(windows, axis=1)  12 us
    ppermute x2, waiting for transfers between devices, gather_weights(): fetched = lax.ppermute(mine, 'row', pairs)  6.66 us
    ppermute x2, starting transfers between devices, padded_2(): lax.ppermute(lax.slice_in_dim(block, block.shape[dim] - width, None, axis...  5.26 us
    broadcast_in_dim x4, local copies, waits for them, and re-layouts, expand(): return jnp.repeat(values, per_group, axis=1)[:, None, None, :]  5.06 us
    another operation x1, other arithmetic, gather_weights(): mates = lax.ppermute(jnp.stack(kernels), 'row', mate_pairs)  4.46 us
  transfers between devices with their start and end apart: 11, of which 3 were waited for; matrix products, arithmetic and copies ran while one was open for 53% of the time, Pallas kernels for 0%

profile of v4, /device:TPU:1, one launch (start us, length us, event | category | flops | bytes accessed | tf_op | source)
XLA Modules:
  0.0 152.9 jit_solution(892708190020706488)
XLA Ops:
  0.0 2.2 %dynamic-slice_bitcast_fusion.1 = bf16[3,3,80,640]{3,2,1,0:T(8,128)(2,1)} fusion(bf16[3,3,2,80,640]{4,3,2,1,0:T(8,128)(2,1)} %bitcast.75, s32[]{:T(128)S(6)} %select_n.125), kind=kLoop, calls=%fused_computation.36 | loop fusion | bytes 1843204 | tf_op jit(solution)/shard_map/jit(dynamic_index_in_dim)/squeeze | solution.py:33
  2.2 2.0 %collective-permute-start.5 = (bf16[3,3,80,640]{3,2,1,0:T(8,128)(2,1)}, bf16[3,3,80,640]{3,2,1,0:T(8,128)(2,1)}, u32[]{:S(2)}, u32[]{:S(2)}) collective-permute-start(bf16[3,3,80,640]{3,2,1,0:T(8,128)(2,1)} %dynamic-slice_bitcast_fusion.1), channel_id=1, source_target_pairs={{8,0},{12,4},{0,8},{4,12},{9,1},{13,5},{1,9},{5,13},{10,2},{14,6},... | collective-permute-start | bytes 2764808 | tf_op jit(solution)/shard_map/ppermute | solution.py:37
  4.2 4.5 %pad_maximum_fusion.2 = bf16[2,3,3,160,640]{4,3,2,1,0:T(8,128)(2,1)} fusion(bf16[1,3,3,160,640]{4,3,2,1,0:T(8,128)(2,1)} %bitcast.77, bf16[1,3,3,160,640]{4,3,2,1,0:T(8,128)(2,1)} %bitcast.76), kind=kLoop, calls=%fused_computation.5 | loop fusion | flops 1843200 | bytes 7372800 | tf_op jit(solution)/shard_map/stack | solution.py:28
  8.7 1.0 collective-permute-start.4
  10.4 1.1 pad_maximum_fusion.6
  11.4 2.0 %collective-permute-start = (bf16[2,24,1,8,640]{4,1,3,2,0:T(8,128)(2,1)}, bf16[2,24,1,8,640]{4,1,3,2,0:T(8,128)(2,1)S(1)}, u32[]{:S(2)}, u32[]{:S(2)}) collective-permute-start(bf16[2,24,1,8,640]{4,1,3,2,0:T(8,128)(2,1)} %get-tuple-element.13), channel_id=1, source_target_pairs={{0,4},{4,8},{8,12},{1,5},{5,9},{9,13},{2,6},{6,10},{10,14},{3,7},{... | collective-permute-start | bytes 1474568 | tf_op jit(solution)/shard_map/ppermute | solution.py:14
  13.5 2.4 %collective-permute-start.1 = (bf16[2,24,1,8,640]{4,1,3,2,0:T(8,128)(2,1)}, bf16[2,24,1,8,640]{4,1,3,2,0:T(8,128)(2,1)}, u32[]{:S(2)}, u32[]{:S(2)}) collective-permute-start(bf16[2,24,1,8,640]{4,1,3,2,0:T(8,128)(2,1)} %get-tuple-element.14), channel_id=1, source_target_pairs={{4,0},{8,4},{12,8},{5,1},{9,5},{13,9},{6,2},{10,6},{14,10},{7,3},{... | collective-permute-start | bytes 1474568 | tf_op jit(solution)/shard_map/ppermute | solution.py:17
  15.9 1.0 dynamic-slice_bitcast_fusion
  18.1 6.7 %collective-permute-done.5 = bf16[3,3,80,640]{3,2,1,0:T(8,128)(2,1)} collective-permute-done((bf16[3,3,80,640]{3,2,1,0:T(8,128)(2,1)}, bf16[3,3,80,640]{3,2,1,0:T(8,128)(2,1)}, u32[]{:S(2)}, u32[]{:S(2)}) %collective-permute-start.5) | collective-permute-done | bytes 921632 | tf_op jit(solution)/shard_map/ppermute | solution.py:37
  24.7 1.2 collective-permute-start.6
  25.9 2.9 %constant_dynamic-update-slice_fusion.3 = bf16[3,3,640,640]{3,2,1,0:T(8,128)(2,1)} fusion(bf16[3,3,160,640]{3,2,1,0:T(8,128)(2,1)} %param.25), kind=kLoop, calls=%fused_computation.48 | loop fusion | bytes 3686400
  29.4 0.9 broadcast_in_dim.72
  30.3 1.8 %mul.112 = f32[24,640]{1,0:T(8,128)} reshape(f32[24,32,20]{2,1,0:T(8,128)} %broadcast_in_dim.72) | data formatting | bytes 122880 | tf_op jit(solution)/shard_map/mul | solution.py:130
  32.2 0.9 broadcast_in_dim.71
  33.1 1.8 %sub.56 = f32[24,640]{1,0:T(8,128)} reshape(f32[24,32,20]{2,1,0:T(8,128)} %broadcast_in_dim.71) | data formatting | bytes 122880 | tf_op jit(solution)/shard_map/sub | solution.py:130
  35.0 1.6 %broadcast_in_dim.76 = f32[24,32,20]{2,1,0:T(8,128)} broadcast(f32[24,32]{1,0:T(8,128)} %param.29), dimensions={0,1} | broadcast | bytes 64512 | tf_op jit(solution)/shard_map/broadcast_in_dim | solution.py:112
  36.7 1.8 %mul.125 = f32[24,640]{1,0:T(8,128)} reshape(f32[24,32,20]{2,1,0:T(8,128)} %broadcast_in_dim.76) | data formatting | bytes 122880 | tf_op jit(solution)/shard_map/mul | solution.py:156
  38.5 0.9 mul.126
  40.1 1.6 %broadcast_in_dim.75 = f32[24,32,20]{2,1,0:T(8,128)} broadcast(f32[24,32]{1,0:T(8,128)} %param.28), dimensions={0,1} | broadcast | bytes 64512 | tf_op jit(solution)/shard_map/broadcast_in_dim | solution.py:112
  41.8 1.8 %sub.66 = f32[24,640]{1,0:T(8,128)} reshape(f32[24,32,20]{2,1,0:T(8,128)} %broadcast_in_dim.75) | data formatting | bytes 122880 | tf_op jit(solution)/shard_map/sub | solution.py:156
  43.6 0.9 sub.67
  45.2 1.7 %constant_dynamic-update-slice_fusion.7 = bf16[3,3,640,640]{3,2,1,0:T(8,128)(2,1)S(1)} fusion(bf16[3,3,160,640]{3,2,1,0:T(8,128)(2,1)} %param.32), kind=kLoop, calls=%fused_computation.52 | loop fusion | bytes 3686400
  47.6 1.0 pad_maximum_fusion.10
  48.6 3.2 %collective-permute-start.2 = (bf16[2,24,6,1,640]{4,1,3,2,0:T(8,128)(2,1)S(1)}, bf16[2,24,6,1,640]{4,1,3,2,0:T(8,128)(2,1)S(1)}, u32[]{:S(2)}, u32[]{:S(2)}) collective-permute-start(bf16[2,24,6,1,640]{4,1,3,2,0:T(8,128)(2,1)S(1)} %get-tuple-element.11), channel_id=1, source_target_pairs={{0,1},{1,2},{2,3},{4,5},{5,6},{6,7},{8,9},{9,10},{10,11},{12,13},{... | collective-permute-start | bytes 1105928 | tf_op jit(solution)/shard_map/ppermute | solution.py:14
  51.8 1.3 collective-permute-start.3
  53.2 1.6 %pad_maximum_fusion.3 = bf16[3,3,160,640]{3,2,1,0:T(8,128)(2,1)S(1)} fusion(bf16[3,3,80,640]{3,2,1,0:T(8,128)(2,1)} %collective-permute-done.6, bf16[3,3,80,640]{3,2,1,0:T(8,128)(2,1)} %collective-permute-done.5), kind=kLoop, calls=%fused_computation.25 | loop fusion | flops 3686400 | bytes 3686400 | tf_op jit(solution)/shard_map/concatenate | solution.py:39
  54.8 3.3 %collective-permute-start.7 = (bf16[3,3,160,640]{3,2,1,0:T(8,128)(2,1)S(1)}, bf16[3,3,160,640]{3,2,1,0:T(8,128)(2,1)S(1)}, u32[]{:S(2)}, u32[]{:S(2)}) collective-permute-start(bf16[3,3,160,640]{3,2,1,0:T(8,128)(2,1)S(1)} %pad_maximum_fusion.3), channel_id=1, source_target_pairs={{0,4},{4,0},{8,12},{12,8},{1,5},{5,1},{9,13},{13,9},{2,6},{6,2},{1... | collective-permute-start | bytes 5529608 | tf_op jit(solution)/shard_map/ppermute | solution.py:40
  58.5 2.0 %collective-permute-done.3 = bf16[2,24,6,1,640]{4,1,3,2,0:T(8,128)(2,1)S(1)} collective-permute-done((bf16[2,24,6,1,640]{4,1,3,2,0:T(8,128)(2,1)S(1)}, bf16[2,24,6,1,640]{4,1,3,2,0:T(8,128)(2,1)S(1)}, u32[]{:S(2)}, u32[]{:S(2)}) %collective-permute-start.3) | collective-permute-done | bytes 368672 | tf_op jit(solution)/shard_map/ppermute | solution.py:17
  60.5 2.9 %pad_maximum_fusion.1 = bf16[2,24,6,10,640]{4,1,3,2,0:T(8,128)(2,1)S(1)} fusion(bf16[2,24,6,1,640]{4,1,3,2,0:T(8,128)(2,1)S(1)} %collective-permute-done.3, bf16[2,24,1,8,640]{4,1,3,2,0:T(8,128)(2,1)} %collective-permute-done.1, bf16[1,24,4,8,640]{4,1,3,2,0:T(8,128)(2,1)S(1)} %get-tuple-element.17, bf16[1,24,4,8,640]{4,1,3,2,0:T(8,128)(2,1)S(1)} %get-tuple-element.18, ...), kind=kLoop, calls=%fused_computation.4 | loop fusion | flops 9216000 | bytes 7372800 | tf_op jit(solution)/shard_map/concatenate | solution.py:18
  63.4 3.7 %fusion.9 = (f32[24,6,10,640]{3,0,2,1:T(8,128)}, f32[24,6,10,640]{3,0,2,1:T(8,128)}) fusion(bf16[2,24,6,10,640]{4,1,3,2,0:T(8,128)(2,1)S(1)} %pad_maximum_fusion.1), kind=kLoop, calls=%fused_computation.20 | loop fusion | flops 1843200 | bytes 11059200 | tf_op jit(solution)/shard_map/convert_element_type | solution.py:117
  67.5 12.8 %collective-permute-done.9 = bf16[3,3,80,640]{3,2,1,0:T(8,128)(2,1)S(1)} collective-permute-done((bf16[3,3,80,640]{3,2,1,0:T(8,128)(2,1)S(1)}, bf16[3,3,80,640]{3,2,1,0:T(8,128)(2,1)S(1)}, u32[]{:S(2)}, u32[]{:S(2)}) %collective-permute-start.9) | collective-permute-done | bytes 921632 | tf_op jit(solution)/shard_map/ppermute | solution.py:38
  80.3 1.6 %pad_maximum_fusion.4 = bf16[3,3,160,640]{3,2,1,0:T(8,128)(2,1)} fusion(bf16[3,3,80,640]{3,2,1,0:T(8,128)(2,1)S(1)} %collective-permute-done.9, bf16[3,3,80,640]{3,2,1,0:T(8,128)(2,1)S(1)} %collective-permute-done.8), kind=kLoop, calls=%fused_computation.26 | loop fusion | flops 3686400 | bytes 3686400 | tf_op jit(solution)/shard_map/concatenate | solution.py:39
  81.9 0.8 collective-permute-start.10
  82.7 3.7 %fusion.10 = (bf16[3,3,640,640]{3,2,1,0:T(8,128)(2,1)}, bf16[3,3,640,640]{3,2,1,0:T(8,128)(2,1)S(1)}) fusion(bf16[3,3,640,640]{3,2,1,0:T(8,128)(2,1)} %constant_dynamic-update-slice_fusion.3, bf16[2,3,3,160,640]{4,3,2,1,0:T(8,128)(2,1)} %collective-permute-done.4, bf16[3,3,640,640]{3,2,1,0:T(8,128)(2,1)S(1)} %constant_dynamic-update-slice_fusion.7), kind=kLoop, calls=%fused_computation.22 | loop fusion | bytes 7372800
  86.4 3.3 %constant_dynamic-update-slice_fusion.2 = bf16[3,3,640,640]{3,2,1,0:T(8,128)(2,1)} fusion(bf16[3,3,640,640]{3,2,1,0:T(8,128)(2,1)} %get-tuple-element.9, bf16[3,3,80,640]{3,2,1,0:T(8,128)(2,1)} %collective-permute-done.5), kind=kLoop, calls=%fused_computation.47 | loop fusion | bytes 1843200
  89.7 2.2 %constant_dynamic-update-slice_fusion.1 = bf16[3,3,640,640]{3,2,1,0:T(8,128)(2,1)} fusion(bf16[3,3,640,640]{3,2,1,0:T(8,128)(2,1)} %constant_dynamic-update-slice_fusion.2, bf16[3,3,80,640]{3,2,1,0:T(8,128)(2,1)} %collective-permute-done.6), kind=kLoop, calls=%fused_computation.46 | loop fusion | bytes 1843200
  91.9 1.4 constant_dynamic-update-slice_fusion
  93.3 13.9 %add_add_fusion = f32[24,4,8,640]{3,0,2,1:T(8,128)S(1)} fusion(bf16[3,3,640,640]{3,2,1,0:T(8,128)(2,1)} %constant_dynamic-update-slice_fusion, f32[24,640]{1,0:T(8,128)S(1)} %copy-done.21, f32[640]{0:T(1024)S(1)} %copy-done.22, f32[6,10]{1,0:T(8,128)S(1)} %and_convert_fusion.1, f32[640]{0:T(1024)S(1)} %copy-done.23, f32[640]{0:T(1024)S(1)} %copy-done.24, ...), kind=kOutput, calls=%fused_computation.16 | convolution fusion | flops 6854410240 | bytes 11376880 | tf_op jit(solution)/shard_map/conv_general_dilated | solution.py:70
  107.3 2.7 %fusion.1 = (f32[24,1,6,6,640]{4,0,3,2,1:T(8,128)S(1)}, f32[24,1,6,6,640]{4,0,3,2,1:T(8,128)S(1)}) fusion(f32[24,4,8,640]{3,0,2,1:T(8,128)S(1)} %add_add_fusion, f32[24,6,10,640]{3,0,2,1:T(8,128)} %get-tuple-element.7, pred[6,6]{1,0:T(8,128)(4,1)S(1)} %broadcast_and_fusion), kind=kLoop, calls=%fused_computation.8 | loop fusion | flops 1105920 | bytes 10813476 | tf_op jit(solution)/shard_map/stack | solution.py:151
  110.3 5.7 %copy.40 = f32[24,2,6,6,640]{4,1,0,3,2:T(2,128)} copy(f32[24,2,6,6,640]{4,0,3,2,1:T(8,128)S(1)} %pad_maximum_fusion) | data formatting | bytes 8847360 | tf_op jit(solution)/shard_map/stack | solution.py:151
  116.0 6.3 %stack.47 = f32[48,6,6,640]{3,0,2,1:T(8,128)} reshape(f32[24,2,6,6,640]{4,1,0,3,2:T(2,128)} %copy.40) | data formatting | bytes 8847360 | tf_op jit(solution)/shard_map/stack | solution.py:151
  122.3 1.0 constant_dynamic-update-slice_fusion.6
  123.3 1.0 constant_dynamic-update-slice_fusion.5
  124.4 2.9 %constant_dynamic-update-slice_fusion.4 = bf16[3,3,640,640]{3,2,1,0:T(8,128)(2,1)} fusion(bf16[3,3,640,640]{3,2,1,0:T(8,128)(2,1)} %constant_dynamic-update-slice_fusion.5, bf16[3,3,160,640]{3,2,1,0:T(8,128)(2,1)} %collective-permute-done.10), kind=kLoop, calls=%fused_computation.49 | loop fusion | bytes 3686400 | tf_op jit(solution)/shard_map/concatenate | solution.py:41
  127.3 19.2 %fusion.4 = f32[48,4,4,640]{3,0,2,1:T(8,128)} fusion(bf16[3,3,640,640]{3,2,1,0:T(8,128)(2,1)} %constant_dynamic-update-slice_fusion.4, f32[48,6,6,640]{3,0,2,1:T(8,128)} %stack.47, f32[48,6,6]{0,2,1:T(8,128)S(1)} %copy.41, f32[640]{0:T(1024)S(1)} %copy-done.25, f32[640]{0:T(1024)S(1)} %copy-done.26, f32[48,640]{1,0:T(8,128)S(1)} %copy-done.9, ...), kind=kOutput, calls=%fused_computation.11 | convolution fusion | flops 7090462720 | bytes 14022912 | tf_op jit(solution)/shard_map/conv_general_dilated | solution.py:70
  146.5 2.5 %reshape.255 = f32[24,1,2,4,4,640]{5,2,0,4,3,1:T(2,128)S(1)} reshape(f32[48,4,4,640]{3,0,2,1:T(8,128)} %fusion.4) | data formatting | bytes 3932160 | tf_op jit(solution)/shard_map/reshape | solution.py:160
  149.3 1.8 %copy-done.2 = f32[24,6,10,640]{3,0,2,1:T(8,128)S(1)} copy-done((f32[24,6,10,640]{3,0,2,1:T(8,128)S(1)}, f32[24,6,10,640]{3,0,2,1:T(8,128)}, u32[]{:S(2)}) %copy-start.2) | copy-done | bytes 3686424
  151.8 1.1 copy.45
  (83 shorter events, 6.8 us)
Async XLA Ops:
  2.2 22.5 %collective-permute-start.5 = (bf16[3,3,80,640]{3,2,1,0:T(8,128)(2,1)}, bf16[3,3,80,640]{3,2,1,0:T(8,128)(2,1)}, u32[]{:S(2)}, u32[]{:S(2)}) collective-permute-start(bf16[3,3,80,640]{3,2,1,0:T(8,128)(2,1)} %dynamic-slice_bitcast_fusion.1), channel_id=1, source_target_pairs={{8,0},{12,4},{0,8},{4,12},{9,1},{13,5},{1,9},{5,13},{10,2},{14,6},... | collective-permute-start | bytes 2764808 | tf_op jit(solution)/shard_map/ppermute | solution.py:37
  4.2 5.4 %copy-start.6 = (bf16[24,4,8,640]{3,2,1,0:T(8,128)(2,1)S(1)}, bf16[24,4,8,640]{3,2,1,0:T(8,128)(2,1)}, u32[]{:S(2)}) copy-start(bf16[24,4,8,640]{3,2,1,0:T(8,128)(2,1)} %param.18) | copy-start | bytes 2949124
  4.2 5.4 %copy-start.7 = (bf16[24,4,8,640]{3,2,1,0:T(8,128)(2,1)S(1)}, bf16[24,4,8,640]{3,2,1,0:T(8,128)(2,1)}, u32[]{:S(2)}) copy-start(bf16[24,4,8,640]{3,2,1,0:T(8,128)(2,1)} %param.17) | copy-start | bytes 2949124
  8.7 7.2 %copy-start.1 = (bf16[3,3,160,640]{3,2,1,0:T(8,128)(2,1)S(1)}, bf16[3,3,160,640]{3,2,1,0:T(8,128)(2,1)}, u32[]{:S(2)}) copy-start(bf16[3,3,160,640]{3,2,1,0:T(8,128)(2,1)} %param.32) | copy-start | bytes 5529604
  8.7 74.0 %collective-permute-start.4 = (bf16[2,3,3,160,640]{4,3,2,1,0:T(8,128)(2,1)}, bf16[2,3,3,160,640]{4,3,2,1,0:T(8,128)(2,1)}, u32[]{:S(2)}, u32[]{:S(2)}) collective-permute-start(bf16[2,3,3,160,640]{4,3,2,1,0:T(8,128)(2,1)} %pad_maximum_fusion.2), channel_id=1, source_target_pairs={{0,4},{4,0},{8,12},{12,8},{1,5},{5,1},{9,13},{13,9},{2,6},{6,2},{1... | collective-permute-start | bytes 11059208 | tf_op jit(solution)/shard_map/ppermute | solution.py:28
  10.4 19.1 %copy-start.13 = (f32[24,32]{1,0:T(8,128)S(1)}, f32[24,32]{1,0:T(8,128)}, u32[]{:S(2)}) copy-start(f32[24,32]{1,0:T(8,128)} %param.22) | copy-start | bytes 9220
  11.4 20.7 %copy-start.14 = (f32[24,32]{1,0:T(8,128)S(1)}, f32[24,32]{1,0:T(8,128)}, u32[]{:S(2)}) copy-start(f32[24,32]{1,0:T(8,128)} %param.21) | copy-start | bytes 9220
  11.4 36.2 %collective-permute-start = (bf16[2,24,1,8,640]{4,1,3,2,0:T(8,128)(2,1)}, bf16[2,24,1,8,640]{4,1,3,2,0:T(8,128)(2,1)S(1)}, u32[]{:S(2)}, u32[]{:S(2)}) collective-permute-start(bf16[2,24,1,8,640]{4,1,3,2,0:T(8,128)(2,1)} %get-tuple-element.13), channel_id=1, source_target_pairs={{0,4},{4,8},{8,12},{1,5},{5,9},{9,13},{2,6},{6,10},{10,14},{3,7},{... | collective-permute-start | bytes 1474568 | tf_op jit(solution)/shard_map/ppermute | solution.py:14
  13.5 34.1 %collective-permute-start.1 = (bf16[2,24,1,8,640]{4,1,3,2,0:T(8,128)(2,1)}, bf16[2,24,1,8,640]{4,1,3,2,0:T(8,128)(2,1)}, u32[]{:S(2)}, u32[]{:S(2)}) collective-permute-start(bf16[2,24,1,8,640]{4,1,3,2,0:T(8,128)(2,1)} %get-tuple-element.14), channel_id=1, source_target_pairs={{4,0},{8,4},{12,8},{5,1},{9,5},{13,9},{6,2},{10,6},{14,10},{7,3},{... | collective-permute-start | bytes 1474568 | tf_op jit(solution)/shard_map/ppermute | solution.py:17
  16.9 41.3 %collective-permute-start.8 = (bf16[3,3,80,640]{3,2,1,0:T(8,128)(2,1)}, bf16[3,3,80,640]{3,2,1,0:T(8,128)(2,1)S(1)}, u32[]{:S(2)}, u32[]{:S(2)}) collective-permute-start(bf16[3,3,80,640]{3,2,1,0:T(8,128)(2,1)} %dynamic-slice_bitcast_fusion), channel_id=1, source_target_pairs={{8,0},{12,4},{0,8},{4,12},{9,1},{13,5},{1,9},{5,13},{10,2},{14,6},... | collective-permute-start | bytes 2764808 | tf_op jit(solution)/shard_map/ppermute | solution.py:37
  17.4 0.5 copy-start.17
  17.5 15.6 %copy-start.18 = (pred[10]{0:T(512)(128)(4,1)}, pred[10]{0:T(512)(128)(4,1)S(1)}, u32[]{:S(2)}) copy-start(pred[10]{0:T(512)(128)(4,1)S(1)} %compare_and_fusion) | copy-start | bytes 34
  24.7 28.5 %collective-permute-start.6 = (bf16[3,3,80,640]{3,2,1,0:T(8,128)(2,1)}, bf16[3,3,80,640]{3,2,1,0:T(8,128)(2,1)}, u32[]{:S(2)}, u32[]{:S(2)}) collective-permute-start(bf16[3,3,80,640]{3,2,1,0:T(8,128)(2,1)} %collective-permute-done.5), channel_id=1, source_target_pairs={{0,16},{16,0},{1,17},{17,1},{2,18},{18,2},{3,19},{19,3},{4,20},{20... | collective-permute-start | bytes 2764808 | tf_op jit(solution)/shard_map/ppermute | solution.py:38
  35.0 11.9 %copy-start.19 = (pred[10]{0:T(512)(128)(4,1)S(1)}, pred[10]{0:T(512)(128)(4,1)}, u32[]{:S(2)}) copy-start(pred[10]{0:T(512)(128)(4,1)} %copy-done.18) | copy-start | bytes 34
  45.2 7.9 %copy-start.15 = (s32[24,16]{0,1:T(8,128)S(1)}, s32[24,16]{0,1:T(8,128)}, u32[]{:S(2)}) copy-start(s32[24,16]{0,1:T(8,128)} %param.20) | copy-start | bytes 4612
  45.2 7.9 %copy-start.20 = (s32[2]{0:T(128)S(1)}, s32[2]{0:T(128)}, u32[]{:S(2)}) copy-start(s32[2]{0:T(128)} %add_add_fusion.1) | copy-start | bytes 28
  48.6 9.9 %collective-permute-start.2 = (bf16[2,24,6,1,640]{4,1,3,2,0:T(8,128)(2,1)S(1)}, bf16[2,24,6,1,640]{4,1,3,2,0:T(8,128)(2,1)S(1)}, u32[]{:S(2)}, u32[]{:S(2)}) collective-permute-start(bf16[2,24,6,1,640]{4,1,3,2,0:T(8,128)(2,1)S(1)} %get-tuple-element.11), channel_id=1, source_target_pairs={{0,1},{1,2},{2,3},{4,5},{5,6},{6,7},{8,9},{9,10},{10,11},{12,13},{... | collective-permute-start | bytes 1105928 | tf_op jit(solution)/shard_map/ppermute | solution.py:14
  51.8 8.7 %collective-permute-start.3 = (bf16[2,24,6,1,640]{4,1,3,2,0:T(8,128)(2,1)S(1)}, bf16[2,24,6,1,640]{4,1,3,2,0:T(8,128)(2,1)S(1)}, u32[]{:S(2)}, u32[]{:S(2)}) collective-permute-start(bf16[2,24,6,1,640]{4,1,3,2,0:T(8,128)(2,1)S(1)} %get-tuple-element.12), channel_id=1, source_target_pairs={{1,0},{2,1},{3,2},{5,4},{6,5},{7,6},{9,8},{10,9},{11,10},{13,12},{... | collective-permute-start | bytes 1105928 | tf_op jit(solution)/shard_map/ppermute | solution.py:17
  54.8 37.0 %collective-permute-start.7 = (bf16[3,3,160,640]{3,2,1,0:T(8,128)(2,1)S(1)}, bf16[3,3,160,640]{3,2,1,0:T(8,128)(2,1)S(1)}, u32[]{:S(2)}, u32[]{:S(2)}) collective-permute-start(bf16[3,3,160,640]{3,2,1,0:T(8,128)(2,1)S(1)} %pad_maximum_fusion.3), channel_id=1, source_target_pairs={{0,4},{4,0},{8,12},{12,8},{1,5},{5,1},{9,13},{13,9},{2,6},{6,2},{1... | collective-permute-start | bytes 5529608 | tf_op jit(solution)/shard_map/ppermute | solution.py:40
  58.2 22.1 %collective-permute-start.9 = (bf16[3,3,80,640]{3,2,1,0:T(8,128)(2,1)S(1)}, bf16[3,3,80,640]{3,2,1,0:T(8,128)(2,1)S(1)}, u32[]{:S(2)}, u32[]{:S(2)}) collective-permute-start(bf16[3,3,80,640]{3,2,1,0:T(8,128)(2,1)S(1)} %collective-permute-done.8), channel_id=1, source_target_pairs={{0,16},{16,0},{1,17},{17,1},{2,18},{18,2},{3,19},{19,3},{4,20},{20... | collective-permute-start | bytes 2764808 | tf_op jit(solution)/shard_map/ppermute | solution.py:38
  63.4 4.1 %copy-start = (bf16[2,24,6,10,640]{4,1,3,2,0:T(8,128)(2,1)}, bf16[2,24,6,10,640]{4,1,3,2,0:T(8,128)(2,1)S(1)}, u32[]{:S(2)}) copy-start(bf16[2,24,6,10,640]{4,1,3,2,0:T(8,128)(2,1)S(1)} %pad_maximum_fusion.1) | copy-start | bytes 11059204
  80.3 6.1 %copy-start.3 = (bf16[3,3,80,640]{3,2,1,0:T(8,128)(2,1)}, bf16[3,3,80,640]{3,2,1,0:T(8,128)(2,1)S(1)}, u32[]{:S(2)}) copy-start(bf16[3,3,80,640]{3,2,1,0:T(8,128)(2,1)S(1)} %collective-permute-done.9) | copy-start | bytes 2764804
  81.9 42.5 %collective-permute-start.10 = (bf16[3,3,160,640]{3,2,1,0:T(8,128)(2,1)}, bf16[3,3,160,640]{3,2,1,0:T(8,128)(2,1)}, u32[]{:S(2)}, u32[]{:S(2)}) collective-permute-start(bf16[3,3,160,640]{3,2,1,0:T(8,128)(2,1)} %pad_maximum_fusion.4), channel_id=1, source_target_pairs={{0,4},{4,0},{8,12},{12,8},{1,5},{5,1},{9,13},{13,9},{2,6},{6,2},{1... | collective-permute-start | bytes 5529608 | tf_op jit(solution)/shard_map/ppermute | solution.py:40
  86.4 5.5 %copy-start.8 = (bf16[3,3,640,640]{3,2,1,0:T(8,128)(2,1)}, bf16[3,3,640,640]{3,2,1,0:T(8,128)(2,1)S(1)}, u32[]{:S(2)}) copy-start(bf16[3,3,640,640]{3,2,1,0:T(8,128)(2,1)S(1)} %get-tuple-element.10) | copy-start | bytes 22118404
  86.4 6.9 %copy-start.11 = (f32[24,640]{1,0:T(8,128)S(1)}, f32[24,640]{1,0:T(8,128)}, u32[]{:S(2)}) copy-start(f32[24,640]{1,0:T(8,128)} %mul.112) | copy-start | bytes 184324
  86.4 6.9 %copy-start.12 = (f32[24,640]{1,0:T(8,128)S(1)}, f32[24,640]{1,0:T(8,128)}, u32[]{:S(2)}) copy-start(f32[24,640]{1,0:T(8,128)} %sub.56) | copy-start | bytes 184324
  86.4 6.9 %copy-start.21 = (f32[24,640]{1,0:T(8,128)S(1)}, f32[24,640]{1,0:T(8,128)}, u32[]{:S(2)}) copy-start(f32[24,640]{1,0:T(8,128)} %param.27) | copy-start | bytes 184324
  86.4 6.9 %copy-start.22 = (f32[640]{0:T(1024)S(1)}, f32[640]{0:T(1024)}, u32[]{:S(2)}) copy-start(f32[640]{0:T(1024)} %param.26) | copy-start | bytes 7684
  86.4 6.9 %copy-start.23 = (f32[640]{0:T(1024)S(1)}, f32[640]{0:T(1024)}, u32[]{:S(2)}) copy-start(f32[640]{0:T(1024)} %param.24) | copy-start | bytes 7684
  86.4 6.9 %copy-start.24 = (f32[640]{0:T(1024)S(1)}, f32[640]{0:T(1024)}, u32[]{:S(2)}) copy-start(f32[640]{0:T(1024)} %param.23) | copy-start | bytes 7684
  116.0 7.4 %copy-start.4 = (bf16[3,3,80,640]{3,2,1,0:T(8,128)(2,1)S(1)}, bf16[3,3,80,640]{3,2,1,0:T(8,128)(2,1)}, u32[]{:S(2)}) copy-start(bf16[3,3,80,640]{3,2,1,0:T(8,128)(2,1)} %copy-done.3) | copy-start | bytes 2764804
  122.3 5.0 %copy-start.9 = (f32[48,640]{1,0:T(8,128)S(1)}, f32[48,640]{1,0:T(8,128)}, u32[]{:S(2)}) copy-start(f32[48,640]{1,0:T(8,128)} %mul.127) | copy-start | bytes 368644
  122.3 5.0 %copy-start.10 = (f32[48,640]{1,0:T(8,128)S(1)}, f32[48,640]{1,0:T(8,128)}, u32[]{:S(2)}) copy-start(f32[48,640]{1,0:T(8,128)} %sub.68) | copy-start | bytes 368644
  122.3 5.0 %copy-start.25 = (f32[640]{0:T(1024)S(1)}, f32[640]{0:T(1024)}, u32[]{:S(2)}) copy-start(f32[640]{0:T(1024)} %param.31) | copy-start | bytes 7684
  122.3 5.0 %copy-start.26 = (f32[640]{0:T(1024)S(1)}, f32[640]{0:T(1024)}, u32[]{:S(2)}) copy-start(f32[640]{0:T(1024)} %param.30) | copy-start | bytes 7684
  146.5 2.8 %copy-start.5 = (bf16[24,4,8,640]{3,2,1,0:T(8,128)(2,1)S(1)}, bf16[24,4,8,640]{3,2,1,0:T(8,128)(2,1)}, u32[]{:S(2)}) copy-start(bf16[24,4,8,640]{3,2,1,0:T(8,128)(2,1)} %param.19) | copy-start | bytes 2949124
  146.5 2.8 %copy-start.16 = (f32[640]{0:T(1024)S(1)}, f32[640]{0:T(1024)}, u32[]{:S(2)}) copy-start(f32[640]{0:T(1024)} %param.33) | copy-start | bytes 7684
  149.0 2.0 %copy-start.2 = (f32[24,6,10,640]{3,0,2,1:T(8,128)S(1)}, f32[24,6,10,640]{3,0,2,1:T(8,128)}, u32[]{:S(2)}) copy-start(f32[24,6,10,640]{3,0,2,1:T(8,128)} %get-tuple-element.8) | copy-start | bytes 11059204

commit v5 on v4

--- a/solution.py
+++ b/solution.py
@@ -25,19 +25,26 @@
     y_pairs = [(i, i ^ 1) for i in range(lax.axis_size("groups"))]
     mate_pairs = [(i, i ^ 1) for i in range(count)]
     parity = lax.axis_index("groups") % 2
-    mates = lax.ppermute(jnp.stack(kernels), "row", mate_pairs)
     wholes = []
-    for index, shard in enumerate(kernels):
+    previous = None
+    for shard in kernels:
         depth = shard.shape[2]
         halves = shard.reshape(shard.shape[:2] + (2, depth // 2) + shard.shape[3:])
         mine = lax.dynamic_index_in_dim(halves, parity, axis=2, keepdims=False)
-        held = [shard, mates[index]]
+        held = [shard, lax.ppermute(shard, "row", mate_pairs)]
         for step in range(1, chips):
+            if previous is not None:
+                mine, _ = lax.optimization_barrier((mine, previous))
             pairs = [(((i // 2 + step) % chips) * 2 + i % 2, i) for i in range(count)]
             fetched = lax.ppermute(mine, "row", pairs)
+            previous = fetched
             other = lax.ppermute(fetched, "groups", y_pairs)
-            remote = jnp.concatenate([fetched, other], axis=2)
-            held += [remote, lax.ppermute(remote, "row", mate_pairs)]
+            relayed = lax.ppermute(fetched, "row", mate_pairs)
+            other_relayed = lax.ppermute(other, "row", mate_pairs)
+            held += [
+                jnp.concatenate([fetched, other], axis=2),
+                jnp.concatenate([relayed, other_relayed], axis=2),
+            ]
         wholes.append(jnp.concatenate(held, axis=2))
     return wholes
 
@@ -59,11 +66,15 @@
     return source * depth + jnp.where(block >= 2, shuffled, within)
 
 
-def conv_relative(activation, kernel, order):
+def to_relative(activation, order):
     natural = jnp.arange(activation.shape[-1], dtype=jnp.int32)[:, None]
     chooser = (natural == order[None, :]).astype(activation.dtype)
     moved = jnp.dot(activation, chooser, preferred_element_type=jnp.float32)
-    return conv_valid(moved.astype(activation.dtype), kernel)
+    return moved.astype(activation.dtype)
+
+
+def conv_relative(activation, kernel, order):
+    return conv_valid(to_relative(activation, order), kernel)
 
 
 def conv_valid(activation, kernel):
@@ -135,32 +146,31 @@
         conv_relative(first_act, first_whole, order) + conv1_bias + step_embed[:, None, None, :]
     )
 
-    fresh_pad = jnp.pad(fresh_mid, ((0, 0), (1, 1), (1, 1), (0, 0)))
-    edge = jnp.arange(TILE + 2, dtype=jnp.int32)
-    interior = ((edge >= 1) & (edge <= TILE))[:, None] & ((edge >= 1) & (edge <= TILE))[None, :]
-    interior = interior[None, :, :, None]
-    windows = []
-    masks = []
-    for tile_down in range(tiles_down):
-        for tile_across in range(tiles_across):
-            r0 = tile_down * TILE
-            c0 = tile_across * TILE
-            cut = (slice(None), slice(r0, r0 + TILE + 2), slice(c0, c0 + TILE + 2))
-            windows.append(jnp.where(interior, fresh_pad[cut], margins_pad[cut]))
-            masks.append(inside[cut])
-    middle = jnp.stack(windows, axis=1)
-    border = jnp.stack(masks, axis=1)
-    second_mean = expand(norm2_mean)[:, None]
-    second_rstd = expand(norm2_rstd)[:, None]
-    second_act = (
-        jax.nn.silu((middle - second_mean) * second_rstd * norm2_gain + norm2_shift) * border
-    ).astype(jnp.bfloat16)
-    second_act = second_act.reshape((-1,) + second_act.shape[2:])
-    second_sum = conv_relative(second_act, second_whole, order)
-    second_sum = second_sum.reshape(requests, tiles_down, tiles_across, TILE, TILE, channels)
-    second_sum = jnp.transpose(second_sum, (0, 1, 3, 2, 4, 5)).reshape(
-        requests, rows_dev, cols_dev, channels
-    )
+    if tiles_down != 1:
+        raise ValueError("tiles_down")
+    second_mean = expand(norm2_mean)
+    second_rstd = expand(norm2_rstd)
+
+    def second_norm(values):
+        return jax.nn.silu((values - second_mean) * second_rstd * norm2_gain + norm2_shift)
+
+    cached_act = to_relative((second_norm(margins_pad) * inside).astype(jnp.bfloat16), order)
+    fresh_act = to_relative(second_norm(fresh_mid).astype(jnp.bfloat16), order)
+    blended = lax.dynamic_update_slice(cached_act, fresh_act, (0, 1, 1, 0))
+    second_sum = conv_valid(blended, second_whole)
+    fixes = jnp.zeros_like(second_sum)
+    for boundary in range(1, tiles_across):
+        edge_col = boundary * TILE
+        for out_col, in_col, tap in ((edge_col - 1, edge_col + 1, 2), (edge_col, edge_col, 0)):
+            pair = jnp.concatenate(
+                [cached_act[:, :, in_col : in_col + 1], blended[:, :, in_col : in_col + 1]]
+            )
+            moved = conv_valid(pair, second_whole[:, tap : tap + 1])
+            change = moved[:requests] - moved[requests:]
+            fixes = fixes + jnp.pad(
+                change, ((0, 0), (0, 0), (out_col, cols_dev - out_col - 1), (0, 0))
+            )
+    second_sum = second_sum + fixes
     renewed = (
         second_sum + conv2_bias + inputs_pad[:, 1 : 1 + rows_dev, 1 : 1 + cols_dev]
     ).astype(jnp.bfloat16)

time: 154 us -> 131 us (0.85)
  local copies, waits for them, and re-layouts: 58.3 us -> 31.7 us
  other arithmetic: 21.6 us -> 7.21 us
  waiting for transfers between devices: 21.5 us -> 33.8 us
  starting transfers between devices: 18.1 us -> 23.8 us
    dot_general x0 -> x3, matrix products: none -> 21.3 us  [to_relative(): moved = jnp.dot(activation, chooser, preferred_element_type=jnp.float32)]
    conv_general_dilated x2 -> x3, matrix products: 33.1 us -> 12.6 us  [conv_valid(): lax.conv_general_dilated(activation, kernel, window_strides=(1, 1), paddi...]
    ppermute x2, waiting for transfers between devices: 0.01 us -> 12.3 us  [padded_2(): lax.ppermute(lax.slice_in_dim(block, block.shape[dim] - width, None, axis...]
    another operation x3 -> x0, local copies, waits for them, and re-layouts: 12.1 us -> none  [the longest x2 12 us: body(): middle = jnp.stack(windows, axis=1)]
    another operation x3 -> x0, other arithmetic: 7.48 us -> none  [the longest x1 4.46 us: gather_weights(): mates = lax.ppermute(jnp.stack(kernels), 'row', mate_pairs)]
    ppermute x2, waiting for transfers between devices: 6.66 us -> 0.01 us  [gather_weights(): fetched = lax.ppermute(mine, 'row', pairs)]
    broadcast_in_dim x4, local copies, waits for them, and re-layouts: 5.06 us -> 0.62 us  [expand(): return jnp.repeat(values, per_group, axis=1)[:, None, None, :]]
    ppermute x2, waiting for transfers between devices: 12.8 us -> 17 us  [gather_weights(): other = lax.ppermute(fetched, 'groups', y_pairs)]
  transfers between devices with their start and end apart: 11 -> 14, of which waited for: 3 -> 5; matrix products, arithmetic and copies ran while one was open for 53% -> 43% of each run, Pallas kernels for 0% -> 0%
where the time goes in v5:
time: 131 us
  waiting for transfers between devices  33.8 us (26%)
  matrix products  33.8 us (26%)
  local copies, waits for them, and re-layouts  31.7 us (24%)
  starting transfers between devices  23.8 us (18%)
  other arithmetic  7.21 us (6%)
    dot_general x3, matrix products, to_relative(): moved = jnp.dot(activation, chooser, preferred_element_type=jnp.float32)  21.3 us
    unnamed x46, local copies, waits for them, and re-layouts  19.5 us
    ppermute x2, waiting for transfers between devices, gather_weights(): other = lax.ppermute(fetched, 'groups', y_pairs)  17 us
    conv_general_dilated x3, matrix products, conv_valid(): lax.conv_general_dilated(activation, kernel, window_strides=(1, 1), paddi...  12.6 us
    ppermute x2, waiting for transfers between devices, padded_2(): lax.ppermute(lax.slice_in_dim(block, block.shape[dim] - width, None, axis...  12.3 us
    ppermute x2, starting transfers between devices, padded_2(): lax.ppermute(lax.slice_in_dim(block, block.shape[dim] - width, None, axis...  6.1 us
    ppermute x2, starting transfers between devices, gather_weights(): other_relayed = lax.ppermute(other, 'row', mate_pairs)  4.84 us
    ppermute x2, waiting for transfers between devices, padded_2(): lax.ppermute(lax.slice_in_dim(block, 0, width, axis=dim), axis, backward)  4.44 us
  transfers between devices with their start and end apart: 14, of which 5 were waited for; matrix products, arithmetic and copies ran while one was open for 43% of the time, Pallas kernels for 0%

profile of v5, /device:TPU:1, one launch (start us, length us, event | category | flops | bytes accessed | tf_op | source)
XLA Modules:
  0.0 130.6 jit_solution(11154012502495927931)
XLA Ops:
  0.1 2.2 %dynamic-slice_bitcast_fusion.1 = bf16[3,3,80,640]{3,2,1,0:T(8,128)(2,1)} fusion(bf16[3,3,2,80,640]{4,3,2,1,0:T(8,128)(2,1)} %bitcast.46, s32[]{:T(128)S(6)} %select_n.118), kind=kLoop, calls=%fused_computation.49 | loop fusion | bytes 1843204 | tf_op jit(solution)/shard_map/jit(dynamic_index_in_dim)/squeeze | solution.py:33
  2.2 2.7 %collective-permute-start.5 = (bf16[3,3,80,640]{3,2,1,0:T(8,128)(2,1)}, bf16[3,3,80,640]{3,2,1,0:T(8,128)(2,1)}, u32[]{:S(2)}, u32[]{:S(2)}) collective-permute-start(bf16[3,3,80,640]{3,2,1,0:T(8,128)(2,1)} %dynamic-slice_bitcast_fusion.1), channel_id=1, source_target_pairs={{8,0},{12,4},{0,8},{4,12},{9,1},{13,5},{1,9},{5,13},{10,2},{14,6},... | collective-permute-start | bytes 2764808 | tf_op jit(solution)/shard_map/ppermute | solution.py:39
  4.9 2.1 %copy_bitcast_fusion = (bf16[1,24,4,8,640]{4,1,3,2,0:T(8,128)(2,1)S(1)}, bf16[1,24,4,8,640]{4,1,3,2,0:T(8,128)(2,1)S(1)}) fusion(bf16[24,4,8,640]{3,2,1,0:T(8,128)(2,1)} %param.18, bf16[24,4,8,640]{3,2,1,0:T(8,128)(2,1)} %param.17), kind=kLoop, calls=%fused_computation.40 | loop fusion | bytes 3932160 | tf_op jit(solution)/shard_map/stack | solution.py:125
  7.1 0.9 pad_maximum_fusion.2
  8.0 1.9 %collective-permute-start = (bf16[2,24,1,8,640]{4,1,3,2,0:T(8,128)(2,1)}, bf16[2,24,1,8,640]{4,1,3,2,0:T(8,128)(2,1)S(1)}, u32[]{:S(2)}, u32[]{:S(2)}) collective-permute-start(bf16[2,24,1,8,640]{4,1,3,2,0:T(8,128)(2,1)} %get-tuple-element.9), channel_id=1, source_target_pairs={{0,4},{4,8},{8,12},{1,5},{5,9},{9,13},{2,6},{6,10},{10,14},{3,7},{... | collective-permute-start | bytes 1474568 | tf_op jit(solution)/shard_map/ppermute | solution.py:14
  9.9 2.4 %collective-permute-start.1 = (bf16[2,24,1,8,640]{4,1,3,2,0:T(8,128)(2,1)S(1)}, bf16[2,24,1,8,640]{4,1,3,2,0:T(8,128)(2,1)S(1)}, u32[]{:S(2)}, u32[]{:S(2)}) collective-permute-start(bf16[2,24,1,8,640]{4,1,3,2,0:T(8,128)(2,1)S(1)} %get-tuple-element.10), channel_id=1, source_target_pairs={{4,0},{8,4},{12,8},{5,1},{9,5},{13,9},{6,2},{10,6},{14,10},{7,3},{... | collective-permute-start | bytes 1474568 | tf_op jit(solution)/shard_map/ppermute | solution.py:17
  12.6 2.9 %constant_dynamic-update-slice_fusion.5 = bf16[3,3,640,640]{3,2,1,0:T(8,128)(2,1)} fusion(bf16[3,3,160,640]{3,2,1,0:T(8,128)(2,1)} %param.25), kind=kLoop, calls=%fused_computation.72 | loop fusion | bytes 3686400
  15.5 2.9 %constant_dynamic-update-slice_fusion.11 = bf16[3,3,640,640]{3,2,1,0:T(8,128)(2,1)} fusion(bf16[3,3,160,640]{3,2,1,0:T(8,128)(2,1)} %param.32), kind=kLoop, calls=%fused_computation.78 | loop fusion | bytes 3686400
  18.4 12.3 %collective-permute-done = bf16[2,24,1,8,640]{4,1,3,2,0:T(8,128)(2,1)S(1)} collective-permute-done((bf16[2,24,1,8,640]{4,1,3,2,0:T(8,128)(2,1)}, bf16[2,24,1,8,640]{4,1,3,2,0:T(8,128)(2,1)S(1)}, u32[]{:S(2)}, u32[]{:S(2)}) %collective-permute-start) | collective-permute-done | bytes 491552 | tf_op jit(solution)/shard_map/ppermute | solution.py:14
  30.7 0.7 collective-permute-done.1
  31.5 1.0 pad_maximum_fusion.6
  32.5 4.2 %collective-permute-start.2 = (bf16[2,24,6,1,640]{4,1,3,2,0:T(8,128)(2,1)}, bf16[2,24,6,1,640]{4,1,3,2,0:T(8,128)(2,1)}, u32[]{:S(2)}, u32[]{:S(2)}) collective-permute-start(bf16[2,24,6,1,640]{4,1,3,2,0:T(8,128)(2,1)} %get-tuple-element.7), channel_id=1, source_target_pairs={{0,1},{1,2},{2,3},{4,5},{5,6},{6,7},{8,9},{9,10},{10,11},{12,13},{... | collective-permute-start | bytes 1105928 | tf_op jit(solution)/shard_map/ppermute | solution.py:14
  36.7 1.3 collective-permute-start.3
  38.0 0.2 broadcast_in_dim.29
  38.2 0.2 mul.115
  38.6 0.2 sub.65
  38.9 0.2 mul.128
  39.3 0.8 sub.75
  40.2 1.3 dynamic-slice_bitcast_fusion
  41.5 3.7 %collective-permute-done.3 = bf16[2,24,6,1,640]{4,1,3,2,0:T(8,128)(2,1)} collective-permute-done((bf16[2,24,6,1,640]{4,1,3,2,0:T(8,128)(2,1)}, bf16[2,24,6,1,640]{4,1,3,2,0:T(8,128)(2,1)}, u32[]{:S(2)}, u32[]{:S(2)}) %collective-permute-start.3) | collective-permute-done | bytes 368672 | tf_op jit(solution)/shard_map/ppermute | solution.py:17
  45.2 3.0 %pad_maximum_fusion = bf16[2,24,6,10,640]{4,1,3,2,0:T(8,128)(2,1)S(1)} fusion(bf16[2,24,6,1,640]{4,1,3,2,0:T(8,128)(2,1)} %collective-permute-done.3, bf16[2,24,1,8,640]{4,1,3,2,0:T(8,128)(2,1)S(1)} %collective-permute-done.1, bf16[1,24,4,8,640]{4,1,3,2,0:T(8,128)(2,1)S(1)} %get-tuple-element.15, bf16[1,24,4,8,640]{4,1,3,2,0:T(8,128)(2,1)S(1)} %get-tuple-element.16, ...), kind=kLoop, calls=%fused_computation | loop fusion | flops 9216000 | bytes 7372800 | tf_op jit(solution)/shard_map/concatenate | solution.py:18
  48.2 3.3 %fusion.27 = bf16[24,6,10,640]{3,0,2,1:T(8,128)(2,1)S(1)} fusion(bf16[2,24,6,10,640]{4,1,3,2,0:T(8,128)(2,1)S(1)} %pad_maximum_fusion, f32[6,10]{1,0:T(8,128)S(1)} %and_convert_fusion, f32[640]{0:T(1024)S(1)} %copy-done.14, f32[640]{0:T(1024)S(1)} %copy-done.15, f32[24,640]{1,0:T(8,128)S(1)} %mul.115, f32[24,640]{1,0:T(8,128)S(1)} %sub.65, s32[640]{0:T(1024)S(1)} %fusion.73), kind=kOutput, calls=%fused_computation.33 | convolution fusion | flops 1191116800 | bytes 3825664 | tf_op jit(solution)/shard_map/dot_general | solution.py:72
  51.7 1.3 collective-permute-start.6
  53.0 2.1 %fusion.17 = f32[24,6,10,640]{3,0,2,1:T(8,128)} fusion(bf16[2,24,6,10,640]{4,1,3,2,0:T(8,128)(2,1)S(1)} %pad_maximum_fusion), kind=kLoop, calls=%fused_computation.22 | loop fusion | flops 921600 | bytes 5529600 | tf_op jit(solution)/shard_map/convert_element_type | solution.py:127
  55.0 4.6 %fusion.26 = bf16[24,6,10,640]{3,0,2,1:T(8,128)(2,1)} fusion(f32[640]{0:T(1024)S(1)} %copy-done.12, f32[640]{0:T(1024)S(1)} %copy-done.13, f32[24,640]{1,0:T(8,128)S(1)} %mul.128, f32[24,640]{1,0:T(8,128)S(1)} %copy-done.4, f32[6,10]{1,0:T(8,128)S(1)} %and_convert_fusion, s32[640]{0:T(1024)S(1)} %fusion.73, bf16[2,24,6,10,640]{4,1,3,2,0:T(8,128)(2,1)S(1)} %pad_maximum_fusion), kind=kOutput, calls=%fused_computation.32 | convolution fusion | flops 1190195200 | bytes 3825664 | tf_op jit(solution)/shard_map/dot_general | solution.py:72
  59.6 3.4 %collective-permute-start.7 = (bf16[3,3,80,640]{3,2,1,0:T(8,128)(2,1)}, bf16[3,3,80,640]{3,2,1,0:T(8,128)(2,1)S(1)}, u32[]{:S(2)}, u32[]{:S(2)}) collective-permute-start(bf16[3,3,80,640]{3,2,1,0:T(8,128)(2,1)} %collective-permute-done.5), channel_id=1, source_target_pairs={{0,4},{4,0},{8,12},{12,8},{1,5},{5,1},{9,13},{13,9},{2,6},{6,2},{1... | collective-permute-start | bytes 2764808 | tf_op jit(solution)/shard_map/ppermute | solution.py:42
  63.1 7.7 %collective-permute-done.6 = bf16[3,3,80,640]{3,2,1,0:T(8,128)(2,1)S(1)} collective-permute-done((bf16[3,3,80,640]{3,2,1,0:T(8,128)(2,1)}, bf16[3,3,80,640]{3,2,1,0:T(8,128)(2,1)S(1)}, u32[]{:S(2)}, u32[]{:S(2)}) %collective-permute-start.6) | collective-permute-done | bytes 921632 | tf_op jit(solution)/shard_map/ppermute | solution.py:41
  70.7 4.1 %collective-permute-start.8 = (bf16[3,3,80,640]{3,2,1,0:T(8,128)(2,1)S(1)}, bf16[3,3,80,640]{3,2,1,0:T(8,128)(2,1)S(1)}, u32[]{:S(2)}, u32[]{:S(2)}) collective-permute-start(bf16[3,3,80,640]{3,2,1,0:T(8,128)(2,1)S(1)} %collective-permute-done.6), channel_id=1, source_target_pairs={{0,4},{4,0},{8,12},{12,8},{1,5},{5,1},{9,13},{13,9},{2,6},{6,2},{1... | collective-permute-start | bytes 2764808 | tf_op jit(solution)/shard_map/ppermute | solution.py:43
  74.8 1.2 collective-permute-start.11
  76.1 0.3 collective-permute-start.12
  76.4 2.9 %constant_dynamic-update-slice_fusion.4 = bf16[3,3,640,640]{3,2,1,0:T(8,128)(2,1)} fusion(bf16[3,3,640,640]{3,2,1,0:T(8,128)(2,1)} %constant_dynamic-update-slice_fusion.5, bf16[3,3,160,640]{3,2,1,0:T(8,128)(2,1)} %collective-permute-done.4), kind=kLoop, calls=%fused_computation.71 | loop fusion | bytes 3686400
  79.3 2.2 %constant_dynamic-update-slice_fusion.3 = bf16[3,3,640,640]{3,2,1,0:T(8,128)(2,1)} fusion(bf16[3,3,640,640]{3,2,1,0:T(8,128)(2,1)} %constant_dynamic-update-slice_fusion.4, bf16[3,3,80,640]{3,2,1,0:T(8,128)(2,1)} %collective-permute-done.5), kind=kLoop, calls=%fused_computation.70 | loop fusion | bytes 1843200
  81.5 1.0 constant_dynamic-update-slice_fusion.2
  82.5 2.9 %constant_dynamic-update-slice_fusion.10 = bf16[3,3,640,640]{3,2,1,0:T(8,128)(2,1)} fusion(bf16[3,3,640,640]{3,2,1,0:T(8,128)(2,1)} %constant_dynamic-update-slice_fusion.11, bf16[3,3,160,640]{3,2,1,0:T(8,128)(2,1)} %collective-permute-done.9), kind=kLoop, calls=%fused_computation.77 | loop fusion | bytes 3686400
  85.5 1.1 constant_dynamic-update-slice_fusion.9
  86.5 1.0 constant_dynamic-update-slice_fusion.1
  87.6 9.3 %collective-permute-done.11 = bf16[3,3,80,640]{3,2,1,0:T(8,128)(2,1)S(1)} collective-permute-done((bf16[3,3,80,640]{3,2,1,0:T(8,128)(2,1)S(1)}, bf16[3,3,80,640]{3,2,1,0:T(8,128)(2,1)S(1)}, u32[]{:S(2)}, u32[]{:S(2)}) %collective-permute-start.11) | collective-permute-done | bytes 921632 | tf_op jit(solution)/shard_map/ppermute | solution.py:41
  96.9 0.8 collective-permute-start.13
  97.7 1.0 constant_dynamic-update-slice_fusion
  98.7 13.4 %fusion.38 = bf16[24,6,10,640]{3,0,2,1:T(8,128)(2,1)} fusion(bf16[24,6,10,640]{3,0,2,1:T(8,128)(2,1)} %copy-done.2, bf16[3,3,640,640]{3,2,1,0:T(8,128)(2,1)} %constant_dynamic-update-slice_fusion, bf16[24,6,10,640]{3,0,2,1:T(8,128)(2,1)} %fusion.26, f32[640]{0:T(1024)S(1)} %copy-done.14, f32[640]{0:T(1024)S(1)} %copy-done.15, f32[24,640]{1,0:T(8,128)S(1)} %mul.115, ...), kind=kOutput, calls=%fused_computation.38 | convolution fusion | flops 6297763840 | bytes 10393600 | tf_op jit(solution)/shard_map/dot_general | solution.py:72
  112.1 1.0 constant_dynamic-update-slice_fusion.8
  113.1 1.0 constant_dynamic-update-slice_fusion.7
  114.2 2.3 %constant_dynamic-update-slice_fusion.6 = bf16[3,3,640,640]{3,2,1,0:T(8,128)(2,1)} fusion(bf16[3,3,640,640]{3,2,1,0:T(8,128)(2,1)} %constant_dynamic-update-slice_fusion.7, bf16[3,3,80,640]{3,2,1,0:T(8,128)(2,1)} %collective-permute-done.13), kind=kLoop, calls=%fused_computation.73 | loop fusion | bytes 1843200 | tf_op jit(solution)/shard_map/concatenate | solution.py:48
  116.5 2.6 %fusion.12 = f32[48,4,1,640]{3,0,2,1:T(8,128)S(1)} fusion(bf16[3,3,640,640]{3,2,1,0:T(8,128)(2,1)} %constant_dynamic-update-slice_fusion.6, bf16[24,6,1,640]{3,0,2,1:T(8,128)(2,1)S(1)} %get-tuple-element.13, bf16[24,6,1,640]{3,0,2,1:T(8,128)(2,1)S(1)} %get-tuple-element.11), kind=kOutput, calls=%fused_computation.15 | convolution fusion | flops 472596480 | bytes 3317760 | tf_op jit(solution)/shard_map/conv_general_dilated | solution.py:81
  119.1 2.7 %fusion.10 = f32[48,4,1,640]{3,0,2,1:T(8,128)S(1)} fusion(bf16[3,3,640,640]{3,2,1,0:T(8,128)(2,1)} %constant_dynamic-update-slice_fusion.6, bf16[24,6,1,640]{3,0,2,1:T(8,128)(2,1)S(1)} %get-tuple-element.14, bf16[24,6,1,640]{3,0,2,1:T(8,128)(2,1)S(1)} %get-tuple-element.12), kind=kOutput, calls=%fused_computation.13 | convolution fusion | flops 472596480 | bytes 3317760 | tf_op jit(solution)/shard_map/conv_general_dilated | solution.py:81
  121.9 0.4 copy-done
  122.3 7.2 %fusion.43 = bf16[24,4,8,640]{3,0,2,1:T(8,128)(2,1)S(1)} fusion(f32[24,6,10,640]{3,0,2,1:T(8,128)S(1)} %copy-done, f32[24,4,1,640]{3,0,2,1:T(8,128)S(1)} %slice_subtract_fusion, f32[24,4,1,640]{3,0,2,1:T(8,128)S(1)} %slice_subtract_fusion.1, bf16[24,6,10,640]{3,0,2,1:T(8,128)(2,1)S(1)} %copy-done.3, bf16[3,3,640,640]{3,2,1,0:T(8,128)(2,1)S(1)} %copy-done.1, ...), kind=kOutput, calls=%fused_computation.39 | convolution fusion | flops 5665259520 | bytes 13642432 | tf_op jit(solution)/shard_map/conv_general_dilated | solution.py:81
  129.6 1.1 copy.43
  (61 shorter events, 1.1 us)
Async XLA Ops:
  0.0 76.1 %collective-permute-start.4 = (bf16[3,3,160,640]{3,2,1,0:T(8,128)(2,1)}, bf16[3,3,160,640]{3,2,1,0:T(8,128)(2,1)}, u32[]{:S(2)}, u32[]{:S(2)}) collective-permute-start(bf16[3,3,160,640]{3,2,1,0:T(8,128)(2,1)} %param.25), channel_id=1, source_target_pairs={{0,4},{4,0},{8,12},{12,8},{1,5},{5,1},{9,13},{13,9},{2,6},{6,2},{1... | collective-permute-start | bytes 5529608 | tf_op jit(solution)/shard_map/ppermute | solution.py:34
  2.2 10.2 %copy-start.9 = (s32[24,16]{0,1:T(8,128)S(1)}, s32[24,16]{0,1:T(8,128)}, u32[]{:S(2)}) copy-start(s32[24,16]{0,1:T(8,128)} %param.20) | copy-start | bytes 4612
  2.2 49.3 %collective-permute-start.5 = (bf16[3,3,80,640]{3,2,1,0:T(8,128)(2,1)}, bf16[3,3,80,640]{3,2,1,0:T(8,128)(2,1)}, u32[]{:S(2)}, u32[]{:S(2)}) collective-permute-start(bf16[3,3,80,640]{3,2,1,0:T(8,128)(2,1)} %dynamic-slice_bitcast_fusion.1), channel_id=1, source_target_pairs={{8,0},{12,4},{0,8},{4,12},{9,1},{13,5},{1,9},{5,13},{10,2},{14,6},... | collective-permute-start | bytes 2764808 | tf_op jit(solution)/shard_map/ppermute | solution.py:39
  8.0 22.8 %collective-permute-start = (bf16[2,24,1,8,640]{4,1,3,2,0:T(8,128)(2,1)}, bf16[2,24,1,8,640]{4,1,3,2,0:T(8,128)(2,1)S(1)}, u32[]{:S(2)}, u32[]{:S(2)}) collective-permute-start(bf16[2,24,1,8,640]{4,1,3,2,0:T(8,128)(2,1)} %get-tuple-element.9), channel_id=1, source_target_pairs={{0,4},{4,8},{8,12},{1,5},{5,9},{9,13},{2,6},{6,10},{10,14},{3,7},{... | collective-permute-start | bytes 1474568 | tf_op jit(solution)/shard_map/ppermute | solution.py:14
  9.9 21.6 %collective-permute-start.1 = (bf16[2,24,1,8,640]{4,1,3,2,0:T(8,128)(2,1)S(1)}, bf16[2,24,1,8,640]{4,1,3,2,0:T(8,128)(2,1)S(1)}, u32[]{:S(2)}, u32[]{:S(2)}) collective-permute-start(bf16[2,24,1,8,640]{4,1,3,2,0:T(8,128)(2,1)S(1)} %get-tuple-element.10), channel_id=1, source_target_pairs={{4,0},{8,4},{12,8},{5,1},{9,5},{13,9},{6,2},{10,6},{14,10},{7,3},{... | collective-permute-start | bytes 1474568 | tf_op jit(solution)/shard_map/ppermute | solution.py:17
  12.3 70.2 %collective-permute-start.9 = (bf16[3,3,160,640]{3,2,1,0:T(8,128)(2,1)}, bf16[3,3,160,640]{3,2,1,0:T(8,128)(2,1)}, u32[]{:S(2)}, u32[]{:S(2)}) collective-permute-start(bf16[3,3,160,640]{3,2,1,0:T(8,128)(2,1)} %param.32), channel_id=1, source_target_pairs={{0,4},{4,0},{8,12},{12,8},{1,5},{5,1},{9,13},{13,9},{2,6},{6,2},{1... | collective-permute-start | bytes 5529608 | tf_op jit(solution)/shard_map/ppermute | solution.py:34
  15.5 22.5 %copy-start.5 = (f32[24,32]{1,0:T(8,128)S(1)}, f32[24,32]{1,0:T(8,128)}, u32[]{:S(2)}) copy-start(f32[24,32]{1,0:T(8,128)} %param.29) | copy-start | bytes 9220
  15.5 22.9 %copy-start.6 = (f32[24,32]{1,0:T(8,128)S(1)}, f32[24,32]{1,0:T(8,128)}, u32[]{:S(2)}) copy-start(f32[24,32]{1,0:T(8,128)} %param.28) | copy-start | bytes 9220
  15.5 23.3 %copy-start.7 = (f32[24,32]{1,0:T(8,128)S(1)}, f32[24,32]{1,0:T(8,128)}, u32[]{:S(2)}) copy-start(f32[24,32]{1,0:T(8,128)} %param.22) | copy-start | bytes 9220
  18.4 20.8 %copy-start.8 = (f32[24,32]{1,0:T(8,128)S(1)}, f32[24,32]{1,0:T(8,128)}, u32[]{:S(2)}) copy-start(f32[24,32]{1,0:T(8,128)} %param.21) | copy-start | bytes 9220
  32.5 9.0 %collective-permute-start.2 = (bf16[2,24,6,1,640]{4,1,3,2,0:T(8,128)(2,1)}, bf16[2,24,6,1,640]{4,1,3,2,0:T(8,128)(2,1)}, u32[]{:S(2)}, u32[]{:S(2)}) collective-permute-start(bf16[2,24,6,1,640]{4,1,3,2,0:T(8,128)(2,1)} %get-tuple-element.7), channel_id=1, source_target_pairs={{0,1},{1,2},{2,3},{4,5},{5,6},{6,7},{8,9},{9,10},{10,11},{12,13},{... | collective-permute-start | bytes 1105928 | tf_op jit(solution)/shard_map/ppermute | solution.py:14
  36.7 8.6 %collective-permute-start.3 = (bf16[2,24,6,1,640]{4,1,3,2,0:T(8,128)(2,1)}, bf16[2,24,6,1,640]{4,1,3,2,0:T(8,128)(2,1)}, u32[]{:S(2)}, u32[]{:S(2)}) collective-permute-start(bf16[2,24,6,1,640]{4,1,3,2,0:T(8,128)(2,1)} %get-tuple-element.8), channel_id=1, source_target_pairs={{1,0},{2,1},{3,2},{5,4},{6,5},{7,6},{9,8},{10,9},{11,10},{13,12},{... | collective-permute-start | bytes 1105928 | tf_op jit(solution)/shard_map/ppermute | solution.py:17
  41.5 6.7 %copy-start.14 = (f32[640]{0:T(1024)S(1)}, f32[640]{0:T(1024)}, u32[]{:S(2)}) copy-start(f32[640]{0:T(1024)} %param.31) | copy-start | bytes 7684
  41.5 6.7 %copy-start.15 = (f32[640]{0:T(1024)S(1)}, f32[640]{0:T(1024)}, u32[]{:S(2)}) copy-start(f32[640]{0:T(1024)} %param.30) | copy-start | bytes 7684
  51.5 24.5 %copy-start.2 = (bf16[24,6,10,640]{3,0,2,1:T(8,128)(2,1)}, bf16[24,6,10,640]{3,0,2,1:T(8,128)(2,1)S(1)}, u32[]{:S(2)}) copy-start(bf16[24,6,10,640]{3,0,2,1:T(8,128)(2,1)S(1)} %fusion.27) | copy-start | bytes 5529604
  51.5 3.5 %copy-start.4 = (f32[24,640]{1,0:T(8,128)S(1)}, f32[24,640]{1,0:T(8,128)}, u32[]{:S(2)}) copy-start(f32[24,640]{1,0:T(8,128)} %sub.75) | copy-start | bytes 184324
  51.5 3.5 %copy-start.12 = (f32[640]{0:T(1024)S(1)}, f32[640]{0:T(1024)}, u32[]{:S(2)}) copy-start(f32[640]{0:T(1024)} %param.24) | copy-start | bytes 7684
  51.6 3.5 %copy-start.13 = (f32[640]{0:T(1024)S(1)}, f32[640]{0:T(1024)}, u32[]{:S(2)}) copy-start(f32[640]{0:T(1024)} %param.23) | copy-start | bytes 7684
  51.6 23.2 %collective-permute-start.10 = (bf16[3,3,80,640]{3,2,1,0:T(8,128)(2,1)S(1)}, bf16[3,3,80,640]{3,2,1,0:T(8,128)(2,1)S(1)}, u32[]{:S(2)}, u32[]{:S(2)}) collective-permute-start(bf16[3,3,80,640]{3,2,1,0:T(8,128)(2,1)S(1)} %dynamic-slice_bitcast_fusion), channel_id=1, source_target_pairs={{8,0},{12,4},{0,8},{4,12},{9,1},{13,5},{1,9},{5,13},{10,2},{14,6},... | collective-permute-start | bytes 2764808 | tf_op jit(solution)/shard_map/ppermute | solution.py:39
  51.7 19.1 %collective-permute-start.6 = (bf16[3,3,80,640]{3,2,1,0:T(8,128)(2,1)}, bf16[3,3,80,640]{3,2,1,0:T(8,128)(2,1)S(1)}, u32[]{:S(2)}, u32[]{:S(2)}) collective-permute-start(bf16[3,3,80,640]{3,2,1,0:T(8,128)(2,1)} %collective-permute-done.5), channel_id=1, source_target_pairs={{0,16},{16,0},{1,17},{17,1},{2,18},{18,2},{3,19},{19,3},{4,20},{20... | collective-permute-start | bytes 2764808 | tf_op jit(solution)/shard_map/ppermute | solution.py:41
  59.6 26.9 %collective-permute-start.7 = (bf16[3,3,80,640]{3,2,1,0:T(8,128)(2,1)}, bf16[3,3,80,640]{3,2,1,0:T(8,128)(2,1)S(1)}, u32[]{:S(2)}, u32[]{:S(2)}) collective-permute-start(bf16[3,3,80,640]{3,2,1,0:T(8,128)(2,1)} %collective-permute-done.5), channel_id=1, source_target_pairs={{0,4},{4,0},{8,12},{12,8},{1,5},{5,1},{9,13},{13,9},{2,6},{6,2},{1... | collective-permute-start | bytes 2764808 | tf_op jit(solution)/shard_map/ppermute | solution.py:42
  70.7 26.9 %collective-permute-start.8 = (bf16[3,3,80,640]{3,2,1,0:T(8,128)(2,1)S(1)}, bf16[3,3,80,640]{3,2,1,0:T(8,128)(2,1)S(1)}, u32[]{:S(2)}, u32[]{:S(2)}) collective-permute-start(bf16[3,3,80,640]{3,2,1,0:T(8,128)(2,1)S(1)} %collective-permute-done.6), channel_id=1, source_target_pairs={{0,4},{4,0},{8,12},{12,8},{1,5},{5,1},{9,13},{13,9},{2,6},{6,2},{1... | collective-permute-start | bytes 2764808 | tf_op jit(solution)/shard_map/ppermute | solution.py:43
  74.8 22.1 %collective-permute-start.11 = (bf16[3,3,80,640]{3,2,1,0:T(8,128)(2,1)S(1)}, bf16[3,3,80,640]{3,2,1,0:T(8,128)(2,1)S(1)}, u32[]{:S(2)}, u32[]{:S(2)}) collective-permute-start(bf16[3,3,80,640]{3,2,1,0:T(8,128)(2,1)S(1)} %collective-permute-done.10), channel_id=1, source_target_pairs={{0,16},{16,0},{1,17},{17,1},{2,18},{18,2},{3,19},{19,3},{4,20},{20... | collective-permute-start | bytes 2764808 | tf_op jit(solution)/shard_map/ppermute | solution.py:41
  76.1 37.0 %collective-permute-start.12 = (bf16[3,3,80,640]{3,2,1,0:T(8,128)(2,1)S(1)}, bf16[3,3,80,640]{3,2,1,0:T(8,128)(2,1)S(1)}, u32[]{:S(2)}, u32[]{:S(2)}) collective-permute-start(bf16[3,3,80,640]{3,2,1,0:T(8,128)(2,1)S(1)} %collective-permute-done.10), channel_id=1, source_target_pairs={{0,4},{4,0},{8,12},{12,8},{1,5},{5,1},{9,13},{13,9},{2,6},{6,2},{1... | collective-permute-start | bytes 2764808 | tf_op jit(solution)/shard_map/ppermute | solution.py:42
  85.5 13.2 %copy-start.11 = (f32[24,640]{1,0:T(8,128)S(1)}, f32[24,640]{1,0:T(8,128)}, u32[]{:S(2)}) copy-start(f32[24,640]{1,0:T(8,128)} %param.27) | copy-start | bytes 184324
  85.5 13.2 %copy-start.16 = (f32[640]{0:T(1024)S(1)}, f32[640]{0:T(1024)}, u32[]{:S(2)}) copy-start(f32[640]{0:T(1024)} %param.26) | copy-start | bytes 7684
  96.9 17.3 %collective-permute-start.13 = (bf16[3,3,80,640]{3,2,1,0:T(8,128)(2,1)S(1)}, bf16[3,3,80,640]{3,2,1,0:T(8,128)(2,1)}, u32[]{:S(2)}, u32[]{:S(2)}) collective-permute-start(bf16[3,3,80,640]{3,2,1,0:T(8,128)(2,1)S(1)} %collective-permute-done.11), channel_id=1, source_target_pairs={{0,4},{4,0},{8,12},{12,8},{1,5},{5,1},{9,13},{13,9},{2,6},{6,2},{1... | collective-permute-start | bytes 2764808 | tf_op jit(solution)/shard_map/ppermute | solution.py:43
  112.1 2.0 %copy-start.3 = (bf16[24,6,10,640]{3,0,2,1:T(8,128)(2,1)S(1)}, bf16[24,6,10,640]{3,0,2,1:T(8,128)(2,1)}, u32[]{:S(2)}) copy-start(bf16[24,6,10,640]{3,0,2,1:T(8,128)(2,1)} %fusion.38) | copy-start | bytes 5529604
  114.1 7.7 %copy-start.10 = (bf16[24,4,8,640]{3,2,1,0:T(8,128)(2,1)S(1)}, bf16[24,4,8,640]{3,2,1,0:T(8,128)(2,1)}, u32[]{:S(2)}) copy-start(bf16[24,4,8,640]{3,2,1,0:T(8,128)(2,1)} %param.19) | copy-start | bytes 2949124
  116.4 5.4 %copy-start.1 = (bf16[3,3,640,640]{3,2,1,0:T(8,128)(2,1)S(1)}, bf16[3,3,640,640]{3,2,1,0:T(8,128)(2,1)}, u32[]{:S(2)}) copy-start(bf16[3,3,640,640]{3,2,1,0:T(8,128)(2,1)} %constant_dynamic-update-slice_fusion.6) | copy-start | bytes 22118404
  119.1 3.3 %copy-start = (f32[24,6,10,640]{3,0,2,1:T(8,128)S(1)}, f32[24,6,10,640]{3,0,2,1:T(8,128)}, u32[]{:S(2)}) copy-start(f32[24,6,10,640]{3,0,2,1:T(8,128)} %fusion.17) | copy-start | bytes 11059204
  119.1 3.3 %copy-start.17 = (f32[640]{0:T(1024)S(1)}, f32[640]{0:T(1024)}, u32[]{:S(2)}) copy-start(f32[640]{0:T(1024)} %param.33) | copy-start | bytes 7684

commit v6 on v5

--- a/solution.py
+++ b/solution.py
@@ -19,15 +19,15 @@
     return block
 
 
-def gather_weights(kernels):
+def gather_weights(kernels, swap_axes):
     count = lax.axis_size("row")
     chips = count // 2
-    y_pairs = [(i, i ^ 1) for i in range(lax.axis_size("groups"))]
     mate_pairs = [(i, i ^ 1) for i in range(count)]
-    parity = lax.axis_index("groups") % 2
     wholes = []
     previous = None
-    for shard in kernels:
+    for shard, swap_axis in zip(kernels, swap_axes):
+        swap_pairs = [(i, i ^ 1) for i in range(lax.axis_size(swap_axis))]
+        parity = lax.axis_index(swap_axis) % 2
         depth = shard.shape[2]
         halves = shard.reshape(shard.shape[:2] + (2, depth // 2) + shard.shape[3:])
         mine = lax.dynamic_index_in_dim(halves, parity, axis=2, keepdims=False)
@@ -38,7 +38,7 @@
             pairs = [(((i // 2 + step) % chips) * 2 + i % 2, i) for i in range(count)]
             fetched = lax.ppermute(mine, "row", pairs)
             previous = fetched
-            other = lax.ppermute(fetched, "groups", y_pairs)
+            other = lax.ppermute(fetched, swap_axis, swap_pairs)
             relayed = lax.ppermute(fetched, "row", mate_pairs)
             other_relayed = lax.ppermute(other, "row", mate_pairs)
             held += [
@@ -49,7 +49,7 @@
     return wholes
 
 
-def relative_order(channels):
+def relative_order(channels, swap_axis):
     count = lax.axis_size("row")
     chips = count // 2
     depth = channels // count
@@ -61,7 +61,7 @@
     within = position % depth
     source = 2 * ((chip + block // 2) % chips) + jnp.where(block % 2 == 0, core, 1 - core)
     half = depth // 2
-    parity = lax.axis_index("groups") % 2
+    parity = lax.axis_index(swap_axis) % 2
     shuffled = (parity ^ (within // half)) * half + within % half
     return source * depth + jnp.where(block >= 2, shuffled, within)
 
@@ -116,8 +116,9 @@
     groups_total = norm1_mean.shape[1]
     per_group = channels // groups_total
 
-    first_whole, second_whole = gather_weights([conv1_weight, conv2_weight])
-    order = relative_order(channels)
+    first_whole, second_whole = gather_weights([conv1_weight, conv2_weight], ("groups", "col"))
+    first_order = relative_order(channels, "groups")
+    order = relative_order(channels, "col")
 
     def expand(values):
         return jnp.repeat(values, per_group, axis=1)[:, None, None, :]
@@ -143,7 +144,7 @@
         * inside
     ).astype(jnp.bfloat16)
     fresh_mid = (
-        conv_relative(first_act, first_whole, order) + conv1_bias + step_embed[:, None, None, :]
+        conv_relative(first_act, first_whole, first_order) + conv1_bias + step_embed[:, None, None, :]
     )
 
     if tiles_down != 1:

time: 131 us -> 131 us (level)
  transfers between devices with their start and end apart: 14 -> 14, of which waited for: 5 -> 5; matrix products, arithmetic and copies ran while one was open for 43% -> 44% of each run, Pallas kernels for 0% -> 0%
where the time goes in v6:
time: 131 us
  matrix products  33.8 us (26%)
  waiting for transfers between devices  33.1 us (25%)
  local copies, waits for them, and re-layouts  31.7 us (24%)
  starting transfers between devices  23.2 us (18%)
  other arithmetic  8.49 us (6%)
    dot_general x3, matrix products, to_relative(): moved = jnp.dot(activation, chooser, preferred_element_type=jnp.float32)  21.3 us
    unnamed x46, local copies, waits for them, and re-layouts  19.5 us
    ppermute x2, waiting for transfers between devices, gather_weights(): other = lax.ppermute(fetched, swap_axis, swap_pairs)  17.6 us
    conv_general_dilated x3, matrix products, conv_valid(): lax.conv_general_dilated(activation, kernel, window_strides=(1, 1), paddi...  12.6 us
    ppermute x2, waiting for transfers between devices, padded_2(): lax.ppermute(lax.slice_in_dim(block, block.shape[dim] - width, None, axis...  12.3 us
    ppermute x2, starting transfers between devices, padded_2(): lax.ppermute(lax.slice_in_dim(block, block.shape[dim] - width, None, axis...  6.1 us
    ppermute x2, starting transfers between devices, gather_weights(): other_relayed = lax.ppermute(other, 'row', mate_pairs)  4.84 us
    ppermute x2, starting transfers between devices, gather_weights(): relayed = lax.ppermute(fetched, 'row', mate_pairs)  3.77 us
  transfers between devices with their start and end apart: 14, of which 5 were waited for; matrix products, arithmetic and copies ran while one was open for 44% of the time, Pallas kernels for 0%

profile of v6, /device:TPU:1, one launch (start us, length us, event | category | flops | bytes accessed | tf_op | source)
XLA Modules:
  0.0 130.6 jit_solution(4408962918522963043)
XLA Ops:
  0.1 2.2 %dynamic-slice_bitcast_fusion.1 = bf16[3,3,80,640]{3,2,1,0:T(8,128)(2,1)} fusion(bf16[3,3,2,80,640]{4,3,2,1,0:T(8,128)(2,1)} %bitcast.50, s32[]{:T(128)S(6)} %select_n.186), kind=kLoop, calls=%fused_computation.51 | loop fusion | bytes 1843204 | tf_op jit(solution)/shard_map/jit(dynamic_index_in_dim)/squeeze | solution.py:33
  2.2 2.7 %collective-permute-start.5 = (bf16[3,3,80,640]{3,2,1,0:T(8,128)(2,1)}, bf16[3,3,80,640]{3,2,1,0:T(8,128)(2,1)}, u32[]{:S(2)}, u32[]{:S(2)}) collective-permute-start(bf16[3,3,80,640]{3,2,1,0:T(8,128)(2,1)} %dynamic-slice_bitcast_fusion.1), channel_id=1, source_target_pairs={{8,0},{12,4},{0,8},{4,12},{9,1},{13,5},{1,9},{5,13},{10,2},{14,6},... | collective-permute-start | bytes 2764808 | tf_op jit(solution)/shard_map/ppermute | solution.py:39
  4.9 2.1 %copy_bitcast_fusion = (bf16[1,24,4,8,640]{4,1,3,2,0:T(8,128)(2,1)S(1)}, bf16[1,24,4,8,640]{4,1,3,2,0:T(8,128)(2,1)S(1)}) fusion(bf16[24,4,8,640]{3,2,1,0:T(8,128)(2,1)} %param.18, bf16[24,4,8,640]{3,2,1,0:T(8,128)(2,1)} %param.17), kind=kLoop, calls=%fused_computation.42 | loop fusion | bytes 3932160 | tf_op jit(solution)/shard_map/stack | solution.py:126
  7.1 0.9 pad_maximum_fusion.2
  8.0 1.9 %collective-permute-start = (bf16[2,24,1,8,640]{4,1,3,2,0:T(8,128)(2,1)}, bf16[2,24,1,8,640]{4,1,3,2,0:T(8,128)(2,1)S(1)}, u32[]{:S(2)}, u32[]{:S(2)}) collective-permute-start(bf16[2,24,1,8,640]{4,1,3,2,0:T(8,128)(2,1)} %get-tuple-element.9), channel_id=1, source_target_pairs={{0,4},{4,8},{8,12},{1,5},{5,9},{9,13},{2,6},{6,10},{10,14},{3,7},{... | collective-permute-start | bytes 1474568 | tf_op jit(solution)/shard_map/ppermute | solution.py:14
  9.9 2.4 %collective-permute-start.1 = (bf16[2,24,1,8,640]{4,1,3,2,0:T(8,128)(2,1)S(1)}, bf16[2,24,1,8,640]{4,1,3,2,0:T(8,128)(2,1)S(1)}, u32[]{:S(2)}, u32[]{:S(2)}) collective-permute-start(bf16[2,24,1,8,640]{4,1,3,2,0:T(8,128)(2,1)S(1)} %get-tuple-element.10), channel_id=1, source_target_pairs={{4,0},{8,4},{12,8},{5,1},{9,5},{13,9},{6,2},{10,6},{14,10},{7,3},{... | collective-permute-start | bytes 1474568 | tf_op jit(solution)/shard_map/ppermute | solution.py:17
  12.6 2.9 %constant_dynamic-update-slice_fusion.5 = bf16[3,3,640,640]{3,2,1,0:T(8,128)(2,1)} fusion(bf16[3,3,160,640]{3,2,1,0:T(8,128)(2,1)} %param.25), kind=kLoop, calls=%fused_computation.74 | loop fusion | bytes 3686400
  15.5 2.9 %constant_dynamic-update-slice_fusion.11 = bf16[3,3,640,640]{3,2,1,0:T(8,128)(2,1)} fusion(bf16[3,3,160,640]{3,2,1,0:T(8,128)(2,1)} %param.32), kind=kLoop, calls=%fused_computation.80 | loop fusion | bytes 3686400
  18.5 12.3 %collective-permute-done = bf16[2,24,1,8,640]{4,1,3,2,0:T(8,128)(2,1)S(1)} collective-permute-done((bf16[2,24,1,8,640]{4,1,3,2,0:T(8,128)(2,1)}, bf16[2,24,1,8,640]{4,1,3,2,0:T(8,128)(2,1)S(1)}, u32[]{:S(2)}, u32[]{:S(2)}) %collective-permute-start) | collective-permute-done | bytes 491552 | tf_op jit(solution)/shard_map/ppermute | solution.py:14
  30.7 0.7 collective-permute-done.1
  31.5 1.0 pad_maximum_fusion.6
  32.5 4.2 %collective-permute-start.2 = (bf16[2,24,6,1,640]{4,1,3,2,0:T(8,128)(2,1)}, bf16[2,24,6,1,640]{4,1,3,2,0:T(8,128)(2,1)}, u32[]{:S(2)}, u32[]{:S(2)}) collective-permute-start(bf16[2,24,6,1,640]{4,1,3,2,0:T(8,128)(2,1)} %get-tuple-element.7), channel_id=1, source_target_pairs={{0,1},{1,2},{2,3},{4,5},{5,6},{6,7},{8,9},{9,10},{10,11},{12,13},{... | collective-permute-start | bytes 1105928 | tf_op jit(solution)/shard_map/ppermute | solution.py:14
  36.7 1.3 collective-permute-start.3
  38.0 0.6 compare_and_fusion
  38.7 0.2 mul.128
  39.1 0.2 sub.77
  39.9 0.8 sub.87
  40.8 1.3 dynamic-slice_bitcast_fusion
  42.0 0.7 and_convert_fusion
  42.8 2.5 %collective-permute-done.3 = bf16[2,24,6,1,640]{4,1,3,2,0:T(8,128)(2,1)} collective-permute-done((bf16[2,24,6,1,640]{4,1,3,2,0:T(8,128)(2,1)}, bf16[2,24,6,1,640]{4,1,3,2,0:T(8,128)(2,1)}, u32[]{:S(2)}, u32[]{:S(2)}) %collective-permute-start.3) | collective-permute-done | bytes 368672 | tf_op jit(solution)/shard_map/ppermute | solution.py:17
  45.2 3.0 %pad_maximum_fusion = bf16[2,24,6,10,640]{4,1,3,2,0:T(8,128)(2,1)S(1)} fusion(bf16[2,24,6,1,640]{4,1,3,2,0:T(8,128)(2,1)} %collective-permute-done.3, bf16[2,24,1,8,640]{4,1,3,2,0:T(8,128)(2,1)S(1)} %collective-permute-done.1, bf16[1,24,4,8,640]{4,1,3,2,0:T(8,128)(2,1)S(1)} %get-tuple-element.15, bf16[1,24,4,8,640]{4,1,3,2,0:T(8,128)(2,1)S(1)} %get-tuple-element.16, ...), kind=kLoop, calls=%fused_computation | loop fusion | flops 9216000 | bytes 7372800 | tf_op jit(solution)/shard_map/concatenate | solution.py:18
  48.2 3.3 %fusion.27 = bf16[24,6,10,640]{3,0,2,1:T(8,128)(2,1)S(1)} fusion(bf16[2,24,6,10,640]{4,1,3,2,0:T(8,128)(2,1)S(1)} %pad_maximum_fusion, f32[6,10]{1,0:T(8,128)S(1)} %and_convert_fusion, f32[640]{0:T(1024)S(1)} %copy-done.14, f32[640]{0:T(1024)S(1)} %copy-done.15, f32[24,640]{1,0:T(8,128)S(1)} %mul.128, f32[24,640]{1,0:T(8,128)S(1)} %sub.77, s32[640]{0:T(1024)S(1)} %fusion.83), kind=kOutput, calls=%fused_computation.33 | convolution fusion | flops 1191116800 | bytes 3825664 | tf_op jit(solution)/shard_map/dot_general | solution.py:72
  51.7 1.3 collective-permute-start.6
  53.0 2.1 %fusion.17 = f32[24,6,10,640]{3,0,2,1:T(8,128)} fusion(bf16[2,24,6,10,640]{4,1,3,2,0:T(8,128)(2,1)S(1)} %pad_maximum_fusion), kind=kLoop, calls=%fused_computation.22 | loop fusion | flops 921600 | bytes 5529600 | tf_op jit(solution)/shard_map/convert_element_type | solution.py:128
  55.0 4.6 %fusion.26 = bf16[24,6,10,640]{3,0,2,1:T(8,128)(2,1)} fusion(f32[640]{0:T(1024)S(1)} %copy-done.12, f32[640]{0:T(1024)S(1)} %copy-done.13, f32[24,640]{1,0:T(8,128)S(1)} %mul.141, f32[24,640]{1,0:T(8,128)S(1)} %copy-done.4, f32[6,10]{1,0:T(8,128)S(1)} %and_convert_fusion, s32[640]{0:T(1024)S(1)} %fusion.84, bf16[2,24,6,10,640]{4,1,3,2,0:T(8,128)(2,1)S(1)} %pad_maximum_fusion), kind=kOutput, calls=%fused_computation.32 | convolution fusion | flops 1190195200 | bytes 3825664 | tf_op jit(solution)/shard_map/dot_general | solution.py:72
  59.6 3.4 %collective-permute-start.7 = (bf16[3,3,80,640]{3,2,1,0:T(8,128)(2,1)}, bf16[3,3,80,640]{3,2,1,0:T(8,128)(2,1)S(1)}, u32[]{:S(2)}, u32[]{:S(2)}) collective-permute-start(bf16[3,3,80,640]{3,2,1,0:T(8,128)(2,1)} %collective-permute-done.5), channel_id=1, source_target_pairs={{0,4},{4,0},{8,12},{12,8},{1,5},{5,1},{9,13},{13,9},{2,6},{6,2},{1... | collective-permute-start | bytes 2764808 | tf_op jit(solution)/shard_map/ppermute | solution.py:42
  63.1 7.7 %collective-permute-done.6 = bf16[3,3,80,640]{3,2,1,0:T(8,128)(2,1)S(1)} collective-permute-done((bf16[3,3,80,640]{3,2,1,0:T(8,128)(2,1)}, bf16[3,3,80,640]{3,2,1,0:T(8,128)(2,1)S(1)}, u32[]{:S(2)}, u32[]{:S(2)}) %collective-permute-start.6) | collective-permute-done | bytes 921632 | tf_op jit(solution)/shard_map/ppermute | solution.py:41
  70.7 4.1 %collective-permute-start.8 = (bf16[3,3,80,640]{3,2,1,0:T(8,128)(2,1)S(1)}, bf16[3,3,80,640]{3,2,1,0:T(8,128)(2,1)S(1)}, u32[]{:S(2)}, u32[]{:S(2)}) collective-permute-start(bf16[3,3,80,640]{3,2,1,0:T(8,128)(2,1)S(1)} %collective-permute-done.6), channel_id=1, source_target_pairs={{0,4},{4,0},{8,12},{12,8},{1,5},{5,1},{9,13},{13,9},{2,6},{6,2},{1... | collective-permute-start | bytes 2764808 | tf_op jit(solution)/shard_map/ppermute | solution.py:43
  74.8 0.6 collective-permute-start.11
  75.4 0.3 collective-permute-start.12
  75.8 2.9 %constant_dynamic-update-slice_fusion.4 = bf16[3,3,640,640]{3,2,1,0:T(8,128)(2,1)} fusion(bf16[3,3,640,640]{3,2,1,0:T(8,128)(2,1)} %constant_dynamic-update-slice_fusion.5, bf16[3,3,160,640]{3,2,1,0:T(8,128)(2,1)} %collective-permute-done.4), kind=kLoop, calls=%fused_computation.73 | loop fusion | bytes 3686400
  78.6 2.2 %constant_dynamic-update-slice_fusion.3 = bf16[3,3,640,640]{3,2,1,0:T(8,128)(2,1)} fusion(bf16[3,3,640,640]{3,2,1,0:T(8,128)(2,1)} %constant_dynamic-update-slice_fusion.4, bf16[3,3,80,640]{3,2,1,0:T(8,128)(2,1)} %collective-permute-done.5), kind=kLoop, calls=%fused_computation.72 | loop fusion | bytes 1843200
  80.9 1.0 constant_dynamic-update-slice_fusion.2
  81.9 2.9 %constant_dynamic-update-slice_fusion.10 = bf16[3,3,640,640]{3,2,1,0:T(8,128)(2,1)} fusion(bf16[3,3,640,640]{3,2,1,0:T(8,128)(2,1)} %constant_dynamic-update-slice_fusion.11, bf16[3,3,160,640]{3,2,1,0:T(8,128)(2,1)} %collective-permute-done.9), kind=kLoop, calls=%fused_computation.79 | loop fusion | bytes 3686400
  84.8 1.1 constant_dynamic-update-slice_fusion.9
  85.9 1.0 constant_dynamic-update-slice_fusion.1
  86.9 10.0 %collective-permute-done.11 = bf16[3,3,80,640]{3,2,1,0:T(8,128)(2,1)S(1)} collective-permute-done((bf16[3,3,80,640]{3,2,1,0:T(8,128)(2,1)S(1)}, bf16[3,3,80,640]{3,2,1,0:T(8,128)(2,1)S(1)}, u32[]{:S(2)}, u32[]{:S(2)}) %collective-permute-start.11) | collective-permute-done | bytes 921632 | tf_op jit(solution)/shard_map/ppermute | solution.py:41
  96.9 0.8 collective-permute-start.13
  97.7 1.0 constant_dynamic-update-slice_fusion
  98.7 13.4 %fusion.39 = bf16[24,6,10,640]{3,0,2,1:T(8,128)(2,1)} fusion(bf16[24,6,10,640]{3,0,2,1:T(8,128)(2,1)} %copy-done.2, bf16[3,3,640,640]{3,2,1,0:T(8,128)(2,1)} %constant_dynamic-update-slice_fusion, bf16[24,6,10,640]{3,0,2,1:T(8,128)(2,1)} %fusion.26, f32[640]{0:T(1024)S(1)} %copy-done.14, f32[640]{0:T(1024)S(1)} %copy-done.15, f32[24,640]{1,0:T(8,128)S(1)} %mul.128, ...), kind=kOutput, calls=%fused_computation.40 | convolution fusion | flops 6297763840 | bytes 10393600 | tf_op jit(solution)/shard_map/dot_general | solution.py:72
  112.1 1.0 constant_dynamic-update-slice_fusion.8
  113.1 1.0 constant_dynamic-update-slice_fusion.7
  114.2 2.3 %constant_dynamic-update-slice_fusion.6 = bf16[3,3,640,640]{3,2,1,0:T(8,128)(2,1)} fusion(bf16[3,3,640,640]{3,2,1,0:T(8,128)(2,1)} %constant_dynamic-update-slice_fusion.7, bf16[3,3,80,640]{3,2,1,0:T(8,128)(2,1)} %collective-permute-done.13), kind=kLoop, calls=%fused_computation.75 | loop fusion | bytes 1843200 | tf_op jit(solution)/shard_map/concatenate | solution.py:48
  116.5 2.6 %fusion.12 = f32[48,4,1,640]{3,0,2,1:T(8,128)S(1)} fusion(bf16[3,3,640,640]{3,2,1,0:T(8,128)(2,1)} %constant_dynamic-update-slice_fusion.6, bf16[24,6,1,640]{3,0,2,1:T(8,128)(2,1)S(1)} %get-tuple-element.13, bf16[24,6,1,640]{3,0,2,1:T(8,128)(2,1)S(1)} %get-tuple-element.11), kind=kOutput, calls=%fused_computation.15 | convolution fusion | flops 472596480 | bytes 3317760 | tf_op jit(solution)/shard_map/conv_general_dilated | solution.py:81
  119.1 2.7 %fusion.10 = f32[48,4,1,640]{3,0,2,1:T(8,128)S(1)} fusion(bf16[3,3,640,640]{3,2,1,0:T(8,128)(2,1)} %constant_dynamic-update-slice_fusion.6, bf16[24,6,1,640]{3,0,2,1:T(8,128)(2,1)S(1)} %get-tuple-element.14, bf16[24,6,1,640]{3,0,2,1:T(8,128)(2,1)S(1)} %get-tuple-element.12), kind=kOutput, calls=%fused_computation.13 | convolution fusion | flops 472596480 | bytes 3317760 | tf_op jit(solution)/shard_map/conv_general_dilated | solution.py:81
  121.9 0.4 copy-done
  122.3 7.2 %fusion.44 = bf16[24,4,8,640]{3,0,2,1:T(8,128)(2,1)S(1)} fusion(f32[24,6,10,640]{3,0,2,1:T(8,128)S(1)} %copy-done, f32[24,4,1,640]{3,0,2,1:T(8,128)S(1)} %slice_subtract_fusion, f32[24,4,1,640]{3,0,2,1:T(8,128)S(1)} %slice_subtract_fusion.1, bf16[24,6,10,640]{3,0,2,1:T(8,128)(2,1)S(1)} %copy-done.3, bf16[3,3,640,640]{3,2,1,0:T(8,128)(2,1)S(1)} %copy-done.1, ...), kind=kOutput, calls=%fused_computation.41 | convolution fusion | flops 5665259520 | bytes 13642432 | tf_op jit(solution)/shard_map/conv_general_dilated | solution.py:81
  129.6 1.1 copy.43
  (62 shorter events, 1.4 us)
Async XLA Ops:
  0.0 75.4 %collective-permute-start.4 = (bf16[3,3,160,640]{3,2,1,0:T(8,128)(2,1)}, bf16[3,3,160,640]{3,2,1,0:T(8,128)(2,1)}, u32[]{:S(2)}, u32[]{:S(2)}) collective-permute-start(bf16[3,3,160,640]{3,2,1,0:T(8,128)(2,1)} %param.25), channel_id=1, source_target_pairs={{0,4},{4,0},{8,12},{12,8},{1,5},{5,1},{9,13},{13,9},{2,6},{6,2},{1... | collective-permute-start | bytes 5529608 | tf_op jit(solution)/shard_map/ppermute | solution.py:34
  2.2 10.3 %copy-start.9 = (s32[24,16]{0,1:T(8,128)S(1)}, s32[24,16]{0,1:T(8,128)}, u32[]{:S(2)}) copy-start(s32[24,16]{0,1:T(8,128)} %param.20) | copy-start | bytes 4612
  2.2 49.3 %collective-permute-start.5 = (bf16[3,3,80,640]{3,2,1,0:T(8,128)(2,1)}, bf16[3,3,80,640]{3,2,1,0:T(8,128)(2,1)}, u32[]{:S(2)}, u32[]{:S(2)}) collective-permute-start(bf16[3,3,80,640]{3,2,1,0:T(8,128)(2,1)} %dynamic-slice_bitcast_fusion.1), channel_id=1, source_target_pairs={{8,0},{12,4},{0,8},{4,12},{9,1},{13,5},{1,9},{5,13},{10,2},{14,6},... | collective-permute-start | bytes 2764808 | tf_op jit(solution)/shard_map/ppermute | solution.py:39
  8.0 22.8 %collective-permute-start = (bf16[2,24,1,8,640]{4,1,3,2,0:T(8,128)(2,1)}, bf16[2,24,1,8,640]{4,1,3,2,0:T(8,128)(2,1)S(1)}, u32[]{:S(2)}, u32[]{:S(2)}) collective-permute-start(bf16[2,24,1,8,640]{4,1,3,2,0:T(8,128)(2,1)} %get-tuple-element.9), channel_id=1, source_target_pairs={{0,4},{4,8},{8,12},{1,5},{5,9},{9,13},{2,6},{6,10},{10,14},{3,7},{... | collective-permute-start | bytes 1474568 | tf_op jit(solution)/shard_map/ppermute | solution.py:14
  9.9 21.6 %collective-permute-start.1 = (bf16[2,24,1,8,640]{4,1,3,2,0:T(8,128)(2,1)S(1)}, bf16[2,24,1,8,640]{4,1,3,2,0:T(8,128)(2,1)S(1)}, u32[]{:S(2)}, u32[]{:S(2)}) collective-permute-start(bf16[2,24,1,8,640]{4,1,3,2,0:T(8,128)(2,1)S(1)} %get-tuple-element.10), channel_id=1, source_target_pairs={{4,0},{8,4},{12,8},{5,1},{9,5},{13,9},{6,2},{10,6},{14,10},{7,3},{... | collective-permute-start | bytes 1474568 | tf_op jit(solution)/shard_map/ppermute | solution.py:17
  12.3 69.6 %collective-permute-start.9 = (bf16[3,3,160,640]{3,2,1,0:T(8,128)(2,1)}, bf16[3,3,160,640]{3,2,1,0:T(8,128)(2,1)}, u32[]{:S(2)}, u32[]{:S(2)}) collective-permute-start(bf16[3,3,160,640]{3,2,1,0:T(8,128)(2,1)} %param.32), channel_id=1, source_target_pairs={{0,4},{4,0},{8,12},{12,8},{1,5},{5,1},{9,13},{13,9},{2,6},{6,2},{1... | collective-permute-start | bytes 5529608 | tf_op jit(solution)/shard_map/ppermute | solution.py:34
  15.5 23.0 %copy-start.5 = (f32[24,32]{1,0:T(8,128)S(1)}, f32[24,32]{1,0:T(8,128)}, u32[]{:S(2)}) copy-start(f32[24,32]{1,0:T(8,128)} %param.29) | copy-start | bytes 9220
  15.5 23.4 %copy-start.6 = (f32[24,32]{1,0:T(8,128)S(1)}, f32[24,32]{1,0:T(8,128)}, u32[]{:S(2)}) copy-start(f32[24,32]{1,0:T(8,128)} %param.28) | copy-start | bytes 9220
  15.5 23.8 %copy-start.7 = (f32[24,32]{1,0:T(8,128)S(1)}, f32[24,32]{1,0:T(8,128)}, u32[]{:S(2)}) copy-start(f32[24,32]{1,0:T(8,128)} %param.22) | copy-start | bytes 9220
  18.5 21.3 %copy-start.8 = (f32[24,32]{1,0:T(8,128)S(1)}, f32[24,32]{1,0:T(8,128)}, u32[]{:S(2)}) copy-start(f32[24,32]{1,0:T(8,128)} %param.21) | copy-start | bytes 9220
  32.5 10.3 %collective-permute-start.2 = (bf16[2,24,6,1,640]{4,1,3,2,0:T(8,128)(2,1)}, bf16[2,24,6,1,640]{4,1,3,2,0:T(8,128)(2,1)}, u32[]{:S(2)}, u32[]{:S(2)}) collective-permute-start(bf16[2,24,6,1,640]{4,1,3,2,0:T(8,128)(2,1)} %get-tuple-element.7), channel_id=1, source_target_pairs={{0,1},{1,2},{2,3},{4,5},{5,6},{6,7},{8,9},{9,10},{10,11},{12,13},{... | collective-permute-start | bytes 1105928 | tf_op jit(solution)/shard_map/ppermute | solution.py:14
  36.7 8.6 %collective-permute-start.3 = (bf16[2,24,6,1,640]{4,1,3,2,0:T(8,128)(2,1)}, bf16[2,24,6,1,640]{4,1,3,2,0:T(8,128)(2,1)}, u32[]{:S(2)}, u32[]{:S(2)}) collective-permute-start(bf16[2,24,6,1,640]{4,1,3,2,0:T(8,128)(2,1)} %get-tuple-element.8), channel_id=1, source_target_pairs={{1,0},{2,1},{3,2},{5,4},{6,5},{7,6},{9,8},{10,9},{11,10},{13,12},{... | collective-permute-start | bytes 1105928 | tf_op jit(solution)/shard_map/ppermute | solution.py:17
  42.8 5.4 %copy-start.14 = (f32[640]{0:T(1024)S(1)}, f32[640]{0:T(1024)}, u32[]{:S(2)}) copy-start(f32[640]{0:T(1024)} %param.31) | copy-start | bytes 7684
  42.8 5.5 %copy-start.15 = (f32[640]{0:T(1024)S(1)}, f32[640]{0:T(1024)}, u32[]{:S(2)}) copy-start(f32[640]{0:T(1024)} %param.30) | copy-start | bytes 7684
  51.5 23.8 %copy-start.2 = (bf16[24,6,10,640]{3,0,2,1:T(8,128)(2,1)}, bf16[24,6,10,640]{3,0,2,1:T(8,128)(2,1)S(1)}, u32[]{:S(2)}) copy-start(bf16[24,6,10,640]{3,0,2,1:T(8,128)(2,1)S(1)} %fusion.27) | copy-start | bytes 5529604
  51.5 3.5 %copy-start.4 = (f32[24,640]{1,0:T(8,128)S(1)}, f32[24,640]{1,0:T(8,128)}, u32[]{:S(2)}) copy-start(f32[24,640]{1,0:T(8,128)} %sub.87) | copy-start | bytes 184324
  51.5 3.5 %copy-start.12 = (f32[640]{0:T(1024)S(1)}, f32[640]{0:T(1024)}, u32[]{:S(2)}) copy-start(f32[640]{0:T(1024)} %param.24) | copy-start | bytes 7684
  51.6 3.5 %copy-start.13 = (f32[640]{0:T(1024)S(1)}, f32[640]{0:T(1024)}, u32[]{:S(2)}) copy-start(f32[640]{0:T(1024)} %param.23) | copy-start | bytes 7684
  51.6 23.2 %collective-permute-start.10 = (bf16[3,3,80,640]{3,2,1,0:T(8,128)(2,1)S(1)}, bf16[3,3,80,640]{3,2,1,0:T(8,128)(2,1)S(1)}, u32[]{:S(2)}, u32[]{:S(2)}) collective-permute-start(bf16[3,3,80,640]{3,2,1,0:T(8,128)(2,1)S(1)} %dynamic-slice_bitcast_fusion), channel_id=1, source_target_pairs={{8,0},{12,4},{0,8},{4,12},{9,1},{13,5},{1,9},{5,13},{10,2},{14,6},... | collective-permute-start | bytes 2764808 | tf_op jit(solution)/shard_map/ppermute | solution.py:39
  51.7 19.1 %collective-permute-start.6 = (bf16[3,3,80,640]{3,2,1,0:T(8,128)(2,1)}, bf16[3,3,80,640]{3,2,1,0:T(8,128)(2,1)S(1)}, u32[]{:S(2)}, u32[]{:S(2)}) collective-permute-start(bf16[3,3,80,640]{3,2,1,0:T(8,128)(2,1)} %collective-permute-done.5), channel_id=1, source_target_pairs={{0,16},{16,0},{1,17},{17,1},{2,18},{18,2},{3,19},{19,3},{4,20},{20... | collective-permute-start | bytes 2764808 | tf_op jit(solution)/shard_map/ppermute | solution.py:41
  59.6 26.2 %collective-permute-start.7 = (bf16[3,3,80,640]{3,2,1,0:T(8,128)(2,1)}, bf16[3,3,80,640]{3,2,1,0:T(8,128)(2,1)S(1)}, u32[]{:S(2)}, u32[]{:S(2)}) collective-permute-start(bf16[3,3,80,640]{3,2,1,0:T(8,128)(2,1)} %collective-permute-done.5), channel_id=1, source_target_pairs={{0,4},{4,0},{8,12},{12,8},{1,5},{5,1},{9,13},{13,9},{2,6},{6,2},{1... | collective-permute-start | bytes 2764808 | tf_op jit(solution)/shard_map/ppermute | solution.py:42
  70.7 26.9 %collective-permute-start.8 = (bf16[3,3,80,640]{3,2,1,0:T(8,128)(2,1)S(1)}, bf16[3,3,80,640]{3,2,1,0:T(8,128)(2,1)S(1)}, u32[]{:S(2)}, u32[]{:S(2)}) collective-permute-start(bf16[3,3,80,640]{3,2,1,0:T(8,128)(2,1)S(1)} %collective-permute-done.6), channel_id=1, source_target_pairs={{0,4},{4,0},{8,12},{12,8},{1,5},{5,1},{9,13},{13,9},{2,6},{6,2},{1... | collective-permute-start | bytes 2764808 | tf_op jit(solution)/shard_map/ppermute | solution.py:43
  74.8 22.1 %collective-permute-start.11 = (bf16[3,3,80,640]{3,2,1,0:T(8,128)(2,1)S(1)}, bf16[3,3,80,640]{3,2,1,0:T(8,128)(2,1)S(1)}, u32[]{:S(2)}, u32[]{:S(2)}) collective-permute-start(bf16[3,3,80,640]{3,2,1,0:T(8,128)(2,1)S(1)} %collective-permute-done.10), channel_id=1, source_target_pairs={{0,1},{1,0},{2,3},{3,2},{4,5},{5,4},{6,7},{7,6},{8,9},{9,8},{10,11... | collective-permute-start | bytes 2764808 | tf_op jit(solution)/shard_map/ppermute | solution.py:41
  75.4 37.7 %collective-permute-start.12 = (bf16[3,3,80,640]{3,2,1,0:T(8,128)(2,1)S(1)}, bf16[3,3,80,640]{3,2,1,0:T(8,128)(2,1)S(1)}, u32[]{:S(2)}, u32[]{:S(2)}) collective-permute-start(bf16[3,3,80,640]{3,2,1,0:T(8,128)(2,1)S(1)} %collective-permute-done.10), channel_id=1, source_target_pairs={{0,4},{4,0},{8,12},{12,8},{1,5},{5,1},{9,13},{13,9},{2,6},{6,2},{1... | collective-permute-start | bytes 2764808 | tf_op jit(solution)/shard_map/ppermute | solution.py:42
  84.8 13.9 %copy-start.11 = (f32[24,640]{1,0:T(8,128)S(1)}, f32[24,640]{1,0:T(8,128)}, u32[]{:S(2)}) copy-start(f32[24,640]{1,0:T(8,128)} %param.27) | copy-start | bytes 184324
  84.8 13.9 %copy-start.16 = (f32[640]{0:T(1024)S(1)}, f32[640]{0:T(1024)}, u32[]{:S(2)}) copy-start(f32[640]{0:T(1024)} %param.26) | copy-start | bytes 7684
  96.9 17.3 %collective-permute-start.13 = (bf16[3,3,80,640]{3,2,1,0:T(8,128)(2,1)S(1)}, bf16[3,3,80,640]{3,2,1,0:T(8,128)(2,1)}, u32[]{:S(2)}, u32[]{:S(2)}) collective-permute-start(bf16[3,3,80,640]{3,2,1,0:T(8,128)(2,1)S(1)} %collective-permute-done.11), channel_id=1, source_target_pairs={{0,4},{4,0},{8,12},{12,8},{1,5},{5,1},{9,13},{13,9},{2,6},{6,2},{1... | collective-permute-start | bytes 2764808 | tf_op jit(solution)/shard_map/ppermute | solution.py:43
  112.1 2.0 %copy-start.3 = (bf16[24,6,10,640]{3,0,2,1:T(8,128)(2,1)S(1)}, bf16[24,6,10,640]{3,0,2,1:T(8,128)(2,1)}, u32[]{:S(2)}) copy-start(bf16[24,6,10,640]{3,0,2,1:T(8,128)(2,1)} %fusion.39) | copy-start | bytes 5529604
  114.1 7.7 %copy-start.10 = (bf16[24,4,8,640]{3,2,1,0:T(8,128)(2,1)S(1)}, bf16[24,4,8,640]{3,2,1,0:T(8,128)(2,1)}, u32[]{:S(2)}) copy-start(bf16[24,4,8,640]{3,2,1,0:T(8,128)(2,1)} %param.19) | copy-start | bytes 2949124
  116.4 5.4 %copy-start.1 = (bf16[3,3,640,640]{3,2,1,0:T(8,128)(2,1)S(1)}, bf16[3,3,640,640]{3,2,1,0:T(8,128)(2,1)}, u32[]{:S(2)}) copy-start(bf16[3,3,640,640]{3,2,1,0:T(8,128)(2,1)} %constant_dynamic-update-slice_fusion.6) | copy-start | bytes 22118404
  119.1 3.3 %copy-start = (f32[24,6,10,640]{3,0,2,1:T(8,128)S(1)}, f32[24,6,10,640]{3,0,2,1:T(8,128)}, u32[]{:S(2)}) copy-start(f32[24,6,10,640]{3,0,2,1:T(8,128)} %fusion.17) | copy-start | bytes 11059204
  119.1 3.3 %copy-start.17 = (f32[640]{0:T(1024)S(1)}, f32[640]{0:T(1024)}, u32[]{:S(2)}) copy-start(f32[640]{0:T(1024)} %param.33) | copy-start | bytes 7684

commit v7 on v6

--- a/solution.py
+++ b/solution.py
@@ -24,7 +24,6 @@
     chips = count // 2
     mate_pairs = [(i, i ^ 1) for i in range(count)]
     wholes = []
-    previous = None
     for shard, swap_axis in zip(kernels, swap_axes):
         swap_pairs = [(i, i ^ 1) for i in range(lax.axis_size(swap_axis))]
         parity = lax.axis_index(swap_axis) % 2
@@ -33,11 +32,8 @@
         mine = lax.dynamic_index_in_dim(halves, parity, axis=2, keepdims=False)
         held = [shard, lax.ppermute(shard, "row", mate_pairs)]
         for step in range(1, chips):
-            if previous is not None:
-                mine, _ = lax.optimization_barrier((mine, previous))
             pairs = [(((i // 2 + step) % chips) * 2 + i % 2, i) for i in range(count)]
             fetched = lax.ppermute(mine, "row", pairs)
-            previous = fetched
             other = lax.ppermute(fetched, swap_axis, swap_pairs)
             relayed = lax.ppermute(fetched, "row", mate_pairs)
             other_relayed = lax.ppermute(other, "row", mate_pairs)

time: 131 us -> 132 us (level)
  waiting for transfers between devices: 33.1 us -> 38.3 us
  starting transfers between devices: 23.2 us -> 19.4 us
    ppermute x2, waiting for transfers between devices: 0.01 us -> 9.74 us  [gather_weights(): fetched = lax.ppermute(mine, 'row', pairs)]
    ppermute x2, waiting for transfers between devices: 17.6 us -> 13.1 us  [gather_weights(): other = lax.ppermute(fetched, swap_axis, swap_pairs)]
    ppermute x2, starting transfers between devices: 4.84 us -> 2.21 us  [gather_weights(): other_relayed = lax.ppermute(other, 'row', mate_pairs)]
    ppermute x2, starting transfers between devices: 3.77 us -> 1.5 us  [gather_weights(): relayed = lax.ppermute(fetched, 'row', mate_pairs)]
  transfers between devices with their start and end apart: 14 -> 14, of which waited for: 5 -> 6; matrix products, arithmetic and copies ran while one was open for 44% -> 44% of each run, Pallas kernels for 0% -> 0%
where the time goes in v7:
time: 132 us
  waiting for transfers between devices  38.3 us (29%)
  matrix products  33.8 us (26%)
  local copies, waits for them, and re-layouts  31.4 us (24%)
  starting transfers between devices  19.4 us (15%)
  other arithmetic  8.58 us (6%)
    dot_general x3, matrix products, to_relative(): moved = jnp.dot(activation, chooser, preferred_element_type=jnp.float32)  21.2 us
    unnamed x46, local copies, waits for them, and re-layouts  19.5 us
    ppermute x2, waiting for transfers between devices, gather_weights(): other = lax.ppermute(fetched, swap_axis, swap_pairs)  13.1 us
    conv_general_dilated x3, matrix products, conv_valid(): lax.conv_general_dilated(activation, kernel, window_strides=(1, 1), paddi...  12.6 us
    ppermute x2, waiting for transfers between devices, padded_2(): lax.ppermute(lax.slice_in_dim(block, block.shape[dim] - width, None, axis...  12.3 us
    ppermute x2, waiting for transfers between devices, gather_weights(): fetched = lax.ppermute(mine, 'row', pairs)  9.74 us
    ppermute x2, starting transfers between devices, padded_2(): lax.ppermute(lax.slice_in_dim(block, block.shape[dim] - width, None, axis...  6.13 us
    ppermute x2, starting transfers between devices, padded_2(): lax.ppermute(lax.slice_in_dim(block, 0, width, axis=dim), axis, backward)  3.71 us
  transfers between devices with their start and end apart: 14, of which 6 were waited for; matrix products, arithmetic and copies ran while one was open for 44% of the time, Pallas kernels for 0%

profile of v7, /device:TPU:1, one launch (start us, length us, event | category | flops | bytes accessed | tf_op | source)
XLA Modules:
  0.0 131.9 jit_solution(5599786455840670336)
XLA Ops:
  0.1 2.2 %dynamic-slice_bitcast_fusion.1 = bf16[3,3,80,640]{3,2,1,0:T(8,128)(2,1)} fusion(bf16[3,3,2,80,640]{4,3,2,1,0:T(8,128)(2,1)} %bitcast.50, s32[]{:T(128)S(6)} %select_n.186), kind=kLoop, calls=%fused_computation.51 | loop fusion | bytes 1843204 | tf_op jit(solution)/shard_map/jit(dynamic_index_in_dim)/squeeze | solution.py:32
  2.2 2.7 %collective-permute-start.5 = (bf16[3,3,80,640]{3,2,1,0:T(8,128)(2,1)}, bf16[3,3,80,640]{3,2,1,0:T(8,128)(2,1)}, u32[]{:S(2)}, u32[]{:S(2)}) collective-permute-start(bf16[3,3,80,640]{3,2,1,0:T(8,128)(2,1)} %dynamic-slice_bitcast_fusion.1), channel_id=1, source_target_pairs={{8,0},{12,4},{0,8},{4,12},{9,1},{13,5},{1,9},{5,13},{10,2},{14,6},... | collective-permute-start | bytes 2764808 | tf_op jit(solution)/shard_map/ppermute | solution.py:36
  4.9 2.1 %copy_bitcast_fusion = (bf16[1,24,4,8,640]{4,1,3,2,0:T(8,128)(2,1)S(1)}, bf16[1,24,4,8,640]{4,1,3,2,0:T(8,128)(2,1)S(1)}) fusion(bf16[24,4,8,640]{3,2,1,0:T(8,128)(2,1)} %param.18, bf16[24,4,8,640]{3,2,1,0:T(8,128)(2,1)} %param.17), kind=kLoop, calls=%fused_computation.42 | loop fusion | bytes 3932160 | tf_op jit(solution)/shard_map/stack | solution.py:122
  7.1 0.9 pad_maximum_fusion.2
  8.0 1.9 %collective-permute-start = (bf16[2,24,1,8,640]{4,1,3,2,0:T(8,128)(2,1)}, bf16[2,24,1,8,640]{4,1,3,2,0:T(8,128)(2,1)S(1)}, u32[]{:S(2)}, u32[]{:S(2)}) collective-permute-start(bf16[2,24,1,8,640]{4,1,3,2,0:T(8,128)(2,1)} %get-tuple-element.7), channel_id=1, source_target_pairs={{0,4},{4,8},{8,12},{1,5},{5,9},{9,13},{2,6},{6,10},{10,14},{3,7},{... | collective-permute-start | bytes 1474568 | tf_op jit(solution)/shard_map/ppermute | solution.py:14
  9.9 2.4 %collective-permute-start.1 = (bf16[2,24,1,8,640]{4,1,3,2,0:T(8,128)(2,1)S(1)}, bf16[2,24,1,8,640]{4,1,3,2,0:T(8,128)(2,1)S(1)}, u32[]{:S(2)}, u32[]{:S(2)}) collective-permute-start(bf16[2,24,1,8,640]{4,1,3,2,0:T(8,128)(2,1)S(1)} %get-tuple-element.8), channel_id=1, source_target_pairs={{4,0},{8,4},{12,8},{5,1},{9,5},{13,9},{6,2},{10,6},{14,10},{7,3},{... | collective-permute-start | bytes 1474568 | tf_op jit(solution)/shard_map/ppermute | solution.py:17
  12.6 2.9 %constant_dynamic-update-slice_fusion.5 = bf16[3,3,640,640]{3,2,1,0:T(8,128)(2,1)} fusion(bf16[3,3,160,640]{3,2,1,0:T(8,128)(2,1)} %param.25), kind=kLoop, calls=%fused_computation.74 | loop fusion | bytes 3686400
  15.5 2.9 %constant_dynamic-update-slice_fusion.11 = bf16[3,3,640,640]{3,2,1,0:T(8,128)(2,1)} fusion(bf16[3,3,160,640]{3,2,1,0:T(8,128)(2,1)} %param.32), kind=kLoop, calls=%fused_computation.80 | loop fusion | bytes 3686400
  18.5 12.3 %collective-permute-done = bf16[2,24,1,8,640]{4,1,3,2,0:T(8,128)(2,1)S(1)} collective-permute-done((bf16[2,24,1,8,640]{4,1,3,2,0:T(8,128)(2,1)}, bf16[2,24,1,8,640]{4,1,3,2,0:T(8,128)(2,1)S(1)}, u32[]{:S(2)}, u32[]{:S(2)}) %collective-permute-start) | collective-permute-done | bytes 491552 | tf_op jit(solution)/shard_map/ppermute | solution.py:14
  30.7 0.7 collective-permute-done.1
  31.5 1.0 pad_maximum_fusion.6
  32.5 4.2 %collective-permute-start.2 = (bf16[2,24,6,1,640]{4,1,3,2,0:T(8,128)(2,1)}, bf16[2,24,6,1,640]{4,1,3,2,0:T(8,128)(2,1)}, u32[]{:S(2)}, u32[]{:S(2)}) collective-permute-start(bf16[2,24,6,1,640]{4,1,3,2,0:T(8,128)(2,1)} %get-tuple-element.5), channel_id=1, source_target_pairs={{0,1},{1,2},{2,3},{4,5},{5,6},{6,7},{8,9},{9,10},{10,11},{12,13},{... | collective-permute-start | bytes 1105928 | tf_op jit(solution)/shard_map/ppermute | solution.py:14
  36.7 1.3 collective-permute-start.3
  38.0 0.5 compare_and_fusion
  39.1 0.2 sub.77
  39.9 0.8 sub.87
  40.7 1.3 dynamic-slice_bitcast_fusion
  42.0 0.7 and_convert_fusion
  42.8 2.5 %collective-permute-done.3 = bf16[2,24,6,1,640]{4,1,3,2,0:T(8,128)(2,1)} collective-permute-done((bf16[2,24,6,1,640]{4,1,3,2,0:T(8,128)(2,1)}, bf16[2,24,6,1,640]{4,1,3,2,0:T(8,128)(2,1)}, u32[]{:S(2)}, u32[]{:S(2)}) %collective-permute-start.3) | collective-permute-done | bytes 368672 | tf_op jit(solution)/shard_map/ppermute | solution.py:17
  45.3 3.0 %pad_maximum_fusion = bf16[2,24,6,10,640]{4,1,3,2,0:T(8,128)(2,1)S(1)} fusion(bf16[2,24,6,1,640]{4,1,3,2,0:T(8,128)(2,1)} %collective-permute-done.3, bf16[2,24,1,8,640]{4,1,3,2,0:T(8,128)(2,1)S(1)} %collective-permute-done.1, bf16[1,24,4,8,640]{4,1,3,2,0:T(8,128)(2,1)S(1)} %get-tuple-element.13, bf16[1,24,4,8,640]{4,1,3,2,0:T(8,128)(2,1)S(1)} %get-tuple-element.14, ...), kind=kLoop, calls=%fused_computation | loop fusion | flops 9216000 | bytes 7372800 | tf_op jit(solution)/shard_map/concatenate | solution.py:18
  48.3 3.3 %fusion.27 = bf16[24,6,10,640]{3,0,2,1:T(8,128)(2,1)S(1)} fusion(bf16[2,24,6,10,640]{4,1,3,2,0:T(8,128)(2,1)S(1)} %pad_maximum_fusion, f32[6,10]{1,0:T(8,128)S(1)} %and_convert_fusion, f32[640]{0:T(1024)S(1)} %copy-done.14, f32[640]{0:T(1024)S(1)} %copy-done.15, f32[24,640]{1,0:T(8,128)S(1)} %mul.128, f32[24,640]{1,0:T(8,128)S(1)} %sub.77, s32[640]{0:T(1024)S(1)} %fusion.83), kind=kOutput, calls=%fused_computation.33 | convolution fusion | flops 1191116800 | bytes 3825664 | tf_op jit(solution)/shard_map/dot_general | solution.py:68
  51.6 2.2 %fusion.17 = f32[24,6,10,640]{3,0,2,1:T(8,128)} fusion(bf16[2,24,6,10,640]{4,1,3,2,0:T(8,128)(2,1)S(1)} %pad_maximum_fusion), kind=kLoop, calls=%fused_computation.22 | loop fusion | flops 921600 | bytes 5529600 | tf_op jit(solution)/shard_map/convert_element_type | solution.py:124
  53.8 1.2 collective-permute-start.6
  55.1 9.7 %collective-permute-done.10 = bf16[3,3,80,640]{3,2,1,0:T(8,128)(2,1)S(1)} collective-permute-done((bf16[3,3,80,640]{3,2,1,0:T(8,128)(2,1)S(1)}, bf16[3,3,80,640]{3,2,1,0:T(8,128)(2,1)S(1)}, u32[]{:S(2)}, u32[]{:S(2)}) %collective-permute-start.10) | collective-permute-done | bytes 921632 | tf_op jit(solution)/shard_map/ppermute | solution.py:36
  64.8 1.8 %collective-permute-start.11 = (bf16[3,3,80,640]{3,2,1,0:T(8,128)(2,1)S(1)}, bf16[3,3,80,640]{3,2,1,0:T(8,128)(2,1)S(1)}, u32[]{:S(2)}, u32[]{:S(2)}) collective-permute-start(bf16[3,3,80,640]{3,2,1,0:T(8,128)(2,1)S(1)} %collective-permute-done.10), channel_id=1, source_target_pairs={{0,1},{1,0},{2,3},{3,2},{4,5},{5,4},{6,7},{7,6},{8,9},{9,8},{10,11... | collective-permute-start | bytes 2764808 | tf_op jit(solution)/shard_map/ppermute | solution.py:37
  66.6 4.5 %fusion.26 = bf16[24,6,10,640]{3,0,2,1:T(8,128)(2,1)} fusion(f32[640]{0:T(1024)S(1)} %copy-done.12, f32[640]{0:T(1024)S(1)} %copy-done.13, f32[24,640]{1,0:T(8,128)S(1)} %mul.141, f32[24,640]{1,0:T(8,128)S(1)} %copy-done.4, f32[6,10]{1,0:T(8,128)S(1)} %and_convert_fusion, s32[640]{0:T(1024)S(1)} %fusion.84, bf16[2,24,6,10,640]{4,1,3,2,0:T(8,128)(2,1)S(1)} %pad_maximum_fusion), kind=kOutput, calls=%fused_computation.32 | convolution fusion | flops 1190195200 | bytes 3825664 | tf_op jit(solution)/shard_map/dot_general | solution.py:68
  71.1 1.4 %collective-permute-start.7 = (bf16[3,3,80,640]{3,2,1,0:T(8,128)(2,1)}, bf16[3,3,80,640]{3,2,1,0:T(8,128)(2,1)S(1)}, u32[]{:S(2)}, u32[]{:S(2)}) collective-permute-start(bf16[3,3,80,640]{3,2,1,0:T(8,128)(2,1)} %collective-permute-done.5), channel_id=1, source_target_pairs={{0,4},{4,0},{8,12},{12,8},{1,5},{5,1},{9,13},{13,9},{2,6},{6,2},{1... | collective-permute-start | bytes 2764808 | tf_op jit(solution)/shard_map/ppermute | solution.py:38
  72.7 3.8 %collective-permute-done.6 = bf16[3,3,80,640]{3,2,1,0:T(8,128)(2,1)S(1)} collective-permute-done((bf16[3,3,80,640]{3,2,1,0:T(8,128)(2,1)}, bf16[3,3,80,640]{3,2,1,0:T(8,128)(2,1)S(1)}, u32[]{:S(2)}, u32[]{:S(2)}) %collective-permute-start.6) | collective-permute-done | bytes 921632 | tf_op jit(solution)/shard_map/ppermute | solution.py:37
  76.5 0.4 collective-permute-start.8
  76.9 9.3 %collective-permute-done.11 = bf16[3,3,80,640]{3,2,1,0:T(8,128)(2,1)S(1)} collective-permute-done((bf16[3,3,80,640]{3,2,1,0:T(8,128)(2,1)S(1)}, bf16[3,3,80,640]{3,2,1,0:T(8,128)(2,1)S(1)}, u32[]{:S(2)}, u32[]{:S(2)}) %collective-permute-start.11) | collective-permute-done | bytes 921632 | tf_op jit(solution)/shard_map/ppermute | solution.py:37
  86.2 1.8 %collective-permute-start.13 = (bf16[3,3,80,640]{3,2,1,0:T(8,128)(2,1)S(1)}, bf16[3,3,80,640]{3,2,1,0:T(8,128)(2,1)S(1)}, u32[]{:S(2)}, u32[]{:S(2)}) collective-permute-start(bf16[3,3,80,640]{3,2,1,0:T(8,128)(2,1)S(1)} %collective-permute-done.11), channel_id=1, source_target_pairs={{0,4},{4,0},{8,12},{12,8},{1,5},{5,1},{9,13},{13,9},{2,6},{6,2},{1... | collective-permute-start | bytes 2764808 | tf_op jit(solution)/shard_map/ppermute | solution.py:39
  88.0 2.9 %constant_dynamic-update-slice_fusion.4 = bf16[3,3,640,640]{3,2,1,0:T(8,128)(2,1)} fusion(bf16[3,3,640,640]{3,2,1,0:T(8,128)(2,1)} %constant_dynamic-update-slice_fusion.5, bf16[3,3,160,640]{3,2,1,0:T(8,128)(2,1)} %collective-permute-done.4), kind=kLoop, calls=%fused_computation.73 | loop fusion | bytes 3686400
  90.8 2.2 %constant_dynamic-update-slice_fusion.3 = bf16[3,3,640,640]{3,2,1,0:T(8,128)(2,1)} fusion(bf16[3,3,640,640]{3,2,1,0:T(8,128)(2,1)} %constant_dynamic-update-slice_fusion.4, bf16[3,3,80,640]{3,2,1,0:T(8,128)(2,1)} %collective-permute-done.5), kind=kLoop, calls=%fused_computation.72 | loop fusion | bytes 1843200
  93.0 1.0 constant_dynamic-update-slice_fusion.2
  94.1 2.9 %constant_dynamic-update-slice_fusion.10 = bf16[3,3,640,640]{3,2,1,0:T(8,128)(2,1)} fusion(bf16[3,3,640,640]{3,2,1,0:T(8,128)(2,1)} %constant_dynamic-update-slice_fusion.11, bf16[3,3,160,640]{3,2,1,0:T(8,128)(2,1)} %collective-permute-done.9), kind=kLoop, calls=%fused_computation.79 | loop fusion | bytes 3686400
  97.0 1.1 constant_dynamic-update-slice_fusion.9
  98.0 1.0 constant_dynamic-update-slice_fusion.8
  99.1 1.0 constant_dynamic-update-slice_fusion.1
  100.1 1.0 constant_dynamic-update-slice_fusion.7
  101.1 1.0 constant_dynamic-update-slice_fusion
  102.2 13.4 %fusion.39 = bf16[24,6,10,640]{3,0,2,1:T(8,128)(2,1)} fusion(bf16[24,6,10,640]{3,0,2,1:T(8,128)(2,1)} %copy-done.2, bf16[3,3,640,640]{3,2,1,0:T(8,128)(2,1)} %constant_dynamic-update-slice_fusion, bf16[24,6,10,640]{3,0,2,1:T(8,128)(2,1)} %fusion.26, f32[640]{0:T(1024)S(1)} %copy-done.14, f32[640]{0:T(1024)S(1)} %copy-done.15, f32[24,640]{1,0:T(8,128)S(1)} %mul.128, ...), kind=kOutput, calls=%fused_computation.40 | convolution fusion | flops 6297763840 | bytes 10393600 | tf_op jit(solution)/shard_map/dot_general | solution.py:68
  115.6 1.0 fusion.95
  116.7 1.0 constant_dynamic-update-slice_fusion.6
  117.7 2.6 %fusion.12 = f32[48,4,1,640]{3,0,2,1:T(8,128)S(1)} fusion(bf16[3,3,640,640]{3,2,1,0:T(8,128)(2,1)} %constant_dynamic-update-slice_fusion.6, bf16[24,6,1,640]{3,0,2,1:T(8,128)(2,1)S(1)} %get-tuple-element.11, bf16[24,6,1,640]{3,0,2,1:T(8,128)(2,1)S(1)} %get-tuple-element.9), kind=kOutput, calls=%fused_computation.15 | convolution fusion | flops 472596480 | bytes 3317760 | tf_op jit(solution)/shard_map/conv_general_dilated | solution.py:77
  120.4 2.7 %fusion.10 = f32[48,4,1,640]{3,0,2,1:T(8,128)S(1)} fusion(bf16[3,3,640,640]{3,2,1,0:T(8,128)(2,1)} %constant_dynamic-update-slice_fusion.6, bf16[24,6,1,640]{3,0,2,1:T(8,128)(2,1)S(1)} %get-tuple-element.12, bf16[24,6,1,640]{3,0,2,1:T(8,128)(2,1)S(1)} %get-tuple-element.10), kind=kOutput, calls=%fused_computation.13 | convolution fusion | flops 472596480 | bytes 3317760 | tf_op jit(solution)/shard_map/conv_general_dilated | solution.py:77
  123.2 0.4 copy-done
  123.6 7.2 %fusion.44 = bf16[24,4,8,640]{3,0,2,1:T(8,128)(2,1)S(1)} fusion(f32[24,6,10,640]{3,0,2,1:T(8,128)S(1)} %copy-done, f32[24,4,1,640]{3,0,2,1:T(8,128)S(1)} %slice_subtract_fusion, f32[24,4,1,640]{3,0,2,1:T(8,128)S(1)} %slice_subtract_fusion.1, bf16[24,6,10,640]{3,0,2,1:T(8,128)(2,1)S(1)} %copy-done.3, bf16[3,3,640,640]{3,2,1,0:T(8,128)(2,1)S(1)} %copy-done.1, ...), kind=kOutput, calls=%fused_computation.41 | convolution fusion | flops 5665259520 | bytes 13642432 | tf_op jit(solution)/shard_map/conv_general_dilated | solution.py:77
  130.8 1.1 copy.43
  (62 shorter events, 1.7 us)
Async XLA Ops:
  0.0 72.6 %collective-permute-start.4 = (bf16[3,3,160,640]{3,2,1,0:T(8,128)(2,1)}, bf16[3,3,160,640]{3,2,1,0:T(8,128)(2,1)}, u32[]{:S(2)}, u32[]{:S(2)}) collective-permute-start(bf16[3,3,160,640]{3,2,1,0:T(8,128)(2,1)} %param.25), channel_id=1, source_target_pairs={{0,4},{4,0},{8,12},{12,8},{1,5},{5,1},{9,13},{13,9},{2,6},{6,2},{1... | collective-permute-start | bytes 5529608 | tf_op jit(solution)/shard_map/ppermute | solution.py:33
  2.2 10.3 %copy-start.9 = (s32[24,16]{0,1:T(8,128)S(1)}, s32[24,16]{0,1:T(8,128)}, u32[]{:S(2)}) copy-start(s32[24,16]{0,1:T(8,128)} %param.20) | copy-start | bytes 4612
  2.2 51.6 %collective-permute-start.5 = (bf16[3,3,80,640]{3,2,1,0:T(8,128)(2,1)}, bf16[3,3,80,640]{3,2,1,0:T(8,128)(2,1)}, u32[]{:S(2)}, u32[]{:S(2)}) collective-permute-start(bf16[3,3,80,640]{3,2,1,0:T(8,128)(2,1)} %dynamic-slice_bitcast_fusion.1), channel_id=1, source_target_pairs={{8,0},{12,4},{0,8},{4,12},{9,1},{13,5},{1,9},{5,13},{10,2},{14,6},... | collective-permute-start | bytes 2764808 | tf_op jit(solution)/shard_map/ppermute | solution.py:36
  8.0 22.8 %collective-permute-start = (bf16[2,24,1,8,640]{4,1,3,2,0:T(8,128)(2,1)}, bf16[2,24,1,8,640]{4,1,3,2,0:T(8,128)(2,1)S(1)}, u32[]{:S(2)}, u32[]{:S(2)}) collective-permute-start(bf16[2,24,1,8,640]{4,1,3,2,0:T(8,128)(2,1)} %get-tuple-element.7), channel_id=1, source_target_pairs={{0,4},{4,8},{8,12},{1,5},{5,9},{9,13},{2,6},{6,10},{10,14},{3,7},{... | collective-permute-start | bytes 1474568 | tf_op jit(solution)/shard_map/ppermute | solution.py:14
  9.9 21.6 %collective-permute-start.1 = (bf16[2,24,1,8,640]{4,1,3,2,0:T(8,128)(2,1)S(1)}, bf16[2,24,1,8,640]{4,1,3,2,0:T(8,128)(2,1)S(1)}, u32[]{:S(2)}, u32[]{:S(2)}) collective-permute-start(bf16[2,24,1,8,640]{4,1,3,2,0:T(8,128)(2,1)S(1)} %get-tuple-element.8), channel_id=1, source_target_pairs={{4,0},{8,4},{12,8},{5,1},{9,5},{13,9},{6,2},{10,6},{14,10},{7,3},{... | collective-permute-start | bytes 1474568 | tf_op jit(solution)/shard_map/ppermute | solution.py:17
  12.3 81.8 %collective-permute-start.9 = (bf16[3,3,160,640]{3,2,1,0:T(8,128)(2,1)}, bf16[3,3,160,640]{3,2,1,0:T(8,128)(2,1)}, u32[]{:S(2)}, u32[]{:S(2)}) collective-permute-start(bf16[3,3,160,640]{3,2,1,0:T(8,128)(2,1)} %param.32), channel_id=1, source_target_pairs={{0,4},{4,0},{8,12},{12,8},{1,5},{5,1},{9,13},{13,9},{2,6},{6,2},{1... | collective-permute-start | bytes 5529608 | tf_op jit(solution)/shard_map/ppermute | solution.py:33
  15.5 23.0 %copy-start.5 = (f32[24,32]{1,0:T(8,128)S(1)}, f32[24,32]{1,0:T(8,128)}, u32[]{:S(2)}) copy-start(f32[24,32]{1,0:T(8,128)} %param.29) | copy-start | bytes 9220
  15.5 23.4 %copy-start.6 = (f32[24,32]{1,0:T(8,128)S(1)}, f32[24,32]{1,0:T(8,128)}, u32[]{:S(2)}) copy-start(f32[24,32]{1,0:T(8,128)} %param.28) | copy-start | bytes 9220
  15.5 23.8 %copy-start.7 = (f32[24,32]{1,0:T(8,128)S(1)}, f32[24,32]{1,0:T(8,128)}, u32[]{:S(2)}) copy-start(f32[24,32]{1,0:T(8,128)} %param.22) | copy-start | bytes 9220
  18.5 21.3 %copy-start.8 = (f32[24,32]{1,0:T(8,128)S(1)}, f32[24,32]{1,0:T(8,128)}, u32[]{:S(2)}) copy-start(f32[24,32]{1,0:T(8,128)} %param.21) | copy-start | bytes 9220
  32.5 10.2 %collective-permute-start.2 = (bf16[2,24,6,1,640]{4,1,3,2,0:T(8,128)(2,1)}, bf16[2,24,6,1,640]{4,1,3,2,0:T(8,128)(2,1)}, u32[]{:S(2)}, u32[]{:S(2)}) collective-permute-start(bf16[2,24,6,1,640]{4,1,3,2,0:T(8,128)(2,1)} %get-tuple-element.5), channel_id=1, source_target_pairs={{0,1},{1,2},{2,3},{4,5},{5,6},{6,7},{8,9},{9,10},{10,11},{12,13},{... | collective-permute-start | bytes 1105928 | tf_op jit(solution)/shard_map/ppermute | solution.py:14
  36.7 8.6 %collective-permute-start.3 = (bf16[2,24,6,1,640]{4,1,3,2,0:T(8,128)(2,1)}, bf16[2,24,6,1,640]{4,1,3,2,0:T(8,128)(2,1)}, u32[]{:S(2)}, u32[]{:S(2)}) collective-permute-start(bf16[2,24,6,1,640]{4,1,3,2,0:T(8,128)(2,1)} %get-tuple-element.6), channel_id=1, source_target_pairs={{1,0},{2,1},{3,2},{5,4},{6,5},{7,6},{9,8},{10,9},{11,10},{13,12},{... | collective-permute-start | bytes 1105928 | tf_op jit(solution)/shard_map/ppermute | solution.py:17
  42.7 5.5 %copy-start.14 = (f32[640]{0:T(1024)S(1)}, f32[640]{0:T(1024)}, u32[]{:S(2)}) copy-start(f32[640]{0:T(1024)} %param.31) | copy-start | bytes 7684
  42.7 5.5 %copy-start.15 = (f32[640]{0:T(1024)S(1)}, f32[640]{0:T(1024)}, u32[]{:S(2)}) copy-start(f32[640]{0:T(1024)} %param.30) | copy-start | bytes 7684
  42.7 22.1 %collective-permute-start.10 = (bf16[3,3,80,640]{3,2,1,0:T(8,128)(2,1)S(1)}, bf16[3,3,80,640]{3,2,1,0:T(8,128)(2,1)S(1)}, u32[]{:S(2)}, u32[]{:S(2)}) collective-permute-start(bf16[3,3,80,640]{3,2,1,0:T(8,128)(2,1)S(1)} %dynamic-slice_bitcast_fusion), channel_id=1, source_target_pairs={{8,0},{12,4},{0,8},{4,12},{9,1},{13,5},{1,9},{5,13},{10,2},{14,6},... | collective-permute-start | bytes 2764808 | tf_op jit(solution)/shard_map/ppermute | solution.py:36
  51.6 21.0 %copy-start.2 = (bf16[24,6,10,640]{3,0,2,1:T(8,128)(2,1)}, bf16[24,6,10,640]{3,0,2,1:T(8,128)(2,1)S(1)}, u32[]{:S(2)}) copy-start(bf16[24,6,10,640]{3,0,2,1:T(8,128)(2,1)S(1)} %fusion.27) | copy-start | bytes 5529604
  51.6 15.0 %copy-start.4 = (f32[24,640]{1,0:T(8,128)S(1)}, f32[24,640]{1,0:T(8,128)}, u32[]{:S(2)}) copy-start(f32[24,640]{1,0:T(8,128)} %sub.87) | copy-start | bytes 184324
  51.6 15.0 %copy-start.12 = (f32[640]{0:T(1024)S(1)}, f32[640]{0:T(1024)}, u32[]{:S(2)}) copy-start(f32[640]{0:T(1024)} %param.24) | copy-start | bytes 7684
  51.6 15.0 %copy-start.13 = (f32[640]{0:T(1024)S(1)}, f32[640]{0:T(1024)}, u32[]{:S(2)}) copy-start(f32[640]{0:T(1024)} %param.23) | copy-start | bytes 7684
  53.8 22.6 %collective-permute-start.6 = (bf16[3,3,80,640]{3,2,1,0:T(8,128)(2,1)}, bf16[3,3,80,640]{3,2,1,0:T(8,128)(2,1)S(1)}, u32[]{:S(2)}, u32[]{:S(2)}) collective-permute-start(bf16[3,3,80,640]{3,2,1,0:T(8,128)(2,1)} %collective-permute-done.5), channel_id=1, source_target_pairs={{0,16},{16,0},{1,17},{17,1},{2,18},{18,2},{3,19},{19,3},{4,20},{20... | collective-permute-start | bytes 2764808 | tf_op jit(solution)/shard_map/ppermute | solution.py:37
  64.8 21.4 %collective-permute-start.11 = (bf16[3,3,80,640]{3,2,1,0:T(8,128)(2,1)S(1)}, bf16[3,3,80,640]{3,2,1,0:T(8,128)(2,1)S(1)}, u32[]{:S(2)}, u32[]{:S(2)}) collective-permute-start(bf16[3,3,80,640]{3,2,1,0:T(8,128)(2,1)S(1)} %collective-permute-done.10), channel_id=1, source_target_pairs={{0,1},{1,0},{2,3},{3,2},{4,5},{5,4},{6,7},{7,6},{8,9},{9,8},{10,11... | collective-permute-start | bytes 2764808 | tf_op jit(solution)/shard_map/ppermute | solution.py:37
  71.1 28.0 %collective-permute-start.7 = (bf16[3,3,80,640]{3,2,1,0:T(8,128)(2,1)}, bf16[3,3,80,640]{3,2,1,0:T(8,128)(2,1)S(1)}, u32[]{:S(2)}, u32[]{:S(2)}) collective-permute-start(bf16[3,3,80,640]{3,2,1,0:T(8,128)(2,1)} %collective-permute-done.5), channel_id=1, source_target_pairs={{0,4},{4,0},{8,12},{12,8},{1,5},{5,1},{9,13},{13,9},{2,6},{6,2},{1... | collective-permute-start | bytes 2764808 | tf_op jit(solution)/shard_map/ppermute | solution.py:38
  72.6 27.5 %collective-permute-start.12 = (bf16[3,3,80,640]{3,2,1,0:T(8,128)(2,1)S(1)}, bf16[3,3,80,640]{3,2,1,0:T(8,128)(2,1)S(1)}, u32[]{:S(2)}, u32[]{:S(2)}) collective-permute-start(bf16[3,3,80,640]{3,2,1,0:T(8,128)(2,1)S(1)} %collective-permute-done.10), channel_id=1, source_target_pairs={{0,4},{4,0},{8,12},{12,8},{1,5},{5,1},{9,13},{13,9},{2,6},{6,2},{1... | collective-permute-start | bytes 2764808 | tf_op jit(solution)/shard_map/ppermute | solution.py:38
  76.5 24.7 %collective-permute-start.8 = (bf16[3,3,80,640]{3,2,1,0:T(8,128)(2,1)S(1)}, bf16[3,3,80,640]{3,2,1,0:T(8,128)(2,1)S(1)}, u32[]{:S(2)}, u32[]{:S(2)}) collective-permute-start(bf16[3,3,80,640]{3,2,1,0:T(8,128)(2,1)S(1)} %collective-permute-done.6), channel_id=1, source_target_pairs={{0,4},{4,0},{8,12},{12,8},{1,5},{5,1},{9,13},{13,9},{2,6},{6,2},{1... | collective-permute-start | bytes 2764808 | tf_op jit(solution)/shard_map/ppermute | solution.py:39
  86.2 30.5 %collective-permute-start.13 = (bf16[3,3,80,640]{3,2,1,0:T(8,128)(2,1)S(1)}, bf16[3,3,80,640]{3,2,1,0:T(8,128)(2,1)S(1)}, u32[]{:S(2)}, u32[]{:S(2)}) collective-permute-start(bf16[3,3,80,640]{3,2,1,0:T(8,128)(2,1)S(1)} %collective-permute-done.11), channel_id=1, source_target_pairs={{0,4},{4,0},{8,12},{12,8},{1,5},{5,1},{9,13},{13,9},{2,6},{6,2},{1... | collective-permute-start | bytes 2764808 | tf_op jit(solution)/shard_map/ppermute | solution.py:39
  98.0 4.1 %copy-start.11 = (f32[24,640]{1,0:T(8,128)S(1)}, f32[24,640]{1,0:T(8,128)}, u32[]{:S(2)}) copy-start(f32[24,640]{1,0:T(8,128)} %param.27) | copy-start | bytes 184324
  98.0 4.1 %copy-start.16 = (f32[640]{0:T(1024)S(1)}, f32[640]{0:T(1024)}, u32[]{:S(2)}) copy-start(f32[640]{0:T(1024)} %param.26) | copy-start | bytes 7684
  102.2 21.0 %copy-start.10 = (bf16[24,4,8,640]{3,2,1,0:T(8,128)(2,1)S(1)}, bf16[24,4,8,640]{3,2,1,0:T(8,128)(2,1)}, u32[]{:S(2)}) copy-start(bf16[24,4,8,640]{3,2,1,0:T(8,128)(2,1)} %param.19) | copy-start | bytes 2949124
  116.7 6.5 %copy-start.3 = (bf16[24,6,10,640]{3,0,2,1:T(8,128)(2,1)S(1)}, bf16[24,6,10,640]{3,0,2,1:T(8,128)(2,1)}, u32[]{:S(2)}) copy-start(bf16[24,6,10,640]{3,0,2,1:T(8,128)(2,1)} %fusion.39) | copy-start | bytes 5529604
  117.7 5.4 %copy-start.1 = (bf16[3,3,640,640]{3,2,1,0:T(8,128)(2,1)S(1)}, bf16[3,3,640,640]{3,2,1,0:T(8,128)(2,1)}, u32[]{:S(2)}) copy-start(bf16[3,3,640,640]{3,2,1,0:T(8,128)(2,1)} %constant_dynamic-update-slice_fusion.6) | copy-start | bytes 22118404
  120.3 3.3 %copy-start = (f32[24,6,10,640]{3,0,2,1:T(8,128)S(1)}, f32[24,6,10,640]{3,0,2,1:T(8,128)}, u32[]{:S(2)}) copy-start(f32[24,6,10,640]{3,0,2,1:T(8,128)} %fusion.17) | copy-start | bytes 11059204
  120.3 3.3 %copy-start.17 = (f32[640]{0:T(1024)S(1)}, f32[640]{0:T(1024)}, u32[]{:S(2)}) copy-start(f32[640]{0:T(1024)} %param.33) | copy-start | bytes 7684

commit v8 on v7

--- a/solution.py
+++ b/solution.py
@@ -23,26 +23,28 @@
     count = lax.axis_size("row")
     chips = count // 2
     mate_pairs = [(i, i ^ 1) for i in range(count)]
-    wholes = []
+    mates = lax.ppermute(jnp.stack(kernels), "row", mate_pairs)
+    mine = []
     for shard, swap_axis in zip(kernels, swap_axes):
-        swap_pairs = [(i, i ^ 1) for i in range(lax.axis_size(swap_axis))]
-        parity = lax.axis_index(swap_axis) % 2
         depth = shard.shape[2]
         halves = shard.reshape(shard.shape[:2] + (2, depth // 2) + shard.shape[3:])
-        mine = lax.dynamic_index_in_dim(halves, parity, axis=2, keepdims=False)
-        held = [shard, lax.ppermute(shard, "row", mate_pairs)]
-        for step in range(1, chips):
-            pairs = [(((i // 2 + step) % chips) * 2 + i % 2, i) for i in range(count)]
-            fetched = lax.ppermute(mine, "row", pairs)
-            other = lax.ppermute(fetched, swap_axis, swap_pairs)
-            relayed = lax.ppermute(fetched, "row", mate_pairs)
+        parity = lax.axis_index(swap_axis) % 2
+        mine.append(lax.dynamic_index_in_dim(halves, parity, axis=2, keepdims=False))
+    mine = jnp.stack(mine)
+    held = [[shard, mates[index]] for index, shard in enumerate(kernels)]
+    for step in range(1, chips):
+        pairs = [(((i // 2 + step) % chips) * 2 + i % 2, i) for i in range(count)]
+        fetched = lax.ppermute(mine, "row", pairs)
+        relayed = lax.ppermute(fetched, "row", mate_pairs)
+        for index, swap_axis in enumerate(swap_axes):
+            swap_pairs = [(i, i ^ 1) for i in range(lax.axis_size(swap_axis))]
+            other = lax.ppermute(fetched[index], swap_axis, swap_pairs)
             other_relayed = lax.ppermute(other, "row", mate_pairs)
-            held += [
-                jnp.concatenate([fetched, other], axis=2),
-                jnp.concatenate([relayed, other_relayed], axis=2),
+            held[index] += [
+                jnp.concatenate([fetched[index], other], axis=2),
+                jnp.concatenate([relayed[index], other_relayed], axis=2),
             ]
-        wholes.append(jnp.concatenate(held, axis=2))
-    return wholes
+    return [jnp.concatenate(pieces, axis=2) for pieces in held]
 
 
 def relative_order(channels, swap_axis):

time: 132 us -> 133 us (level); the launches traced: 132 us -> 131 us
  local copies, waits for them, and re-layouts: 31.4 us -> 26.4 us
  waiting for transfers between devices: 38.3 us -> 42.8 us
  other arithmetic: 8.58 us -> 12.5 us
  starting transfers between devices: 19.4 us -> 15.5 us
    ppermute x2, waiting for transfers between devices: 12.3 us -> 34.8 us  [padded_2(): lax.ppermute(lax.slice_in_dim(block, block.shape[dim] - width, None, axis...]
    ppermute x2 -> x1, waiting for transfers between devices: 9.74 us -> 0.01 us  [gather_weights(): fetched = lax.ppermute(mine, 'row', pairs)]
    ppermute x4 -> x3, waiting for transfers between devices: 13.1 us -> 6.44 us  [the longest x2 6.44 us: gather_weights(): other = lax.ppermute(fetched[index], swap_axis, swap_pairs)]
    unnamed x46 -> x52, local copies, waits for them, and re-layouts: 19.5 us -> 15.3 us
    another operation x0 -> x2, other arithmetic: none -> 3.69 us  [the longest x1 2.25 us: gather_weights(): mates = lax.ppermute(jnp.stack(kernels), 'row', mate_pairs)]
    another operation x0 -> x1, local copies, waits for them, and re-layouts: none -> 1.77 us  [gather_weights(): mine = jnp.stack(mine)]
    ppermute x2, starting transfers between devices: 2.21 us -> 0.51 us  [gather_weights(): other_relayed = lax.ppermute(other, 'row', mate_pairs)]
    ppermute x2, waiting for transfers between devices: 3.21 us -> 1.55 us  [padded_2(): lax.ppermute(lax.slice_in_dim(block, 0, width, axis=dim), axis, backward)]
  transfers between devices with their start and end apart: 14 -> 11, of which waited for: 6 -> 5; matrix products, arithmetic and copies ran while one was open for 44% -> 41% of each run, Pallas kernels for 0% -> 0%
where the time goes in v8:
time: 133 us; the launch traced here: 131 us
  waiting for transfers between devices  42.8 us (32%)
  matrix products  33.8 us (25%)
  local copies, waits for them, and re-layouts  26.4 us (20%)
  starting transfers between devices  15.5 us (12%)
  other arithmetic  12.5 us (9%)
    ppermute x2, waiting for transfers between devices, padded_2(): lax.ppermute(lax.slice_in_dim(block, block.shape[dim] - width, None, axis...  34.8 us
    dot_general x3, matrix products, to_relative(): moved = jnp.dot(activation, chooser, preferred_element_type=jnp.float32)  21.3 us
    unnamed x52, local copies, waits for them, and re-layouts  15.3 us
    conv_general_dilated x3, matrix products, conv_valid(): lax.conv_general_dilated(activation, kernel, window_strides=(1, 1), paddi...  12.6 us
    ppermute x2, waiting for transfers between devices, gather_weights(): other = lax.ppermute(fetched[index], swap_axis, swap_pairs)  6.44 us
    ppermute x2, starting transfers between devices, padded_2(): lax.ppermute(lax.slice_in_dim(block, block.shape[dim] - width, None, axis...  6.1 us
    ppermute x2, starting transfers between devices, padded_2(): lax.ppermute(lax.slice_in_dim(block, 0, width, axis=dim), axis, backward)  3.71 us
    concatenate x1, other arithmetic, padded_2(): block = jnp.concatenate([low, block, high], axis=dim)  2.97 us
  transfers between devices with their start and end apart: 11, of which 5 were waited for; matrix products, arithmetic and copies ran while one was open for 41% of the time, Pallas kernels for 0%

profile of v8, /device:TPU:1, one launch (start us, length us, event | category | flops | bytes accessed | tf_op | source)
XLA Modules:
  0.0 131.5 jit_solution(2140543041951782236)
XLA Ops:
  0.0 1.8 %dynamic-slice_bitcast_fusion = (bf16[1,3,3,80,640]{4,3,2,1,0:T(8,128)(2,1)S(1)}, bf16[1,3,3,80,640]{4,3,2,1,0:T(8,128)(2,1)S(1)}) fusion(bf16[3,3,2,80,640]{4,3,2,1,0:T(8,128)(2,1)} %bitcast.78, s32[]{:T(128)S(6)} %select_n.187, bf16[3,3,2,80,640]{4,3,2,1,0:T(8,128)(2,1)} %bitcast.76, s32[]{:T(128)S(6)} %select_n.186), kind=kLoop, calls=%fused_computation.62 | loop fusion | bytes 3686408 | tf_op jit(solution)/shard_map/stack | solution.py:33
  1.8 1.4 %pad_maximum_fusion.2 = bf16[2,3,3,80,640]{4,3,2,1,0:T(8,128)(2,1)} fusion(bf16[1,3,3,80,640]{4,3,2,1,0:T(8,128)(2,1)S(1)} %get-tuple-element.25, bf16[1,3,3,80,640]{4,3,2,1,0:T(8,128)(2,1)S(1)} %get-tuple-element.26), kind=kLoop, calls=%fused_computation.29 | loop fusion | flops 921600 | bytes 3686400 | tf_op jit(solution)/shard_map/stack | solution.py:33
  3.2 2.0 %collective-permute-start.5 = (bf16[2,3,3,80,640]{4,3,2,1,0:T(8,128)(2,1)}, bf16[2,3,3,80,640]{4,3,2,1,0:T(8,128)(2,1)}, u32[]{:S(2)}, u32[]{:S(2)}) collective-permute-start(bf16[2,3,3,80,640]{4,3,2,1,0:T(8,128)(2,1)} %pad_maximum_fusion.2), channel_id=1, source_target_pairs={{8,0},{12,4},{0,8},{4,12},{9,1},{13,5},{1,9},{5,13},{10,2},{14,6},... | collective-permute-start | bytes 5529608 | tf_op jit(solution)/shard_map/ppermute | solution.py:37
  5.3 2.2 %pad_maximum_fusion.1 = bf16[2,3,3,160,640]{4,3,2,1,0:T(8,128)(2,1)} fusion(bf16[1,3,3,160,640]{4,3,2,1,0:T(8,128)(2,1)S(1)} %bitcast.79, bf16[1,3,3,160,640]{4,3,2,1,0:T(8,128)(2,1)S(1)} %bitcast.77), kind=kLoop, calls=%fused_computation.1 | loop fusion | flops 1843200 | bytes 7372800 | tf_op jit(solution)/shard_map/stack | solution.py:26
  7.5 1.0 collective-permute-start.4
  8.5 0.7 copy_bitcast_fusion
  9.2 0.9 pad_maximum_fusion.4
  10.0 1.9 %collective-permute-start = (bf16[2,24,1,8,640]{4,1,3,2,0:T(8,128)(2,1)}, bf16[2,24,1,8,640]{4,1,3,2,0:T(8,128)(2,1)S(1)}, u32[]{:S(2)}, u32[]{:S(2)}) collective-permute-start(bf16[2,24,1,8,640]{4,1,3,2,0:T(8,128)(2,1)} %get-tuple-element.9), channel_id=1, source_target_pairs={{0,4},{4,8},{8,12},{1,5},{5,9},{9,13},{2,6},{6,10},{10,14},{3,7},{... | collective-permute-start | bytes 1474568 | tf_op jit(solution)/shard_map/ppermute | solution.py:14
  12.0 2.4 %collective-permute-start.1 = (bf16[2,24,1,8,640]{4,1,3,2,0:T(8,128)(2,1)S(1)}, bf16[2,24,1,8,640]{4,1,3,2,0:T(8,128)(2,1)S(1)}, u32[]{:S(2)}, u32[]{:S(2)}) collective-permute-start(bf16[2,24,1,8,640]{4,1,3,2,0:T(8,128)(2,1)S(1)} %get-tuple-element.10), channel_id=1, source_target_pairs={{4,0},{8,4},{12,8},{5,1},{9,5},{13,9},{6,2},{10,6},{14,10},{7,3},{... | collective-permute-start | bytes 1474568 | tf_op jit(solution)/shard_map/ppermute | solution.py:17
  14.5 4.2 %constant_dynamic-update-slice_fusion.3 = (bf16[3,3,640,640]{3,2,1,0:T(8,128)(2,1)}, bf16[3,3,640,640]{3,2,1,0:T(8,128)(2,1)}) fusion(bf16[3,3,160,640]{3,2,1,0:T(8,128)(2,1)} %param.25, bf16[3,3,160,640]{3,2,1,0:T(8,128)(2,1)} %param.32), kind=kLoop, calls=%fused_computation.84 | loop fusion | bytes 7372800
  18.8 32.1 %collective-permute-done = bf16[2,24,1,8,640]{4,1,3,2,0:T(8,128)(2,1)S(1)} collective-permute-done((bf16[2,24,1,8,640]{4,1,3,2,0:T(8,128)(2,1)}, bf16[2,24,1,8,640]{4,1,3,2,0:T(8,128)(2,1)S(1)}, u32[]{:S(2)}, u32[]{:S(2)}) %collective-permute-start) | collective-permute-done | bytes 491552 | tf_op jit(solution)/shard_map/ppermute | solution.py:14
  50.8 0.3 collective-permute-done.1
  51.2 1.0 pad_maximum_fusion.8
  52.2 4.2 %collective-permute-start.2 = (bf16[2,24,6,1,640]{4,1,3,2,0:T(8,128)(2,1)}, bf16[2,24,6,1,640]{4,1,3,2,0:T(8,128)(2,1)}, u32[]{:S(2)}, u32[]{:S(2)}) collective-permute-start(bf16[2,24,6,1,640]{4,1,3,2,0:T(8,128)(2,1)} %get-tuple-element.7), channel_id=1, source_target_pairs={{0,1},{1,2},{2,3},{4,5},{5,6},{6,7},{8,9},{9,10},{10,11},{12,13},{... | collective-permute-start | bytes 1105928 | tf_op jit(solution)/shard_map/ppermute | solution.py:14
  56.4 1.3 collective-permute-start.3
  57.7 0.6 fusion.88
  58.3 0.5 add_add_fusion
  59.0 0.2 mul.128
  59.4 0.2 sub.77
  59.6 0.2 broadcast_in_dim.65
  59.8 0.2 mul.141
  60.2 0.9 sub.87
  61.0 0.7 compare_reduce_fusion
  61.7 2.7 %collective-permute-done.2 = bf16[2,24,6,1,640]{4,1,3,2,0:T(8,128)(2,1)} collective-permute-done((bf16[2,24,6,1,640]{4,1,3,2,0:T(8,128)(2,1)}, bf16[2,24,6,1,640]{4,1,3,2,0:T(8,128)(2,1)}, u32[]{:S(2)}, u32[]{:S(2)}) %collective-permute-start.2) | collective-permute-done | bytes 368672 | tf_op jit(solution)/shard_map/ppermute | solution.py:14
  64.4 1.2 collective-permute-done.3
  65.6 3.0 %pad_maximum_fusion = bf16[2,24,6,10,640]{4,1,3,2,0:T(8,128)(2,1)S(1)} fusion(bf16[2,24,6,1,640]{4,1,3,2,0:T(8,128)(2,1)} %collective-permute-done.3, bf16[2,24,1,8,640]{4,1,3,2,0:T(8,128)(2,1)S(1)} %collective-permute-done.1, bf16[1,24,4,8,640]{4,1,3,2,0:T(8,128)(2,1)S(1)} %get-tuple-element.21, bf16[1,24,4,8,640]{4,1,3,2,0:T(8,128)(2,1)S(1)} %get-tuple-element.22, ...), kind=kLoop, calls=%fused_computation | loop fusion | flops 9216000 | bytes 7372800 | tf_op jit(solution)/shard_map/concatenate | solution.py:18
  68.6 2.1 %fusion.19 = f32[24,6,10,640]{3,0,2,1:T(8,128)} fusion(bf16[2,24,6,10,640]{4,1,3,2,0:T(8,128)(2,1)S(1)} %pad_maximum_fusion), kind=kLoop, calls=%fused_computation.27 | loop fusion | flops 921600 | bytes 5529600 | tf_op jit(solution)/shard_map/convert_element_type | solution.py:126
  70.7 3.3 %fusion.29 = bf16[24,6,10,640]{3,0,2,1:T(8,128)(2,1)S(1)} fusion(bf16[2,24,6,10,640]{4,1,3,2,0:T(8,128)(2,1)S(1)} %pad_maximum_fusion, f32[6,10]{1,0:T(8,128)S(1)} %and_convert_fusion, f32[640]{0:T(1024)S(1)} %copy-done.19, f32[640]{0:T(1024)S(1)} %copy-done.20, f32[24,640]{1,0:T(8,128)S(1)} %mul.128, f32[24,640]{1,0:T(8,128)S(1)} %sub.77, s32[640]{0:T(1024)S(1)} %fusion.87), kind=kOutput, calls=%fused_computation.39 | convolution fusion | flops 1191116800 | bytes 3825664 | tf_op jit(solution)/shard_map/dot_general | solution.py:70
  74.0 2.3 %slice_bitcast_fusion.8 = (bf16[3,3,80,640]{3,2,1,0:T(8,128)(2,1)S(1)}, bf16[3,3,80,640]{3,2,1,0:T(8,128)(2,1)S(1)}) fusion(bf16[2,3,3,80,640]{4,3,2,1,0:T(8,128)(2,1)} %collective-permute-done.5), kind=kLoop, calls=%fused_computation.61 | loop fusion | bytes 3686400 | tf_op jit(solution)/shard_map/squeeze | solution.py:44
  76.3 1.0 collective-permute-start.9
  77.3 1.2 collective-permute-start.6
  78.6 4.5 %fusion.28 = bf16[24,6,10,640]{3,0,2,1:T(8,128)(2,1)} fusion(f32[640]{0:T(1024)S(1)} %copy-done.17, f32[640]{0:T(1024)S(1)} %copy-done.18, f32[24,640]{1,0:T(8,128)S(1)} %mul.141, f32[24,640]{1,0:T(8,128)S(1)} %copy-done.8, f32[6,10]{1,0:T(8,128)S(1)} %and_convert_fusion, s32[640]{0:T(1024)S(1)} %copy-done.14, ...), kind=kOutput, calls=%fused_computation.38 | convolution fusion | flops 1190195200 | bytes 3825664 | tf_op jit(solution)/shard_map/dot_general | solution.py:70
  83.1 6.4 %collective-permute-done.6 = bf16[3,3,80,640]{3,2,1,0:T(8,128)(2,1)S(1)} collective-permute-done((bf16[3,3,80,640]{3,2,1,0:T(8,128)(2,1)S(1)}, bf16[3,3,80,640]{3,2,1,0:T(8,128)(2,1)S(1)}, u32[]{:S(2)}, u32[]{:S(2)}) %collective-permute-start.6) | collective-permute-done | bytes 921632 | tf_op jit(solution)/shard_map/ppermute | solution.py:41
  89.6 0.5 collective-permute-start.10
  90.1 4.2 %fusion.18 = (bf16[3,3,640,640]{3,2,1,0:T(8,128)(2,1)}, bf16[3,3,640,640]{3,2,1,0:T(8,128)(2,1)}) fusion(bf16[3,3,640,640]{3,2,1,0:T(8,128)(2,1)} %get-tuple-element.23, bf16[2,3,3,160,640]{4,3,2,1,0:T(8,128)(2,1)} %collective-permute-done.4, bf16[3,3,640,640]{3,2,1,0:T(8,128)(2,1)} %get-tuple-element.24), kind=kLoop, calls=%fused_computation.25 | loop fusion | bytes 7372800
  94.3 2.9 %constant_dynamic-update-slice_fusion.2 = (bf16[3,3,640,640]{3,2,1,0:T(8,128)(2,1)}, bf16[3,3,640,640]{3,2,1,0:T(8,128)(2,1)}) fusion(bf16[3,3,640,640]{3,2,1,0:T(8,128)(2,1)} %get-tuple-element.5, bf16[2,3,3,80,640]{4,3,2,1,0:T(8,128)(2,1)} %collective-permute-done.5, bf16[3,3,640,640]{3,2,1,0:T(8,128)(2,1)} %get-tuple-element.6), kind=kLoop, calls=%fused_computation.83 | loop fusion | bytes 3686400
  97.2 1.0 constant_dynamic-update-slice_fusion.5
  98.3 1.0 constant_dynamic-update-slice_fusion.1
  99.3 1.4 %fusion.56 = (bf16[3,3,640,640]{3,2,1,0:T(8,128)(2,1)}, bf16[3,3,640,640]{3,2,1,0:T(8,128)(2,1)}) fusion(bf16[3,3,640,640]{3,2,1,0:T(8,128)(2,1)} %constant_dynamic-update-slice_fusion.1, bf16[2,3,3,80,640]{4,3,2,1,0:T(8,128)(2,1)S(1)} %collective-permute-done.7, bf16[3,3,640,640]{3,2,1,0:T(8,128)(2,1)} %constant_dynamic-update-slice_fusion.5), kind=kLoop, calls=%fused_computation.60 | loop fusion | bytes 3686400
  100.7 1.0 constant_dynamic-update-slice_fusion
  101.7 13.5 %fusion.41 = bf16[24,6,10,640]{3,0,2,1:T(8,128)(2,1)} fusion(bf16[24,6,10,640]{3,0,2,1:T(8,128)(2,1)} %copy-done.6, bf16[3,3,640,640]{3,2,1,0:T(8,128)(2,1)} %constant_dynamic-update-slice_fusion, bf16[24,6,10,640]{3,0,2,1:T(8,128)(2,1)} %fusion.28, f32[640]{0:T(1024)S(1)} %copy-done.19, f32[640]{0:T(1024)S(1)} %copy-done.20, f32[24,640]{1,0:T(8,128)S(1)} %mul.128, ...), kind=kOutput, calls=%fused_computation.46 | convolution fusion | flops 6297763840 | bytes 10393600 | tf_op jit(solution)/shard_map/dot_general | solution.py:70
  115.2 1.0 fusion.99
  116.2 1.0 constant_dynamic-update-slice_fusion.4
  117.3 2.6 %fusion.12 = f32[48,4,1,640]{3,0,2,1:T(8,128)S(1)} fusion(bf16[3,3,640,640]{3,2,1,0:T(8,128)(2,1)} %constant_dynamic-update-slice_fusion.4, bf16[24,6,1,640]{3,0,2,1:T(8,128)(2,1)S(1)} %get-tuple-element.13, bf16[24,6,1,640]{3,0,2,1:T(8,128)(2,1)S(1)} %get-tuple-element.11), kind=kOutput, calls=%fused_computation.16 | convolution fusion | flops 472596480 | bytes 3317760 | tf_op jit(solution)/shard_map/conv_general_dilated | solution.py:79
  119.9 2.7 %fusion.10 = f32[48,4,1,640]{3,0,2,1:T(8,128)S(1)} fusion(bf16[3,3,640,640]{3,2,1,0:T(8,128)(2,1)} %constant_dynamic-update-slice_fusion.4, bf16[24,6,1,640]{3,0,2,1:T(8,128)(2,1)S(1)} %get-tuple-element.14, bf16[24,6,1,640]{3,0,2,1:T(8,128)(2,1)S(1)} %get-tuple-element.12), kind=kOutput, calls=%fused_computation.14 | convolution fusion | flops 472596480 | bytes 3317760 | tf_op jit(solution)/shard_map/conv_general_dilated | solution.py:79
  122.7 0.4 copy-done.2
  123.1 7.2 %fusion.46 = bf16[24,4,8,640]{3,0,2,1:T(8,128)(2,1)S(1)} fusion(f32[24,6,10,640]{3,0,2,1:T(8,128)S(1)} %copy-done.2, f32[24,4,1,640]{3,0,2,1:T(8,128)S(1)} %slice_subtract_fusion, f32[24,4,1,640]{3,0,2,1:T(8,128)S(1)} %slice_subtract_fusion.1, bf16[24,6,10,640]{3,0,2,1:T(8,128)(2,1)S(1)} %copy-done.7, bf16[3,3,640,640]{3,2,1,0:T(8,128)(2,1)S(1)} %copy-done.5, ...), kind=kOutput, calls=%fused_computation.47 | convolution fusion | flops 5665259520 | bytes 13642432 | tf_op jit(solution)/shard_map/conv_general_dilated | solution.py:79
  130.4 1.1 copy.43
  (64 shorter events, 0.8 us)
Async XLA Ops:
  0.0 5.3 %copy-start = (bf16[3,3,160,640]{3,2,1,0:T(8,128)(2,1)S(1)}, bf16[3,3,160,640]{3,2,1,0:T(8,128)(2,1)}, u32[]{:S(2)}) copy-start(bf16[3,3,160,640]{3,2,1,0:T(8,128)(2,1)} %param.25) | copy-start | bytes 5529604
  0.0 5.3 %copy-start.1 = (bf16[3,3,160,640]{3,2,1,0:T(8,128)(2,1)S(1)}, bf16[3,3,160,640]{3,2,1,0:T(8,128)(2,1)}, u32[]{:S(2)}) copy-start(bf16[3,3,160,640]{3,2,1,0:T(8,128)(2,1)} %param.32) | copy-start | bytes 5529604
  3.2 70.8 %collective-permute-start.5 = (bf16[2,3,3,80,640]{4,3,2,1,0:T(8,128)(2,1)}, bf16[2,3,3,80,640]{4,3,2,1,0:T(8,128)(2,1)}, u32[]{:S(2)}, u32[]{:S(2)}) collective-permute-start(bf16[2,3,3,80,640]{4,3,2,1,0:T(8,128)(2,1)} %pad_maximum_fusion.2), channel_id=1, source_target_pairs={{8,0},{12,4},{0,8},{4,12},{9,1},{13,5},{1,9},{5,13},{10,2},{14,6},... | collective-permute-start | bytes 5529608 | tf_op jit(solution)/shard_map/ppermute | solution.py:37
  5.3 3.2 %copy-start.3 = (bf16[24,4,8,640]{3,2,1,0:T(8,128)(2,1)S(1)}, bf16[24,4,8,640]{3,2,1,0:T(8,128)(2,1)}, u32[]{:S(2)}) copy-start(bf16[24,4,8,640]{3,2,1,0:T(8,128)(2,1)} %param.18) | copy-start | bytes 2949124
  5.3 3.2 %copy-start.4 = (bf16[24,4,8,640]{3,2,1,0:T(8,128)(2,1)S(1)}, bf16[24,4,8,640]{3,2,1,0:T(8,128)(2,1)}, u32[]{:S(2)}) copy-start(bf16[24,4,8,640]{3,2,1,0:T(8,128)(2,1)} %param.17) | copy-start | bytes 2949124
  7.5 82.6 %collective-permute-start.4 = (bf16[2,3,3,160,640]{4,3,2,1,0:T(8,128)(2,1)}, bf16[2,3,3,160,640]{4,3,2,1,0:T(8,128)(2,1)}, u32[]{:S(2)}, u32[]{:S(2)}) collective-permute-start(bf16[2,3,3,160,640]{4,3,2,1,0:T(8,128)(2,1)} %pad_maximum_fusion.1), channel_id=1, source_target_pairs={{0,4},{4,0},{8,12},{12,8},{1,5},{5,1},{9,13},{13,9},{2,6},{6,2},{1... | collective-permute-start | bytes 11059208 | tf_op jit(solution)/shard_map/ppermute | solution.py:26
  10.0 40.8 %collective-permute-start = (bf16[2,24,1,8,640]{4,1,3,2,0:T(8,128)(2,1)}, bf16[2,24,1,8,640]{4,1,3,2,0:T(8,128)(2,1)S(1)}, u32[]{:S(2)}, u32[]{:S(2)}) collective-permute-start(bf16[2,24,1,8,640]{4,1,3,2,0:T(8,128)(2,1)} %get-tuple-element.9), channel_id=1, source_target_pairs={{0,4},{4,8},{8,12},{1,5},{5,9},{9,13},{2,6},{6,10},{10,14},{3,7},{... | collective-permute-start | bytes 1474568 | tf_op jit(solution)/shard_map/ppermute | solution.py:14
  12.0 39.2 %collective-permute-start.1 = (bf16[2,24,1,8,640]{4,1,3,2,0:T(8,128)(2,1)S(1)}, bf16[2,24,1,8,640]{4,1,3,2,0:T(8,128)(2,1)S(1)}, u32[]{:S(2)}, u32[]{:S(2)}) collective-permute-start(bf16[2,24,1,8,640]{4,1,3,2,0:T(8,128)(2,1)S(1)} %get-tuple-element.10), channel_id=1, source_target_pairs={{4,0},{8,4},{12,8},{5,1},{9,5},{13,9},{6,2},{10,6},{14,10},{7,3},{... | collective-permute-start | bytes 1474568 | tf_op jit(solution)/shard_map/ppermute | solution.py:17
  18.7 40.1 %copy-start.9 = (f32[24,32]{1,0:T(8,128)S(1)}, f32[24,32]{1,0:T(8,128)}, u32[]{:S(2)}) copy-start(f32[24,32]{1,0:T(8,128)} %param.29) | copy-start | bytes 9220
  18.7 40.5 %copy-start.10 = (f32[24,32]{1,0:T(8,128)S(1)}, f32[24,32]{1,0:T(8,128)}, u32[]{:S(2)}) copy-start(f32[24,32]{1,0:T(8,128)} %param.28) | copy-start | bytes 9220
  18.7 40.9 %copy-start.11 = (f32[24,32]{1,0:T(8,128)S(1)}, f32[24,32]{1,0:T(8,128)}, u32[]{:S(2)}) copy-start(f32[24,32]{1,0:T(8,128)} %param.22) | copy-start | bytes 9220
  18.7 41.2 %copy-start.12 = (f32[24,32]{1,0:T(8,128)S(1)}, f32[24,32]{1,0:T(8,128)}, u32[]{:S(2)}) copy-start(f32[24,32]{1,0:T(8,128)} %param.21) | copy-start | bytes 9220
  18.8 42.3 %copy-start.13 = (s32[24,16]{0,1:T(8,128)S(1)}, s32[24,16]{0,1:T(8,128)}, u32[]{:S(2)}) copy-start(s32[24,16]{0,1:T(8,128)} %param.20) | copy-start | bytes 4612
  52.2 12.2 %collective-permute-start.2 = (bf16[2,24,6,1,640]{4,1,3,2,0:T(8,128)(2,1)}, bf16[2,24,6,1,640]{4,1,3,2,0:T(8,128)(2,1)}, u32[]{:S(2)}, u32[]{:S(2)}) collective-permute-start(bf16[2,24,6,1,640]{4,1,3,2,0:T(8,128)(2,1)} %get-tuple-element.7), channel_id=1, source_target_pairs={{0,1},{1,2},{2,3},{4,5},{5,6},{6,7},{8,9},{9,10},{10,11},{12,13},{... | collective-permute-start | bytes 1105928 | tf_op jit(solution)/shard_map/ppermute | solution.py:14
  56.4 9.2 %collective-permute-start.3 = (bf16[2,24,6,1,640]{4,1,3,2,0:T(8,128)(2,1)}, bf16[2,24,6,1,640]{4,1,3,2,0:T(8,128)(2,1)}, u32[]{:S(2)}, u32[]{:S(2)}) collective-permute-start(bf16[2,24,6,1,640]{4,1,3,2,0:T(8,128)(2,1)} %get-tuple-element.8), channel_id=1, source_target_pairs={{1,0},{2,1},{3,2},{5,4},{6,5},{7,6},{9,8},{10,9},{11,10},{13,12},{... | collective-permute-start | bytes 1105928 | tf_op jit(solution)/shard_map/ppermute | solution.py:17
  68.6 2.1 %copy-start.19 = (f32[640]{0:T(1024)S(1)}, f32[640]{0:T(1024)}, u32[]{:S(2)}) copy-start(f32[640]{0:T(1024)} %param.31) | copy-start | bytes 7684
  68.6 2.1 %copy-start.20 = (f32[640]{0:T(1024)S(1)}, f32[640]{0:T(1024)}, u32[]{:S(2)}) copy-start(f32[640]{0:T(1024)} %param.30) | copy-start | bytes 7684
  74.0 9.2 %copy-start.6 = (bf16[24,6,10,640]{3,0,2,1:T(8,128)(2,1)}, bf16[24,6,10,640]{3,0,2,1:T(8,128)(2,1)S(1)}, u32[]{:S(2)}) copy-start(bf16[24,6,10,640]{3,0,2,1:T(8,128)(2,1)S(1)} %fusion.29) | copy-start | bytes 5529604
  74.0 4.6 %copy-start.8 = (f32[24,640]{1,0:T(8,128)S(1)}, f32[24,640]{1,0:T(8,128)}, u32[]{:S(2)}) copy-start(f32[24,640]{1,0:T(8,128)} %sub.87) | copy-start | bytes 184324
  74.0 4.6 %copy-start.14 = (s32[640]{0:T(1024)S(1)}, s32[640]{0:T(1024)}, u32[]{:S(2)}) copy-start(s32[640]{0:T(1024)} %fusion.88) | copy-start | bytes 7684
  74.0 4.6 %copy-start.17 = (f32[640]{0:T(1024)S(1)}, f32[640]{0:T(1024)}, u32[]{:S(2)}) copy-start(f32[640]{0:T(1024)} %param.24) | copy-start | bytes 7684
  74.0 4.6 %copy-start.18 = (f32[640]{0:T(1024)S(1)}, f32[640]{0:T(1024)}, u32[]{:S(2)}) copy-start(f32[640]{0:T(1024)} %param.23) | copy-start | bytes 7684
  76.3 13.2 %collective-permute-start.9 = (bf16[3,3,80,640]{3,2,1,0:T(8,128)(2,1)S(1)}, bf16[3,3,80,640]{3,2,1,0:T(8,128)(2,1)S(1)}, u32[]{:S(2)}, u32[]{:S(2)}) collective-permute-start(bf16[3,3,80,640]{3,2,1,0:T(8,128)(2,1)S(1)} %get-tuple-element.18), channel_id=1, source_target_pairs={{0,1},{1,0},{2,3},{3,2},{4,5},{5,4},{6,7},{7,6},{8,9},{9,8},{10,11... | collective-permute-start | bytes 2764808 | tf_op jit(solution)/shard_map/ppermute | solution.py:41
  77.3 12.3 %collective-permute-start.6 = (bf16[3,3,80,640]{3,2,1,0:T(8,128)(2,1)S(1)}, bf16[3,3,80,640]{3,2,1,0:T(8,128)(2,1)S(1)}, u32[]{:S(2)}, u32[]{:S(2)}) collective-permute-start(bf16[3,3,80,640]{3,2,1,0:T(8,128)(2,1)S(1)} %get-tuple-element.17), channel_id=1, source_target_pairs={{0,16},{16,0},{1,17},{17,1},{2,18},{18,2},{3,19},{19,3},{4,20},{20... | collective-permute-start | bytes 2764808 | tf_op jit(solution)/shard_map/ppermute | solution.py:41
  78.5 20.8 %collective-permute-start.7 = (bf16[2,3,3,80,640]{4,3,2,1,0:T(8,128)(2,1)}, bf16[2,3,3,80,640]{4,3,2,1,0:T(8,128)(2,1)S(1)}, u32[]{:S(2)}, u32[]{:S(2)}) collective-permute-start(bf16[2,3,3,80,640]{4,3,2,1,0:T(8,128)(2,1)} %collective-permute-done.5), channel_id=1, source_target_pairs={{0,4},{4,0},{8,12},{12,8},{1,5},{5,1},{9,13},{13,9},{2,6},{6,2},{1... | collective-permute-start | bytes 5529608 | tf_op jit(solution)/shard_map/ppermute | solution.py:38
  89.6 11.1 %collective-permute-start.8 = (bf16[3,3,80,640]{3,2,1,0:T(8,128)(2,1)S(1)}, bf16[3,3,80,640]{3,2,1,0:T(8,128)(2,1)S(1)}, u32[]{:S(2)}, u32[]{:S(2)}) collective-permute-start(bf16[3,3,80,640]{3,2,1,0:T(8,128)(2,1)S(1)} %collective-permute-done.6), channel_id=1, source_target_pairs={{0,4},{4,0},{8,12},{12,8},{1,5},{5,1},{9,13},{13,9},{2,6},{6,2},{1... | collective-permute-start | bytes 2764808 | tf_op jit(solution)/shard_map/ppermute | solution.py:42
  89.6 26.7 %collective-permute-start.10 = (bf16[3,3,80,640]{3,2,1,0:T(8,128)(2,1)S(1)}, bf16[3,3,80,640]{3,2,1,0:T(8,128)(2,1)S(1)}, u32[]{:S(2)}, u32[]{:S(2)}) collective-permute-start(bf16[3,3,80,640]{3,2,1,0:T(8,128)(2,1)S(1)} %collective-permute-done.9), channel_id=1, source_target_pairs={{0,4},{4,0},{8,12},{12,8},{1,5},{5,1},{9,13},{13,9},{2,6},{6,2},{1... | collective-permute-start | bytes 2764808 | tf_op jit(solution)/shard_map/ppermute | solution.py:42
  98.3 3.4 %copy-start.16 = (f32[24,640]{1,0:T(8,128)S(1)}, f32[24,640]{1,0:T(8,128)}, u32[]{:S(2)}) copy-start(f32[24,640]{1,0:T(8,128)} %param.27) | copy-start | bytes 184324
  98.3 3.4 %copy-start.21 = (f32[640]{0:T(1024)S(1)}, f32[640]{0:T(1024)}, u32[]{:S(2)}) copy-start(f32[640]{0:T(1024)} %param.26) | copy-start | bytes 7684
  101.7 21.0 %copy-start.15 = (bf16[24,4,8,640]{3,2,1,0:T(8,128)(2,1)S(1)}, bf16[24,4,8,640]{3,2,1,0:T(8,128)(2,1)}, u32[]{:S(2)}) copy-start(bf16[24,4,8,640]{3,2,1,0:T(8,128)(2,1)} %param.19) | copy-start | bytes 2949124
  116.2 6.5 %copy-start.7 = (bf16[24,6,10,640]{3,0,2,1:T(8,128)(2,1)S(1)}, bf16[24,6,10,640]{3,0,2,1:T(8,128)(2,1)}, u32[]{:S(2)}) copy-start(bf16[24,6,10,640]{3,0,2,1:T(8,128)(2,1)} %fusion.41) | copy-start | bytes 5529604
  117.3 5.4 %copy-start.5 = (bf16[3,3,640,640]{3,2,1,0:T(8,128)(2,1)S(1)}, bf16[3,3,640,640]{3,2,1,0:T(8,128)(2,1)}, u32[]{:S(2)}) copy-start(bf16[3,3,640,640]{3,2,1,0:T(8,128)(2,1)} %constant_dynamic-update-slice_fusion.4) | copy-start | bytes 22118404
  119.9 3.3 %copy-start.2 = (f32[24,6,10,640]{3,0,2,1:T(8,128)S(1)}, f32[24,6,10,640]{3,0,2,1:T(8,128)}, u32[]{:S(2)}) copy-start(f32[24,6,10,640]{3,0,2,1:T(8,128)} %fusion.19) | copy-start | bytes 11059204
  119.9 3.2 %copy-start.22 = (f32[640]{0:T(1024)S(1)}, f32[640]{0:T(1024)}, u32[]{:S(2)}) copy-start(f32[640]{0:T(1024)} %param.33) | copy-start | bytes 7684

commit v9 on v6

--- a/solution.py
+++ b/solution.py
@@ -23,28 +23,35 @@
     count = lax.axis_size("row")
     chips = count // 2
     mate_pairs = [(i, i ^ 1) for i in range(count)]
+    mates = lax.ppermute(jnp.stack(kernels), "row", mate_pairs)
     wholes = []
     previous = None
-    for shard, swap_axis in zip(kernels, swap_axes):
-        swap_pairs = [(i, i ^ 1) for i in range(lax.axis_size(swap_axis))]
-        parity = lax.axis_index(swap_axis) % 2
-        depth = shard.shape[2]
-        halves = shard.reshape(shard.shape[:2] + (2, depth // 2) + shard.shape[3:])
-        mine = lax.dynamic_index_in_dim(halves, parity, axis=2, keepdims=False)
-        held = [shard, lax.ppermute(shard, "row", mate_pairs)]
+    for index, (shard, swap_axis) in enumerate(zip(kernels, swap_axes)):
+        if swap_axis is None:
+            mine = shard
+        else:
+            depth = shard.shape[2]
+            halves = shard.reshape(shard.shape[:2] + (2, depth // 2) + shard.shape[3:])
+            parity = lax.axis_index(swap_axis) % 2
+            mine = lax.dynamic_index_in_dim(halves, parity, axis=2, keepdims=False)
+        held = [shard, mates[index]]
         for step in range(1, chips):
             if previous is not None:
                 mine, _ = lax.optimization_barrier((mine, previous))
             pairs = [(((i // 2 + step) % chips) * 2 + i % 2, i) for i in range(count)]
             fetched = lax.ppermute(mine, "row", pairs)
             previous = fetched
-            other = lax.ppermute(fetched, swap_axis, swap_pairs)
             relayed = lax.ppermute(fetched, "row", mate_pairs)
-            other_relayed = lax.ppermute(other, "row", mate_pairs)
-            held += [
-                jnp.concatenate([fetched, other], axis=2),
-                jnp.concatenate([relayed, other_relayed], axis=2),
-            ]
+            if swap_axis is None:
+                held += [fetched, relayed]
+            else:
+                swap_pairs = [(i, i ^ 1) for i in range(lax.axis_size(swap_axis))]
+                other = lax.ppermute(fetched, swap_axis, swap_pairs)
+                other_relayed = lax.ppermute(other, "row", mate_pairs)
+                held += [
+                    jnp.concatenate([fetched, other], axis=2),
+                    jnp.concatenate([relayed, other_relayed], axis=2),
+                ]
         wholes.append(jnp.concatenate(held, axis=2))
     return wholes
 
@@ -60,6 +67,8 @@
     block = position // depth
     within = position % depth
     source = 2 * ((chip + block // 2) % chips) + jnp.where(block % 2 == 0, core, 1 - core)
+    if swap_axis is None:
+        return source * depth + within
     half = depth // 2
     parity = lax.axis_index(swap_axis) % 2
     shuffled = (parity ^ (within // half)) * half + within % half
@@ -116,9 +125,9 @@
     groups_total = norm1_mean.shape[1]
     per_group = channels // groups_total
 
-    first_whole, second_whole = gather_weights([conv1_weight, conv2_weight], ("groups", "col"))
-    first_order = relative_order(channels, "groups")
-    order = relative_order(channels, "col")
+    first_whole, second_whole = gather_weights([conv1_weight, conv2_weight], (None, "groups"))
+    first_order = relative_order(channels, None)
+    order = relative_order(channels, "groups")
 
     def expand(values):
         return jnp.repeat(values, per_group, axis=1)[:, None, None, :]

time: 131 us -> 149 us (1.14)
  waiting for transfers between devices: 33.1 us -> 56 us
  local copies, waits for them, and re-layouts: 31.7 us -> 22.2 us
  other arithmetic: 8.49 us -> 12.9 us
    ppermute x2, waiting for transfers between devices: 12.3 us -> 31.1 us  [padded_2(): lax.ppermute(lax.slice_in_dim(block, block.shape[dim] - width, None, axis...]
    ppermute x2, waiting for transfers between devices: 0.01 us -> 11 us  [gather_weights(): fetched = lax.ppermute(mine, 'row', pairs)]
    unnamed x46 -> x47, local copies, waits for them, and re-layouts: 19.5 us -> 11.8 us
    ppermute x2 -> x1, waiting for transfers between devices: 17.6 us -> 10.8 us  [gather_weights(): other = lax.ppermute(fetched, swap_axis, swap_pairs)]
    another operation x0 -> x1, other arithmetic: none -> 4.4 us  [gather_weights(): mates = lax.ppermute(jnp.stack(kernels), 'row', mate_pairs)]
    squeeze x0 -> x1, local copies, waits for them, and re-layouts: none -> 2.89 us  [gather_weights(): held = [shard, mates[index]]]
    ppermute x2, starting transfers between devices: 3.77 us -> 6.4 us  [gather_weights(): relayed = lax.ppermute(fetched, 'row', mate_pairs)]
    squeeze x2 -> x1, local copies, waits for them, and re-layouts: 3.44 us -> 1.26 us  [gather_weights(): mine = lax.dynamic_index_in_dim(halves, parity, axis=2, keepdims=False)]
  transfers between devices with their start and end apart: 14 -> 11, of which waited for: 5 -> 5; matrix products, arithmetic and copies ran while one was open for 44% -> 35% of each run, Pallas kernels for 0% -> 0%
where the time goes in v9:
time: 149 us
  waiting for transfers between devices  56 us (38%)
  matrix products  33.3 us (22%)
  starting transfers between devices  24 us (16%)
  local copies, waits for them, and re-layouts  22.2 us (15%)
  other arithmetic  12.9 us (9%)
    ppermute x2, waiting for transfers between devices, padded_2(): lax.ppermute(lax.slice_in_dim(block, block.shape[dim] - width, None, axis...  31.1 us
    dot_general x3, matrix products, to_relative(): moved = jnp.dot(activation, chooser, preferred_element_type=jnp.float32)  20.8 us
    conv_general_dilated x3, matrix products, conv_valid(): lax.conv_general_dilated(activation, kernel, window_strides=(1, 1), paddi...  12.5 us
    unnamed x47, local copies, waits for them, and re-layouts  11.8 us
    ppermute x2, waiting for transfers between devices, gather_weights(): fetched = lax.ppermute(mine, 'row', pairs)  11 us
    ppermute x1, waiting for transfers between devices, gather_weights(): other = lax.ppermute(fetched, swap_axis, swap_pairs)  10.8 us
    ppermute x2, starting transfers between devices, gather_weights(): relayed = lax.ppermute(fetched, 'row', mate_pairs)  6.4 us
    ppermute x2, starting transfers between devices, padded_2(): lax.ppermute(lax.slice_in_dim(block, block.shape[dim] - width, None, axis...  6.11 us
  transfers between devices with their start and end apart: 11, of which 5 were waited for; matrix products, arithmetic and copies ran while one was open for 35% of the time, Pallas kernels for 0%

profile of v9, /device:TPU:1, one launch (start us, length us, event | category | flops | bytes accessed | tf_op | source)
XLA Modules:
  0.0 148.8 jit_solution(9112230535017749321)
XLA Ops:
  0.0 2.0 %collective-permute-start.5 = (bf16[3,3,160,640]{3,2,1,0:T(8,128)(2,1)}, bf16[3,3,160,640]{3,2,1,0:T(8,128)(2,1)}, u32[]{:S(2)}, u32[]{:S(2)}) collective-permute-start(bf16[3,3,160,640]{3,2,1,0:T(8,128)(2,1)} %param.25), channel_id=1, source_target_pairs={{8,0},{12,4},{0,8},{4,12},{9,1},{13,5},{1,9},{5,13},{10,2},{14,6},... | collective-permute-start | bytes 5529608 | tf_op jit(solution)/shard_map/ppermute | solution.py:42
  2.0 4.4 %pad_maximum_fusion.1 = bf16[2,3,3,160,640]{4,3,2,1,0:T(8,128)(2,1)} fusion(bf16[1,3,3,160,640]{4,3,2,1,0:T(8,128)(2,1)} %bitcast.52, bf16[1,3,3,160,640]{4,3,2,1,0:T(8,128)(2,1)} %bitcast.54), kind=kLoop, calls=%fused_computation.9 | loop fusion | flops 1843200 | bytes 7372800 | tf_op jit(solution)/shard_map/stack | solution.py:26
  6.4 1.0 collective-permute-start.4
  7.4 0.7 copy_bitcast_fusion
  8.1 0.9 pad_maximum_fusion.3
  9.0 1.9 %collective-permute-start = (bf16[2,24,1,8,640]{4,1,3,2,0:T(8,128)(2,1)}, bf16[2,24,1,8,640]{4,1,3,2,0:T(8,128)(2,1)S(1)}, u32[]{:S(2)}, u32[]{:S(2)}) collective-permute-start(bf16[2,24,1,8,640]{4,1,3,2,0:T(8,128)(2,1)} %get-tuple-element.9), channel_id=1, source_target_pairs={{0,4},{4,8},{8,12},{1,5},{5,9},{9,13},{2,6},{6,10},{10,14},{3,7},{... | collective-permute-start | bytes 1474568 | tf_op jit(solution)/shard_map/ppermute | solution.py:14
  10.9 2.4 %collective-permute-start.1 = (bf16[2,24,1,8,640]{4,1,3,2,0:T(8,128)(2,1)S(1)}, bf16[2,24,1,8,640]{4,1,3,2,0:T(8,128)(2,1)S(1)}, u32[]{:S(2)}, u32[]{:S(2)}) collective-permute-start(bf16[2,24,1,8,640]{4,1,3,2,0:T(8,128)(2,1)S(1)} %get-tuple-element.10), channel_id=1, source_target_pairs={{4,0},{8,4},{12,8},{5,1},{9,5},{13,9},{6,2},{10,6},{14,10},{7,3},{... | collective-permute-start | bytes 1474568 | tf_op jit(solution)/shard_map/ppermute | solution.py:17
  13.5 0.1 compare_reduce_fusion
  13.6 2.9 %constant_dynamic-update-slice_fusion.4 = bf16[3,3,640,640]{3,2,1,0:T(8,128)(2,1)} fusion(bf16[3,3,160,640]{3,2,1,0:T(8,128)(2,1)} %param.32), kind=kLoop, calls=%fused_computation.78 | loop fusion | bytes 3686400
  16.5 31.1 %collective-permute-done = bf16[2,24,1,8,640]{4,1,3,2,0:T(8,128)(2,1)S(1)} collective-permute-done((bf16[2,24,1,8,640]{4,1,3,2,0:T(8,128)(2,1)}, bf16[2,24,1,8,640]{4,1,3,2,0:T(8,128)(2,1)S(1)}, u32[]{:S(2)}, u32[]{:S(2)}) %collective-permute-start) | collective-permute-done | bytes 491552 | tf_op jit(solution)/shard_map/ppermute | solution.py:14
  47.6 0.3 collective-permute-done.1
  48.0 1.0 pad_maximum_fusion.7
  49.0 4.2 %collective-permute-start.2 = (bf16[2,24,6,1,640]{4,1,3,2,0:T(8,128)(2,1)}, bf16[2,24,6,1,640]{4,1,3,2,0:T(8,128)(2,1)}, u32[]{:S(2)}, u32[]{:S(2)}) collective-permute-start(bf16[2,24,6,1,640]{4,1,3,2,0:T(8,128)(2,1)} %get-tuple-element.7), channel_id=1, source_target_pairs={{0,1},{1,2},{2,3},{4,5},{5,6},{6,7},{8,9},{9,10},{10,11},{12,13},{... | collective-permute-start | bytes 1105928 | tf_op jit(solution)/shard_map/ppermute | solution.py:14
  53.2 1.3 collective-permute-start.3
  54.5 0.5 compare_and_fusion
  54.9 0.2 broadcast_in_dim.31
  55.1 0.2 mul.122
  55.3 0.2 broadcast_in_dim.30
  55.5 0.2 sub.71
  55.7 0.2 broadcast_in_dim.65
  55.9 0.2 mul.135
  56.1 0.2 broadcast_in_dim.64
  56.3 0.8 sub.81
  57.1 1.3 dynamic-slice_bitcast_fusion
  58.4 0.6 and_convert_fusion
  59.1 2.7 %collective-permute-done.3 = bf16[2,24,6,1,640]{4,1,3,2,0:T(8,128)(2,1)} collective-permute-done((bf16[2,24,6,1,640]{4,1,3,2,0:T(8,128)(2,1)}, bf16[2,24,6,1,640]{4,1,3,2,0:T(8,128)(2,1)}, u32[]{:S(2)}, u32[]{:S(2)}) %collective-permute-start.3) | collective-permute-done | bytes 368672 | tf_op jit(solution)/shard_map/ppermute | solution.py:17
  61.7 3.0 %pad_maximum_fusion = bf16[2,24,6,10,640]{4,1,3,2,0:T(8,128)(2,1)S(1)} fusion(bf16[2,24,6,1,640]{4,1,3,2,0:T(8,128)(2,1)} %collective-permute-done.3, bf16[2,24,1,8,640]{4,1,3,2,0:T(8,128)(2,1)S(1)} %collective-permute-done.1, bf16[1,24,4,8,640]{4,1,3,2,0:T(8,128)(2,1)S(1)} %get-tuple-element.15, bf16[1,24,4,8,640]{4,1,3,2,0:T(8,128)(2,1)S(1)} %get-tuple-element.16, ...), kind=kLoop, calls=%fused_computation.8 | loop fusion | flops 9216000 | bytes 7372800 | tf_op jit(solution)/shard_map/concatenate | solution.py:18
  64.8 3.6 %collective-permute-start.6 = (bf16[3,3,160,640]{3,2,1,0:T(8,128)(2,1)}, bf16[3,3,160,640]{3,2,1,0:T(8,128)(2,1)}, u32[]{:S(2)}, u32[]{:S(2)}) collective-permute-start(bf16[3,3,160,640]{3,2,1,0:T(8,128)(2,1)} %collective-permute-done.5), channel_id=1, source_target_pairs={{0,4},{4,0},{8,12},{12,8},{1,5},{5,1},{9,13},{13,9},{2,6},{6,2},{1... | collective-permute-start | bytes 5529608 | tf_op jit(solution)/shard_map/ppermute | solution.py:44
  68.4 3.3 %fusion.35 = bf16[24,6,10,640]{3,0,2,1:T(8,128)(2,1)S(1)} fusion(bf16[2,24,6,10,640]{4,1,3,2,0:T(8,128)(2,1)S(1)} %pad_maximum_fusion, f32[6,10]{1,0:T(8,128)S(1)} %and_convert_fusion, f32[640]{0:T(1024)S(1)} %copy-done.17, f32[640]{0:T(1024)S(1)} %copy-done.18, f32[24,640]{1,0:T(8,128)S(1)} %mul.122, f32[24,640]{1,0:T(8,128)S(1)} %sub.71, s32[640]{0:T(1024)S(1)} %fusion.85), kind=kOutput, calls=%fused_computation.44 | convolution fusion | flops 1191116800 | bytes 3825664 | tf_op jit(solution)/shard_map/dot_general | solution.py:81
  71.7 2.3 %fusion.26 = f32[24,6,10,640]{3,0,2,1:T(8,128)} fusion(bf16[2,24,6,10,640]{4,1,3,2,0:T(8,128)(2,1)S(1)} %pad_maximum_fusion), kind=kLoop, calls=%fused_computation.34 | loop fusion | flops 921600 | bytes 5529600 | tf_op jit(solution)/shard_map/convert_element_type | solution.py:137
  74.1 11.0 %collective-permute-done.7 = bf16[3,3,80,640]{3,2,1,0:T(8,128)(2,1)S(1)} collective-permute-done((bf16[3,3,80,640]{3,2,1,0:T(8,128)(2,1)S(1)}, bf16[3,3,80,640]{3,2,1,0:T(8,128)(2,1)S(1)}, u32[]{:S(2)}, u32[]{:S(2)}) %collective-permute-start.7) | collective-permute-done | bytes 921632 | tf_op jit(solution)/shard_map/ppermute | solution.py:42
  85.1 1.2 collective-permute-start.8
  86.5 4.6 %fusion.34 = bf16[24,6,10,640]{3,0,2,1:T(8,128)(2,1)} fusion(f32[640]{0:T(1024)S(1)} %copy-done.15, f32[640]{0:T(1024)S(1)} %copy-done.16, f32[24,640]{1,0:T(8,128)S(1)} %mul.135, f32[24,640]{1,0:T(8,128)S(1)} %copy-done.7, f32[6,10]{1,0:T(8,128)S(1)} %and_convert_fusion, s32[640]{0:T(1024)S(1)} %fusion.86, bf16[2,24,6,10,640]{4,1,3,2,0:T(8,128)(2,1)S(1)} %pad_maximum_fusion), kind=kOutput, calls=%fused_computation.43 | convolution fusion | flops 1190195200 | bytes 3825664 | tf_op jit(solution)/shard_map/dot_general | solution.py:81
  91.1 2.8 %collective-permute-start.9 = (bf16[3,3,80,640]{3,2,1,0:T(8,128)(2,1)S(1)}, bf16[3,3,80,640]{3,2,1,0:T(8,128)(2,1)}, u32[]{:S(2)}, u32[]{:S(2)}) collective-permute-start(bf16[3,3,80,640]{3,2,1,0:T(8,128)(2,1)S(1)} %collective-permute-done.7), channel_id=1, source_target_pairs={{0,4},{4,0},{8,12},{12,8},{1,5},{5,1},{9,13},{13,9},{2,6},{6,2},{1... | collective-permute-start | bytes 2764808 | tf_op jit(solution)/shard_map/ppermute | solution.py:44
  93.9 10.8 %collective-permute-done.8 = bf16[3,3,80,640]{3,2,1,0:T(8,128)(2,1)} collective-permute-done((bf16[3,3,80,640]{3,2,1,0:T(8,128)(2,1)S(1)}, bf16[3,3,80,640]{3,2,1,0:T(8,128)(2,1)}, u32[]{:S(2)}, u32[]{:S(2)}) %collective-permute-start.8) | collective-permute-done | bytes 921632 | tf_op jit(solution)/shard_map/ppermute | solution.py:49
  104.6 3.4 %collective-permute-start.10 = (bf16[3,3,80,640]{3,2,1,0:T(8,128)(2,1)}, bf16[3,3,80,640]{3,2,1,0:T(8,128)(2,1)}, u32[]{:S(2)}, u32[]{:S(2)}) collective-permute-start(bf16[3,3,80,640]{3,2,1,0:T(8,128)(2,1)} %collective-permute-done.8), channel_id=1, source_target_pairs={{0,4},{4,0},{8,12},{12,8},{1,5},{5,1},{9,13},{13,9},{2,6},{6,2},{1... | collective-permute-start | bytes 2764808 | tf_op jit(solution)/shard_map/ppermute | solution.py:50
  108.1 2.9 %slice_bitcast_fusion.1 = bf16[3,3,160,640]{3,2,1,0:T(8,128)(2,1)} fusion(bf16[2,3,3,160,640]{4,3,2,1,0:T(8,128)(2,1)} %collective-permute-done.4), kind=kLoop, calls=%fused_computation.32 | loop fusion | bytes 3686400 | tf_op jit(solution)/shard_map/squeeze | solution.py:37
  111.0 12.9 %fusion.47 = bf16[24,6,10,640]{3,0,2,1:T(8,128)(2,1)} fusion(bf16[24,6,10,640]{3,0,2,1:T(8,128)(2,1)} %copy-done.5, f32[640]{0:T(1024)S(1)} %copy-done.17, f32[640]{0:T(1024)S(1)} %copy-done.18, f32[24,640]{1,0:T(8,128)S(1)} %mul.122, f32[24,640]{1,0:T(8,128)S(1)} %sub.71, f32[24,640]{1,0:T(8,128)S(1)} %copy-done.14, f32[640]{0:T(1024)S(1)} %copy-done.19, ...), kind=kOutput, calls=%fused_computation.51 | convolution fusion | flops 6327255040 | bytes 10393600 | tf_op jit(solution)/shard_map/dot_general | solution.py:81
  123.9 2.9 %fusion.25 = bf16[3,3,640,640]{3,2,1,0:T(8,128)(2,1)} fusion(bf16[3,3,640,640]{3,2,1,0:T(8,128)(2,1)} %constant_dynamic-update-slice_fusion.4, bf16[2,3,3,160,640]{4,3,2,1,0:T(8,128)(2,1)} %collective-permute-done.4), kind=kLoop, calls=%fused_computation.31 | loop fusion | bytes 3686400
  126.8 1.1 constant_dynamic-update-slice_fusion.3
  127.9 2.2 %constant_dynamic-update-slice_fusion.2 = bf16[3,3,640,640]{3,2,1,0:T(8,128)(2,1)} fusion(bf16[3,3,640,640]{3,2,1,0:T(8,128)(2,1)} %constant_dynamic-update-slice_fusion.3, bf16[3,3,80,640]{3,2,1,0:T(8,128)(2,1)} %collective-permute-done.8), kind=kLoop, calls=%fused_computation.76 | loop fusion | bytes 1843200
  130.0 2.2 %constant_dynamic-update-slice_fusion.1 = bf16[3,3,640,640]{3,2,1,0:T(8,128)(2,1)} fusion(bf16[3,3,640,640]{3,2,1,0:T(8,128)(2,1)} %constant_dynamic-update-slice_fusion.2, bf16[3,3,80,640]{3,2,1,0:T(8,128)(2,1)} %collective-permute-done.9), kind=kLoop, calls=%fused_computation.75 | loop fusion | bytes 1843200
  132.3 2.3 %constant_dynamic-update-slice_fusion = bf16[3,3,640,640]{3,2,1,0:T(8,128)(2,1)} fusion(bf16[3,3,640,640]{3,2,1,0:T(8,128)(2,1)} %constant_dynamic-update-slice_fusion.1, bf16[3,3,80,640]{3,2,1,0:T(8,128)(2,1)} %collective-permute-done.10), kind=kLoop, calls=%fused_computation.74 | loop fusion | bytes 1843200 | tf_op jit(solution)/shard_map/concatenate | solution.py:55
  134.6 2.6 %fusion.20 = f32[48,4,1,640]{3,0,2,1:T(8,128)S(1)} fusion(bf16[3,3,640,640]{3,2,1,0:T(8,128)(2,1)} %constant_dynamic-update-slice_fusion, bf16[24,6,1,640]{3,0,2,1:T(8,128)(2,1)S(1)} %get-tuple-element.13, bf16[24,6,1,640]{3,0,2,1:T(8,128)(2,1)S(1)} %get-tuple-element.11), kind=kOutput, calls=%fused_computation.24 | convolution fusion | flops 472596480 | bytes 3317760 | tf_op jit(solution)/shard_map/conv_general_dilated | solution.py:90
  137.3 2.7 %fusion.18 = f32[48,4,1,640]{3,0,2,1:T(8,128)S(1)} fusion(bf16[3,3,640,640]{3,2,1,0:T(8,128)(2,1)} %constant_dynamic-update-slice_fusion, bf16[24,6,1,640]{3,0,2,1:T(8,128)(2,1)S(1)} %get-tuple-element.14, bf16[24,6,1,640]{3,0,2,1:T(8,128)(2,1)S(1)} %get-tuple-element.12), kind=kOutput, calls=%fused_computation.22 | convolution fusion | flops 472596480 | bytes 3317760 | tf_op jit(solution)/shard_map/conv_general_dilated | solution.py:90
  140.0 0.4 copy-done
  140.5 7.2 %fusion.50 = bf16[24,4,8,640]{3,0,2,1:T(8,128)(2,1)S(1)} fusion(f32[24,6,10,640]{3,0,2,1:T(8,128)S(1)} %copy-done, f32[24,4,1,640]{3,0,2,1:T(8,128)S(1)} %slice_subtract_fusion, f32[24,4,1,640]{3,0,2,1:T(8,128)S(1)} %slice_subtract_fusion.1, bf16[24,6,10,640]{3,0,2,1:T(8,128)(2,1)S(1)} %copy-done.6, bf16[3,3,640,640]{3,2,1,0:T(8,128)(2,1)S(1)} %copy-done.4, ...), kind=kOutput, calls=%fused_computation.52 | convolution fusion | flops 5665259520 | bytes 13642432 | tf_op jit(solution)/shard_map/conv_general_dilated | solution.py:90
  147.7 1.1 copy.40
  (57 shorter events, 0.4 us)
Async XLA Ops:
  0.0 64.7 %collective-permute-start.5 = (bf16[3,3,160,640]{3,2,1,0:T(8,128)(2,1)}, bf16[3,3,160,640]{3,2,1,0:T(8,128)(2,1)}, u32[]{:S(2)}, u32[]{:S(2)}) collective-permute-start(bf16[3,3,160,640]{3,2,1,0:T(8,128)(2,1)} %param.25), channel_id=1, source_target_pairs={{8,0},{12,4},{0,8},{4,12},{9,1},{13,5},{1,9},{5,13},{10,2},{14,6},... | collective-permute-start | bytes 5529608 | tf_op jit(solution)/shard_map/ppermute | solution.py:42
  2.0 5.4 %copy-start.2 = (bf16[24,4,8,640]{3,2,1,0:T(8,128)(2,1)S(1)}, bf16[24,4,8,640]{3,2,1,0:T(8,128)(2,1)}, u32[]{:S(2)}) copy-start(bf16[24,4,8,640]{3,2,1,0:T(8,128)(2,1)} %param.18) | copy-start | bytes 2949124
  2.0 5.4 %copy-start.3 = (bf16[24,4,8,640]{3,2,1,0:T(8,128)(2,1)S(1)}, bf16[24,4,8,640]{3,2,1,0:T(8,128)(2,1)}, u32[]{:S(2)}) copy-start(bf16[24,4,8,640]{3,2,1,0:T(8,128)(2,1)} %param.17) | copy-start | bytes 2949124
  6.4 7.0 %copy-start.12 = (s32[24,16]{0,1:T(8,128)S(1)}, s32[24,16]{0,1:T(8,128)}, u32[]{:S(2)}) copy-start(s32[24,16]{0,1:T(8,128)} %param.20) | copy-start | bytes 4612
  6.4 101.6 %collective-permute-start.4 = (bf16[2,3,3,160,640]{4,3,2,1,0:T(8,128)(2,1)}, bf16[2,3,3,160,640]{4,3,2,1,0:T(8,128)(2,1)}, u32[]{:S(2)}, u32[]{:S(2)}) collective-permute-start(bf16[2,3,3,160,640]{4,3,2,1,0:T(8,128)(2,1)} %pad_maximum_fusion.1), channel_id=1, source_target_pairs={{0,4},{4,0},{8,12},{12,8},{1,5},{5,1},{9,13},{13,9},{2,6},{6,2},{1... | collective-permute-start | bytes 11059208 | tf_op jit(solution)/shard_map/ppermute | solution.py:26
  9.0 38.7 %collective-permute-start = (bf16[2,24,1,8,640]{4,1,3,2,0:T(8,128)(2,1)}, bf16[2,24,1,8,640]{4,1,3,2,0:T(8,128)(2,1)S(1)}, u32[]{:S(2)}, u32[]{:S(2)}) collective-permute-start(bf16[2,24,1,8,640]{4,1,3,2,0:T(8,128)(2,1)} %get-tuple-element.9), channel_id=1, source_target_pairs={{0,4},{4,8},{8,12},{1,5},{5,9},{9,13},{2,6},{6,10},{10,14},{3,7},{... | collective-permute-start | bytes 1474568 | tf_op jit(solution)/shard_map/ppermute | solution.py:14
  10.9 37.1 %collective-permute-start.1 = (bf16[2,24,1,8,640]{4,1,3,2,0:T(8,128)(2,1)S(1)}, bf16[2,24,1,8,640]{4,1,3,2,0:T(8,128)(2,1)S(1)}, u32[]{:S(2)}, u32[]{:S(2)}) collective-permute-start(bf16[2,24,1,8,640]{4,1,3,2,0:T(8,128)(2,1)S(1)} %get-tuple-element.10), channel_id=1, source_target_pairs={{4,0},{8,4},{12,8},{5,1},{9,5},{13,9},{6,2},{10,6},{14,10},{7,3},{... | collective-permute-start | bytes 1474568 | tf_op jit(solution)/shard_map/ppermute | solution.py:17
  13.6 41.4 %copy-start.8 = (f32[24,32]{1,0:T(8,128)S(1)}, f32[24,32]{1,0:T(8,128)}, u32[]{:S(2)}) copy-start(f32[24,32]{1,0:T(8,128)} %param.29) | copy-start | bytes 9220
  13.6 41.8 %copy-start.9 = (f32[24,32]{1,0:T(8,128)S(1)}, f32[24,32]{1,0:T(8,128)}, u32[]{:S(2)}) copy-start(f32[24,32]{1,0:T(8,128)} %param.28) | copy-start | bytes 9220
  13.6 42.2 %copy-start.10 = (f32[24,32]{1,0:T(8,128)S(1)}, f32[24,32]{1,0:T(8,128)}, u32[]{:S(2)}) copy-start(f32[24,32]{1,0:T(8,128)} %param.22) | copy-start | bytes 9220
  16.5 39.6 %copy-start.11 = (f32[24,32]{1,0:T(8,128)S(1)}, f32[24,32]{1,0:T(8,128)}, u32[]{:S(2)}) copy-start(f32[24,32]{1,0:T(8,128)} %param.21) | copy-start | bytes 9220
  49.0 10.1 %collective-permute-start.2 = (bf16[2,24,6,1,640]{4,1,3,2,0:T(8,128)(2,1)}, bf16[2,24,6,1,640]{4,1,3,2,0:T(8,128)(2,1)}, u32[]{:S(2)}, u32[]{:S(2)}) collective-permute-start(bf16[2,24,6,1,640]{4,1,3,2,0:T(8,128)(2,1)} %get-tuple-element.7), channel_id=1, source_target_pairs={{0,1},{1,2},{2,3},{4,5},{5,6},{6,7},{8,9},{9,10},{10,11},{12,13},{... | collective-permute-start | bytes 1105928 | tf_op jit(solution)/shard_map/ppermute | solution.py:14
  53.2 8.6 %collective-permute-start.3 = (bf16[2,24,6,1,640]{4,1,3,2,0:T(8,128)(2,1)}, bf16[2,24,6,1,640]{4,1,3,2,0:T(8,128)(2,1)}, u32[]{:S(2)}, u32[]{:S(2)}) collective-permute-start(bf16[2,24,6,1,640]{4,1,3,2,0:T(8,128)(2,1)} %get-tuple-element.8), channel_id=1, source_target_pairs={{1,0},{2,1},{3,2},{5,4},{6,5},{7,6},{9,8},{10,9},{11,10},{13,12},{... | collective-permute-start | bytes 1105928 | tf_op jit(solution)/shard_map/ppermute | solution.py:17
  59.1 9.3 %copy-start.17 = (f32[640]{0:T(1024)S(1)}, f32[640]{0:T(1024)}, u32[]{:S(2)}) copy-start(f32[640]{0:T(1024)} %param.31) | copy-start | bytes 7684
  59.1 9.3 %copy-start.18 = (f32[640]{0:T(1024)S(1)}, f32[640]{0:T(1024)}, u32[]{:S(2)}) copy-start(f32[640]{0:T(1024)} %param.30) | copy-start | bytes 7684
  64.7 20.4 %collective-permute-start.7 = (bf16[3,3,80,640]{3,2,1,0:T(8,128)(2,1)S(1)}, bf16[3,3,80,640]{3,2,1,0:T(8,128)(2,1)S(1)}, u32[]{:S(2)}, u32[]{:S(2)}) collective-permute-start(bf16[3,3,80,640]{3,2,1,0:T(8,128)(2,1)S(1)} %dynamic-slice_bitcast_fusion), channel_id=1, source_target_pairs={{8,0},{12,4},{0,8},{4,12},{9,1},{13,5},{1,9},{5,13},{10,2},{14,6},... | collective-permute-start | bytes 2764808 | tf_op jit(solution)/shard_map/ppermute | solution.py:42
  64.8 46.2 %collective-permute-start.6 = (bf16[3,3,160,640]{3,2,1,0:T(8,128)(2,1)}, bf16[3,3,160,640]{3,2,1,0:T(8,128)(2,1)}, u32[]{:S(2)}, u32[]{:S(2)}) collective-permute-start(bf16[3,3,160,640]{3,2,1,0:T(8,128)(2,1)} %collective-permute-done.5), channel_id=1, source_target_pairs={{0,4},{4,0},{8,12},{12,8},{1,5},{5,1},{9,13},{13,9},{2,6},{6,2},{1... | collective-permute-start | bytes 5529608 | tf_op jit(solution)/shard_map/ppermute | solution.py:44
  71.7 14.7 %copy-start.5 = (bf16[24,6,10,640]{3,0,2,1:T(8,128)(2,1)}, bf16[24,6,10,640]{3,0,2,1:T(8,128)(2,1)S(1)}, u32[]{:S(2)}) copy-start(bf16[24,6,10,640]{3,0,2,1:T(8,128)(2,1)S(1)} %fusion.35) | copy-start | bytes 5529604
  71.7 14.7 %copy-start.7 = (f32[24,640]{1,0:T(8,128)S(1)}, f32[24,640]{1,0:T(8,128)}, u32[]{:S(2)}) copy-start(f32[24,640]{1,0:T(8,128)} %sub.81) | copy-start | bytes 184324
  71.7 14.7 %copy-start.15 = (f32[640]{0:T(1024)S(1)}, f32[640]{0:T(1024)}, u32[]{:S(2)}) copy-start(f32[640]{0:T(1024)} %param.24) | copy-start | bytes 7684
  71.7 14.7 %copy-start.16 = (f32[640]{0:T(1024)S(1)}, f32[640]{0:T(1024)}, u32[]{:S(2)}) copy-start(f32[640]{0:T(1024)} %param.23) | copy-start | bytes 7684
  85.1 19.5 %collective-permute-start.8 = (bf16[3,3,80,640]{3,2,1,0:T(8,128)(2,1)S(1)}, bf16[3,3,80,640]{3,2,1,0:T(8,128)(2,1)}, u32[]{:S(2)}, u32[]{:S(2)}) collective-permute-start(bf16[3,3,80,640]{3,2,1,0:T(8,128)(2,1)S(1)} %collective-permute-done.7), channel_id=1, source_target_pairs={{0,16},{16,0},{1,17},{17,1},{2,18},{18,2},{3,19},{19,3},{4,20},{20... | collective-permute-start | bytes 2764808 | tf_op jit(solution)/shard_map/ppermute | solution.py:49
  86.4 24.6 %copy-start.1 = (bf16[3,3,160,640]{3,2,1,0:T(8,128)(2,1)S(1)}, bf16[3,3,160,640]{3,2,1,0:T(8,128)(2,1)}, u32[]{:S(2)}) copy-start(bf16[3,3,160,640]{3,2,1,0:T(8,128)(2,1)} %param.25) | copy-start | bytes 5529604
  86.4 24.5 %copy-start.14 = (f32[24,640]{1,0:T(8,128)S(1)}, f32[24,640]{1,0:T(8,128)}, u32[]{:S(2)}) copy-start(f32[24,640]{1,0:T(8,128)} %param.27) | copy-start | bytes 184324
  86.4 24.5 %copy-start.19 = (f32[640]{0:T(1024)S(1)}, f32[640]{0:T(1024)}, u32[]{:S(2)}) copy-start(f32[640]{0:T(1024)} %param.26) | copy-start | bytes 7684
  91.1 39.0 %collective-permute-start.9 = (bf16[3,3,80,640]{3,2,1,0:T(8,128)(2,1)S(1)}, bf16[3,3,80,640]{3,2,1,0:T(8,128)(2,1)}, u32[]{:S(2)}, u32[]{:S(2)}) collective-permute-start(bf16[3,3,80,640]{3,2,1,0:T(8,128)(2,1)S(1)} %collective-permute-done.7), channel_id=1, source_target_pairs={{0,4},{4,0},{8,12},{12,8},{1,5},{5,1},{9,13},{13,9},{2,6},{6,2},{1... | collective-permute-start | bytes 2764808 | tf_op jit(solution)/shard_map/ppermute | solution.py:44
  104.6 27.7 %collective-permute-start.10 = (bf16[3,3,80,640]{3,2,1,0:T(8,128)(2,1)}, bf16[3,3,80,640]{3,2,1,0:T(8,128)(2,1)}, u32[]{:S(2)}, u32[]{:S(2)}) collective-permute-start(bf16[3,3,80,640]{3,2,1,0:T(8,128)(2,1)} %collective-permute-done.8), channel_id=1, source_target_pairs={{0,4},{4,0},{8,12},{12,8},{1,5},{5,1},{9,13},{13,9},{2,6},{6,2},{1... | collective-permute-start | bytes 2764808 | tf_op jit(solution)/shard_map/ppermute | solution.py:50
  126.8 5.5 %copy-start.6 = (bf16[24,6,10,640]{3,0,2,1:T(8,128)(2,1)S(1)}, bf16[24,6,10,640]{3,0,2,1:T(8,128)(2,1)}, u32[]{:S(2)}) copy-start(bf16[24,6,10,640]{3,0,2,1:T(8,128)(2,1)} %fusion.47) | copy-start | bytes 5529604
  132.3 7.7 %copy-start.13 = (bf16[24,4,8,640]{3,2,1,0:T(8,128)(2,1)S(1)}, bf16[24,4,8,640]{3,2,1,0:T(8,128)(2,1)}, u32[]{:S(2)}) copy-start(bf16[24,4,8,640]{3,2,1,0:T(8,128)(2,1)} %param.19) | copy-start | bytes 2949124
  134.6 5.4 %copy-start.4 = (bf16[3,3,640,640]{3,2,1,0:T(8,128)(2,1)S(1)}, bf16[3,3,640,640]{3,2,1,0:T(8,128)(2,1)}, u32[]{:S(2)}) copy-start(bf16[3,3,640,640]{3,2,1,0:T(8,128)(2,1)} %constant_dynamic-update-slice_fusion) | copy-start | bytes 22118404
  137.2 3.3 %copy-start = (f32[24,6,10,640]{3,0,2,1:T(8,128)S(1)}, f32[24,6,10,640]{3,0,2,1:T(8,128)}, u32[]{:S(2)}) copy-start(f32[24,6,10,640]{3,0,2,1:T(8,128)} %fusion.26) | copy-start | bytes 11059204
  137.2 3.3 %copy-start.20 = (f32[640]{0:T(1024)S(1)}, f32[640]{0:T(1024)}, u32[]{:S(2)}) copy-start(f32[640]{0:T(1024)} %param.33) | copy-start | bytes 7684

commit v10 on v6

--- a/solution.py
+++ b/solution.py
@@ -37,8 +37,8 @@
                 mine, _ = lax.optimization_barrier((mine, previous))
             pairs = [(((i // 2 + step) % chips) * 2 + i % 2, i) for i in range(count)]
             fetched = lax.ppermute(mine, "row", pairs)
-            previous = fetched
             other = lax.ppermute(fetched, swap_axis, swap_pairs)
+            previous = other
             relayed = lax.ppermute(fetched, "row", mate_pairs)
             other_relayed = lax.ppermute(other, "row", mate_pairs)
             held += [

time: 131 us -> 134 us (1.023)
  starting transfers between devices: 23.2 us -> 24.7 us
    ppermute x2, waiting for transfers between devices: 0.01 us -> 10.8 us  [gather_weights(): fetched = lax.ppermute(mine, 'row', pairs)]
    ppermute x2, waiting for transfers between devices: 17.6 us -> 8.21 us  [gather_weights(): other = lax.ppermute(fetched, swap_axis, swap_pairs)]
    ppermute x2, starting transfers between devices: 3.77 us -> 5.88 us  [gather_weights(): relayed = lax.ppermute(fetched, 'row', mate_pairs)]
    ppermute x2, starting transfers between devices: 4.84 us -> 3.04 us  [gather_weights(): other_relayed = lax.ppermute(other, 'row', mate_pairs)]
  transfers between devices with their start and end apart: 14 -> 14, of which waited for: 5 -> 6; matrix products, arithmetic and copies ran while one was open for 44% -> 44% of each run, Pallas kernels for 0% -> 0%
where the time goes in v10:
time: 134 us; the launch traced here: 133 us
  matrix products  33.8 us (25%)
  waiting for transfers between devices  33.3 us (25%)
  local copies, waits for them, and re-layouts  32.7 us (24%)
  starting transfers between devices  24.7 us (18%)
  other arithmetic  8.41 us (6%)
    dot_general x3, matrix products, to_relative(): moved = jnp.dot(activation, chooser, preferred_element_type=jnp.float32)  21.2 us
    unnamed x46, local copies, waits for them, and re-layouts  19.5 us
    conv_general_dilated x3, matrix products, conv_valid(): lax.conv_general_dilated(activation, kernel, window_strides=(1, 1), paddi...  12.6 us
    ppermute x2, waiting for transfers between devices, padded_2(): lax.ppermute(lax.slice_in_dim(block, block.shape[dim] - width, None, axis...  12.3 us
    ppermute x2, waiting for transfers between devices, gather_weights(): fetched = lax.ppermute(mine, 'row', pairs)  10.8 us
    ppermute x2, waiting for transfers between devices, gather_weights(): other = lax.ppermute(fetched, swap_axis, swap_pairs)  8.21 us
    ppermute x2, starting transfers between devices, padded_2(): lax.ppermute(lax.slice_in_dim(block, block.shape[dim] - width, None, axis...  6.13 us
    ppermute x2, starting transfers between devices, gather_weights(): relayed = lax.ppermute(fetched, 'row', mate_pairs)  5.88 us
  transfers between devices with their start and end apart: 14, of which 6 were waited for; matrix products, arithmetic and copies ran while one was open for 44% of the time, Pallas kernels for 0%

profile of v10, /device:TPU:1, one launch (start us, length us, event | category | flops | bytes accessed | tf_op | source)
XLA Modules:
  0.0 133.3 jit_solution(10594603143487007446)
XLA Ops:
  0.1 2.2 %dynamic-slice_bitcast_fusion.1 = bf16[3,3,80,640]{3,2,1,0:T(8,128)(2,1)} fusion(bf16[3,3,2,80,640]{4,3,2,1,0:T(8,128)(2,1)} %bitcast.50, s32[]{:T(128)S(6)} %select_n.186), kind=kLoop, calls=%fused_computation.51 | loop fusion | bytes 1843204 | tf_op jit(solution)/shard_map/jit(dynamic_index_in_dim)/squeeze | solution.py:33
  2.2 2.7 %collective-permute-start.5 = (bf16[3,3,80,640]{3,2,1,0:T(8,128)(2,1)}, bf16[3,3,80,640]{3,2,1,0:T(8,128)(2,1)}, u32[]{:S(2)}, u32[]{:S(2)}) collective-permute-start(bf16[3,3,80,640]{3,2,1,0:T(8,128)(2,1)} %dynamic-slice_bitcast_fusion.1), channel_id=1, source_target_pairs={{8,0},{12,4},{0,8},{4,12},{9,1},{13,5},{1,9},{5,13},{10,2},{14,6},... | collective-permute-start | bytes 2764808 | tf_op jit(solution)/shard_map/ppermute | solution.py:39
  4.9 2.1 %copy_bitcast_fusion = (bf16[1,24,4,8,640]{4,1,3,2,0:T(8,128)(2,1)S(1)}, bf16[1,24,4,8,640]{4,1,3,2,0:T(8,128)(2,1)S(1)}) fusion(bf16[24,4,8,640]{3,2,1,0:T(8,128)(2,1)} %param.18, bf16[24,4,8,640]{3,2,1,0:T(8,128)(2,1)} %param.17), kind=kLoop, calls=%fused_computation.42 | loop fusion | bytes 3932160 | tf_op jit(solution)/shard_map/stack | solution.py:126
  7.1 0.9 pad_maximum_fusion.2
  8.0 1.9 %collective-permute-start = (bf16[2,24,1,8,640]{4,1,3,2,0:T(8,128)(2,1)}, bf16[2,24,1,8,640]{4,1,3,2,0:T(8,128)(2,1)S(1)}, u32[]{:S(2)}, u32[]{:S(2)}) collective-permute-start(bf16[2,24,1,8,640]{4,1,3,2,0:T(8,128)(2,1)} %get-tuple-element.9), channel_id=1, source_target_pairs={{0,4},{4,8},{8,12},{1,5},{5,9},{9,13},{2,6},{6,10},{10,14},{3,7},{... | collective-permute-start | bytes 1474568 | tf_op jit(solution)/shard_map/ppermute | solution.py:14
  9.9 2.4 %collective-permute-start.1 = (bf16[2,24,1,8,640]{4,1,3,2,0:T(8,128)(2,1)S(1)}, bf16[2,24,1,8,640]{4,1,3,2,0:T(8,128)(2,1)S(1)}, u32[]{:S(2)}, u32[]{:S(2)}) collective-permute-start(bf16[2,24,1,8,640]{4,1,3,2,0:T(8,128)(2,1)S(1)} %get-tuple-element.10), channel_id=1, source_target_pairs={{4,0},{8,4},{12,8},{5,1},{9,5},{13,9},{6,2},{10,6},{14,10},{7,3},{... | collective-permute-start | bytes 1474568 | tf_op jit(solution)/shard_map/ppermute | solution.py:17
  12.6 2.9 %constant_dynamic-update-slice_fusion.5 = bf16[3,3,640,640]{3,2,1,0:T(8,128)(2,1)} fusion(bf16[3,3,160,640]{3,2,1,0:T(8,128)(2,1)} %param.25), kind=kLoop, calls=%fused_computation.74 | loop fusion | bytes 3686400
  15.5 2.9 %constant_dynamic-update-slice_fusion.11 = bf16[3,3,640,640]{3,2,1,0:T(8,128)(2,1)} fusion(bf16[3,3,160,640]{3,2,1,0:T(8,128)(2,1)} %param.32), kind=kLoop, calls=%fused_computation.80 | loop fusion | bytes 3686400
  18.5 12.3 %collective-permute-done = bf16[2,24,1,8,640]{4,1,3,2,0:T(8,128)(2,1)S(1)} collective-permute-done((bf16[2,24,1,8,640]{4,1,3,2,0:T(8,128)(2,1)}, bf16[2,24,1,8,640]{4,1,3,2,0:T(8,128)(2,1)S(1)}, u32[]{:S(2)}, u32[]{:S(2)}) %collective-permute-start) | collective-permute-done | bytes 491552 | tf_op jit(solution)/shard_map/ppermute | solution.py:14
  30.7 0.7 collective-permute-done.1
  31.5 1.0 pad_maximum_fusion.6
  32.5 4.2 %collective-permute-start.2 = (bf16[2,24,6,1,640]{4,1,3,2,0:T(8,128)(2,1)}, bf16[2,24,6,1,640]{4,1,3,2,0:T(8,128)(2,1)}, u32[]{:S(2)}, u32[]{:S(2)}) collective-permute-start(bf16[2,24,6,1,640]{4,1,3,2,0:T(8,128)(2,1)} %get-tuple-element.7), channel_id=1, source_target_pairs={{0,1},{1,2},{2,3},{4,5},{5,6},{6,7},{8,9},{9,10},{10,11},{12,13},{... | collective-permute-start | bytes 1105928 | tf_op jit(solution)/shard_map/ppermute | solution.py:14
  36.7 1.3 collective-permute-start.3
  38.0 0.5 compare_and_fusion
  38.7 0.2 mul.128
  39.9 0.8 sub.87
  40.8 1.3 dynamic-slice_bitcast_fusion
  42.0 0.7 and_convert_fusion
  42.7 1.3 collective-permute-start.6
  44.0 1.2 collective-permute-done.3
  45.3 3.0 %pad_maximum_fusion = bf16[2,24,6,10,640]{4,1,3,2,0:T(8,128)(2,1)S(1)} fusion(bf16[2,24,6,1,640]{4,1,3,2,0:T(8,128)(2,1)} %collective-permute-done.3, bf16[2,24,1,8,640]{4,1,3,2,0:T(8,128)(2,1)S(1)} %collective-permute-done.1, bf16[1,24,4,8,640]{4,1,3,2,0:T(8,128)(2,1)S(1)} %get-tuple-element.15, bf16[1,24,4,8,640]{4,1,3,2,0:T(8,128)(2,1)S(1)} %get-tuple-element.16, ...), kind=kLoop, calls=%fused_computation | loop fusion | flops 9216000 | bytes 7372800 | tf_op jit(solution)/shard_map/concatenate | solution.py:18
  48.3 3.3 %fusion.27 = bf16[24,6,10,640]{3,0,2,1:T(8,128)(2,1)S(1)} fusion(bf16[2,24,6,10,640]{4,1,3,2,0:T(8,128)(2,1)S(1)} %pad_maximum_fusion, f32[6,10]{1,0:T(8,128)S(1)} %and_convert_fusion, f32[640]{0:T(1024)S(1)} %copy-done.14, f32[640]{0:T(1024)S(1)} %copy-done.15, f32[24,640]{1,0:T(8,128)S(1)} %mul.128, f32[24,640]{1,0:T(8,128)S(1)} %sub.77, s32[640]{0:T(1024)S(1)} %fusion.83), kind=kOutput, calls=%fused_computation.33 | convolution fusion | flops 1191116800 | bytes 3825664 | tf_op jit(solution)/shard_map/dot_general | solution.py:72
  51.6 3.7 %collective-permute-done.6 = bf16[3,3,80,640]{3,2,1,0:T(8,128)(2,1)S(1)} collective-permute-done((bf16[3,3,80,640]{3,2,1,0:T(8,128)(2,1)}, bf16[3,3,80,640]{3,2,1,0:T(8,128)(2,1)S(1)}, u32[]{:S(2)}, u32[]{:S(2)}) %collective-permute-start.6) | collective-permute-done | bytes 921632 | tf_op jit(solution)/shard_map/ppermute | solution.py:40
  55.3 4.6 %fusion.26 = bf16[24,6,10,640]{3,0,2,1:T(8,128)(2,1)} fusion(f32[640]{0:T(1024)S(1)} %copy-done.12, f32[640]{0:T(1024)S(1)} %copy-done.13, f32[24,640]{1,0:T(8,128)S(1)} %mul.141, f32[24,640]{1,0:T(8,128)S(1)} %copy-done.4, f32[6,10]{1,0:T(8,128)S(1)} %and_convert_fusion, s32[640]{0:T(1024)S(1)} %fusion.84, bf16[2,24,6,10,640]{4,1,3,2,0:T(8,128)(2,1)S(1)} %pad_maximum_fusion), kind=kOutput, calls=%fused_computation.32 | convolution fusion | flops 1190195200 | bytes 3825664 | tf_op jit(solution)/shard_map/dot_general | solution.py:72
  59.9 3.2 %collective-permute-start.7 = (bf16[3,3,80,640]{3,2,1,0:T(8,128)(2,1)}, bf16[3,3,80,640]{3,2,1,0:T(8,128)(2,1)S(1)}, u32[]{:S(2)}, u32[]{:S(2)}) collective-permute-start(bf16[3,3,80,640]{3,2,1,0:T(8,128)(2,1)} %collective-permute-done.5), channel_id=1, source_target_pairs={{0,4},{4,0},{8,12},{12,8},{1,5},{5,1},{9,13},{13,9},{2,6},{6,2},{1... | collective-permute-start | bytes 2764808 | tf_op jit(solution)/shard_map/ppermute | solution.py:42
  63.1 2.1 %fusion.17 = f32[24,6,10,640]{3,0,2,1:T(8,128)} fusion(bf16[2,24,6,10,640]{4,1,3,2,0:T(8,128)(2,1)S(1)} %pad_maximum_fusion), kind=kLoop, calls=%fused_computation.22 | loop fusion | flops 921600 | bytes 5529600 | tf_op jit(solution)/shard_map/convert_element_type | solution.py:128
  65.2 10.8 %collective-permute-done.10 = bf16[3,3,80,640]{3,2,1,0:T(8,128)(2,1)S(1)} collective-permute-done((bf16[3,3,80,640]{3,2,1,0:T(8,128)(2,1)S(1)}, bf16[3,3,80,640]{3,2,1,0:T(8,128)(2,1)S(1)}, u32[]{:S(2)}, u32[]{:S(2)}) %collective-permute-start.10) | collective-permute-done | bytes 921632 | tf_op jit(solution)/shard_map/ppermute | solution.py:39
  76.0 1.8 %collective-permute-start.11 = (bf16[3,3,80,640]{3,2,1,0:T(8,128)(2,1)S(1)}, bf16[3,3,80,640]{3,2,1,0:T(8,128)(2,1)S(1)}, u32[]{:S(2)}, u32[]{:S(2)}) collective-permute-start(bf16[3,3,80,640]{3,2,1,0:T(8,128)(2,1)S(1)} %collective-permute-done.10), channel_id=1, source_target_pairs={{0,1},{1,0},{2,3},{3,2},{4,5},{5,4},{6,7},{7,6},{8,9},{9,8},{10,11... | collective-permute-start | bytes 2764808 | tf_op jit(solution)/shard_map/ppermute | solution.py:40
  77.9 2.9 %constant_dynamic-update-slice_fusion.4 = bf16[3,3,640,640]{3,2,1,0:T(8,128)(2,1)} fusion(bf16[3,3,640,640]{3,2,1,0:T(8,128)(2,1)} %constant_dynamic-update-slice_fusion.5, bf16[3,3,160,640]{3,2,1,0:T(8,128)(2,1)} %collective-permute-done.4), kind=kLoop, calls=%fused_computation.73 | loop fusion | bytes 3686400
  80.8 2.2 %constant_dynamic-update-slice_fusion.3 = bf16[3,3,640,640]{3,2,1,0:T(8,128)(2,1)} fusion(bf16[3,3,640,640]{3,2,1,0:T(8,128)(2,1)} %constant_dynamic-update-slice_fusion.4, bf16[3,3,80,640]{3,2,1,0:T(8,128)(2,1)} %collective-permute-done.5), kind=kLoop, calls=%fused_computation.72 | loop fusion | bytes 1843200
  83.0 1.0 constant_dynamic-update-slice_fusion.2
  84.0 1.0 constant_dynamic-update-slice_fusion.1
  85.1 2.9 %constant_dynamic-update-slice_fusion.10 = bf16[3,3,640,640]{3,2,1,0:T(8,128)(2,1)} fusion(bf16[3,3,640,640]{3,2,1,0:T(8,128)(2,1)} %constant_dynamic-update-slice_fusion.11, bf16[3,3,160,640]{3,2,1,0:T(8,128)(2,1)} %collective-permute-done.9), kind=kLoop, calls=%fused_computation.79 | loop fusion | bytes 3686400
  88.0 2.7 %collective-permute-start.12 = (bf16[3,3,80,640]{3,2,1,0:T(8,128)(2,1)S(1)}, bf16[3,3,80,640]{3,2,1,0:T(8,128)(2,1)S(1)}, u32[]{:S(2)}, u32[]{:S(2)}) collective-permute-start(bf16[3,3,80,640]{3,2,1,0:T(8,128)(2,1)S(1)} %collective-permute-done.10), channel_id=1, source_target_pairs={{0,4},{4,0},{8,12},{12,8},{1,5},{5,1},{9,13},{13,9},{2,6},{6,2},{1... | collective-permute-start | bytes 2764808 | tf_op jit(solution)/shard_map/ppermute | solution.py:42
  90.6 1.0 constant_dynamic-update-slice_fusion
  91.7 4.5 %collective-permute-done.11 = bf16[3,3,80,640]{3,2,1,0:T(8,128)(2,1)S(1)} collective-permute-done((bf16[3,3,80,640]{3,2,1,0:T(8,128)(2,1)S(1)}, bf16[3,3,80,640]{3,2,1,0:T(8,128)(2,1)S(1)}, u32[]{:S(2)}, u32[]{:S(2)}) %collective-permute-start.11) | collective-permute-done | bytes 921632 | tf_op jit(solution)/shard_map/ppermute | solution.py:40
  96.2 3.0 %collective-permute-start.13 = (bf16[3,3,80,640]{3,2,1,0:T(8,128)(2,1)S(1)}, bf16[3,3,80,640]{3,2,1,0:T(8,128)(2,1)}, u32[]{:S(2)}, u32[]{:S(2)}) collective-permute-start(bf16[3,3,80,640]{3,2,1,0:T(8,128)(2,1)S(1)} %collective-permute-done.11), channel_id=1, source_target_pairs={{0,4},{4,0},{8,12},{12,8},{1,5},{5,1},{9,13},{13,9},{2,6},{6,2},{1... | collective-permute-start | bytes 2764808 | tf_op jit(solution)/shard_map/ppermute | solution.py:43
  99.2 13.4 %fusion.39 = bf16[24,6,10,640]{3,0,2,1:T(8,128)(2,1)} fusion(bf16[24,6,10,640]{3,0,2,1:T(8,128)(2,1)} %copy-done.2, bf16[3,3,640,640]{3,2,1,0:T(8,128)(2,1)} %constant_dynamic-update-slice_fusion, bf16[24,6,10,640]{3,0,2,1:T(8,128)(2,1)} %fusion.26, f32[640]{0:T(1024)S(1)} %copy-done.14, f32[640]{0:T(1024)S(1)} %copy-done.15, f32[24,640]{1,0:T(8,128)S(1)} %mul.128, ...), kind=kOutput, calls=%fused_computation.40 | convolution fusion | flops 6297763840 | bytes 10393600 | tf_op jit(solution)/shard_map/dot_general | solution.py:72
  112.6 1.1 constant_dynamic-update-slice_fusion.9
  113.7 1.0 fusion.95
  114.7 1.0 constant_dynamic-update-slice_fusion.8
  115.7 1.0 constant_dynamic-update-slice_fusion.7
  116.7 2.3 %constant_dynamic-update-slice_fusion.6 = bf16[3,3,640,640]{3,2,1,0:T(8,128)(2,1)} fusion(bf16[3,3,640,640]{3,2,1,0:T(8,128)(2,1)} %constant_dynamic-update-slice_fusion.7, bf16[3,3,80,640]{3,2,1,0:T(8,128)(2,1)} %collective-permute-done.13), kind=kLoop, calls=%fused_computation.75 | loop fusion | bytes 1843200 | tf_op jit(solution)/shard_map/concatenate | solution.py:48
  119.1 2.6 %fusion.12 = f32[48,4,1,640]{3,0,2,1:T(8,128)S(1)} fusion(bf16[3,3,640,640]{3,2,1,0:T(8,128)(2,1)} %constant_dynamic-update-slice_fusion.6, bf16[24,6,1,640]{3,0,2,1:T(8,128)(2,1)S(1)} %get-tuple-element.13, bf16[24,6,1,640]{3,0,2,1:T(8,128)(2,1)S(1)} %get-tuple-element.11), kind=kOutput, calls=%fused_computation.15 | convolution fusion | flops 472596480 | bytes 3317760 | tf_op jit(solution)/shard_map/conv_general_dilated | solution.py:81
  121.8 2.7 %fusion.10 = f32[48,4,1,640]{3,0,2,1:T(8,128)S(1)} fusion(bf16[3,3,640,640]{3,2,1,0:T(8,128)(2,1)} %constant_dynamic-update-slice_fusion.6, bf16[24,6,1,640]{3,0,2,1:T(8,128)(2,1)S(1)} %get-tuple-element.14, bf16[24,6,1,640]{3,0,2,1:T(8,128)(2,1)S(1)} %get-tuple-element.12), kind=kOutput, calls=%fused_computation.13 | convolution fusion | flops 472596480 | bytes 3317760 | tf_op jit(solution)/shard_map/conv_general_dilated | solution.py:81
  124.5 0.4 copy-done
  125.0 7.2 %fusion.44 = bf16[24,4,8,640]{3,0,2,1:T(8,128)(2,1)S(1)} fusion(f32[24,6,10,640]{3,0,2,1:T(8,128)S(1)} %copy-done, f32[24,4,1,640]{3,0,2,1:T(8,128)S(1)} %slice_subtract_fusion, f32[24,4,1,640]{3,0,2,1:T(8,128)S(1)} %slice_subtract_fusion.1, bf16[24,6,10,640]{3,0,2,1:T(8,128)(2,1)S(1)} %copy-done.3, bf16[3,3,640,640]{3,2,1,0:T(8,128)(2,1)S(1)} %copy-done.1, ...), kind=kOutput, calls=%fused_computation.41 | convolution fusion | flops 5665259520 | bytes 13642432 | tf_op jit(solution)/shard_map/conv_general_dilated | solution.py:81
  132.2 1.1 copy.43
  (62 shorter events, 1.6 us)
Async XLA Ops:
  0.0 77.9 %collective-permute-start.4 = (bf16[3,3,160,640]{3,2,1,0:T(8,128)(2,1)}, bf16[3,3,160,640]{3,2,1,0:T(8,128)(2,1)}, u32[]{:S(2)}, u32[]{:S(2)}) collective-permute-start(bf16[3,3,160,640]{3,2,1,0:T(8,128)(2,1)} %param.25), channel_id=1, source_target_pairs={{0,4},{4,0},{8,12},{12,8},{1,5},{5,1},{9,13},{13,9},{2,6},{6,2},{1... | collective-permute-start | bytes 5529608 | tf_op jit(solution)/shard_map/ppermute | solution.py:34
  2.2 10.2 %copy-start.9 = (s32[24,16]{0,1:T(8,128)S(1)}, s32[24,16]{0,1:T(8,128)}, u32[]{:S(2)}) copy-start(s32[24,16]{0,1:T(8,128)} %param.20) | copy-start | bytes 4612
  2.2 40.5 %collective-permute-start.5 = (bf16[3,3,80,640]{3,2,1,0:T(8,128)(2,1)}, bf16[3,3,80,640]{3,2,1,0:T(8,128)(2,1)}, u32[]{:S(2)}, u32[]{:S(2)}) collective-permute-start(bf16[3,3,80,640]{3,2,1,0:T(8,128)(2,1)} %dynamic-slice_bitcast_fusion.1), channel_id=1, source_target_pairs={{8,0},{12,4},{0,8},{4,12},{9,1},{13,5},{1,9},{5,13},{10,2},{14,6},... | collective-permute-start | bytes 2764808 | tf_op jit(solution)/shard_map/ppermute | solution.py:39
  8.0 22.8 %collective-permute-start = (bf16[2,24,1,8,640]{4,1,3,2,0:T(8,128)(2,1)}, bf16[2,24,1,8,640]{4,1,3,2,0:T(8,128)(2,1)S(1)}, u32[]{:S(2)}, u32[]{:S(2)}) collective-permute-start(bf16[2,24,1,8,640]{4,1,3,2,0:T(8,128)(2,1)} %get-tuple-element.9), channel_id=1, source_target_pairs={{0,4},{4,8},{8,12},{1,5},{5,9},{9,13},{2,6},{6,10},{10,14},{3,7},{... | collective-permute-start | bytes 1474568 | tf_op jit(solution)/shard_map/ppermute | solution.py:14
  9.9 21.6 %collective-permute-start.1 = (bf16[2,24,1,8,640]{4,1,3,2,0:T(8,128)(2,1)S(1)}, bf16[2,24,1,8,640]{4,1,3,2,0:T(8,128)(2,1)S(1)}, u32[]{:S(2)}, u32[]{:S(2)}) collective-permute-start(bf16[2,24,1,8,640]{4,1,3,2,0:T(8,128)(2,1)S(1)} %get-tuple-element.10), channel_id=1, source_target_pairs={{4,0},{8,4},{12,8},{5,1},{9,5},{13,9},{6,2},{10,6},{14,10},{7,3},{... | collective-permute-start | bytes 1474568 | tf_op jit(solution)/shard_map/ppermute | solution.py:17
  12.3 72.7 %collective-permute-start.9 = (bf16[3,3,160,640]{3,2,1,0:T(8,128)(2,1)}, bf16[3,3,160,640]{3,2,1,0:T(8,128)(2,1)}, u32[]{:S(2)}, u32[]{:S(2)}) collective-permute-start(bf16[3,3,160,640]{3,2,1,0:T(8,128)(2,1)} %param.32), channel_id=1, source_target_pairs={{0,4},{4,0},{8,12},{12,8},{1,5},{5,1},{9,13},{13,9},{2,6},{6,2},{1... | collective-permute-start | bytes 5529608 | tf_op jit(solution)/shard_map/ppermute | solution.py:34
  15.5 23.0 %copy-start.5 = (f32[24,32]{1,0:T(8,128)S(1)}, f32[24,32]{1,0:T(8,128)}, u32[]{:S(2)}) copy-start(f32[24,32]{1,0:T(8,128)} %param.29) | copy-start | bytes 9220
  15.5 23.4 %copy-start.6 = (f32[24,32]{1,0:T(8,128)S(1)}, f32[24,32]{1,0:T(8,128)}, u32[]{:S(2)}) copy-start(f32[24,32]{1,0:T(8,128)} %param.28) | copy-start | bytes 9220
  15.5 23.8 %copy-start.7 = (f32[24,32]{1,0:T(8,128)S(1)}, f32[24,32]{1,0:T(8,128)}, u32[]{:S(2)}) copy-start(f32[24,32]{1,0:T(8,128)} %param.22) | copy-start | bytes 9220
  18.5 21.3 %copy-start.8 = (f32[24,32]{1,0:T(8,128)S(1)}, f32[24,32]{1,0:T(8,128)}, u32[]{:S(2)}) copy-start(f32[24,32]{1,0:T(8,128)} %param.21) | copy-start | bytes 9220
  32.5 11.5 %collective-permute-start.2 = (bf16[2,24,6,1,640]{4,1,3,2,0:T(8,128)(2,1)}, bf16[2,24,6,1,640]{4,1,3,2,0:T(8,128)(2,1)}, u32[]{:S(2)}, u32[]{:S(2)}) collective-permute-start(bf16[2,24,6,1,640]{4,1,3,2,0:T(8,128)(2,1)} %get-tuple-element.7), channel_id=1, source_target_pairs={{0,1},{1,2},{2,3},{4,5},{5,6},{6,7},{8,9},{9,10},{10,11},{12,13},{... | collective-permute-start | bytes 1105928 | tf_op jit(solution)/shard_map/ppermute | solution.py:14
  36.7 8.6 %collective-permute-start.3 = (bf16[2,24,6,1,640]{4,1,3,2,0:T(8,128)(2,1)}, bf16[2,24,6,1,640]{4,1,3,2,0:T(8,128)(2,1)}, u32[]{:S(2)}, u32[]{:S(2)}) collective-permute-start(bf16[2,24,6,1,640]{4,1,3,2,0:T(8,128)(2,1)} %get-tuple-element.8), channel_id=1, source_target_pairs={{1,0},{2,1},{3,2},{5,4},{6,5},{7,6},{9,8},{10,9},{11,10},{13,12},{... | collective-permute-start | bytes 1105928 | tf_op jit(solution)/shard_map/ppermute | solution.py:17
  42.7 5.5 %copy-start.14 = (f32[640]{0:T(1024)S(1)}, f32[640]{0:T(1024)}, u32[]{:S(2)}) copy-start(f32[640]{0:T(1024)} %param.31) | copy-start | bytes 7684
  42.7 5.5 %copy-start.15 = (f32[640]{0:T(1024)S(1)}, f32[640]{0:T(1024)}, u32[]{:S(2)}) copy-start(f32[640]{0:T(1024)} %param.30) | copy-start | bytes 7684
  42.7 12.6 %collective-permute-start.6 = (bf16[3,3,80,640]{3,2,1,0:T(8,128)(2,1)}, bf16[3,3,80,640]{3,2,1,0:T(8,128)(2,1)S(1)}, u32[]{:S(2)}, u32[]{:S(2)}) collective-permute-start(bf16[3,3,80,640]{3,2,1,0:T(8,128)(2,1)} %collective-permute-done.5), channel_id=1, source_target_pairs={{0,16},{16,0},{1,17},{17,1},{2,18},{18,2},{3,19},{19,3},{4,20},{20... | collective-permute-start | bytes 2764808 | tf_op jit(solution)/shard_map/ppermute | solution.py:40
  48.3 7.0 %copy-start.4 = (f32[24,640]{1,0:T(8,128)S(1)}, f32[24,640]{1,0:T(8,128)}, u32[]{:S(2)}) copy-start(f32[24,640]{1,0:T(8,128)} %sub.87) | copy-start | bytes 184324
  48.3 7.0 %copy-start.12 = (f32[640]{0:T(1024)S(1)}, f32[640]{0:T(1024)}, u32[]{:S(2)}) copy-start(f32[640]{0:T(1024)} %param.24) | copy-start | bytes 7684
  48.3 7.0 %copy-start.13 = (f32[640]{0:T(1024)S(1)}, f32[640]{0:T(1024)}, u32[]{:S(2)}) copy-start(f32[640]{0:T(1024)} %param.23) | copy-start | bytes 7684
  51.6 26.2 %copy-start.2 = (bf16[24,6,10,640]{3,0,2,1:T(8,128)(2,1)}, bf16[24,6,10,640]{3,0,2,1:T(8,128)(2,1)S(1)}, u32[]{:S(2)}) copy-start(bf16[24,6,10,640]{3,0,2,1:T(8,128)(2,1)S(1)} %fusion.27) | copy-start | bytes 5529604
  55.3 20.7 %collective-permute-start.10 = (bf16[3,3,80,640]{3,2,1,0:T(8,128)(2,1)S(1)}, bf16[3,3,80,640]{3,2,1,0:T(8,128)(2,1)S(1)}, u32[]{:S(2)}, u32[]{:S(2)}) collective-permute-start(bf16[3,3,80,640]{3,2,1,0:T(8,128)(2,1)S(1)} %dynamic-slice_bitcast_fusion), channel_id=1, source_target_pairs={{8,0},{12,4},{0,8},{4,12},{9,1},{13,5},{1,9},{5,13},{10,2},{14,6},... | collective-permute-start | bytes 2764808 | tf_op jit(solution)/shard_map/ppermute | solution.py:39
  59.9 24.1 %collective-permute-start.7 = (bf16[3,3,80,640]{3,2,1,0:T(8,128)(2,1)}, bf16[3,3,80,640]{3,2,1,0:T(8,128)(2,1)S(1)}, u32[]{:S(2)}, u32[]{:S(2)}) collective-permute-start(bf16[3,3,80,640]{3,2,1,0:T(8,128)(2,1)} %collective-permute-done.5), channel_id=1, source_target_pairs={{0,4},{4,0},{8,12},{12,8},{1,5},{5,1},{9,13},{13,9},{2,6},{6,2},{1... | collective-permute-start | bytes 2764808 | tf_op jit(solution)/shard_map/ppermute | solution.py:42
  65.2 25.5 %collective-permute-start.8 = (bf16[3,3,80,640]{3,2,1,0:T(8,128)(2,1)S(1)}, bf16[3,3,80,640]{3,2,1,0:T(8,128)(2,1)S(1)}, u32[]{:S(2)}, u32[]{:S(2)}) collective-permute-start(bf16[3,3,80,640]{3,2,1,0:T(8,128)(2,1)S(1)} %collective-permute-done.6), channel_id=1, source_target_pairs={{0,4},{4,0},{8,12},{12,8},{1,5},{5,1},{9,13},{13,9},{2,6},{6,2},{1... | collective-permute-start | bytes 2764808 | tf_op jit(solution)/shard_map/ppermute | solution.py:43
  76.0 20.2 %collective-permute-start.11 = (bf16[3,3,80,640]{3,2,1,0:T(8,128)(2,1)S(1)}, bf16[3,3,80,640]{3,2,1,0:T(8,128)(2,1)S(1)}, u32[]{:S(2)}, u32[]{:S(2)}) collective-permute-start(bf16[3,3,80,640]{3,2,1,0:T(8,128)(2,1)S(1)} %collective-permute-done.10), channel_id=1, source_target_pairs={{0,1},{1,0},{2,3},{3,2},{4,5},{5,4},{6,7},{7,6},{8,9},{9,8},{10,11... | collective-permute-start | bytes 2764808 | tf_op jit(solution)/shard_map/ppermute | solution.py:40
  84.0 15.2 %copy-start.11 = (f32[24,640]{1,0:T(8,128)S(1)}, f32[24,640]{1,0:T(8,128)}, u32[]{:S(2)}) copy-start(f32[24,640]{1,0:T(8,128)} %param.27) | copy-start | bytes 184324
  84.0 15.2 %copy-start.16 = (f32[640]{0:T(1024)S(1)}, f32[640]{0:T(1024)}, u32[]{:S(2)}) copy-start(f32[640]{0:T(1024)} %param.26) | copy-start | bytes 7684
  88.0 27.8 %collective-permute-start.12 = (bf16[3,3,80,640]{3,2,1,0:T(8,128)(2,1)S(1)}, bf16[3,3,80,640]{3,2,1,0:T(8,128)(2,1)S(1)}, u32[]{:S(2)}, u32[]{:S(2)}) collective-permute-start(bf16[3,3,80,640]{3,2,1,0:T(8,128)(2,1)S(1)} %collective-permute-done.10), channel_id=1, source_target_pairs={{0,4},{4,0},{8,12},{12,8},{1,5},{5,1},{9,13},{13,9},{2,6},{6,2},{1... | collective-permute-start | bytes 2764808 | tf_op jit(solution)/shard_map/ppermute | solution.py:42
  96.2 20.5 %collective-permute-start.13 = (bf16[3,3,80,640]{3,2,1,0:T(8,128)(2,1)S(1)}, bf16[3,3,80,640]{3,2,1,0:T(8,128)(2,1)}, u32[]{:S(2)}, u32[]{:S(2)}) collective-permute-start(bf16[3,3,80,640]{3,2,1,0:T(8,128)(2,1)S(1)} %collective-permute-done.11), channel_id=1, source_target_pairs={{0,4},{4,0},{8,12},{12,8},{1,5},{5,1},{9,13},{13,9},{2,6},{6,2},{1... | collective-permute-start | bytes 2764808 | tf_op jit(solution)/shard_map/ppermute | solution.py:43
  115.7 8.8 %copy-start.10 = (bf16[24,4,8,640]{3,2,1,0:T(8,128)(2,1)S(1)}, bf16[24,4,8,640]{3,2,1,0:T(8,128)(2,1)}, u32[]{:S(2)}) copy-start(bf16[24,4,8,640]{3,2,1,0:T(8,128)(2,1)} %param.19) | copy-start | bytes 2949124
  116.7 7.8 %copy-start.3 = (bf16[24,6,10,640]{3,0,2,1:T(8,128)(2,1)S(1)}, bf16[24,6,10,640]{3,0,2,1:T(8,128)(2,1)}, u32[]{:S(2)}) copy-start(bf16[24,6,10,640]{3,0,2,1:T(8,128)(2,1)} %fusion.39) | copy-start | bytes 5529604
  119.1 5.5 %copy-start.1 = (bf16[3,3,640,640]{3,2,1,0:T(8,128)(2,1)S(1)}, bf16[3,3,640,640]{3,2,1,0:T(8,128)(2,1)}, u32[]{:S(2)}) copy-start(bf16[3,3,640,640]{3,2,1,0:T(8,128)(2,1)} %constant_dynamic-update-slice_fusion.6) | copy-start | bytes 22118404
  121.7 3.3 %copy-start = (f32[24,6,10,640]{3,0,2,1:T(8,128)S(1)}, f32[24,6,10,640]{3,0,2,1:T(8,128)}, u32[]{:S(2)}) copy-start(f32[24,6,10,640]{3,0,2,1:T(8,128)} %fusion.17) | copy-start | bytes 11059204
  121.7 3.3 %copy-start.17 = (f32[640]{0:T(1024)S(1)}, f32[640]{0:T(1024)}, u32[]{:S(2)}) copy-start(f32[640]{0:T(1024)} %param.33) | copy-start | bytes 7684

commit v11 on v5

--- a/solution.py
+++ b/solution.py
@@ -162,11 +162,16 @@
     for boundary in range(1, tiles_across):
         edge_col = boundary * TILE
         for out_col, in_col, tap in ((edge_col - 1, edge_col + 1, 2), (edge_col, edge_col, 0)):
-            pair = jnp.concatenate(
-                [cached_act[:, :, in_col : in_col + 1], blended[:, :, in_col : in_col + 1]]
-            )
-            moved = conv_valid(pair, second_whole[:, tap : tap + 1])
-            change = moved[:requests] - moved[requests:]
+            pair = jnp.stack([cached_act[:, :, in_col], blended[:, :, in_col]])
+            moved = None
+            for tap_row in range(3):
+                term = jnp.dot(
+                    pair[:, :, tap_row : tap_row + rows_dev],
+                    second_whole[tap_row, tap],
+                    preferred_element_type=jnp.float32,
+                )
+                moved = term if moved is None else moved + term
+            change = (moved[0] - moved[1])[:, :, None, :]
             fixes = fixes + jnp.pad(
                 change, ((0, 0), (0, 0), (out_col, cols_dev - out_col - 1), (0, 0))
             )

time: 131 us -> 140 us (1.069)
  matrix products: 33.8 us -> 39.4 us
  local copies, waits for them, and re-layouts: 31.7 us -> 33.8 us
    dot_general x3 -> x2, matrix products: 21.3 us -> 4.49 us  [to_relative(): moved = jnp.dot(activation, chooser, preferred_element_type=jnp.float32)]
    conv_general_dilated x3 -> x2, matrix products: 12.6 us -> 25.6 us  [conv_valid(): lax.conv_general_dilated(activation, kernel, window_strides=(1, 1), paddi...]
    dot_general x0 -> x6, matrix products: none -> 9.37 us  [body(): jnp.dot(pair[:, :, tap_row:tap_row + rows_dev], second_whole[tap_row, tap...]
    unnamed x46 -> x44, local copies, waits for them, and re-layouts: 19.5 us -> 21.5 us
  transfers between devices with their start and end apart: 14 -> 14, of which waited for: 5 -> 5; matrix products, arithmetic and copies ran while one was open for 43% -> 41% of each run, Pallas kernels for 0% -> 0%
where the time goes in v11:
time: 140 us
  matrix products  39.4 us (28%)
  waiting for transfers between devices  35 us (25%)
  local copies, waits for them, and re-layouts  33.8 us (24%)
  starting transfers between devices  23.8 us (17%)
  other arithmetic  7.2 us (5%)
    conv_general_dilated x2, matrix products, conv_valid(): lax.conv_general_dilated(activation, kernel, window_strides=(1, 1), paddi...  25.6 us
    unnamed x44, local copies, waits for them, and re-layouts  21.5 us
    ppermute x2, waiting for transfers between devices, gather_weights(): other = lax.ppermute(fetched, 'groups', y_pairs)  18.2 us
    ppermute x2, waiting for transfers between devices, padded_2(): lax.ppermute(lax.slice_in_dim(block, block.shape[dim] - width, None, axis...  12.3 us
    dot_general x6, matrix products, body(): jnp.dot(pair[:, :, tap_row:tap_row + rows_dev], second_whole[tap_row, tap...  9.37 us
    ppermute x2, starting transfers between devices, padded_2(): lax.ppermute(lax.slice_in_dim(block, block.shape[dim] - width, None, axis...  6.11 us
    ppermute x2, starting transfers between devices, gather_weights(): other_relayed = lax.ppermute(other, 'row', mate_pairs)  4.84 us
    dot_general x2, matrix products, to_relative(): moved = jnp.dot(activation, chooser, preferred_element_type=jnp.float32)  4.49 us
  transfers between devices with their start and end apart: 14, of which 5 were waited for; matrix products, arithmetic and copies ran while one was open for 41% of the time, Pallas kernels for 0%

profile of v11, /device:TPU:1, one launch (start us, length us, event | category | flops | bytes accessed | tf_op | source)
XLA Modules:
  0.0 139.7 jit_solution(5366660355756268707)
XLA Ops:
  0.1 2.2 %dynamic-slice_bitcast_fusion.1 = bf16[3,3,80,640]{3,2,1,0:T(8,128)(2,1)} fusion(bf16[3,3,2,80,640]{4,3,2,1,0:T(8,128)(2,1)} %bitcast.104, s32[]{:T(128)S(6)} %select_n.118), kind=kLoop, calls=%fused_computation.47 | loop fusion | bytes 1843204 | tf_op jit(solution)/shard_map/jit(dynamic_index_in_dim)/squeeze | solution.py:33
  2.2 2.7 %collective-permute-start.5 = (bf16[3,3,80,640]{3,2,1,0:T(8,128)(2,1)}, bf16[3,3,80,640]{3,2,1,0:T(8,128)(2,1)}, u32[]{:S(2)}, u32[]{:S(2)}) collective-permute-start(bf16[3,3,80,640]{3,2,1,0:T(8,128)(2,1)} %dynamic-slice_bitcast_fusion.1), channel_id=1, source_target_pairs={{8,0},{12,4},{0,8},{4,12},{9,1},{13,5},{1,9},{5,13},{10,2},{14,6},... | collective-permute-start | bytes 2764808 | tf_op jit(solution)/shard_map/ppermute | solution.py:39
  4.9 2.1 %copy_bitcast_fusion = (bf16[1,24,4,8,640]{4,1,3,2,0:T(8,128)(2,1)S(1)}, bf16[1,24,4,8,640]{4,1,3,2,0:T(8,128)(2,1)S(1)}) fusion(bf16[24,4,8,640]{3,2,1,0:T(8,128)(2,1)} %param.18, bf16[24,4,8,640]{3,2,1,0:T(8,128)(2,1)} %param.17), kind=kLoop, calls=%fused_computation.44 | loop fusion | bytes 3932160 | tf_op jit(solution)/shard_map/stack | solution.py:125
  7.1 0.9 pad_maximum_fusion.2
  8.0 1.9 %collective-permute-start = (bf16[2,24,1,8,640]{4,1,3,2,0:T(8,128)(2,1)}, bf16[2,24,1,8,640]{4,1,3,2,0:T(8,128)(2,1)S(1)}, u32[]{:S(2)}, u32[]{:S(2)}) collective-permute-start(bf16[2,24,1,8,640]{4,1,3,2,0:T(8,128)(2,1)} %get-tuple-element.9), channel_id=1, source_target_pairs={{0,4},{4,8},{8,12},{1,5},{5,9},{9,13},{2,6},{6,10},{10,14},{3,7},{... | collective-permute-start | bytes 1474568 | tf_op jit(solution)/shard_map/ppermute | solution.py:14
  9.9 2.4 %collective-permute-start.1 = (bf16[2,24,1,8,640]{4,1,3,2,0:T(8,128)(2,1)S(1)}, bf16[2,24,1,8,640]{4,1,3,2,0:T(8,128)(2,1)S(1)}, u32[]{:S(2)}, u32[]{:S(2)}) collective-permute-start(bf16[2,24,1,8,640]{4,1,3,2,0:T(8,128)(2,1)S(1)} %get-tuple-element.10), channel_id=1, source_target_pairs={{4,0},{8,4},{12,8},{5,1},{9,5},{13,9},{6,2},{10,6},{14,10},{7,3},{... | collective-permute-start | bytes 1474568 | tf_op jit(solution)/shard_map/ppermute | solution.py:17
  12.6 2.9 %constant_dynamic-update-slice_fusion.5 = bf16[3,3,640,640]{3,2,1,0:T(8,128)(2,1)} fusion(bf16[3,3,160,640]{3,2,1,0:T(8,128)(2,1)} %param.25), kind=kLoop, calls=%fused_computation.82 | loop fusion | bytes 3686400
  15.5 2.9 %constant_dynamic-update-slice_fusion.11 = bf16[3,3,640,640]{3,2,1,0:T(8,128)(2,1)} fusion(bf16[3,3,160,640]{3,2,1,0:T(8,128)(2,1)} %param.32), kind=kLoop, calls=%fused_computation.88 | loop fusion | bytes 3686400
  18.4 12.3 %collective-permute-done = bf16[2,24,1,8,640]{4,1,3,2,0:T(8,128)(2,1)S(1)} collective-permute-done((bf16[2,24,1,8,640]{4,1,3,2,0:T(8,128)(2,1)}, bf16[2,24,1,8,640]{4,1,3,2,0:T(8,128)(2,1)S(1)}, u32[]{:S(2)}, u32[]{:S(2)}) %collective-permute-start) | collective-permute-done | bytes 491552 | tf_op jit(solution)/shard_map/ppermute | solution.py:14
  30.7 0.7 collective-permute-done.1
  31.5 1.0 pad_maximum_fusion.6
  32.5 4.2 %collective-permute-start.2 = (bf16[2,24,6,1,640]{4,1,3,2,0:T(8,128)(2,1)}, bf16[2,24,6,1,640]{4,1,3,2,0:T(8,128)(2,1)}, u32[]{:S(2)}, u32[]{:S(2)}) collective-permute-start(bf16[2,24,6,1,640]{4,1,3,2,0:T(8,128)(2,1)} %get-tuple-element.7), channel_id=1, source_target_pairs={{0,1},{1,2},{2,3},{4,5},{5,6},{6,7},{8,9},{9,10},{10,11},{12,13},{... | collective-permute-start | bytes 1105928 | tf_op jit(solution)/shard_map/ppermute | solution.py:14
  36.7 1.3 collective-permute-start.3
  39.0 0.2 mul.128
  39.4 0.8 sub.95
  40.2 1.3 dynamic-slice_bitcast_fusion
  41.5 3.7 %collective-permute-done.3 = bf16[2,24,6,1,640]{4,1,3,2,0:T(8,128)(2,1)} collective-permute-done((bf16[2,24,6,1,640]{4,1,3,2,0:T(8,128)(2,1)}, bf16[2,24,6,1,640]{4,1,3,2,0:T(8,128)(2,1)}, u32[]{:S(2)}, u32[]{:S(2)}) %collective-permute-start.3) | collective-permute-done | bytes 368672 | tf_op jit(solution)/shard_map/ppermute | solution.py:17
  45.3 3.0 %pad_maximum_fusion = bf16[2,24,6,10,640]{4,1,3,2,0:T(8,128)(2,1)S(1)} fusion(bf16[2,24,6,1,640]{4,1,3,2,0:T(8,128)(2,1)} %collective-permute-done.3, bf16[2,24,1,8,640]{4,1,3,2,0:T(8,128)(2,1)S(1)} %collective-permute-done.1, bf16[1,24,4,8,640]{4,1,3,2,0:T(8,128)(2,1)S(1)} %get-tuple-element.13, bf16[1,24,4,8,640]{4,1,3,2,0:T(8,128)(2,1)S(1)} %get-tuple-element.14, ...), kind=kLoop, calls=%fused_computation | loop fusion | flops 9216000 | bytes 7372800 | tf_op jit(solution)/shard_map/concatenate | solution.py:18
  48.3 1.3 collective-permute-start.6
  49.6 3.3 %fusion.25 = bf16[24,6,10,640]{3,0,2,1:T(8,128)(2,1)S(1)} fusion(bf16[2,24,6,10,640]{4,1,3,2,0:T(8,128)(2,1)S(1)} %pad_maximum_fusion, f32[6,10]{1,0:T(8,128)S(1)} %and_convert_fusion, f32[640]{0:T(1024)S(1)} %copy-done.10, f32[640]{0:T(1024)S(1)} %copy-done.11, f32[24,640]{1,0:T(8,128)S(1)} %mul.115, f32[24,640]{1,0:T(8,128)S(1)} %sub.85, s32[640]{0:T(1024)S(1)} %fusion.76), kind=kOutput, calls=%fused_computation.31 | convolution fusion | flops 1191116800 | bytes 3825664 | tf_op jit(solution)/shard_map/dot_general | solution.py:72
  53.0 2.1 %fusion.13 = f32[24,6,10,640]{3,0,2,1:T(8,128)} fusion(bf16[2,24,6,10,640]{4,1,3,2,0:T(8,128)(2,1)S(1)} %pad_maximum_fusion), kind=kLoop, calls=%fused_computation.18 | loop fusion | flops 921600 | bytes 5529600 | tf_op jit(solution)/shard_map/convert_element_type | solution.py:127
  55.0 3.4 %collective-permute-start.7 = (bf16[3,3,80,640]{3,2,1,0:T(8,128)(2,1)}, bf16[3,3,80,640]{3,2,1,0:T(8,128)(2,1)S(1)}, u32[]{:S(2)}, u32[]{:S(2)}) collective-permute-start(bf16[3,3,80,640]{3,2,1,0:T(8,128)(2,1)} %collective-permute-done.5), channel_id=1, source_target_pairs={{0,4},{4,0},{8,12},{12,8},{1,5},{5,1},{9,13},{13,9},{2,6},{6,2},{1... | collective-permute-start | bytes 2764808 | tf_op jit(solution)/shard_map/ppermute | solution.py:42
  58.4 9.0 %collective-permute-done.6 = bf16[3,3,80,640]{3,2,1,0:T(8,128)(2,1)S(1)} collective-permute-done((bf16[3,3,80,640]{3,2,1,0:T(8,128)(2,1)}, bf16[3,3,80,640]{3,2,1,0:T(8,128)(2,1)S(1)}, u32[]{:S(2)}, u32[]{:S(2)}) %collective-permute-start.6) | collective-permute-done | bytes 921632 | tf_op jit(solution)/shard_map/ppermute | solution.py:41
  67.4 4.1 %collective-permute-start.8 = (bf16[3,3,80,640]{3,2,1,0:T(8,128)(2,1)S(1)}, bf16[3,3,80,640]{3,2,1,0:T(8,128)(2,1)S(1)}, u32[]{:S(2)}, u32[]{:S(2)}) collective-permute-start(bf16[3,3,80,640]{3,2,1,0:T(8,128)(2,1)S(1)} %collective-permute-done.6), channel_id=1, source_target_pairs={{0,4},{4,0},{8,12},{12,8},{1,5},{5,1},{9,13},{13,9},{2,6},{6,2},{1... | collective-permute-start | bytes 2764808 | tf_op jit(solution)/shard_map/ppermute | solution.py:43
  71.5 1.2 collective-permute-start.11
  72.9 0.3 collective-permute-start.12
  73.2 2.9 %constant_dynamic-update-slice_fusion.4 = bf16[3,3,640,640]{3,2,1,0:T(8,128)(2,1)} fusion(bf16[3,3,640,640]{3,2,1,0:T(8,128)(2,1)} %constant_dynamic-update-slice_fusion.5, bf16[3,3,160,640]{3,2,1,0:T(8,128)(2,1)} %collective-permute-done.4), kind=kLoop, calls=%fused_computation.81 | loop fusion | bytes 3686400
  76.1 2.2 %constant_dynamic-update-slice_fusion.3 = bf16[3,3,640,640]{3,2,1,0:T(8,128)(2,1)} fusion(bf16[3,3,640,640]{3,2,1,0:T(8,128)(2,1)} %constant_dynamic-update-slice_fusion.4, bf16[3,3,80,640]{3,2,1,0:T(8,128)(2,1)} %collective-permute-done.5), kind=kLoop, calls=%fused_computation.80 | loop fusion | bytes 1843200
  78.3 1.0 constant_dynamic-update-slice_fusion.2
  79.4 2.9 %constant_dynamic-update-slice_fusion.10 = bf16[3,3,640,640]{3,2,1,0:T(8,128)(2,1)} fusion(bf16[3,3,640,640]{3,2,1,0:T(8,128)(2,1)} %constant_dynamic-update-slice_fusion.11, bf16[3,3,160,640]{3,2,1,0:T(8,128)(2,1)} %collective-permute-done.9), kind=kLoop, calls=%fused_computation.87 | loop fusion | bytes 3686400
  82.3 1.0 constant_dynamic-update-slice_fusion.9
  83.3 1.1 constant_dynamic-update-slice_fusion.1
  84.4 9.3 %collective-permute-done.11 = bf16[3,3,80,640]{3,2,1,0:T(8,128)(2,1)} collective-permute-done((bf16[3,3,80,640]{3,2,1,0:T(8,128)(2,1)S(1)}, bf16[3,3,80,640]{3,2,1,0:T(8,128)(2,1)}, u32[]{:S(2)}, u32[]{:S(2)}) %collective-permute-start.11) | collective-permute-done | bytes 921632 | tf_op jit(solution)/shard_map/ppermute | solution.py:41
  93.6 0.8 collective-permute-start.13
  94.4 1.0 constant_dynamic-update-slice_fusion
  95.5 15.2 %multiply_convert_fusion.1 = bf16[24,4,8,640]{3,0,2,1:T(8,128)(2,1)} fusion(bf16[3,3,640,640]{3,2,1,0:T(8,128)(2,1)} %constant_dynamic-update-slice_fusion, f32[640]{0:T(1024)S(1)} %copy-done.10, f32[640]{0:T(1024)S(1)} %copy-done.11, f32[24,640]{1,0:T(8,128)S(1)} %mul.115, f32[24,640]{1,0:T(8,128)S(1)} %sub.85, f32[24,640]{1,0:T(8,128)S(1)} %copy-done.9, ...), kind=kOutput, calls=%fused_computation.15 | convolution fusion | flops 6858833920 | bytes 10521840 | tf_op jit(solution)/shard_map/conv_general_dilated | solution.py:81
  110.7 2.3 %constant_dynamic-update-slice_fusion.8 = bf16[3,3,640,640]{3,2,1,0:T(8,128)(2,1)} fusion(bf16[3,3,640,640]{3,2,1,0:T(8,128)(2,1)} %constant_dynamic-update-slice_fusion.9, bf16[3,3,80,640]{3,2,1,0:T(8,128)(2,1)} %collective-permute-done.11), kind=kLoop, calls=%fused_computation.85 | loop fusion | bytes 1843200
  113.1 2.2 %constant_dynamic-update-slice_fusion.7 = bf16[3,3,640,640]{3,2,1,0:T(8,128)(2,1)} fusion(bf16[3,3,640,640]{3,2,1,0:T(8,128)(2,1)} %constant_dynamic-update-slice_fusion.8, bf16[3,3,80,640]{3,2,1,0:T(8,128)(2,1)} %collective-permute-done.12), kind=kLoop, calls=%fused_computation.84 | loop fusion | bytes 1843200
  115.3 1.2 fusion.37
  116.5 2.2 %constant_dynamic-update-slice_fusion.6 = bf16[3,3,640,640]{3,2,1,0:T(8,128)(2,1)} fusion(bf16[3,3,640,640]{3,2,1,0:T(8,128)(2,1)} %constant_dynamic-update-slice_fusion.7, bf16[3,3,80,640]{3,2,1,0:T(8,128)(2,1)} %collective-permute-done.13), kind=kLoop, calls=%fused_computation.83 | loop fusion | bytes 1843200 | tf_op jit(solution)/shard_map/concatenate | solution.py:48
  118.7 1.5 %fusion.53 = f32[2,24,4,640]{3,1,2,0:T(8,128)S(1)} fusion(bf16[3,3,640,640]{3,2,1,0:T(8,128)(2,1)} %constant_dynamic-update-slice_fusion.6, bf16[1,24,6,640]{3,1,2,0:T(8,128)(2,1)S(1)} %get-tuple-element.11, bf16[1,24,6,640]{3,1,2,0:T(8,128)(2,1)S(1)} %slice_bitcast_fusion.18), kind=kOutput, calls=%fused_computation.56 | convolution fusion | flops 158023680 | bytes 1679360 | tf_op jit(solution)/shard_map/dot_general | solution.py:168
  120.3 1.5 %fusion.52 = f32[2,24,4,640]{3,1,2,0:T(8,128)S(1)} fusion(bf16[3,3,640,640]{3,2,1,0:T(8,128)(2,1)} %constant_dynamic-update-slice_fusion.6, bf16[1,24,6,640]{3,1,2,0:T(8,128)(2,1)S(1)} %get-tuple-element.11, bf16[1,24,6,640]{3,1,2,0:T(8,128)(2,1)S(1)} %slice_bitcast_fusion.18), kind=kOutput, calls=%fused_computation.54 | convolution fusion | flops 158023680 | bytes 1679360 | tf_op jit(solution)/shard_map/dot_general | solution.py:168
  121.8 1.5 %fusion.51 = f32[2,24,4,640]{3,1,2,0:T(8,128)S(1)} fusion(bf16[3,3,640,640]{3,2,1,0:T(8,128)(2,1)} %constant_dynamic-update-slice_fusion.6, bf16[1,24,6,640]{3,1,2,0:T(8,128)(2,1)S(1)} %get-tuple-element.12, bf16[1,24,6,640]{3,1,2,0:T(8,128)(2,1)S(1)} %slice_bitcast_fusion.16), kind=kOutput, calls=%fused_computation.51 | convolution fusion | flops 158023680 | bytes 1679360 | tf_op jit(solution)/shard_map/dot_general | solution.py:168
  123.3 1.5 %fusion.50 = f32[2,24,4,640]{3,1,2,0:T(8,128)S(1)} fusion(bf16[3,3,640,640]{3,2,1,0:T(8,128)(2,1)} %constant_dynamic-update-slice_fusion.6, bf16[1,24,6,640]{3,1,2,0:T(8,128)(2,1)S(1)} %get-tuple-element.12, bf16[1,24,6,640]{3,1,2,0:T(8,128)(2,1)S(1)} %slice_bitcast_fusion.16), kind=kOutput, calls=%fused_computation.49 | convolution fusion | flops 158023680 | bytes 1679360 | tf_op jit(solution)/shard_map/dot_general | solution.py:168
  124.9 1.7 %fusion.43 = f32[2,24,4,640]{3,1,2,0:T(8,128)S(1)} fusion(f32[2,24,4,640]{3,1,2,0:T(8,128)S(1)} %fusion.52, f32[2,24,4,640]{3,1,2,0:T(8,128)S(1)} %fusion.53, bf16[3,3,640,640]{3,2,1,0:T(8,128)(2,1)} %constant_dynamic-update-slice_fusion.6, bf16[1,24,6,640]{3,1,2,0:T(8,128)(2,1)S(1)} %get-tuple-element.11, bf16[1,24,6,640]{3,1,2,0:T(8,128)(2,1)S(1)} %slice_bitcast_fusion.18), kind=kOutput, calls=%fused_computation.41 | convolution fusion | flops 158269440 | bytes 2662400 | tf_op jit(solution)/shard_map/dot_general | solution.py:168
  126.6 1.5 %fusion.42 = f32[2,24,4,640]{3,1,2,0:T(8,128)S(1)} fusion(f32[2,24,4,640]{3,1,2,0:T(8,128)S(1)} %fusion.50, f32[2,24,4,640]{3,1,2,0:T(8,128)S(1)} %fusion.51, bf16[3,3,640,640]{3,2,1,0:T(8,128)(2,1)} %constant_dynamic-update-slice_fusion.6, bf16[1,24,6,640]{3,1,2,0:T(8,128)(2,1)S(1)} %get-tuple-element.12, bf16[1,24,6,640]{3,1,2,0:T(8,128)(2,1)S(1)} %slice_bitcast_fusion.16), kind=kOutput, calls=%fused_computation.39 | convolution fusion | flops 158269440 | bytes 2662400 | tf_op jit(solution)/shard_map/dot_general | solution.py:168
  128.3 10.3 %fusion.46 = bf16[24,4,8,640]{3,0,2,1:T(8,128)(2,1)S(1)} fusion(f32[24,6,10,640]{3,0,2,1:T(8,128)S(1)} %copy-done.1, f32[24,4,1,640]{3,0,2,1:T(8,128)S(1)} %fusion.63, f32[24,4,1,640]{3,0,2,1:T(8,128)S(1)} %fusion.64, bf16[3,3,640,640]{3,2,1,0:T(8,128)(2,1)} %constant_dynamic-update-slice_fusion.6, bf16[24,6,10,640]{3,0,1,2:T(8,128)(2,1)S(1)} %fusion.37, ...), kind=kOutput, calls=%fused_computation.42 | convolution fusion | flops 5665259520 | bytes 13642432 | tf_op jit(solution)/shard_map/conv_general_dilated | solution.py:81
  138.6 1.1 copy.52
  (65 shorter events, 1.9 us)
Async XLA Ops:
  0.0 72.9 %collective-permute-start.4 = (bf16[3,3,160,640]{3,2,1,0:T(8,128)(2,1)}, bf16[3,3,160,640]{3,2,1,0:T(8,128)(2,1)}, u32[]{:S(2)}, u32[]{:S(2)}) collective-permute-start(bf16[3,3,160,640]{3,2,1,0:T(8,128)(2,1)} %param.25), channel_id=1, source_target_pairs={{0,4},{4,0},{8,12},{12,8},{1,5},{5,1},{9,13},{13,9},{2,6},{6,2},{1... | collective-permute-start | bytes 5529608 | tf_op jit(solution)/shard_map/ppermute | solution.py:34
  2.2 10.2 %copy-start.7 = (s32[24,16]{0,1:T(8,128)S(1)}, s32[24,16]{0,1:T(8,128)}, u32[]{:S(2)}) copy-start(s32[24,16]{0,1:T(8,128)} %param.20) | copy-start | bytes 4612
  2.2 46.0 %collective-permute-start.5 = (bf16[3,3,80,640]{3,2,1,0:T(8,128)(2,1)}, bf16[3,3,80,640]{3,2,1,0:T(8,128)(2,1)}, u32[]{:S(2)}, u32[]{:S(2)}) collective-permute-start(bf16[3,3,80,640]{3,2,1,0:T(8,128)(2,1)} %dynamic-slice_bitcast_fusion.1), channel_id=1, source_target_pairs={{8,0},{12,4},{0,8},{4,12},{9,1},{13,5},{1,9},{5,13},{10,2},{14,6},... | collective-permute-start | bytes 2764808 | tf_op jit(solution)/shard_map/ppermute | solution.py:39
  8.0 22.8 %collective-permute-start = (bf16[2,24,1,8,640]{4,1,3,2,0:T(8,128)(2,1)}, bf16[2,24,1,8,640]{4,1,3,2,0:T(8,128)(2,1)S(1)}, u32[]{:S(2)}, u32[]{:S(2)}) collective-permute-start(bf16[2,24,1,8,640]{4,1,3,2,0:T(8,128)(2,1)} %get-tuple-element.9), channel_id=1, source_target_pairs={{0,4},{4,8},{8,12},{1,5},{5,9},{9,13},{2,6},{6,10},{10,14},{3,7},{... | collective-permute-start | bytes 1474568 | tf_op jit(solution)/shard_map/ppermute | solution.py:14
  9.9 21.6 %collective-permute-start.1 = (bf16[2,24,1,8,640]{4,1,3,2,0:T(8,128)(2,1)S(1)}, bf16[2,24,1,8,640]{4,1,3,2,0:T(8,128)(2,1)S(1)}, u32[]{:S(2)}, u32[]{:S(2)}) collective-permute-start(bf16[2,24,1,8,640]{4,1,3,2,0:T(8,128)(2,1)S(1)} %get-tuple-element.10), channel_id=1, source_target_pairs={{4,0},{8,4},{12,8},{5,1},{9,5},{13,9},{6,2},{10,6},{14,10},{7,3},{... | collective-permute-start | bytes 1474568 | tf_op jit(solution)/shard_map/ppermute | solution.py:17
  12.3 67.1 %collective-permute-start.9 = (bf16[3,3,160,640]{3,2,1,0:T(8,128)(2,1)}, bf16[3,3,160,640]{3,2,1,0:T(8,128)(2,1)}, u32[]{:S(2)}, u32[]{:S(2)}) collective-permute-start(bf16[3,3,160,640]{3,2,1,0:T(8,128)(2,1)} %param.32), channel_id=1, source_target_pairs={{0,4},{4,0},{8,12},{12,8},{1,5},{5,1},{9,13},{13,9},{2,6},{6,2},{1... | collective-permute-start | bytes 5529608 | tf_op jit(solution)/shard_map/ppermute | solution.py:34
  15.5 22.5 %copy-start.3 = (f32[24,32]{1,0:T(8,128)S(1)}, f32[24,32]{1,0:T(8,128)}, u32[]{:S(2)}) copy-start(f32[24,32]{1,0:T(8,128)} %param.29) | copy-start | bytes 9220
  15.5 22.9 %copy-start.4 = (f32[24,32]{1,0:T(8,128)S(1)}, f32[24,32]{1,0:T(8,128)}, u32[]{:S(2)}) copy-start(f32[24,32]{1,0:T(8,128)} %param.28) | copy-start | bytes 9220
  15.5 23.3 %copy-start.5 = (f32[24,32]{1,0:T(8,128)S(1)}, f32[24,32]{1,0:T(8,128)}, u32[]{:S(2)}) copy-start(f32[24,32]{1,0:T(8,128)} %param.22) | copy-start | bytes 9220
  18.4 20.8 %copy-start.6 = (f32[24,32]{1,0:T(8,128)S(1)}, f32[24,32]{1,0:T(8,128)}, u32[]{:S(2)}) copy-start(f32[24,32]{1,0:T(8,128)} %param.21) | copy-start | bytes 9220
  32.5 9.1 %collective-permute-start.2 = (bf16[2,24,6,1,640]{4,1,3,2,0:T(8,128)(2,1)}, bf16[2,24,6,1,640]{4,1,3,2,0:T(8,128)(2,1)}, u32[]{:S(2)}, u32[]{:S(2)}) collective-permute-start(bf16[2,24,6,1,640]{4,1,3,2,0:T(8,128)(2,1)} %get-tuple-element.7), channel_id=1, source_target_pairs={{0,1},{1,2},{2,3},{4,5},{5,6},{6,7},{8,9},{9,10},{10,11},{12,13},{... | collective-permute-start | bytes 1105928 | tf_op jit(solution)/shard_map/ppermute | solution.py:14
  36.7 8.6 %collective-permute-start.3 = (bf16[2,24,6,1,640]{4,1,3,2,0:T(8,128)(2,1)}, bf16[2,24,6,1,640]{4,1,3,2,0:T(8,128)(2,1)}, u32[]{:S(2)}, u32[]{:S(2)}) collective-permute-start(bf16[2,24,6,1,640]{4,1,3,2,0:T(8,128)(2,1)} %get-tuple-element.8), channel_id=1, source_target_pairs={{1,0},{2,1},{3,2},{5,4},{6,5},{7,6},{9,8},{10,9},{11,10},{13,12},{... | collective-permute-start | bytes 1105928 | tf_op jit(solution)/shard_map/ppermute | solution.py:17
  41.5 8.1 %copy-start.10 = (f32[640]{0:T(1024)S(1)}, f32[640]{0:T(1024)}, u32[]{:S(2)}) copy-start(f32[640]{0:T(1024)} %param.31) | copy-start | bytes 7684
  41.5 8.1 %copy-start.11 = (f32[640]{0:T(1024)S(1)}, f32[640]{0:T(1024)}, u32[]{:S(2)}) copy-start(f32[640]{0:T(1024)} %param.30) | copy-start | bytes 7684
  48.2 4.7 %copy-start = (bf16[2,24,6,10,640]{4,1,3,2,0:T(8,128)(2,1)}, bf16[2,24,6,10,640]{4,1,3,2,0:T(8,128)(2,1)S(1)}, u32[]{:S(2)}) copy-start(bf16[2,24,6,10,640]{4,1,3,2,0:T(8,128)(2,1)S(1)} %pad_maximum_fusion) | copy-start | bytes 11059204
  48.2 23.2 %collective-permute-start.10 = (bf16[3,3,80,640]{3,2,1,0:T(8,128)(2,1)S(1)}, bf16[3,3,80,640]{3,2,1,0:T(8,128)(2,1)S(1)}, u32[]{:S(2)}, u32[]{:S(2)}) collective-permute-start(bf16[3,3,80,640]{3,2,1,0:T(8,128)(2,1)S(1)} %dynamic-slice_bitcast_fusion), channel_id=1, source_target_pairs={{8,0},{12,4},{0,8},{4,12},{9,1},{13,5},{1,9},{5,13},{10,2},{14,6},... | collective-permute-start | bytes 2764808 | tf_op jit(solution)/shard_map/ppermute | solution.py:39
  48.3 19.1 %collective-permute-start.6 = (bf16[3,3,80,640]{3,2,1,0:T(8,128)(2,1)}, bf16[3,3,80,640]{3,2,1,0:T(8,128)(2,1)S(1)}, u32[]{:S(2)}, u32[]{:S(2)}) collective-permute-start(bf16[3,3,80,640]{3,2,1,0:T(8,128)(2,1)} %collective-permute-done.5), channel_id=1, source_target_pairs={{0,16},{16,0},{1,17},{17,1},{2,18},{18,2},{3,19},{19,3},{4,20},{20... | collective-permute-start | bytes 2764808 | tf_op jit(solution)/shard_map/ppermute | solution.py:41
  55.0 28.3 %collective-permute-start.7 = (bf16[3,3,80,640]{3,2,1,0:T(8,128)(2,1)}, bf16[3,3,80,640]{3,2,1,0:T(8,128)(2,1)S(1)}, u32[]{:S(2)}, u32[]{:S(2)}) collective-permute-start(bf16[3,3,80,640]{3,2,1,0:T(8,128)(2,1)} %collective-permute-done.5), channel_id=1, source_target_pairs={{0,4},{4,0},{8,12},{12,8},{1,5},{5,1},{9,13},{13,9},{2,6},{6,2},{1... | collective-permute-start | bytes 2764808 | tf_op jit(solution)/shard_map/ppermute | solution.py:42
  67.4 27.0 %collective-permute-start.8 = (bf16[3,3,80,640]{3,2,1,0:T(8,128)(2,1)S(1)}, bf16[3,3,80,640]{3,2,1,0:T(8,128)(2,1)S(1)}, u32[]{:S(2)}, u32[]{:S(2)}) collective-permute-start(bf16[3,3,80,640]{3,2,1,0:T(8,128)(2,1)S(1)} %collective-permute-done.6), channel_id=1, source_target_pairs={{0,4},{4,0},{8,12},{12,8},{1,5},{5,1},{9,13},{13,9},{2,6},{6,2},{1... | collective-permute-start | bytes 2764808 | tf_op jit(solution)/shard_map/ppermute | solution.py:43
  71.5 22.2 %collective-permute-start.11 = (bf16[3,3,80,640]{3,2,1,0:T(8,128)(2,1)S(1)}, bf16[3,3,80,640]{3,2,1,0:T(8,128)(2,1)}, u32[]{:S(2)}, u32[]{:S(2)}) collective-permute-start(bf16[3,3,80,640]{3,2,1,0:T(8,128)(2,1)S(1)} %collective-permute-done.10), channel_id=1, source_target_pairs={{0,16},{16,0},{1,17},{17,1},{2,18},{18,2},{3,19},{19,3},{4,20},{20... | collective-permute-start | bytes 2764808 | tf_op jit(solution)/shard_map/ppermute | solution.py:41
  72.9 40.2 %collective-permute-start.12 = (bf16[3,3,80,640]{3,2,1,0:T(8,128)(2,1)S(1)}, bf16[3,3,80,640]{3,2,1,0:T(8,128)(2,1)}, u32[]{:S(2)}, u32[]{:S(2)}) collective-permute-start(bf16[3,3,80,640]{3,2,1,0:T(8,128)(2,1)S(1)} %collective-permute-done.10), channel_id=1, source_target_pairs={{0,4},{4,0},{8,12},{12,8},{1,5},{5,1},{9,13},{13,9},{2,6},{6,2},{1... | collective-permute-start | bytes 2764808 | tf_op jit(solution)/shard_map/ppermute | solution.py:42
  82.3 13.2 %copy-start.2 = (f32[24,640]{1,0:T(8,128)S(1)}, f32[24,640]{1,0:T(8,128)}, u32[]{:S(2)}) copy-start(f32[24,640]{1,0:T(8,128)} %sub.95) | copy-start | bytes 184324
  82.3 13.2 %copy-start.9 = (f32[24,640]{1,0:T(8,128)S(1)}, f32[24,640]{1,0:T(8,128)}, u32[]{:S(2)}) copy-start(f32[24,640]{1,0:T(8,128)} %param.27) | copy-start | bytes 184324
  82.3 13.2 %copy-start.12 = (f32[640]{0:T(1024)S(1)}, f32[640]{0:T(1024)}, u32[]{:S(2)}) copy-start(f32[640]{0:T(1024)} %param.26) | copy-start | bytes 7684
  82.3 13.2 %copy-start.13 = (f32[640]{0:T(1024)S(1)}, f32[640]{0:T(1024)}, u32[]{:S(2)}) copy-start(f32[640]{0:T(1024)} %param.24) | copy-start | bytes 7684
  82.3 13.2 %copy-start.14 = (f32[640]{0:T(1024)S(1)}, f32[640]{0:T(1024)}, u32[]{:S(2)}) copy-start(f32[640]{0:T(1024)} %param.23) | copy-start | bytes 7684
  93.6 22.9 %collective-permute-start.13 = (bf16[3,3,80,640]{3,2,1,0:T(8,128)(2,1)}, bf16[3,3,80,640]{3,2,1,0:T(8,128)(2,1)}, u32[]{:S(2)}, u32[]{:S(2)}) collective-permute-start(bf16[3,3,80,640]{3,2,1,0:T(8,128)(2,1)} %collective-permute-done.11), channel_id=1, source_target_pairs={{0,4},{4,0},{8,12},{12,8},{1,5},{5,1},{9,13},{13,9},{2,6},{6,2},{1... | collective-permute-start | bytes 2764808 | tf_op jit(solution)/shard_map/ppermute | solution.py:43
  110.7 4.5 %copy-start.16 = (bf16[24,4,8,640]{3,0,2,1:T(8,128)(2,1)S(1)}, bf16[24,4,8,640]{3,0,2,1:T(8,128)(2,1)}, u32[]{:S(2)}) copy-start(bf16[24,4,8,640]{3,0,2,1:T(8,128)(2,1)} %multiply_convert_fusion.1) | copy-start | bytes 2949124
  124.9 3.4 %copy-start.1 = (f32[24,6,10,640]{3,0,2,1:T(8,128)S(1)}, f32[24,6,10,640]{3,0,2,1:T(8,128)}, u32[]{:S(2)}) copy-start(f32[24,6,10,640]{3,0,2,1:T(8,128)} %fusion.13) | copy-start | bytes 11059204
  124.9 3.4 %copy-start.8 = (bf16[24,4,8,640]{3,2,1,0:T(8,128)(2,1)S(1)}, bf16[24,4,8,640]{3,2,1,0:T(8,128)(2,1)}, u32[]{:S(2)}) copy-start(bf16[24,4,8,640]{3,2,1,0:T(8,128)(2,1)} %param.19) | copy-start | bytes 2949124
  124.9 3.4 %copy-start.15 = (f32[640]{0:T(1024)S(1)}, f32[640]{0:T(1024)}, u32[]{:S(2)}) copy-start(f32[640]{0:T(1024)} %param.33) | copy-start | bytes 7684

commit v12 on v5

--- a/solution.py
+++ b/solution.py
@@ -22,9 +22,8 @@
 def gather_weights(kernels):
     count = lax.axis_size("row")
     chips = count // 2
-    y_pairs = [(i, i ^ 1) for i in range(lax.axis_size("groups"))]
     mate_pairs = [(i, i ^ 1) for i in range(count)]
-    parity = lax.axis_index("groups") % 2
+    parity = lax.axis_index("groups")
     wholes = []
     previous = None
     for shard in kernels:
@@ -38,13 +37,8 @@
             pairs = [(((i // 2 + step) % chips) * 2 + i % 2, i) for i in range(count)]
             fetched = lax.ppermute(mine, "row", pairs)
             previous = fetched
-            other = lax.ppermute(fetched, "groups", y_pairs)
-            relayed = lax.ppermute(fetched, "row", mate_pairs)
-            other_relayed = lax.ppermute(other, "row", mate_pairs)
-            held += [
-                jnp.concatenate([fetched, other], axis=2),
-                jnp.concatenate([relayed, other_relayed], axis=2),
-            ]
+            rebuilt = lax.all_gather(fetched, "groups", axis=2, tiled=True)
+            held += [rebuilt, lax.ppermute(rebuilt, "row", mate_pairs)]
         wholes.append(jnp.concatenate(held, axis=2))
     return wholes
 
@@ -60,10 +54,7 @@
     block = position // depth
     within = position % depth
     source = 2 * ((chip + block // 2) % chips) + jnp.where(block % 2 == 0, core, 1 - core)
-    half = depth // 2
-    parity = lax.axis_index("groups") % 2
-    shuffled = (parity ^ (within // half)) * half + within % half
-    return source * depth + jnp.where(block >= 2, shuffled, within)
+    return source * depth + within
 
 
 def to_relative(activation, order):

time: 131 us -> 141 us (1.076)
  between operations: 0.38 us -> 13.8 us
  local copies, waits for them, and re-layouts: 31.7 us -> 19.6 us
  waiting for transfers between devices: 33.8 us -> 43.3 us
  starting transfers between devices: 23.8 us -> 18.9 us
  matrix products: 33.8 us -> 38.2 us
    ppermute x2, waiting for transfers between devices: 0.01 us -> 18.7 us  [gather_weights(): fetched = lax.ppermute(mine, 'row', pairs)]
    ppermute x6 -> x2, waiting for transfers between devices: 17 us -> 0.01 us  [gather_weights(): held += [rebuilt, lax.ppermute(rebuilt, 'row', mate_pairs)]]
    all_gather x0 -> x2, waiting for transfers between devices: none -> 15.3 us  [gather_weights(): rebuilt = lax.all_gather(fetched, 'groups', axis=2, tiled=True)]
    ppermute x2, waiting for transfers between devices: 12.3 us -> 0.12 us  [padded_2(): lax.ppermute(lax.slice_in_dim(block, block.shape[dim] - width, None, axis...]
    unnamed x46 -> x41, local copies, waits for them, and re-layouts: 19.5 us -> 9.45 us
    ppermute x6 -> x2, starting transfers between devices: 11.1 us -> 2.85 us  [gather_weights(): held += [rebuilt, lax.ppermute(rebuilt, 'row', mate_pairs)]]
    ppermute x2, waiting for transfers between devices: 4.44 us -> 9.23 us  [padded_2(): lax.ppermute(lax.slice_in_dim(block, 0, width, axis=dim), axis, backward)]
    conv_general_dilated x3, matrix products: 12.6 us -> 15.5 us  [conv_valid(): lax.conv_general_dilated(activation, kernel, window_strides=(1, 1), paddi...]
  transfers between devices with their start and end apart: 14 -> 12, of which waited for: 5 -> 6; matrix products, arithmetic and copies ran while one was open for 43% -> 32% of each run, Pallas kernels for 0% -> 0%
where the time goes in v12:
time: 141 us
  waiting for transfers between devices  43.3 us (31%)
  matrix products  38.2 us (27%)
  local copies, waits for them, and re-layouts  19.6 us (14%)
  starting transfers between devices  18.9 us (13%)
  between operations  13.8 us (10%)
  other arithmetic  6.81 us (5%)
    dot_general x3, matrix products, to_relative(): moved = jnp.dot(activation, chooser, preferred_element_type=jnp.float32)  22.7 us
    ppermute x2, waiting for transfers between devices, gather_weights(): fetched = lax.ppermute(mine, 'row', pairs)  18.7 us
    conv_general_dilated x3, matrix products, conv_valid(): lax.conv_general_dilated(activation, kernel, window_strides=(1, 1), paddi...  15.5 us
    all_gather x2, waiting for transfers between devices, gather_weights(): rebuilt = lax.all_gather(fetched, 'groups', axis=2, tiled=True)  15.3 us
    unnamed x41, local copies, waits for them, and re-layouts  9.45 us
    ppermute x2, waiting for transfers between devices, padded_2(): lax.ppermute(lax.slice_in_dim(block, 0, width, axis=dim), axis, backward)  9.23 us
    ppermute x2, starting transfers between devices, padded_2(): lax.ppermute(lax.slice_in_dim(block, block.shape[dim] - width, None, axis...  7.8 us
    ppermute x2, starting transfers between devices, gather_weights(): fetched = lax.ppermute(mine, 'row', pairs)  3.99 us
  transfers between devices with their start and end apart: 12, of which 6 were waited for; matrix products, arithmetic and copies ran while one was open for 32% of the time, Pallas kernels for 0%

profile of v12, /device:TPU:1, one launch (start us, length us, event | category | flops | bytes accessed | tf_op | source)
XLA Modules:
  0.0 140.7 jit_solution(3018284462536701708)
XLA Ops:
  6.5 1.3 dynamic-slice_bitcast_fusion.1
  7.9 2.1 %collective-permute-start.5 = (bf16[3,3,80,640]{3,2,1,0:T(8,128)(2,1)S(1)}, bf16[3,3,80,640]{3,2,1,0:T(8,128)(2,1)}, u32[]{:S(2)}, u32[]{:S(2)}) collective-permute-start(bf16[3,3,80,640]{3,2,1,0:T(8,128)(2,1)S(1)} %dynamic-slice_bitcast_fusion.1), channel_id=1, source_target_pairs={{8,0},{12,4},{0,8},{4,12},{9,1},{13,5},{1,9},{5,13},{10,2},{14,6},... | collective-permute-start | bytes 2764808 | tf_op jit(solution)/shard_map/ppermute | solution.py:38
  10.0 1.0 collective-permute-start.4
  11.0 1.9 %copy_bitcast_fusion = (bf16[1,24,4,8,640]{4,1,3,2,0:T(8,128)(2,1)S(1)}, bf16[1,24,4,8,640]{4,1,3,2,0:T(8,128)(2,1)S(1)}) fusion(bf16[24,4,8,640]{3,2,1,0:T(8,128)(2,1)S(1)} %copy-done.2, bf16[24,4,8,640]{3,2,1,0:T(8,128)(2,1)} %param.17), kind=kLoop, calls=%fused_computation.47 | loop fusion | bytes 3932160 | tf_op jit(solution)/shard_map/stack | solution.py:116
  12.8 17.4 %collective-permute-done.5 = bf16[3,3,80,640]{3,2,1,0:T(8,128)(2,1)} collective-permute-done((bf16[3,3,80,640]{3,2,1,0:T(8,128)(2,1)S(1)}, bf16[3,3,80,640]{3,2,1,0:T(8,128)(2,1)}, u32[]{:S(2)}, u32[]{:S(2)}) %collective-permute-start.5) | collective-permute-done | bytes 921632 | tf_op jit(solution)/shard_map/ppermute | solution.py:38
  30.3 0.0 all-gather.5.cloned.1.call-start
  30.4 1.1 pad_maximum_fusion.2
  31.4 4.6 %collective-permute-start = (bf16[2,24,1,8,640]{4,1,3,2,0:T(8,128)(2,1)}, bf16[2,24,1,8,640]{4,1,3,2,0:T(8,128)(2,1)S(1)}, u32[]{:S(2)}, u32[]{:S(2)}) collective-permute-start(bf16[2,24,1,8,640]{4,1,3,2,0:T(8,128)(2,1)} %get-tuple-element.9), channel_id=1, source_target_pairs={{0,4},{4,8},{8,12},{1,5},{5,9},{9,13},{2,6},{6,10},{10,14},{3,7},{... | collective-permute-start | bytes 1474568 | tf_op jit(solution)/shard_map/ppermute | solution.py:14
  36.0 1.9 %collective-permute-start.1 = (bf16[2,24,1,8,640]{4,1,3,2,0:T(8,128)(2,1)}, bf16[2,24,1,8,640]{4,1,3,2,0:T(8,128)(2,1)S(1)}, u32[]{:S(2)}, u32[]{:S(2)}) collective-permute-start(bf16[2,24,1,8,640]{4,1,3,2,0:T(8,128)(2,1)} %get-tuple-element.10), channel_id=1, source_target_pairs={{4,0},{8,4},{12,8},{5,1},{9,5},{13,9},{6,2},{10,6},{14,10},{7,3},{... | collective-permute-start | bytes 1474568 | tf_op jit(solution)/shard_map/ppermute | solution.py:17
  38.0 0.1 collective-permute-start.7
  38.1 0.2 broadcast_in_dim.29
  38.3 0.2 mul.108
  38.5 0.2 broadcast_in_dim.28
  38.7 0.2 sub.59
  38.9 0.2 broadcast_in_dim.33
  39.1 0.2 mul.120
  39.3 0.2 broadcast_in_dim.32
  39.5 0.9 sub.68
  40.4 0.1 compare_reduce_fusion
  40.5 1.3 dynamic-slice_bitcast_fusion
  41.8 1.9 %collective-permute-start.8 = (bf16[3,3,80,640]{3,2,1,0:T(8,128)(2,1)S(1)}, bf16[3,3,80,640]{3,2,1,0:T(8,128)(2,1)}, u32[]{:S(2)}, u32[]{:S(2)}) collective-permute-start(bf16[3,3,80,640]{3,2,1,0:T(8,128)(2,1)S(1)} %dynamic-slice_bitcast_fusion), channel_id=1, source_target_pairs={{8,0},{12,4},{0,8},{4,12},{9,1},{13,5},{1,9},{5,13},{10,2},{14,6},... | collective-permute-start | bytes 2764808 | tf_op jit(solution)/shard_map/ppermute | solution.py:38
  43.6 4.8 %collective-permute-done.1 = bf16[2,24,1,8,640]{4,1,3,2,0:T(8,128)(2,1)S(1)} collective-permute-done((bf16[2,24,1,8,640]{4,1,3,2,0:T(8,128)(2,1)}, bf16[2,24,1,8,640]{4,1,3,2,0:T(8,128)(2,1)S(1)}, u32[]{:S(2)}, u32[]{:S(2)}) %collective-permute-start.1) | collective-permute-done | bytes 491552 | tf_op jit(solution)/shard_map/ppermute | solution.py:17
  48.5 0.1 pad_maximum_fusion.6
  48.6 3.2 %collective-permute-start.2 = (bf16[2,24,6,1,640]{4,1,3,2,0:T(8,128)(2,1)S(1)}, bf16[2,24,6,1,640]{4,1,3,2,0:T(8,128)(2,1)S(1)}, u32[]{:S(2)}, u32[]{:S(2)}) collective-permute-start(bf16[2,24,6,1,640]{4,1,3,2,0:T(8,128)(2,1)S(1)} %get-tuple-element.7), channel_id=1, source_target_pairs={{0,1},{1,2},{2,3},{4,5},{5,6},{6,7},{8,9},{9,10},{10,11},{12,13},{... | collective-permute-start | bytes 1105928 | tf_op jit(solution)/shard_map/ppermute | solution.py:14
  51.8 1.3 collective-permute-start.3
  53.1 2.9 %constant_dynamic-update-slice_fusion.3 = bf16[3,3,640,640]{3,2,1,0:T(8,128)(2,1)} fusion(bf16[3,3,160,640]{3,2,1,0:T(8,128)(2,1)} %param.32), kind=kLoop, calls=%fused_computation.72 | loop fusion | bytes 3686400
  56.1 0.1 and_convert_fusion
  56.1 0.1 collective-permute-done.2
  56.3 4.4 %collective-permute-done.3 = bf16[2,24,6,1,640]{4,1,3,2,0:T(8,128)(2,1)S(1)} collective-permute-done((bf16[2,24,6,1,640]{4,1,3,2,0:T(8,128)(2,1)S(1)}, bf16[2,24,6,1,640]{4,1,3,2,0:T(8,128)(2,1)S(1)}, u32[]{:S(2)}, u32[]{:S(2)}) %collective-permute-start.3) | collective-permute-done | bytes 368672 | tf_op jit(solution)/shard_map/ppermute | solution.py:17
  60.6 2.9 %pad_maximum_fusion = bf16[2,24,6,10,640]{4,1,3,2,0:T(8,128)(2,1)} fusion(bf16[2,24,6,1,640]{4,1,3,2,0:T(8,128)(2,1)S(1)} %collective-permute-done.3, bf16[2,24,1,8,640]{4,1,3,2,0:T(8,128)(2,1)S(1)} %collective-permute-done.1, bf16[1,24,4,8,640]{4,1,3,2,0:T(8,128)(2,1)S(1)} %get-tuple-element.15, bf16[1,24,4,8,640]{4,1,3,2,0:T(8,128)(2,1)S(1)} %get-tuple-element.16, ...), kind=kLoop, calls=%fused_computation.8 | loop fusion | flops 9216000 | bytes 7372800 | tf_op jit(solution)/shard_map/concatenate | solution.py:18
  63.6 1.2 collective-permute-done.8
  64.9 2.2 %collective-permute-start.6 = (bf16[3,3,160,640]{3,2,1,0:T(8,128)(2,1)}, bf16[3,3,160,640]{3,2,1,0:T(8,128)(2,1)}, u32[]{:S(2)}, u32[]{:S(2)}) collective-permute-start(bf16[3,3,160,640]{3,2,1,0:T(8,128)(2,1)} %all-gather.3.cloned.1.call-done), channel_id=1, source_target_pairs={{0,4},{4,0},{8,12},{12,8},{1,5},{5,1},{9,13},{13,9},{2,6},{6,2},{1... | collective-permute-start | bytes 5529608 | tf_op jit(solution)/shard_map/ppermute | solution.py:41
  67.1 4.8 %fusion.34 = bf16[24,6,10,640]{3,0,2,1:T(8,128)(2,1)S(1)} fusion(bf16[2,24,6,10,640]{4,1,3,2,0:T(8,128)(2,1)} %pad_maximum_fusion, f32[6,10]{1,0:T(8,128)S(1)} %and_convert_fusion, f32[640]{0:T(1024)S(1)} %copy-done.15, f32[640]{0:T(1024)S(1)} %copy-done.16, f32[24,640]{1,0:T(8,128)S(1)} %mul.108, f32[24,640]{1,0:T(8,128)S(1)} %sub.59, s32[640]{0:T(1024)S(1)} %fusion.78), kind=kOutput, calls=%fused_computation.40 | convolution fusion | flops 1191116800 | bytes 3817200 | tf_op jit(solution)/shard_map/dot_general | solution.py:63
  71.9 2.4 %fusion.25 = f32[24,6,10,640]{3,0,2,1:T(8,128)} fusion(bf16[2,24,6,10,640]{4,1,3,2,0:T(8,128)(2,1)S(1)} %copy-done), kind=kLoop, calls=%fused_computation.30 | loop fusion | flops 921600 | bytes 5529600 | tf_op jit(solution)/shard_map/convert_element_type | solution.py:118
  74.4 4.5 %fusion.33 = bf16[24,6,10,640]{3,0,2,1:T(8,128)(2,1)} fusion(f32[640]{0:T(1024)S(1)} %copy-done.13, f32[640]{0:T(1024)S(1)} %copy-done.14, f32[24,640]{1,0:T(8,128)S(1)} %mul.120, f32[24,640]{1,0:T(8,128)S(1)} %copy-done.5, f32[6,10]{1,0:T(8,128)S(1)} %and_convert_fusion, s32[640]{0:T(1024)S(1)} %fusion.78, bf16[2,24,6,10,640]{4,1,3,2,0:T(8,128)(2,1)S(1)} %copy-done), kind=kOutput, calls=%fused_computation.39 | convolution fusion | flops 1190195200 | bytes 3825664 | tf_op jit(solution)/shard_map/dot_general | solution.py:63
  78.9 2.9 %constant_dynamic-update-slice_fusion.2 = bf16[3,3,640,640]{3,2,1,0:T(8,128)(2,1)} fusion(bf16[3,3,640,640]{3,2,1,0:T(8,128)(2,1)} %constant_dynamic-update-slice_fusion.3, bf16[3,3,160,640]{3,2,1,0:T(8,128)(2,1)} %collective-permute-done.7), kind=kLoop, calls=%fused_computation.71 | loop fusion | bytes 3686400
  81.8 15.2 %all-gather.5.cloned.1.call-done = bf16[3,3,160,640]{3,2,1,0:T(8,128)(2,1)} async-done(((bf16[3,3,80,640]{3,2,1,0:T(8,128)(2,1)}), bf16[3,3,160,640]{3,2,1,0:T(8,128)(2,1)}) %all-gather.5.cloned.1.call-update) | async-done | bytes 1843216 | tf_op jit(solution)/shard_map/all_gather | solution.py:40
  97.0 0.7 collective-permute-start.9
  97.7 2.9 %constant_dynamic-update-slice_fusion.1 = bf16[3,3,640,640]{3,2,1,0:T(8,128)(2,1)} fusion(bf16[3,3,640,640]{3,2,1,0:T(8,128)(2,1)} %constant_dynamic-update-slice_fusion.2, bf16[3,3,160,640]{3,2,1,0:T(8,128)(2,1)} %all-gather.5.cloned.1.call-done), kind=kLoop, calls=%fused_computation.70 | loop fusion | bytes 3686400
  100.6 13.4 %fusion.45 = bf16[24,6,10,640]{3,0,2,1:T(8,128)(2,1)} fusion(bf16[24,6,10,640]{3,0,2,1:T(8,128)(2,1)} %copy-done.3, f32[640]{0:T(1024)S(1)} %copy-done.15, f32[640]{0:T(1024)S(1)} %copy-done.16, f32[24,640]{1,0:T(8,128)S(1)} %mul.108, f32[24,640]{1,0:T(8,128)S(1)} %sub.59, f32[24,640]{1,0:T(8,128)S(1)} %copy-done.12, f32[640]{0:T(1024)S(1)} %copy-done.17, ...), kind=kOutput, calls=%fused_computation.45 | convolution fusion | flops 6327255040 | bytes 10393600 | tf_op jit(solution)/shard_map/dot_general | solution.py:63
  114.0 1.0 fusion.90
  115.1 1.4 constant_dynamic-update-slice_fusion
  116.5 2.5 %fusion.20 = f32[48,4,1,640]{3,0,2,1:T(8,128)S(1)} fusion(bf16[3,3,640,640]{3,2,1,0:T(8,128)(2,1)} %constant_dynamic-update-slice_fusion, bf16[24,6,1,640]{3,0,2,1:T(8,128)(2,1)S(1)} %get-tuple-element.13, bf16[24,6,1,640]{3,0,2,1:T(8,128)(2,1)S(1)} %get-tuple-element.11), kind=kOutput, calls=%fused_computation.23 | convolution fusion | flops 472596480 | bytes 3317760 | tf_op jit(solution)/shard_map/conv_general_dilated | solution.py:72
  119.1 2.6 %fusion.18 = f32[48,4,1,640]{3,0,2,1:T(8,128)S(1)} fusion(bf16[3,3,640,640]{3,2,1,0:T(8,128)(2,1)} %constant_dynamic-update-slice_fusion, bf16[24,6,1,640]{3,0,2,1:T(8,128)(2,1)S(1)} %get-tuple-element.14, bf16[24,6,1,640]{3,0,2,1:T(8,128)(2,1)S(1)} %get-tuple-element.12), kind=kOutput, calls=%fused_computation.21 | convolution fusion | flops 472596480 | bytes 3317760 | tf_op jit(solution)/shard_map/conv_general_dilated | solution.py:72
  121.8 0.1 copy-done.1
  121.8 0.6 copy-done.4
  122.4 10.3 %fusion.48 = bf16[24,4,8,640]{3,0,2,1:T(8,128)(2,1)S(1)} fusion(f32[24,6,10,640]{3,0,2,1:T(8,128)S(1)} %copy-done.1, f32[24,4,1,640]{3,0,2,1:T(8,128)S(1)} %slice_subtract_fusion, f32[24,4,1,640]{3,0,2,1:T(8,128)S(1)} %slice_subtract_fusion.1, bf16[24,6,10,640]{3,0,2,1:T(8,128)(2,1)S(1)} %copy-done.4, ...), kind=kOutput, calls=%fused_computation.46 | convolution fusion | flops 5665259520 | bytes 13642432 | tf_op jit(solution)/shard_map/conv_general_dilated | solution.py:72
  132.8 1.1 copy.43
  (53 shorter events, 0.3 us)
Async XLA Ops:
  6.5 4.4 %copy-start.2 = (bf16[24,4,8,640]{3,2,1,0:T(8,128)(2,1)S(1)}, bf16[24,4,8,640]{3,2,1,0:T(8,128)(2,1)}, u32[]{:S(2)}) copy-start(bf16[24,4,8,640]{3,2,1,0:T(8,128)(2,1)} %param.18) | copy-start | bytes 2949124
  6.5 58.3 %all-gather.3.cloned.1.call-start = ((), (), s32[]{:S(2)}) async-start(), calls=%async_computation | async-start | bytes 2764800 | tf_op jit(solution)/shard_map/all_gather | solution.py:40
  7.9 22.4 %collective-permute-start.5 = (bf16[3,3,80,640]{3,2,1,0:T(8,128)(2,1)S(1)}, bf16[3,3,80,640]{3,2,1,0:T(8,128)(2,1)}, u32[]{:S(2)}, u32[]{:S(2)}) collective-permute-start(bf16[3,3,80,640]{3,2,1,0:T(8,128)(2,1)S(1)} %dynamic-slice_bitcast_fusion.1), channel_id=1, source_target_pairs={{8,0},{12,4},{0,8},{4,12},{9,1},{13,5},{1,9},{5,13},{10,2},{14,6},... | collective-permute-start | bytes 2764808 | tf_op jit(solution)/shard_map/ppermute | solution.py:38
  10.0 90.6 %collective-permute-start.4 = (bf16[3,3,160,640]{3,2,1,0:T(8,128)(2,1)}, bf16[3,3,160,640]{3,2,1,0:T(8,128)(2,1)}, u32[]{:S(2)}, u32[]{:S(2)}) collective-permute-start(bf16[3,3,160,640]{3,2,1,0:T(8,128)(2,1)} %param.25), channel_id=1, source_target_pairs={{0,4},{4,0},{8,12},{12,8},{1,5},{5,1},{9,13},{13,9},{2,6},{6,2},{1... | collective-permute-start | bytes 5529608 | tf_op jit(solution)/shard_map/ppermute | solution.py:33
  12.8 25.3 %copy-start.6 = (f32[24,32]{1,0:T(8,128)S(1)}, f32[24,32]{1,0:T(8,128)}, u32[]{:S(2)}) copy-start(f32[24,32]{1,0:T(8,128)} %param.29) | copy-start | bytes 9220
  12.8 25.7 %copy-start.7 = (f32[24,32]{1,0:T(8,128)S(1)}, f32[24,32]{1,0:T(8,128)}, u32[]{:S(2)}) copy-start(f32[24,32]{1,0:T(8,128)} %param.28) | copy-start | bytes 9220
  30.3 8.6 %copy-start.8 = (f32[24,32]{1,0:T(8,128)S(1)}, f32[24,32]{1,0:T(8,128)}, u32[]{:S(2)}) copy-start(f32[24,32]{1,0:T(8,128)} %param.22) | copy-start | bytes 9220
  30.3 66.7 %all-gather.5.cloned.1.call-start = ((), (), s32[]{:S(2)}) async-start(), calls=%async_computation.1 | async-start | bytes 2764800 | tf_op jit(solution)/shard_map/all_gather | solution.py:40
  30.4 8.9 %copy-start.9 = (f32[24,32]{1,0:T(8,128)S(1)}, f32[24,32]{1,0:T(8,128)}, u32[]{:S(2)}) copy-start(f32[24,32]{1,0:T(8,128)} %param.21) | copy-start | bytes 9220
  31.4 8.9 %copy-start.10 = (s32[24,16]{0,1:T(8,128)S(1)}, s32[24,16]{0,1:T(8,128)}, u32[]{:S(2)}) copy-start(s32[24,16]{0,1:T(8,128)} %param.20) | copy-start | bytes 4612
  31.4 12.2 %collective-permute-start = (bf16[2,24,1,8,640]{4,1,3,2,0:T(8,128)(2,1)}, bf16[2,24,1,8,640]{4,1,3,2,0:T(8,128)(2,1)S(1)}, u32[]{:S(2)}, u32[]{:S(2)}) collective-permute-start(bf16[2,24,1,8,640]{4,1,3,2,0:T(8,128)(2,1)} %get-tuple-element.9), channel_id=1, source_target_pairs={{0,4},{4,8},{8,12},{1,5},{5,9},{9,13},{2,6},{6,10},{10,14},{3,7},{... | collective-permute-start | bytes 1474568 | tf_op jit(solution)/shard_map/ppermute | solution.py:14
  36.0 12.5 %collective-permute-start.1 = (bf16[2,24,1,8,640]{4,1,3,2,0:T(8,128)(2,1)}, bf16[2,24,1,8,640]{4,1,3,2,0:T(8,128)(2,1)S(1)}, u32[]{:S(2)}, u32[]{:S(2)}) collective-permute-start(bf16[2,24,1,8,640]{4,1,3,2,0:T(8,128)(2,1)} %get-tuple-element.10), channel_id=1, source_target_pairs={{4,0},{8,4},{12,8},{5,1},{9,5},{13,9},{6,2},{10,6},{14,10},{7,3},{... | collective-permute-start | bytes 1474568 | tf_op jit(solution)/shard_map/ppermute | solution.py:17
  38.0 40.9 %collective-permute-start.7 = (bf16[3,3,160,640]{3,2,1,0:T(8,128)(2,1)}, bf16[3,3,160,640]{3,2,1,0:T(8,128)(2,1)}, u32[]{:S(2)}, u32[]{:S(2)}) collective-permute-start(bf16[3,3,160,640]{3,2,1,0:T(8,128)(2,1)} %param.32), channel_id=1, source_target_pairs={{0,4},{4,0},{8,12},{12,8},{1,5},{5,1},{9,13},{13,9},{2,6},{6,2},{1... | collective-permute-start | bytes 5529608 | tf_op jit(solution)/shard_map/ppermute | solution.py:33
  41.8 23.1 %collective-permute-start.8 = (bf16[3,3,80,640]{3,2,1,0:T(8,128)(2,1)S(1)}, bf16[3,3,80,640]{3,2,1,0:T(8,128)(2,1)}, u32[]{:S(2)}, u32[]{:S(2)}) collective-permute-start(bf16[3,3,80,640]{3,2,1,0:T(8,128)(2,1)S(1)} %dynamic-slice_bitcast_fusion), channel_id=1, source_target_pairs={{8,0},{12,4},{0,8},{4,12},{9,1},{13,5},{1,9},{5,13},{10,2},{14,6},... | collective-permute-start | bytes 2764808 | tf_op jit(solution)/shard_map/ppermute | solution.py:38
  48.6 7.6 %collective-permute-start.2 = (bf16[2,24,6,1,640]{4,1,3,2,0:T(8,128)(2,1)S(1)}, bf16[2,24,6,1,640]{4,1,3,2,0:T(8,128)(2,1)S(1)}, u32[]{:S(2)}, u32[]{:S(2)}) collective-permute-start(bf16[2,24,6,1,640]{4,1,3,2,0:T(8,128)(2,1)S(1)} %get-tuple-element.7), channel_id=1, source_target_pairs={{0,1},{1,2},{2,3},{4,5},{5,6},{6,7},{8,9},{9,10},{10,11},{12,13},{... | collective-permute-start | bytes 1105928 | tf_op jit(solution)/shard_map/ppermute | solution.py:14
  51.8 8.8 %collective-permute-start.3 = (bf16[2,24,6,1,640]{4,1,3,2,0:T(8,128)(2,1)S(1)}, bf16[2,24,6,1,640]{4,1,3,2,0:T(8,128)(2,1)S(1)}, u32[]{:S(2)}, u32[]{:S(2)}) collective-permute-start(bf16[2,24,6,1,640]{4,1,3,2,0:T(8,128)(2,1)S(1)} %get-tuple-element.8), channel_id=1, source_target_pairs={{1,0},{2,1},{3,2},{5,4},{6,5},{7,6},{9,8},{10,9},{11,10},{13,12},{... | collective-permute-start | bytes 1105928 | tf_op jit(solution)/shard_map/ppermute | solution.py:17
  56.1 10.9 %copy-start.15 = (f32[640]{0:T(1024)S(1)}, f32[640]{0:T(1024)}, u32[]{:S(2)}) copy-start(f32[640]{0:T(1024)} %param.31) | copy-start | bytes 7684
  56.1 10.9 %copy-start.16 = (f32[640]{0:T(1024)S(1)}, f32[640]{0:T(1024)}, u32[]{:S(2)}) copy-start(f32[640]{0:T(1024)} %param.30) | copy-start | bytes 7684
  64.9 7.0 %copy-start = (bf16[2,24,6,10,640]{4,1,3,2,0:T(8,128)(2,1)S(1)}, bf16[2,24,6,10,640]{4,1,3,2,0:T(8,128)(2,1)}, u32[]{:S(2)}) copy-start(bf16[2,24,6,10,640]{4,1,3,2,0:T(8,128)(2,1)} %pad_maximum_fusion) | copy-start | bytes 11059204
  64.9 35.7 %collective-permute-start.6 = (bf16[3,3,160,640]{3,2,1,0:T(8,128)(2,1)}, bf16[3,3,160,640]{3,2,1,0:T(8,128)(2,1)}, u32[]{:S(2)}, u32[]{:S(2)}) collective-permute-start(bf16[3,3,160,640]{3,2,1,0:T(8,128)(2,1)} %all-gather.3.cloned.1.call-done), channel_id=1, source_target_pairs={{0,4},{4,0},{8,12},{12,8},{1,5},{5,1},{9,13},{13,9},{2,6},{6,2},{1... | collective-permute-start | bytes 5529608 | tf_op jit(solution)/shard_map/ppermute | solution.py:41
  71.8 2.5 %copy-start.3 = (bf16[24,6,10,640]{3,0,2,1:T(8,128)(2,1)}, bf16[24,6,10,640]{3,0,2,1:T(8,128)(2,1)S(1)}, u32[]{:S(2)}) copy-start(bf16[24,6,10,640]{3,0,2,1:T(8,128)(2,1)S(1)} %fusion.34) | copy-start | bytes 5529604
  71.9 2.5 %copy-start.5 = (f32[24,640]{1,0:T(8,128)S(1)}, f32[24,640]{1,0:T(8,128)}, u32[]{:S(2)}) copy-start(f32[24,640]{1,0:T(8,128)} %sub.68) | copy-start | bytes 184324
  71.9 2.5 %copy-start.13 = (f32[640]{0:T(1024)S(1)}, f32[640]{0:T(1024)}, u32[]{:S(2)}) copy-start(f32[640]{0:T(1024)} %param.24) | copy-start | bytes 7684
  71.9 2.4 %copy-start.14 = (f32[640]{0:T(1024)S(1)}, f32[640]{0:T(1024)}, u32[]{:S(2)}) copy-start(f32[640]{0:T(1024)} %param.23) | copy-start | bytes 7684
  81.8 18.8 %copy-start.12 = (f32[24,640]{1,0:T(8,128)S(1)}, f32[24,640]{1,0:T(8,128)}, u32[]{:S(2)}) copy-start(f32[24,640]{1,0:T(8,128)} %param.27) | copy-start | bytes 184324
  81.8 18.8 %copy-start.17 = (f32[640]{0:T(1024)S(1)}, f32[640]{0:T(1024)}, u32[]{:S(2)}) copy-start(f32[640]{0:T(1024)} %param.26) | copy-start | bytes 7684
  97.0 18.1 %collective-permute-start.9 = (bf16[3,3,160,640]{3,2,1,0:T(8,128)(2,1)}, bf16[3,3,160,640]{3,2,1,0:T(8,128)(2,1)S(1)}, u32[]{:S(2)}, u32[]{:S(2)}) collective-permute-start(bf16[3,3,160,640]{3,2,1,0:T(8,128)(2,1)} %all-gather.5.cloned.1.call-done), channel_id=1, source_target_pairs={{0,4},{4,0},{8,12},{12,8},{1,5},{5,1},{9,13},{13,9},{2,6},{6,2},{1... | collective-permute-start | bytes 5529608 | tf_op jit(solution)/shard_map/ppermute | solution.py:41
  116.5 5.3 %copy-start.11 = (bf16[24,4,8,640]{3,2,1,0:T(8,128)(2,1)S(1)}, bf16[24,4,8,640]{3,2,1,0:T(8,128)(2,1)}, u32[]{:S(2)}) copy-start(bf16[24,4,8,640]{3,2,1,0:T(8,128)(2,1)} %param.19) | copy-start | bytes 2949124
  119.1 2.8 %copy-start.1 = (f32[24,6,10,640]{3,0,2,1:T(8,128)S(1)}, f32[24,6,10,640]{3,0,2,1:T(8,128)}, u32[]{:S(2)}) copy-start(f32[24,6,10,640]{3,0,2,1:T(8,128)} %fusion.25) | copy-start | bytes 11059204
  119.1 3.3 %copy-start.4 = (bf16[24,6,10,640]{3,0,2,1:T(8,128)(2,1)S(1)}, bf16[24,6,10,640]{3,0,2,1:T(8,128)(2,1)}, u32[]{:S(2)}) copy-start(bf16[24,6,10,640]{3,0,2,1:T(8,128)(2,1)} %fusion.45) | copy-start | bytes 5529604
  119.1 3.3 %copy-start.18 = (f32[640]{0:T(1024)S(1)}, f32[640]{0:T(1024)}, u32[]{:S(2)}) copy-start(f32[640]{0:T(1024)} %param.33) | copy-start | bytes 7684
Sparse Core Ops, SparseCore 0:
  30.4 32.4 all-gather.2
  65.0 32.0 all-gather.4

commit v13 on v5

--- a/solution.py
+++ b/solution.py
@@ -156,21 +156,19 @@
 
     cached_act = to_relative((second_norm(margins_pad) * inside).astype(jnp.bfloat16), order)
     fresh_act = to_relative(second_norm(fresh_mid).astype(jnp.bfloat16), order)
-    blended = lax.dynamic_update_slice(cached_act, fresh_act, (0, 1, 1, 0))
-    second_sum = conv_valid(blended, second_whole)
-    fixes = jnp.zeros_like(second_sum)
-    for boundary in range(1, tiles_across):
-        edge_col = boundary * TILE
-        for out_col, in_col, tap in ((edge_col - 1, edge_col + 1, 2), (edge_col, edge_col, 0)):
-            pair = jnp.concatenate(
-                [cached_act[:, :, in_col : in_col + 1], blended[:, :, in_col : in_col + 1]]
-            )
-            moved = conv_valid(pair, second_whole[:, tap : tap + 1])
-            change = moved[:requests] - moved[requests:]
-            fixes = fixes + jnp.pad(
-                change, ((0, 0), (0, 0), (out_col, cols_dev - out_col - 1), (0, 0))
-            )
-    second_sum = second_sum + fixes
+    fresh_pad = jnp.pad(fresh_act, ((0, 0), (1, 1), (1, 1), (0, 0)))
+    edge = jnp.arange(TILE + 2, dtype=jnp.int32)
+    interior = ((edge >= 1) & (edge <= TILE))[:, None] & ((edge >= 1) & (edge <= TILE))[None, :]
+    interior = interior[None, :, :, None]
+    windows = []
+    for tile_across in range(tiles_across):
+        cut = slice(tile_across * TILE, tile_across * TILE + TILE + 2)
+        windows.append(jnp.where(interior, fresh_pad[:, :, cut], cached_act[:, :, cut]))
+    wide_sum = conv_valid(jnp.concatenate(windows, axis=2), second_whole)
+    stride = TILE + 2
+    second_sum = jnp.concatenate(
+        [wide_sum[:, :, t * stride : t * stride + TILE] for t in range(tiles_across)], axis=2
+    )
     renewed = (
         second_sum + conv2_bias + inputs_pad[:, 1 : 1 + rows_dev, 1 : 1 + cols_dev]
     ).astype(jnp.bfloat16)

time: 131 us -> 123 us (0.939)
  waiting for transfers between devices: 33.8 us -> 26.7 us
  matrix products: 33.8 us -> 28.8 us
  other arithmetic: 7.21 us -> 11.3 us
  starting transfers between devices: 23.8 us -> 21.3 us
  local copies, waits for them, and re-layouts: 31.7 us -> 33.6 us
    dot_general x3 -> x2, matrix products: 21.3 us -> 4.33 us  [to_relative(): moved = jnp.dot(activation, chooser, preferred_element_type=jnp.float32)]
    ppermute x2, waiting for transfers between devices: 17 us -> 0.38 us  [gather_weights(): other = lax.ppermute(fetched, 'groups', y_pairs)]
    conv_general_dilated x3 -> x2, matrix products: 12.6 us -> 24.5 us  [conv_valid(): lax.conv_general_dilated(activation, kernel, window_strides=(1, 1), paddi...]
    ppermute x2, waiting for transfers between devices: 0.01 us -> 10.6 us  [gather_weights(): fetched = lax.ppermute(mine, 'row', pairs)]
    ppermute x2, starting transfers between devices: 4.84 us -> 0.02 us  [gather_weights(): other_relayed = lax.ppermute(other, 'row', mate_pairs)]
    unnamed x46 -> x50, local copies, waits for them, and re-layouts: 19.5 us -> 23.1 us
    ppermute x2, starting transfers between devices: 3.77 us -> 6.45 us  [gather_weights(): relayed = lax.ppermute(fetched, 'row', mate_pairs)]
    ppermute x2, waiting for transfers between devices: 4.44 us -> 1.99 us  [padded_2(): lax.ppermute(lax.slice_in_dim(block, 0, width, axis=dim), axis, backward)]
  transfers between devices with their start and end apart: 14 -> 14, of which waited for: 5 -> 5; matrix products, arithmetic and copies ran while one was open for 43% -> 50% of each run, Pallas kernels for 0% -> 0%
where the time goes in v13:
time: 123 us; the launch traced here: 122 us
  local copies, waits for them, and re-layouts  33.6 us (27%)
  matrix products  28.8 us (23%)
  waiting for transfers between devices  26.7 us (22%)
  starting transfers between devices  21.3 us (17%)
  other arithmetic  11.3 us (9%)
    conv_general_dilated x2, matrix products, conv_valid(): lax.conv_general_dilated(activation, kernel, window_strides=(1, 1), paddi...  24.5 us
    unnamed x50, local copies, waits for them, and re-layouts  23.1 us
    ppermute x2, waiting for transfers between devices, padded_2(): lax.ppermute(lax.slice_in_dim(block, block.shape[dim] - width, None, axis...  13.7 us
    ppermute x2, waiting for transfers between devices, gather_weights(): fetched = lax.ppermute(mine, 'row', pairs)  10.6 us
    ppermute x2, starting transfers between devices, gather_weights(): relayed = lax.ppermute(fetched, 'row', mate_pairs)  6.45 us
    ppermute x2, starting transfers between devices, padded_2(): lax.ppermute(lax.slice_in_dim(block, block.shape[dim] - width, None, axis...  5.73 us
    dot_general x2, matrix products, to_relative(): moved = jnp.dot(activation, chooser, preferred_element_type=jnp.float32)  4.33 us
    ppermute x2, starting transfers between devices, padded_2(): lax.ppermute(lax.slice_in_dim(block, 0, width, axis=dim), axis, backward)  3.7 us
  transfers between devices with their start and end apart: 14, of which 5 were waited for; matrix products, arithmetic and copies ran while one was open for 50% of the time, Pallas kernels for 0%

profile of v13, /device:TPU:1, one launch (start us, length us, event | category | flops | bytes accessed | tf_op | source)
XLA Modules:
  0.0 122.2 jit_solution(5412565069082579385)
XLA Ops:
  0.1 2.2 %dynamic-slice_bitcast_fusion.1 = bf16[3,3,80,640]{3,2,1,0:T(8,128)(2,1)} fusion(bf16[3,3,2,80,640]{4,3,2,1,0:T(8,128)(2,1)} %bitcast.45, s32[]{:T(128)S(6)} %select_n.125), kind=kLoop, calls=%fused_computation.47 | loop fusion | bytes 1843204 | tf_op jit(solution)/shard_map/jit(dynamic_index_in_dim)/squeeze | solution.py:33
  2.2 2.7 %collective-permute-start.5 = (bf16[3,3,80,640]{3,2,1,0:T(8,128)(2,1)}, bf16[3,3,80,640]{3,2,1,0:T(8,128)(2,1)}, u32[]{:S(2)}, u32[]{:S(2)}) collective-permute-start(bf16[3,3,80,640]{3,2,1,0:T(8,128)(2,1)} %dynamic-slice_bitcast_fusion.1), channel_id=1, source_target_pairs={{8,0},{12,4},{0,8},{4,12},{9,1},{13,5},{1,9},{5,13},{10,2},{14,6},... | collective-permute-start | bytes 2764808 | tf_op jit(solution)/shard_map/ppermute | solution.py:39
  4.9 2.1 %copy_bitcast_fusion = (bf16[1,24,4,8,640]{4,1,3,2,0:T(8,128)(2,1)S(1)}, bf16[1,24,4,8,640]{4,1,3,2,0:T(8,128)(2,1)S(1)}) fusion(bf16[24,4,8,640]{3,2,1,0:T(8,128)(2,1)} %param.18, bf16[24,4,8,640]{3,2,1,0:T(8,128)(2,1)} %param.17), kind=kLoop, calls=%fused_computation.44 | loop fusion | bytes 3932160 | tf_op jit(solution)/shard_map/stack | solution.py:125
  7.1 0.9 pad_maximum_fusion.3
  8.0 1.9 %collective-permute-start = (bf16[2,24,1,8,640]{4,1,3,2,0:T(8,128)(2,1)}, bf16[2,24,1,8,640]{4,1,3,2,0:T(8,128)(2,1)S(1)}, u32[]{:S(2)}, u32[]{:S(2)}) collective-permute-start(bf16[2,24,1,8,640]{4,1,3,2,0:T(8,128)(2,1)} %get-tuple-element.13), channel_id=1, source_target_pairs={{0,4},{4,8},{8,12},{1,5},{5,9},{9,13},{2,6},{6,10},{10,14},{3,7},{... | collective-permute-start | bytes 1474568 | tf_op jit(solution)/shard_map/ppermute | solution.py:14
  9.9 2.4 %collective-permute-start.1 = (bf16[2,24,1,8,640]{4,1,3,2,0:T(8,128)(2,1)S(1)}, bf16[2,24,1,8,640]{4,1,3,2,0:T(8,128)(2,1)S(1)}, u32[]{:S(2)}, u32[]{:S(2)}) collective-permute-start(bf16[2,24,1,8,640]{4,1,3,2,0:T(8,128)(2,1)S(1)} %get-tuple-element.14), channel_id=1, source_target_pairs={{4,0},{8,4},{12,8},{5,1},{9,5},{13,9},{6,2},{10,6},{14,10},{7,3},{... | collective-permute-start | bytes 1474568 | tf_op jit(solution)/shard_map/ppermute | solution.py:17
  12.4 1.4 %constant_dynamic-update-slice_fusion.5 = bf16[3,3,640,640]{3,2,1,0:T(8,128)(2,1)} fusion(bf16[3,3,160,640]{3,2,1,0:T(8,128)(2,1)S(1)} %copy-done.2), kind=kLoop, calls=%fused_computation.62 | loop fusion | bytes 3686400
  14.0 2.9 %constant_dynamic-update-slice_fusion.11 = bf16[3,3,640,640]{3,2,1,0:T(8,128)(2,1)} fusion(bf16[3,3,160,640]{3,2,1,0:T(8,128)(2,1)} %param.32), kind=kLoop, calls=%fused_computation.68 | loop fusion | bytes 3686400
  17.0 13.7 %collective-permute-done = bf16[2,24,1,8,640]{4,1,3,2,0:T(8,128)(2,1)S(1)} collective-permute-done((bf16[2,24,1,8,640]{4,1,3,2,0:T(8,128)(2,1)}, bf16[2,24,1,8,640]{4,1,3,2,0:T(8,128)(2,1)S(1)}, u32[]{:S(2)}, u32[]{:S(2)}) %collective-permute-start) | collective-permute-done | bytes 491552 | tf_op jit(solution)/shard_map/ppermute | solution.py:14
  30.7 0.7 collective-permute-done.1
  31.5 1.0 pad_maximum_fusion.7
  32.5 3.8 %collective-permute-start.2 = (bf16[2,24,6,1,640]{4,1,3,2,0:T(8,128)(2,1)}, bf16[2,24,6,1,640]{4,1,3,2,0:T(8,128)(2,1)}, u32[]{:S(2)}, u32[]{:S(2)}) collective-permute-start(bf16[2,24,6,1,640]{4,1,3,2,0:T(8,128)(2,1)} %get-tuple-element.9), channel_id=1, source_target_pairs={{0,1},{1,2},{2,3},{4,5},{5,6},{6,7},{8,9},{9,10},{10,11},{12,13},{... | collective-permute-start | bytes 1105928 | tf_op jit(solution)/shard_map/ppermute | solution.py:14
  36.3 1.3 %collective-permute-start.3 = (bf16[2,24,6,1,640]{4,1,3,2,0:T(8,128)(2,1)}, bf16[2,24,6,1,640]{4,1,3,2,0:T(8,128)(2,1)}, u32[]{:S(2)}, u32[]{:S(2)}) collective-permute-start(bf16[2,24,6,1,640]{4,1,3,2,0:T(8,128)(2,1)} %get-tuple-element.10), channel_id=1, source_target_pairs={{1,0},{2,1},{3,2},{5,4},{6,5},{7,6},{9,8},{10,9},{11,10},{13,12},{... | collective-permute-start | bytes 1105928 | tf_op jit(solution)/shard_map/ppermute | solution.py:17
  37.6 0.5 compare_and_fusion
  38.3 0.2 mul.128
  38.7 0.2 sub.69
  39.1 0.2 mul.115
  39.5 0.9 sub.59
  40.3 0.7 and_convert_fusion
  41.0 1.3 %dynamic-slice_bitcast_fusion = bf16[3,3,80,640]{3,2,1,0:T(8,128)(2,1)S(1)} fusion(bf16[3,3,2,80,640]{4,3,2,1,0:T(8,128)(2,1)} %bitcast.10, s32[]{:T(128)S(6)} %select_n.125), kind=kLoop, calls=%fused_computation.46 | loop fusion | bytes 1843204 | tf_op jit(solution)/shard_map/jit(dynamic_index_in_dim)/squeeze | solution.py:33
  42.3 1.3 %collective-permute-start.6 = (bf16[3,3,80,640]{3,2,1,0:T(8,128)(2,1)}, bf16[3,3,80,640]{3,2,1,0:T(8,128)(2,1)S(1)}, u32[]{:S(2)}, u32[]{:S(2)}) collective-permute-start(bf16[3,3,80,640]{3,2,1,0:T(8,128)(2,1)} %collective-permute-done.5), channel_id=1, source_target_pairs={{0,16},{16,0},{1,17},{17,1},{2,18},{18,2},{3,19},{19,3},{4,20},{20... | collective-permute-start | bytes 2764808 | tf_op jit(solution)/shard_map/ppermute | solution.py:41
  43.6 1.3 %collective-permute-done.3 = bf16[2,24,6,1,640]{4,1,3,2,0:T(8,128)(2,1)} collective-permute-done((bf16[2,24,6,1,640]{4,1,3,2,0:T(8,128)(2,1)}, bf16[2,24,6,1,640]{4,1,3,2,0:T(8,128)(2,1)}, u32[]{:S(2)}, u32[]{:S(2)}) %collective-permute-start.3) | collective-permute-done | bytes 368672 | tf_op jit(solution)/shard_map/ppermute | solution.py:17
  44.9 3.0 %pad_maximum_fusion = bf16[2,24,6,10,640]{4,1,3,2,0:T(8,128)(2,1)S(1)} fusion(bf16[2,24,6,1,640]{4,1,3,2,0:T(8,128)(2,1)} %collective-permute-done.3, bf16[2,24,1,8,640]{4,1,3,2,0:T(8,128)(2,1)S(1)} %collective-permute-done.1, bf16[1,24,4,8,640]{4,1,3,2,0:T(8,128)(2,1)S(1)} %get-tuple-element.15, bf16[1,24,4,8,640]{4,1,3,2,0:T(8,128)(2,1)S(1)} %get-tuple-element.16, ...), kind=kLoop, calls=%fused_computation.1 | loop fusion | flops 9216000 | bytes 7372800 | tf_op jit(solution)/shard_map/concatenate | solution.py:18
  47.9 3.3 %fusion.13 = bf16[24,6,10,640]{3,0,2,1:T(8,128)(2,1)S(1)} fusion(bf16[2,24,6,10,640]{4,1,3,2,0:T(8,128)(2,1)S(1)} %pad_maximum_fusion, f32[640]{0:T(1024)S(1)} %copy-done.12, f32[640]{0:T(1024)S(1)} %copy-done.13, f32[24,640]{1,0:T(8,128)S(1)} %mul.128, f32[24,640]{1,0:T(8,128)S(1)} %sub.69, f32[6,10]{1,0:T(8,128)S(1)} %and_convert_fusion, s32[640]{0:T(1024)S(1)} %fusion.59), kind=kOutput, calls=%fused_computation.23 | convolution fusion | flops 1190195200 | bytes 3825664 | tf_op jit(solution)/shard_map/dot_general | solution.py:72
  51.2 3.6 %collective-permute-start.7 = (bf16[3,3,80,640]{3,2,1,0:T(8,128)(2,1)}, bf16[3,3,80,640]{3,2,1,0:T(8,128)(2,1)S(1)}, u32[]{:S(2)}, u32[]{:S(2)}) collective-permute-start(bf16[3,3,80,640]{3,2,1,0:T(8,128)(2,1)} %collective-permute-done.5), channel_id=1, source_target_pairs={{0,4},{4,0},{8,12},{12,8},{1,5},{5,1},{9,13},{13,9},{2,6},{6,2},{1... | collective-permute-start | bytes 2764808 | tf_op jit(solution)/shard_map/ppermute | solution.py:42
  54.9 0.4 collective-permute-done.6
  55.3 2.1 %fusion.15 = f32[24,6,10,640]{3,0,2,1:T(8,128)} fusion(bf16[2,24,6,10,640]{4,1,3,2,0:T(8,128)(2,1)S(1)} %pad_maximum_fusion), kind=kLoop, calls=%fused_computation.26 | loop fusion | flops 921600 | bytes 5529600 | tf_op jit(solution)/shard_map/convert_element_type | solution.py:127
  57.3 0.4 copy.58
  57.8 10.6 %collective-permute-done.10 = bf16[3,3,80,640]{3,2,1,0:T(8,128)(2,1)} collective-permute-done((bf16[3,3,80,640]{3,2,1,0:T(8,128)(2,1)S(1)}, bf16[3,3,80,640]{3,2,1,0:T(8,128)(2,1)}, u32[]{:S(2)}, u32[]{:S(2)}) %collective-permute-start.10) | collective-permute-done | bytes 921632 | tf_op jit(solution)/shard_map/ppermute | solution.py:39
  68.4 1.2 %collective-permute-start.11 = (bf16[3,3,80,640]{3,2,1,0:T(8,128)(2,1)}, bf16[3,3,80,640]{3,2,1,0:T(8,128)(2,1)}, u32[]{:S(2)}, u32[]{:S(2)}) collective-permute-start(bf16[3,3,80,640]{3,2,1,0:T(8,128)(2,1)} %collective-permute-done.10), channel_id=1, source_target_pairs={{0,16},{16,0},{1,17},{17,1},{2,18},{18,2},{3,19},{19,3},{4,20},{20... | collective-permute-start | bytes 2764808 | tf_op jit(solution)/shard_map/ppermute | solution.py:41
  69.6 2.8 %collective-permute-start.12 = (bf16[3,3,80,640]{3,2,1,0:T(8,128)(2,1)}, bf16[3,3,80,640]{3,2,1,0:T(8,128)(2,1)}, u32[]{:S(2)}, u32[]{:S(2)}) collective-permute-start(bf16[3,3,80,640]{3,2,1,0:T(8,128)(2,1)} %collective-permute-done.10), channel_id=1, source_target_pairs={{0,4},{4,0},{8,12},{12,8},{1,5},{5,1},{9,13},{13,9},{2,6},{6,2},{1... | collective-permute-start | bytes 2764808 | tf_op jit(solution)/shard_map/ppermute | solution.py:42
  72.4 2.9 %constant_dynamic-update-slice_fusion.4 = bf16[3,3,640,640]{3,2,1,0:T(8,128)(2,1)} fusion(bf16[3,3,640,640]{3,2,1,0:T(8,128)(2,1)} %constant_dynamic-update-slice_fusion.5, bf16[3,3,160,640]{3,2,1,0:T(8,128)(2,1)} %collective-permute-done.4), kind=kLoop, calls=%fused_computation.61 | loop fusion | bytes 3686400
  75.3 2.2 %constant_dynamic-update-slice_fusion.3 = bf16[3,3,640,640]{3,2,1,0:T(8,128)(2,1)} fusion(bf16[3,3,640,640]{3,2,1,0:T(8,128)(2,1)} %constant_dynamic-update-slice_fusion.4, bf16[3,3,80,640]{3,2,1,0:T(8,128)(2,1)} %collective-permute-done.5), kind=kLoop, calls=%fused_computation.60 | loop fusion | bytes 1843200
  77.5 1.0 constant_dynamic-update-slice_fusion.2
  78.6 2.9 %constant_dynamic-update-slice_fusion.10 = bf16[3,3,640,640]{3,2,1,0:T(8,128)(2,1)} fusion(bf16[3,3,640,640]{3,2,1,0:T(8,128)(2,1)} %constant_dynamic-update-slice_fusion.11, bf16[3,3,160,640]{3,2,1,0:T(8,128)(2,1)} %collective-permute-done.9), kind=kLoop, calls=%fused_computation.67 | loop fusion | bytes 3686400
  81.5 2.3 %constant_dynamic-update-slice_fusion.9 = bf16[3,3,640,640]{3,2,1,0:T(8,128)(2,1)} fusion(bf16[3,3,640,640]{3,2,1,0:T(8,128)(2,1)} %constant_dynamic-update-slice_fusion.10, bf16[3,3,80,640]{3,2,1,0:T(8,128)(2,1)} %collective-permute-done.10), kind=kLoop, calls=%fused_computation.66 | loop fusion | bytes 1843200
  83.8 1.0 constant_dynamic-update-slice_fusion.1
  84.8 1.0 constant_dynamic-update-slice_fusion
  85.8 15.2 %multiply_convert_fusion.1 = bf16[24,4,8,640]{3,0,2,1:T(8,128)(2,1)} fusion(bf16[3,3,640,640]{3,2,1,0:T(8,128)(2,1)} %constant_dynamic-update-slice_fusion, f32[640]{0:T(1024)S(1)} %copy-done.12, f32[640]{0:T(1024)S(1)} %copy-done.13, f32[24,640]{1,0:T(8,128)S(1)} %mul.128, f32[24,640]{1,0:T(8,128)S(1)} %sub.69, f32[24,640]{1,0:T(8,128)S(1)} %copy-done.11, ...), kind=kOutput, calls=%fused_computation.22 | convolution fusion | flops 6858833920 | bytes 10521840 | tf_op jit(solution)/shard_map/conv_general_dilated | solution.py:81
  101.1 2.3 %constant_dynamic-update-slice_fusion.8 = bf16[3,3,640,640]{3,2,1,0:T(8,128)(2,1)} fusion(bf16[3,3,640,640]{3,2,1,0:T(8,128)(2,1)} %constant_dynamic-update-slice_fusion.9, bf16[3,3,80,640]{3,2,1,0:T(8,128)(2,1)} %collective-permute-done.11), kind=kLoop, calls=%fused_computation.65 | loop fusion | bytes 1843200
  103.3 2.2 %constant_dynamic-update-slice_fusion.7 = bf16[3,3,640,640]{3,2,1,0:T(8,128)(2,1)} fusion(bf16[3,3,640,640]{3,2,1,0:T(8,128)(2,1)} %constant_dynamic-update-slice_fusion.8, bf16[3,3,80,640]{3,2,1,0:T(8,128)(2,1)} %collective-permute-done.12), kind=kLoop, calls=%fused_computation.64 | loop fusion | bytes 1843200
  105.5 1.0 fusion.32
  106.6 1.2 fusion.30
  107.8 1.1 pad_maximum_fusion.1
  109.1 9.3 %fusion.10 = f32[24,4,10,640]{3,0,2,1:T(8,128)S(1)} fusion(bf16[3,3,640,640]{3,2,1,0:T(8,128)(2,1)S(1)} %constant_dynamic-update-slice_fusion.6, bf16[24,6,12,640]{3,2,1,0:T(8,128)(2,1)S(1)} %pad_maximum_fusion.1), kind=kOutput, calls=%fused_computation.17 | convolution fusion | flops 7077888000 | bytes 12042240 | tf_op jit(solution)/shard_map/conv_general_dilated | solution.py:81
  118.6 1.8 %copy-done = f32[24,6,10,640]{3,0,2,1:T(8,128)S(1)} copy-done((f32[24,6,10,640]{3,0,2,1:T(8,128)S(1)}, f32[24,6,10,640]{3,0,2,1:T(8,128)}, u32[]{:S(2)}) %copy-start) | copy-done | bytes 3686424
  120.4 0.7 fusion.37
  121.1 1.1 copy.46
  (67 shorter events, 1.5 us)
Async XLA Ops:
  0.0 69.6 %collective-permute-start.4 = (bf16[3,3,160,640]{3,2,1,0:T(8,128)(2,1)}, bf16[3,3,160,640]{3,2,1,0:T(8,128)(2,1)}, u32[]{:S(2)}, u32[]{:S(2)}) collective-permute-start(bf16[3,3,160,640]{3,2,1,0:T(8,128)(2,1)} %param.25), channel_id=1, source_target_pairs={{0,4},{4,0},{8,12},{12,8},{1,5},{5,1},{9,13},{13,9},{2,6},{6,2},{1... | collective-permute-start | bytes 5529608 | tf_op jit(solution)/shard_map/ppermute | solution.py:34
  2.2 10.2 %copy-start.2 = (bf16[3,3,160,640]{3,2,1,0:T(8,128)(2,1)S(1)}, bf16[3,3,160,640]{3,2,1,0:T(8,128)(2,1)}, u32[]{:S(2)}) copy-start(bf16[3,3,160,640]{3,2,1,0:T(8,128)(2,1)} %param.25) | copy-start | bytes 5529604
  2.2 40.0 %collective-permute-start.5 = (bf16[3,3,80,640]{3,2,1,0:T(8,128)(2,1)}, bf16[3,3,80,640]{3,2,1,0:T(8,128)(2,1)}, u32[]{:S(2)}, u32[]{:S(2)}) collective-permute-start(bf16[3,3,80,640]{3,2,1,0:T(8,128)(2,1)} %dynamic-slice_bitcast_fusion.1), channel_id=1, source_target_pairs={{8,0},{12,4},{0,8},{4,12},{9,1},{13,5},{1,9},{5,13},{10,2},{14,6},... | collective-permute-start | bytes 2764808 | tf_op jit(solution)/shard_map/ppermute | solution.py:39
  7.1 6.8 %copy-start.9 = (s32[24,16]{0,1:T(8,128)S(1)}, s32[24,16]{0,1:T(8,128)}, u32[]{:S(2)}) copy-start(s32[24,16]{0,1:T(8,128)} %param.20) | copy-start | bytes 4612
  8.0 22.8 %collective-permute-start = (bf16[2,24,1,8,640]{4,1,3,2,0:T(8,128)(2,1)}, bf16[2,24,1,8,640]{4,1,3,2,0:T(8,128)(2,1)S(1)}, u32[]{:S(2)}, u32[]{:S(2)}) collective-permute-start(bf16[2,24,1,8,640]{4,1,3,2,0:T(8,128)(2,1)} %get-tuple-element.13), channel_id=1, source_target_pairs={{0,4},{4,8},{8,12},{1,5},{5,9},{9,13},{2,6},{6,10},{10,14},{3,7},{... | collective-permute-start | bytes 1474568 | tf_op jit(solution)/shard_map/ppermute | solution.py:14
  9.9 21.6 %collective-permute-start.1 = (bf16[2,24,1,8,640]{4,1,3,2,0:T(8,128)(2,1)S(1)}, bf16[2,24,1,8,640]{4,1,3,2,0:T(8,128)(2,1)S(1)}, u32[]{:S(2)}, u32[]{:S(2)}) collective-permute-start(bf16[2,24,1,8,640]{4,1,3,2,0:T(8,128)(2,1)S(1)} %get-tuple-element.14), channel_id=1, source_target_pairs={{4,0},{8,4},{12,8},{5,1},{9,5},{13,9},{6,2},{10,6},{14,10},{7,3},{... | collective-permute-start | bytes 1474568 | tf_op jit(solution)/shard_map/ppermute | solution.py:17
  12.3 66.3 %collective-permute-start.9 = (bf16[3,3,160,640]{3,2,1,0:T(8,128)(2,1)}, bf16[3,3,160,640]{3,2,1,0:T(8,128)(2,1)}, u32[]{:S(2)}, u32[]{:S(2)}) collective-permute-start(bf16[3,3,160,640]{3,2,1,0:T(8,128)(2,1)} %param.32), channel_id=1, source_target_pairs={{0,4},{4,0},{8,12},{12,8},{1,5},{5,1},{9,13},{13,9},{2,6},{6,2},{1... | collective-permute-start | bytes 5529608 | tf_op jit(solution)/shard_map/ppermute | solution.py:34
  14.0 24.2 %copy-start.5 = (f32[24,32]{1,0:T(8,128)S(1)}, f32[24,32]{1,0:T(8,128)}, u32[]{:S(2)}) copy-start(f32[24,32]{1,0:T(8,128)} %param.29) | copy-start | bytes 9220
  14.0 24.5 %copy-start.6 = (f32[24,32]{1,0:T(8,128)S(1)}, f32[24,32]{1,0:T(8,128)}, u32[]{:S(2)}) copy-start(f32[24,32]{1,0:T(8,128)} %param.28) | copy-start | bytes 9220
  14.0 24.9 %copy-start.7 = (f32[24,32]{1,0:T(8,128)S(1)}, f32[24,32]{1,0:T(8,128)}, u32[]{:S(2)}) copy-start(f32[24,32]{1,0:T(8,128)} %param.22) | copy-start | bytes 9220
  16.9 22.4 %copy-start.8 = (f32[24,32]{1,0:T(8,128)S(1)}, f32[24,32]{1,0:T(8,128)}, u32[]{:S(2)}) copy-start(f32[24,32]{1,0:T(8,128)} %param.21) | copy-start | bytes 9220
  32.5 11.1 %collective-permute-start.2 = (bf16[2,24,6,1,640]{4,1,3,2,0:T(8,128)(2,1)}, bf16[2,24,6,1,640]{4,1,3,2,0:T(8,128)(2,1)}, u32[]{:S(2)}, u32[]{:S(2)}) collective-permute-start(bf16[2,24,6,1,640]{4,1,3,2,0:T(8,128)(2,1)} %get-tuple-element.9), channel_id=1, source_target_pairs={{0,1},{1,2},{2,3},{4,5},{5,6},{6,7},{8,9},{9,10},{10,11},{12,13},{... | collective-permute-start | bytes 1105928 | tf_op jit(solution)/shard_map/ppermute | solution.py:14
  36.3 8.6 %collective-permute-start.3 = (bf16[2,24,6,1,640]{4,1,3,2,0:T(8,128)(2,1)}, bf16[2,24,6,1,640]{4,1,3,2,0:T(8,128)(2,1)}, u32[]{:S(2)}, u32[]{:S(2)}) collective-permute-start(bf16[2,24,6,1,640]{4,1,3,2,0:T(8,128)(2,1)} %get-tuple-element.10), channel_id=1, source_target_pairs={{1,0},{2,1},{3,2},{5,4},{6,5},{7,6},{9,8},{10,9},{11,10},{13,12},{... | collective-permute-start | bytes 1105928 | tf_op jit(solution)/shard_map/ppermute | solution.py:17
  42.3 5.7 %copy-start.12 = (f32[640]{0:T(1024)S(1)}, f32[640]{0:T(1024)}, u32[]{:S(2)}) copy-start(f32[640]{0:T(1024)} %param.31) | copy-start | bytes 7684
  42.3 5.7 %copy-start.13 = (f32[640]{0:T(1024)S(1)}, f32[640]{0:T(1024)}, u32[]{:S(2)}) copy-start(f32[640]{0:T(1024)} %param.30) | copy-start | bytes 7684
  42.3 13.0 %collective-permute-start.6 = (bf16[3,3,80,640]{3,2,1,0:T(8,128)(2,1)}, bf16[3,3,80,640]{3,2,1,0:T(8,128)(2,1)S(1)}, u32[]{:S(2)}, u32[]{:S(2)}) collective-permute-start(bf16[3,3,80,640]{3,2,1,0:T(8,128)(2,1)} %collective-permute-done.5), channel_id=1, source_target_pairs={{0,16},{16,0},{1,17},{17,1},{2,18},{18,2},{3,19},{19,3},{4,20},{20... | collective-permute-start | bytes 2764808 | tf_op jit(solution)/shard_map/ppermute | solution.py:41
  47.8 7.4 %copy-start.1 = (bf16[2,24,6,10,640]{4,1,3,2,0:T(8,128)(2,1)}, bf16[2,24,6,10,640]{4,1,3,2,0:T(8,128)(2,1)S(1)}, u32[]{:S(2)}) copy-start(bf16[2,24,6,10,640]{4,1,3,2,0:T(8,128)(2,1)S(1)} %pad_maximum_fusion) | copy-start | bytes 11059204
  47.8 20.5 %collective-permute-start.10 = (bf16[3,3,80,640]{3,2,1,0:T(8,128)(2,1)S(1)}, bf16[3,3,80,640]{3,2,1,0:T(8,128)(2,1)}, u32[]{:S(2)}, u32[]{:S(2)}) collective-permute-start(bf16[3,3,80,640]{3,2,1,0:T(8,128)(2,1)S(1)} %dynamic-slice_bitcast_fusion), channel_id=1, source_target_pairs={{8,0},{12,4},{0,8},{4,12},{9,1},{13,5},{1,9},{5,13},{10,2},{14,6},... | collective-permute-start | bytes 2764808 | tf_op jit(solution)/shard_map/ppermute | solution.py:39
  51.2 32.5 %collective-permute-start.7 = (bf16[3,3,80,640]{3,2,1,0:T(8,128)(2,1)}, bf16[3,3,80,640]{3,2,1,0:T(8,128)(2,1)S(1)}, u32[]{:S(2)}, u32[]{:S(2)}) collective-permute-start(bf16[3,3,80,640]{3,2,1,0:T(8,128)(2,1)} %collective-permute-done.5), channel_id=1, source_target_pairs={{0,4},{4,0},{8,12},{12,8},{1,5},{5,1},{9,13},{13,9},{2,6},{6,2},{1... | collective-permute-start | bytes 2764808 | tf_op jit(solution)/shard_map/ppermute | solution.py:42
  55.3 29.5 %collective-permute-start.8 = (bf16[3,3,80,640]{3,2,1,0:T(8,128)(2,1)S(1)}, bf16[3,3,80,640]{3,2,1,0:T(8,128)(2,1)S(1)}, u32[]{:S(2)}, u32[]{:S(2)}) collective-permute-start(bf16[3,3,80,640]{3,2,1,0:T(8,128)(2,1)S(1)} %collective-permute-done.6), channel_id=1, source_target_pairs={{0,4},{4,0},{8,12},{12,8},{1,5},{5,1},{9,13},{13,9},{2,6},{6,2},{1... | collective-permute-start | bytes 2764808 | tf_op jit(solution)/shard_map/ppermute | solution.py:43
  68.4 32.7 %collective-permute-start.11 = (bf16[3,3,80,640]{3,2,1,0:T(8,128)(2,1)}, bf16[3,3,80,640]{3,2,1,0:T(8,128)(2,1)}, u32[]{:S(2)}, u32[]{:S(2)}) collective-permute-start(bf16[3,3,80,640]{3,2,1,0:T(8,128)(2,1)} %collective-permute-done.10), channel_id=1, source_target_pairs={{0,16},{16,0},{1,17},{17,1},{2,18},{18,2},{3,19},{19,3},{4,20},{20... | collective-permute-start | bytes 2764808 | tf_op jit(solution)/shard_map/ppermute | solution.py:41
  69.6 33.7 %collective-permute-start.12 = (bf16[3,3,80,640]{3,2,1,0:T(8,128)(2,1)}, bf16[3,3,80,640]{3,2,1,0:T(8,128)(2,1)}, u32[]{:S(2)}, u32[]{:S(2)}) collective-permute-start(bf16[3,3,80,640]{3,2,1,0:T(8,128)(2,1)} %collective-permute-done.10), channel_id=1, source_target_pairs={{0,4},{4,0},{8,12},{12,8},{1,5},{5,1},{9,13},{13,9},{2,6},{6,2},{1... | collective-permute-start | bytes 2764808 | tf_op jit(solution)/shard_map/ppermute | solution.py:42
  81.5 4.3 %copy-start.4 = (f32[24,640]{1,0:T(8,128)S(1)}, f32[24,640]{1,0:T(8,128)}, u32[]{:S(2)}) copy-start(f32[24,640]{1,0:T(8,128)} %sub.59) | copy-start | bytes 184324
  81.5 4.3 %copy-start.11 = (f32[24,640]{1,0:T(8,128)S(1)}, f32[24,640]{1,0:T(8,128)}, u32[]{:S(2)}) copy-start(f32[24,640]{1,0:T(8,128)} %param.27) | copy-start | bytes 184324
  81.5 4.3 %copy-start.14 = (f32[640]{0:T(1024)S(1)}, f32[640]{0:T(1024)}, u32[]{:S(2)}) copy-start(f32[640]{0:T(1024)} %param.26) | copy-start | bytes 7684
  81.5 4.3 %copy-start.15 = (f32[640]{0:T(1024)S(1)}, f32[640]{0:T(1024)}, u32[]{:S(2)}) copy-start(f32[640]{0:T(1024)} %param.24) | copy-start | bytes 7684
  81.5 4.3 %copy-start.16 = (f32[640]{0:T(1024)S(1)}, f32[640]{0:T(1024)}, u32[]{:S(2)}) copy-start(f32[640]{0:T(1024)} %param.23) | copy-start | bytes 7684
  101.0 4.5 %copy-start.17 = (bf16[24,4,8,640]{3,0,2,1:T(8,128)(2,1)S(1)}, bf16[24,4,8,640]{3,0,2,1:T(8,128)(2,1)}, u32[]{:S(2)}) copy-start(bf16[24,4,8,640]{3,0,2,1:T(8,128)(2,1)} %multiply_convert_fusion.1) | copy-start | bytes 2949124
  101.0 7.9 %collective-permute-start.13 = (bf16[3,3,80,640]{3,2,1,0:T(8,128)(2,1)}, bf16[3,3,80,640]{3,2,1,0:T(8,128)(2,1)S(1)}, u32[]{:S(2)}, u32[]{:S(2)}) collective-permute-start(bf16[3,3,80,640]{3,2,1,0:T(8,128)(2,1)} %collective-permute-done.11), channel_id=1, source_target_pairs={{0,4},{4,0},{8,12},{12,8},{1,5},{5,1},{9,13},{13,9},{2,6},{6,2},{1... | collective-permute-start | bytes 2764808 | tf_op jit(solution)/shard_map/ppermute | solution.py:43
  105.5 3.4 %slice-start = ((s8[7372800]{0:T(1024)(128)(4,1)}), s8[4194304]{0:T(1024)(128)(4,1)S(1)}, s32[]{:S(2)}) async-start(s8[7372800]{0:T(1024)(128)(4,1)} %bitcast.46), calls=%async_computation | async-start | bytes 8388608
  106.6 2.4 %slice-start.1 = ((s8[7372800]{0:T(1024)(128)(4,1)}), s8[3178496]{0:T(1024)(128)(4,1)S(1)}, s32[]{:S(2)}) async-start(s8[7372800]{0:T(1024)(128)(4,1)} %bitcast.46), calls=%async_computation.1 | async-start | bytes 6356992
  109.1 9.5 %copy-start.3 = (bf16[24,4,8,640]{3,2,1,0:T(8,128)(2,1)S(1)}, bf16[24,4,8,640]{3,2,1,0:T(8,128)(2,1)}, u32[]{:S(2)}) copy-start(bf16[24,4,8,640]{3,2,1,0:T(8,128)(2,1)} %param.19) | copy-start | bytes 2949124
  118.4 2.0 %copy-start = (f32[24,6,10,640]{3,0,2,1:T(8,128)S(1)}, f32[24,6,10,640]{3,0,2,1:T(8,128)}, u32[]{:S(2)}) copy-start(f32[24,6,10,640]{3,0,2,1:T(8,128)} %fusion.15) | copy-start | bytes 11059204
  118.4 2.0 %copy-start.10 = (f32[640]{0:T(1024)S(1)}, f32[640]{0:T(1024)}, u32[]{:S(2)}) copy-start(f32[640]{0:T(1024)} %param.33) | copy-start | bytes 7684

commit v14 on v13

--- a/solution.py
+++ b/solution.py
@@ -45,7 +45,7 @@
                 jnp.concatenate([fetched, other], axis=2),
                 jnp.concatenate([relayed, other_relayed], axis=2),
             ]
-        wholes.append(jnp.concatenate(held, axis=2))
+        wholes.append(held)
     return wholes
 
 
@@ -116,7 +116,10 @@
     groups_total = norm1_mean.shape[1]
     per_group = channels // groups_total
 
-    first_whole, second_whole = gather_weights([conv1_weight, conv2_weight])
+    first_held, second_held = gather_weights([conv1_weight, conv2_weight])
+    first_whole = jnp.concatenate(first_held, axis=2)
+    second_local = jnp.concatenate(second_held[:2], axis=2)
+    second_remote = jnp.concatenate(second_held[2:], axis=2)
     order = relative_order(channels)
 
     def expand(values):
@@ -164,7 +167,11 @@
     for tile_across in range(tiles_across):
         cut = slice(tile_across * TILE, tile_across * TILE + TILE + 2)
         windows.append(jnp.where(interior, fresh_pad[:, :, cut], cached_act[:, :, cut]))
-    wide_sum = conv_valid(jnp.concatenate(windows, axis=2), second_whole)
+    wide = jnp.concatenate(windows, axis=2)
+    split = second_local.shape[2]
+    wide_sum = conv_valid(wide[..., :split], second_local) + conv_valid(
+        wide[..., split:], second_remote
+    )
     stride = TILE + 2
     second_sum = jnp.concatenate(
         [wide_sum[:, :, t * stride : t * stride + TILE] for t in range(tiles_across)], axis=2

time: 123 us -> 120 us (0.976)
  local copies, waits for them, and re-layouts: 33.6 us -> 22.4 us
  matrix products: 28.8 us -> 35 us
    unnamed x50 -> x37, local copies, waits for them, and re-layouts: 23.1 us -> 12 us
    conv_general_dilated x2 -> x3, matrix products: 24.5 us -> 29.4 us  [conv_valid(): lax.conv_general_dilated(activation, kernel, window_strides=(1, 1), paddi...]
    ppermute x2, waiting for transfers between devices: 13.7 us -> 15.1 us  [padded_2(): lax.ppermute(lax.slice_in_dim(block, block.shape[dim] - width, None, axis...]
  transfers between devices with their start and end apart: 14 -> 14, of which waited for: 5 -> 4; matrix products, arithmetic and copies ran while one was open for 50% -> 49% of each run, Pallas kernels for 0% -> 0%
where the time goes in v14:
time: 120 us; the launch traced here: 119 us
  matrix products  35 us (29%)
  waiting for transfers between devices  27.9 us (23%)
  local copies, waits for them, and re-layouts  22.4 us (19%)
  starting transfers between devices  21.5 us (18%)
  other arithmetic  12.3 us (10%)
    conv_general_dilated x3, matrix products, conv_valid(): lax.conv_general_dilated(activation, kernel, window_strides=(1, 1), paddi...  29.4 us
    ppermute x2, waiting for transfers between devices, padded_2(): lax.ppermute(lax.slice_in_dim(block, block.shape[dim] - width, None, axis...  15.1 us
    unnamed x37, local copies, waits for them, and re-layouts  12 us
    ppermute x2, waiting for transfers between devices, gather_weights(): fetched = lax.ppermute(mine, 'row', pairs)  10.8 us
    ppermute x2, starting transfers between devices, gather_weights(): relayed = lax.ppermute(fetched, 'row', mate_pairs)  6.4 us
    ppermute x2, starting transfers between devices, padded_2(): lax.ppermute(lax.slice_in_dim(block, block.shape[dim] - width, None, axis...  5.86 us
    dot_general x2, matrix products, to_relative(): moved = jnp.dot(activation, chooser, preferred_element_type=jnp.float32)  5.53 us
    ppermute x2, starting transfers between devices, padded_2(): lax.ppermute(lax.slice_in_dim(block, 0, width, axis=dim), axis, backward)  3.71 us
  transfers between devices with their start and end apart: 14, of which 4 were waited for; matrix products, arithmetic and copies ran while one was open for 49% of the time, Pallas kernels for 0%

profile of v14, /device:TPU:1, one launch (start us, length us, event | category | flops | bytes accessed | tf_op | source)
XLA Modules:
  0.0 119.5 jit_solution(16075296964853750164)
XLA Ops:
  0.1 2.2 %dynamic-slice_bitcast_fusion.1 = bf16[3,3,80,640]{3,2,1,0:T(8,128)(2,1)} fusion(bf16[3,3,2,80,640]{4,3,2,1,0:T(8,128)(2,1)} %bitcast.44, s32[]{:T(128)S(6)} %select_n.125), kind=kLoop, calls=%fused_computation.63 | loop fusion | bytes 1843204 | tf_op jit(solution)/shard_map/jit(dynamic_index_in_dim)/squeeze | solution.py:33
  2.2 2.7 %collective-permute-start.5 = (bf16[3,3,80,640]{3,2,1,0:T(8,128)(2,1)}, bf16[3,3,80,640]{3,2,1,0:T(8,128)(2,1)}, u32[]{:S(2)}, u32[]{:S(2)}) collective-permute-start(bf16[3,3,80,640]{3,2,1,0:T(8,128)(2,1)} %dynamic-slice_bitcast_fusion.1), channel_id=1, source_target_pairs={{8,0},{12,4},{0,8},{4,12},{9,1},{13,5},{1,9},{5,13},{10,2},{14,6},... | collective-permute-start | bytes 2764808 | tf_op jit(solution)/shard_map/ppermute | solution.py:39
  4.9 2.1 %copy_bitcast_fusion = (bf16[1,24,4,8,640]{4,1,3,2,0:T(8,128)(2,1)S(1)}, bf16[1,24,4,8,640]{4,1,3,2,0:T(8,128)(2,1)S(1)}) fusion(bf16[24,4,8,640]{3,2,1,0:T(8,128)(2,1)} %param.18, bf16[24,4,8,640]{3,2,1,0:T(8,128)(2,1)} %param.17), kind=kLoop, calls=%fused_computation.60 | loop fusion | bytes 3932160 | tf_op jit(solution)/shard_map/stack | solution.py:128
  7.1 0.9 pad_maximum_fusion.3
  8.0 1.9 %collective-permute-start = (bf16[2,24,1,8,640]{4,1,3,2,0:T(8,128)(2,1)}, bf16[2,24,1,8,640]{4,1,3,2,0:T(8,128)(2,1)S(1)}, u32[]{:S(2)}, u32[]{:S(2)}) collective-permute-start(bf16[2,24,1,8,640]{4,1,3,2,0:T(8,128)(2,1)} %get-tuple-element.15), channel_id=1, source_target_pairs={{0,4},{4,8},{8,12},{1,5},{5,9},{9,13},{2,6},{6,10},{10,14},{3,7},{... | collective-permute-start | bytes 1474568 | tf_op jit(solution)/shard_map/ppermute | solution.py:14
  9.9 2.4 %collective-permute-start.1 = (bf16[2,24,1,8,640]{4,1,3,2,0:T(8,128)(2,1)S(1)}, bf16[2,24,1,8,640]{4,1,3,2,0:T(8,128)(2,1)S(1)}, u32[]{:S(2)}, u32[]{:S(2)}) collective-permute-start(bf16[2,24,1,8,640]{4,1,3,2,0:T(8,128)(2,1)S(1)} %get-tuple-element.16), channel_id=1, source_target_pairs={{4,0},{8,4},{12,8},{5,1},{9,5},{13,9},{6,2},{10,6},{14,10},{7,3},{... | collective-permute-start | bytes 1474568 | tf_op jit(solution)/shard_map/ppermute | solution.py:17
  12.6 2.9 %constant_dynamic-update-slice_fusion.5 = bf16[3,3,640,640]{3,2,1,0:T(8,128)(2,1)} fusion(bf16[3,3,160,640]{3,2,1,0:T(8,128)(2,1)} %param.25), kind=kLoop, calls=%fused_computation.79 | loop fusion | bytes 3686400
  15.6 15.1 %collective-permute-done = bf16[2,24,1,8,640]{4,1,3,2,0:T(8,128)(2,1)S(1)} collective-permute-done((bf16[2,24,1,8,640]{4,1,3,2,0:T(8,128)(2,1)}, bf16[2,24,1,8,640]{4,1,3,2,0:T(8,128)(2,1)S(1)}, u32[]{:S(2)}, u32[]{:S(2)}) %collective-permute-start) | collective-permute-done | bytes 491552 | tf_op jit(solution)/shard_map/ppermute | solution.py:14
  30.7 0.6 collective-permute-done.1
  31.4 1.1 pad_maximum_fusion.7
  32.4 3.9 %collective-permute-start.2 = (bf16[2,24,6,1,640]{4,1,3,2,0:T(8,128)(2,1)}, bf16[2,24,6,1,640]{4,1,3,2,0:T(8,128)(2,1)}, u32[]{:S(2)}, u32[]{:S(2)}) collective-permute-start(bf16[2,24,6,1,640]{4,1,3,2,0:T(8,128)(2,1)} %get-tuple-element.11), channel_id=1, source_target_pairs={{0,1},{1,2},{2,3},{4,5},{5,6},{6,7},{8,9},{9,10},{10,11},{12,13},{... | collective-permute-start | bytes 1105928 | tf_op jit(solution)/shard_map/ppermute | solution.py:14
  36.4 1.3 %collective-permute-start.3 = (bf16[2,24,6,1,640]{4,1,3,2,0:T(8,128)(2,1)}, bf16[2,24,6,1,640]{4,1,3,2,0:T(8,128)(2,1)}, u32[]{:S(2)}, u32[]{:S(2)}) collective-permute-start(bf16[2,24,6,1,640]{4,1,3,2,0:T(8,128)(2,1)} %get-tuple-element.12), channel_id=1, source_target_pairs={{1,0},{2,1},{3,2},{5,4},{6,5},{7,6},{9,8},{10,9},{11,10},{13,12},{... | collective-permute-start | bytes 1105928 | tf_op jit(solution)/shard_map/ppermute | solution.py:17
  37.7 0.5 compare_and_fusion
  38.2 0.2 broadcast_in_dim.80
  38.3 0.2 mul.128
  38.6 0.2 broadcast_in_dim.79
  38.7 0.2 sub.69
  39.0 0.2 broadcast_in_dim.76
  39.1 0.2 mul.115
  39.4 0.2 broadcast_in_dim.42
  39.5 0.8 sub.59
  40.4 0.6 and_convert_fusion
  41.0 1.3 %dynamic-slice_bitcast_fusion = bf16[3,3,80,640]{3,2,1,0:T(8,128)(2,1)S(1)} fusion(bf16[3,3,2,80,640]{4,3,2,1,0:T(8,128)(2,1)} %bitcast.10, s32[]{:T(128)S(6)} %select_n.125), kind=kLoop, calls=%fused_computation.62 | loop fusion | bytes 1843204 | tf_op jit(solution)/shard_map/jit(dynamic_index_in_dim)/squeeze | solution.py:33
  42.3 1.3 %collective-permute-start.6 = (bf16[3,3,80,640]{3,2,1,0:T(8,128)(2,1)}, bf16[3,3,80,640]{3,2,1,0:T(8,128)(2,1)S(1)}, u32[]{:S(2)}, u32[]{:S(2)}) collective-permute-start(bf16[3,3,80,640]{3,2,1,0:T(8,128)(2,1)} %collective-permute-done.5), channel_id=1, source_target_pairs={{0,16},{16,0},{1,17},{17,1},{2,18},{18,2},{3,19},{19,3},{4,20},{20... | collective-permute-start | bytes 2764808 | tf_op jit(solution)/shard_map/ppermute | solution.py:41
  43.6 1.3 %collective-permute-done.3 = bf16[2,24,6,1,640]{4,1,3,2,0:T(8,128)(2,1)} collective-permute-done((bf16[2,24,6,1,640]{4,1,3,2,0:T(8,128)(2,1)}, bf16[2,24,6,1,640]{4,1,3,2,0:T(8,128)(2,1)}, u32[]{:S(2)}, u32[]{:S(2)}) %collective-permute-start.3) | collective-permute-done | bytes 368672 | tf_op jit(solution)/shard_map/ppermute | solution.py:17
  45.0 3.0 %pad_maximum_fusion = bf16[2,24,6,10,640]{4,1,3,2,0:T(8,128)(2,1)S(1)} fusion(bf16[2,24,6,1,640]{4,1,3,2,0:T(8,128)(2,1)} %collective-permute-done.3, bf16[2,24,1,8,640]{4,1,3,2,0:T(8,128)(2,1)S(1)} %collective-permute-done.1, bf16[1,24,4,8,640]{4,1,3,2,0:T(8,128)(2,1)S(1)} %get-tuple-element.17, bf16[1,24,4,8,640]{4,1,3,2,0:T(8,128)(2,1)S(1)} %get-tuple-element.18, ...), kind=kLoop, calls=%fused_computation.1 | loop fusion | flops 9216000 | bytes 7372800 | tf_op jit(solution)/shard_map/concatenate | solution.py:18
  48.0 3.6 %collective-permute-start.7 = (bf16[3,3,80,640]{3,2,1,0:T(8,128)(2,1)}, bf16[3,3,80,640]{3,2,1,0:T(8,128)(2,1)S(1)}, u32[]{:S(2)}, u32[]{:S(2)}) collective-permute-start(bf16[3,3,80,640]{3,2,1,0:T(8,128)(2,1)} %collective-permute-done.5), channel_id=1, source_target_pairs={{0,4},{4,0},{8,12},{12,8},{1,5},{5,1},{9,13},{13,9},{2,6},{6,2},{1... | collective-permute-start | bytes 2764808 | tf_op jit(solution)/shard_map/ppermute | solution.py:42
  51.6 3.3 %fusion.23 = bf16[24,6,10,640]{3,0,2,1:T(8,128)(2,1)S(1)} fusion(bf16[2,24,6,10,640]{4,1,3,2,0:T(8,128)(2,1)S(1)} %pad_maximum_fusion, f32[640]{0:T(1024)S(1)} %copy-done.11, f32[640]{0:T(1024)S(1)} %copy-done.12, f32[24,640]{1,0:T(8,128)S(1)} %mul.128, f32[24,640]{1,0:T(8,128)S(1)} %sub.69, f32[6,10]{1,0:T(8,128)S(1)} %and_convert_fusion, s32[640]{0:T(1024)S(1)} %fusion.75), kind=kOutput, calls=%fused_computation.34 | convolution fusion | flops 1190195200 | bytes 3825664 | tf_op jit(solution)/shard_map/dot_general | solution.py:72
  54.9 0.4 copy.63
  55.5 2.2 %fusion.25 = f32[24,6,10,640]{3,0,2,1:T(8,128)} fusion(bf16[2,24,6,10,640]{4,1,3,2,0:T(8,128)(2,1)S(1)} %pad_maximum_fusion), kind=kLoop, calls=%fused_computation.37 | loop fusion | flops 921600 | bytes 5529600 | tf_op jit(solution)/shard_map/convert_element_type | solution.py:130
  57.6 10.8 %collective-permute-done.10 = bf16[3,3,80,640]{3,2,1,0:T(8,128)(2,1)} collective-permute-done((bf16[3,3,80,640]{3,2,1,0:T(8,128)(2,1)S(1)}, bf16[3,3,80,640]{3,2,1,0:T(8,128)(2,1)}, u32[]{:S(2)}, u32[]{:S(2)}) %collective-permute-start.10) | collective-permute-done | bytes 921632 | tf_op jit(solution)/shard_map/ppermute | solution.py:39
  68.4 1.2 %collective-permute-start.11 = (bf16[3,3,80,640]{3,2,1,0:T(8,128)(2,1)}, bf16[3,3,80,640]{3,2,1,0:T(8,128)(2,1)}, u32[]{:S(2)}, u32[]{:S(2)}) collective-permute-start(bf16[3,3,80,640]{3,2,1,0:T(8,128)(2,1)} %collective-permute-done.10), channel_id=1, source_target_pairs={{0,16},{16,0},{1,17},{17,1},{2,18},{18,2},{3,19},{19,3},{4,20},{20... | collective-permute-start | bytes 2764808 | tf_op jit(solution)/shard_map/ppermute | solution.py:41
  69.7 2.8 %collective-permute-start.12 = (bf16[3,3,80,640]{3,2,1,0:T(8,128)(2,1)}, bf16[3,3,80,640]{3,2,1,0:T(8,128)(2,1)}, u32[]{:S(2)}, u32[]{:S(2)}) collective-permute-start(bf16[3,3,80,640]{3,2,1,0:T(8,128)(2,1)} %collective-permute-done.10), channel_id=1, source_target_pairs={{0,4},{4,0},{8,12},{12,8},{1,5},{5,1},{9,13},{13,9},{2,6},{6,2},{1... | collective-permute-start | bytes 2764808 | tf_op jit(solution)/shard_map/ppermute | solution.py:42
  72.5 2.9 %constant_dynamic-update-slice_fusion.4 = bf16[3,3,640,640]{3,2,1,0:T(8,128)(2,1)} fusion(bf16[3,3,640,640]{3,2,1,0:T(8,128)(2,1)} %constant_dynamic-update-slice_fusion.5, bf16[3,3,160,640]{3,2,1,0:T(8,128)(2,1)} %collective-permute-done.4), kind=kLoop, calls=%fused_computation.78 | loop fusion | bytes 3686400
  75.4 2.3 %constant_dynamic-update-slice_fusion.3 = bf16[3,3,640,640]{3,2,1,0:T(8,128)(2,1)} fusion(bf16[3,3,640,640]{3,2,1,0:T(8,128)(2,1)} %constant_dynamic-update-slice_fusion.4, bf16[3,3,80,640]{3,2,1,0:T(8,128)(2,1)} %collective-permute-done.5), kind=kLoop, calls=%fused_computation.77 | loop fusion | bytes 1843200
  77.7 1.1 constant_dynamic-update-slice_fusion.2
  78.7 1.0 constant_dynamic-update-slice_fusion.1
  79.7 1.0 constant_dynamic-update-slice_fusion
  80.8 15.2 %multiply_convert_fusion.1 = bf16[24,4,8,640]{3,0,2,1:T(8,128)(2,1)} fusion(bf16[3,3,640,640]{3,2,1,0:T(8,128)(2,1)} %constant_dynamic-update-slice_fusion, f32[640]{0:T(1024)S(1)} %copy-done.11, f32[640]{0:T(1024)S(1)} %copy-done.12, f32[24,640]{1,0:T(8,128)S(1)} %mul.128, f32[24,640]{1,0:T(8,128)S(1)} %sub.69, f32[24,640]{1,0:T(8,128)S(1)} %copy-done.10, ...), kind=kOutput, calls=%fused_computation.33 | convolution fusion | flops 6858833920 | bytes 10521840 | tf_op jit(solution)/shard_map/conv_general_dilated | solution.py:81
  96.0 2.2 %fusion.46 = bf16[24,4,8,640]{3,2,1,0:T(8,128)(2,1)S(1)} fusion(bf16[24,4,8,640]{3,0,2,1:T(8,128)(2,1)} %multiply_convert_fusion.1, s32[640]{0:T(1024)S(1)} %fusion.75), kind=kOutput, calls=%fused_computation.55 | convolution fusion | flops 630046720 | bytes 1968640 | tf_op jit(solution)/shard_map/dot_general | solution.py:72
  98.3 1.2 %fusion.45 = (bf16[24,6,6,640]{3,2,1,0:T(8,128)(2,1)S(1)}, bf16[24,6,6,640]{3,2,1,0:T(8,128)(2,1)S(1)}) fusion(bf16[24,4,8,640]{3,2,1,0:T(8,128)(2,1)S(1)} %fusion.46, bf16[24,6,10,640]{3,2,1,0:T(8,128)(2,1)S(1)} %copy.63, pred[6,6]{1,0:T(8,128)(4,1)S(1)} %broadcast_and_fusion), kind=kLoop, calls=%fused_computation.54 | loop fusion | flops 1105920 | bytes 5406756 | tf_op jit(solution)/shard_map/jit(_where)/select_n | solution.py:169
  99.5 2.1 %pad_maximum_fusion.1 = (bf16[24,6,12,320]{3,2,1,0:T(8,128)(2,1)S(1)}, bf16[24,6,12,320]{3,2,1,0:T(8,128)(2,1)S(1)}) fusion(bf16[24,6,6,640]{3,2,1,0:T(8,128)(2,1)S(1)} %get-tuple-element.7, bf16[24,6,6,640]{3,2,1,0:T(8,128)(2,1)S(1)} %get-tuple-element.8), kind=kLoop, calls=%fused_computation.48 | loop fusion | flops 4423680 | bytes 4423680 | tf_op jit(solution)/shard_map/concatenate | solution.py:170
  101.5 7.1 %fusion = f32[24,4,10,640]{3,0,2,1:T(8,128)S(1)} fusion(bf16[3,3,160,640]{3,2,1,0:T(8,128)(2,1)} %collective-permute-done.9, bf16[3,3,160,640]{3,2,1,0:T(8,128)(2,1)} %param.32, bf16[24,6,12,320]{3,2,1,0:T(8,128)(2,1)S(1)} %get-tuple-element.10), kind=kOutput, calls=%fused_computation.2 | convolution fusion | flops 3546316800 | bytes 7249920 | tf_op jit(solution)/shard_map/conv_general_dilated | solution.py:81
  108.7 7.1 %fusion.36 = f32[24,4,10,640]{3,0,2,1:T(8,128)S(1)} fusion(f32[24,4,10,640]{3,0,2,1:T(8,128)S(1)} %fusion, bf16[3,3,80,640]{3,2,1,0:T(8,128)(2,1)S(1)} %collective-permute-done.13, bf16[3,3,80,640]{3,2,1,0:T(8,128)(2,1)} %collective-permute-done.12, bf16[3,3,80,640]{3,2,1,0:T(8,128)(2,1)} %collective-permute-done.11, ...), kind=kOutput, calls=%fused_computation.49 | convolution fusion | flops 3554304000 | bytes 9707520 | tf_op jit(solution)/shard_map/conv_general_dilated | solution.py:81
  115.8 0.1 fusion.97
  116.0 1.8 %copy-done = f32[24,6,10,640]{3,0,2,1:T(8,128)S(1)} copy-done((f32[24,6,10,640]{3,0,2,1:T(8,128)S(1)}, f32[24,6,10,640]{3,0,2,1:T(8,128)}, u32[]{:S(2)}) %copy-start) | copy-done | bytes 3686424
  117.8 0.6 fusion.53
  118.4 1.1 copy.49
  (53 shorter events, 0.6 us)
Async XLA Ops:
  0.0 69.7 %collective-permute-start.4 = (bf16[3,3,160,640]{3,2,1,0:T(8,128)(2,1)}, bf16[3,3,160,640]{3,2,1,0:T(8,128)(2,1)}, u32[]{:S(2)}, u32[]{:S(2)}) collective-permute-start(bf16[3,3,160,640]{3,2,1,0:T(8,128)(2,1)} %param.25), channel_id=1, source_target_pairs={{0,4},{4,0},{8,12},{12,8},{1,5},{5,1},{9,13},{13,9},{2,6},{6,2},{1... | collective-permute-start | bytes 5529608 | tf_op jit(solution)/shard_map/ppermute | solution.py:34
  2.2 10.3 %copy-start.8 = (s32[24,16]{0,1:T(8,128)S(1)}, s32[24,16]{0,1:T(8,128)}, u32[]{:S(2)}) copy-start(s32[24,16]{0,1:T(8,128)} %param.20) | copy-start | bytes 4612
  2.2 40.1 %collective-permute-start.5 = (bf16[3,3,80,640]{3,2,1,0:T(8,128)(2,1)}, bf16[3,3,80,640]{3,2,1,0:T(8,128)(2,1)}, u32[]{:S(2)}, u32[]{:S(2)}) collective-permute-start(bf16[3,3,80,640]{3,2,1,0:T(8,128)(2,1)} %dynamic-slice_bitcast_fusion.1), channel_id=1, source_target_pairs={{8,0},{12,4},{0,8},{4,12},{9,1},{13,5},{1,9},{5,13},{10,2},{14,6},... | collective-permute-start | bytes 2764808 | tf_op jit(solution)/shard_map/ppermute | solution.py:39
  8.0 22.8 %collective-permute-start = (bf16[2,24,1,8,640]{4,1,3,2,0:T(8,128)(2,1)}, bf16[2,24,1,8,640]{4,1,3,2,0:T(8,128)(2,1)S(1)}, u32[]{:S(2)}, u32[]{:S(2)}) collective-permute-start(bf16[2,24,1,8,640]{4,1,3,2,0:T(8,128)(2,1)} %get-tuple-element.15), channel_id=1, source_target_pairs={{0,4},{4,8},{8,12},{1,5},{5,9},{9,13},{2,6},{6,10},{10,14},{3,7},{... | collective-permute-start | bytes 1474568 | tf_op jit(solution)/shard_map/ppermute | solution.py:14
  9.9 21.5 %collective-permute-start.1 = (bf16[2,24,1,8,640]{4,1,3,2,0:T(8,128)(2,1)S(1)}, bf16[2,24,1,8,640]{4,1,3,2,0:T(8,128)(2,1)S(1)}, u32[]{:S(2)}, u32[]{:S(2)}) collective-permute-start(bf16[2,24,1,8,640]{4,1,3,2,0:T(8,128)(2,1)S(1)} %get-tuple-element.16), channel_id=1, source_target_pairs={{4,0},{8,4},{12,8},{5,1},{9,5},{13,9},{6,2},{10,6},{14,10},{7,3},{... | collective-permute-start | bytes 1474568 | tf_op jit(solution)/shard_map/ppermute | solution.py:17
  12.3 89.2 %collective-permute-start.9 = (bf16[3,3,160,640]{3,2,1,0:T(8,128)(2,1)}, bf16[3,3,160,640]{3,2,1,0:T(8,128)(2,1)}, u32[]{:S(2)}, u32[]{:S(2)}) collective-permute-start(bf16[3,3,160,640]{3,2,1,0:T(8,128)(2,1)} %param.32), channel_id=1, source_target_pairs={{0,4},{4,0},{8,12},{12,8},{1,5},{5,1},{9,13},{13,9},{2,6},{6,2},{1... | collective-permute-start | bytes 5529608 | tf_op jit(solution)/shard_map/ppermute | solution.py:34
  12.6 25.6 %copy-start.4 = (f32[24,32]{1,0:T(8,128)S(1)}, f32[24,32]{1,0:T(8,128)}, u32[]{:S(2)}) copy-start(f32[24,32]{1,0:T(8,128)} %param.29) | copy-start | bytes 9220
  12.6 25.9 %copy-start.5 = (f32[24,32]{1,0:T(8,128)S(1)}, f32[24,32]{1,0:T(8,128)}, u32[]{:S(2)}) copy-start(f32[24,32]{1,0:T(8,128)} %param.28) | copy-start | bytes 9220
  15.5 23.4 %copy-start.6 = (f32[24,32]{1,0:T(8,128)S(1)}, f32[24,32]{1,0:T(8,128)}, u32[]{:S(2)}) copy-start(f32[24,32]{1,0:T(8,128)} %param.22) | copy-start | bytes 9220
  15.5 23.8 %copy-start.7 = (f32[24,32]{1,0:T(8,128)S(1)}, f32[24,32]{1,0:T(8,128)}, u32[]{:S(2)}) copy-start(f32[24,32]{1,0:T(8,128)} %param.21) | copy-start | bytes 9220
  32.4 11.2 %collective-permute-start.2 = (bf16[2,24,6,1,640]{4,1,3,2,0:T(8,128)(2,1)}, bf16[2,24,6,1,640]{4,1,3,2,0:T(8,128)(2,1)}, u32[]{:S(2)}, u32[]{:S(2)}) collective-permute-start(bf16[2,24,6,1,640]{4,1,3,2,0:T(8,128)(2,1)} %get-tuple-element.11), channel_id=1, source_target_pairs={{0,1},{1,2},{2,3},{4,5},{5,6},{6,7},{8,9},{9,10},{10,11},{12,13},{... | collective-permute-start | bytes 1105928 | tf_op jit(solution)/shard_map/ppermute | solution.py:14
  36.4 8.6 %collective-permute-start.3 = (bf16[2,24,6,1,640]{4,1,3,2,0:T(8,128)(2,1)}, bf16[2,24,6,1,640]{4,1,3,2,0:T(8,128)(2,1)}, u32[]{:S(2)}, u32[]{:S(2)}) collective-permute-start(bf16[2,24,6,1,640]{4,1,3,2,0:T(8,128)(2,1)} %get-tuple-element.12), channel_id=1, source_target_pairs={{1,0},{2,1},{3,2},{5,4},{6,5},{7,6},{9,8},{10,9},{11,10},{13,12},{... | collective-permute-start | bytes 1105928 | tf_op jit(solution)/shard_map/ppermute | solution.py:17
  42.3 9.3 %copy-start.11 = (f32[640]{0:T(1024)S(1)}, f32[640]{0:T(1024)}, u32[]{:S(2)}) copy-start(f32[640]{0:T(1024)} %param.31) | copy-start | bytes 7684
  42.3 9.3 %copy-start.12 = (f32[640]{0:T(1024)S(1)}, f32[640]{0:T(1024)}, u32[]{:S(2)}) copy-start(f32[640]{0:T(1024)} %param.30) | copy-start | bytes 7684
  42.3 13.1 %collective-permute-start.6 = (bf16[3,3,80,640]{3,2,1,0:T(8,128)(2,1)}, bf16[3,3,80,640]{3,2,1,0:T(8,128)(2,1)S(1)}, u32[]{:S(2)}, u32[]{:S(2)}) collective-permute-start(bf16[3,3,80,640]{3,2,1,0:T(8,128)(2,1)} %collective-permute-done.5), channel_id=1, source_target_pairs={{0,16},{16,0},{1,17},{17,1},{2,18},{18,2},{3,19},{19,3},{4,20},{20... | collective-permute-start | bytes 2764808 | tf_op jit(solution)/shard_map/ppermute | solution.py:41
  47.9 7.5 %copy-start.1 = (bf16[2,24,6,10,640]{4,1,3,2,0:T(8,128)(2,1)}, bf16[2,24,6,10,640]{4,1,3,2,0:T(8,128)(2,1)S(1)}, u32[]{:S(2)}) copy-start(bf16[2,24,6,10,640]{4,1,3,2,0:T(8,128)(2,1)S(1)} %pad_maximum_fusion) | copy-start | bytes 11059204
  47.9 20.5 %collective-permute-start.10 = (bf16[3,3,80,640]{3,2,1,0:T(8,128)(2,1)S(1)}, bf16[3,3,80,640]{3,2,1,0:T(8,128)(2,1)}, u32[]{:S(2)}, u32[]{:S(2)}) collective-permute-start(bf16[3,3,80,640]{3,2,1,0:T(8,128)(2,1)S(1)} %dynamic-slice_bitcast_fusion), channel_id=1, source_target_pairs={{8,0},{12,4},{0,8},{4,12},{9,1},{13,5},{1,9},{5,13},{10,2},{14,6},... | collective-permute-start | bytes 2764808 | tf_op jit(solution)/shard_map/ppermute | solution.py:39
  48.0 30.7 %collective-permute-start.7 = (bf16[3,3,80,640]{3,2,1,0:T(8,128)(2,1)}, bf16[3,3,80,640]{3,2,1,0:T(8,128)(2,1)S(1)}, u32[]{:S(2)}, u32[]{:S(2)}) collective-permute-start(bf16[3,3,80,640]{3,2,1,0:T(8,128)(2,1)} %collective-permute-done.5), channel_id=1, source_target_pairs={{0,4},{4,0},{8,12},{12,8},{1,5},{5,1},{9,13},{13,9},{2,6},{6,2},{1... | collective-permute-start | bytes 2764808 | tf_op jit(solution)/shard_map/ppermute | solution.py:42
  55.4 24.4 %collective-permute-start.8 = (bf16[3,3,80,640]{3,2,1,0:T(8,128)(2,1)S(1)}, bf16[3,3,80,640]{3,2,1,0:T(8,128)(2,1)S(1)}, u32[]{:S(2)}, u32[]{:S(2)}) collective-permute-start(bf16[3,3,80,640]{3,2,1,0:T(8,128)(2,1)S(1)} %collective-permute-done.6), channel_id=1, source_target_pairs={{0,4},{4,0},{8,12},{12,8},{1,5},{5,1},{9,13},{13,9},{2,6},{6,2},{1... | collective-permute-start | bytes 2764808 | tf_op jit(solution)/shard_map/ppermute | solution.py:43
  68.4 27.5 %collective-permute-start.11 = (bf16[3,3,80,640]{3,2,1,0:T(8,128)(2,1)}, bf16[3,3,80,640]{3,2,1,0:T(8,128)(2,1)}, u32[]{:S(2)}, u32[]{:S(2)}) collective-permute-start(bf16[3,3,80,640]{3,2,1,0:T(8,128)(2,1)} %collective-permute-done.10), channel_id=1, source_target_pairs={{0,16},{16,0},{1,17},{17,1},{2,18},{18,2},{3,19},{19,3},{4,20},{20... | collective-permute-start | bytes 2764808 | tf_op jit(solution)/shard_map/ppermute | solution.py:41
  69.7 38.9 %collective-permute-start.12 = (bf16[3,3,80,640]{3,2,1,0:T(8,128)(2,1)}, bf16[3,3,80,640]{3,2,1,0:T(8,128)(2,1)}, u32[]{:S(2)}, u32[]{:S(2)}) collective-permute-start(bf16[3,3,80,640]{3,2,1,0:T(8,128)(2,1)} %collective-permute-done.10), channel_id=1, source_target_pairs={{0,4},{4,0},{8,12},{12,8},{1,5},{5,1},{9,13},{13,9},{2,6},{6,2},{1... | collective-permute-start | bytes 2764808 | tf_op jit(solution)/shard_map/ppermute | solution.py:42
  75.4 5.4 %copy-start.3 = (f32[24,640]{1,0:T(8,128)S(1)}, f32[24,640]{1,0:T(8,128)}, u32[]{:S(2)}) copy-start(f32[24,640]{1,0:T(8,128)} %sub.59) | copy-start | bytes 184324
  75.4 5.4 %copy-start.10 = (f32[24,640]{1,0:T(8,128)S(1)}, f32[24,640]{1,0:T(8,128)}, u32[]{:S(2)}) copy-start(f32[24,640]{1,0:T(8,128)} %param.27) | copy-start | bytes 184324
  75.4 5.4 %copy-start.13 = (f32[640]{0:T(1024)S(1)}, f32[640]{0:T(1024)}, u32[]{:S(2)}) copy-start(f32[640]{0:T(1024)} %param.26) | copy-start | bytes 7684
  75.4 5.4 %copy-start.14 = (f32[640]{0:T(1024)S(1)}, f32[640]{0:T(1024)}, u32[]{:S(2)}) copy-start(f32[640]{0:T(1024)} %param.24) | copy-start | bytes 7684
  75.4 5.4 %copy-start.15 = (f32[640]{0:T(1024)S(1)}, f32[640]{0:T(1024)}, u32[]{:S(2)}) copy-start(f32[640]{0:T(1024)} %param.23) | copy-start | bytes 7684
  96.0 12.6 %collective-permute-start.13 = (bf16[3,3,80,640]{3,2,1,0:T(8,128)(2,1)}, bf16[3,3,80,640]{3,2,1,0:T(8,128)(2,1)S(1)}, u32[]{:S(2)}, u32[]{:S(2)}) collective-permute-start(bf16[3,3,80,640]{3,2,1,0:T(8,128)(2,1)} %collective-permute-done.11), channel_id=1, source_target_pairs={{0,4},{4,0},{8,12},{12,8},{1,5},{5,1},{9,13},{13,9},{2,6},{6,2},{1... | collective-permute-start | bytes 2764808 | tf_op jit(solution)/shard_map/ppermute | solution.py:43
  108.6 7.3 %copy-start.2 = (bf16[24,4,8,640]{3,2,1,0:T(8,128)(2,1)S(1)}, bf16[24,4,8,640]{3,2,1,0:T(8,128)(2,1)}, u32[]{:S(2)}) copy-start(bf16[24,4,8,640]{3,2,1,0:T(8,128)(2,1)} %param.19) | copy-start | bytes 2949124
  115.8 2.0 %copy-start = (f32[24,6,10,640]{3,0,2,1:T(8,128)S(1)}, f32[24,6,10,640]{3,0,2,1:T(8,128)}, u32[]{:S(2)}) copy-start(f32[24,6,10,640]{3,0,2,1:T(8,128)} %fusion.25) | copy-start | bytes 11059204
  115.8 2.0 %copy-start.9 = (f32[640]{0:T(1024)S(1)}, f32[640]{0:T(1024)}, u32[]{:S(2)}) copy-start(f32[640]{0:T(1024)} %param.33) | copy-start | bytes 7684

commit v15 on v14

--- a/solution.py
+++ b/solution.py
@@ -117,7 +117,8 @@
     per_group = channels // groups_total
 
     first_held, second_held = gather_weights([conv1_weight, conv2_weight])
-    first_whole = jnp.concatenate(first_held, axis=2)
+    first_local = jnp.concatenate(first_held[:2], axis=2)
+    first_remote = jnp.concatenate(first_held[2:], axis=2)
     second_local = jnp.concatenate(second_held[:2], axis=2)
     second_remote = jnp.concatenate(second_held[2:], axis=2)
     order = relative_order(channels)
@@ -145,8 +146,13 @@
         )
         * inside
     ).astype(jnp.bfloat16)
+    first_moved = to_relative(first_act, order)
+    first_split = first_local.shape[2]
     fresh_mid = (
-        conv_relative(first_act, first_whole, order) + conv1_bias + step_embed[:, None, None, :]
+        conv_valid(first_moved[..., :first_split], first_local)
+        + conv_valid(first_moved[..., first_split:], first_remote)
+        + conv1_bias
+        + step_embed[:, None, None, :]
     )
 
     if tiles_down != 1:

time: 120 us -> 112 us (0.933)
  local copies, waits for them, and re-layouts: 22.4 us -> 10.9 us
  waiting for transfers between devices: 27.9 us -> 36.9 us
  matrix products: 35 us -> 31.4 us
  starting transfers between devices: 21.5 us -> 19.4 us
    ppermute x2, waiting for transfers between devices: 15.1 us -> 0.01 us  [padded_2(): lax.ppermute(lax.slice_in_dim(block, block.shape[dim] - width, None, axis...]
    ppermute x2, waiting for transfers between devices: 0.01 us -> 14.3 us  [gather_weights(): other = lax.ppermute(fetched, 'groups', y_pairs)]
    unnamed x37 -> x36, local copies, waits for them, and re-layouts: 12 us -> 1.44 us
    ppermute x2, waiting for transfers between devices: 1.97 us -> 7.7 us  [padded_2(): lax.ppermute(lax.slice_in_dim(block, 0, width, axis=dim), axis, backward)]
    conv_general_dilated x3 -> x4, matrix products: 29.4 us -> 23.8 us  [conv_valid(): lax.conv_general_dilated(activation, kernel, window_strides=(1, 1), paddi...]
    ppermute x2, starting transfers between devices: 6.4 us -> 1.84 us  [gather_weights(): relayed = lax.ppermute(fetched, 'row', mate_pairs)]
    ppermute x2, waiting for transfers between devices: 10.8 us -> 14.9 us  [gather_weights(): fetched = lax.ppermute(mine, 'row', pairs)]
    ppermute x2, starting transfers between devices: 5.86 us -> 8.57 us  [padded_2(): lax.ppermute(lax.slice_in_dim(block, block.shape[dim] - width, None, axis...]
  transfers between devices with their start and end apart: 14 -> 14, of which waited for: 4 -> 4; matrix products, arithmetic and copies ran while one was open for 49% -> 39% of each run, Pallas kernels for 0% -> 0%
where the time goes in v15:
time: 112 us; the launch traced here: 111 us
  waiting for transfers between devices  36.9 us (33%)
  matrix products  31.4 us (28%)
  starting transfers between devices  19.4 us (17%)
  other arithmetic  12.2 us (11%)
  local copies, waits for them, and re-layouts  10.9 us (10%)
    conv_general_dilated x4, matrix products, conv_valid(): lax.conv_general_dilated(activation, kernel, window_strides=(1, 1), paddi...  23.8 us
    ppermute x2, waiting for transfers between devices, gather_weights(): fetched = lax.ppermute(mine, 'row', pairs)  14.9 us
    ppermute x2, waiting for transfers between devices, gather_weights(): other = lax.ppermute(fetched, 'groups', y_pairs)  14.3 us
    ppermute x2, starting transfers between devices, padded_2(): lax.ppermute(lax.slice_in_dim(block, block.shape[dim] - width, None, axis...  8.57 us
    ppermute x2, waiting for transfers between devices, padded_2(): lax.ppermute(lax.slice_in_dim(block, 0, width, axis=dim), axis, backward)  7.7 us
    dot_general x3, matrix products, to_relative(): moved = jnp.dot(activation, chooser, preferred_element_type=jnp.float32)  7.62 us
    squeeze x2, local copies, waits for them, and re-layouts, gather_weights(): mine = lax.dynamic_index_in_dim(halves, parity, axis=2, keepdims=False)  3.46 us
    ppermute x2, starting transfers between devices, padded_2(): lax.ppermute(lax.slice_in_dim(block, 0, width, axis=dim), axis, backward)  3.2 us
  transfers between devices with their start and end apart: 14, of which 4 were waited for; matrix products, arithmetic and copies ran while one was open for 39% of the time, Pallas kernels for 0%

profile of v15, /device:TPU:1, one launch (start us, length us, event | category | flops | bytes accessed | tf_op | source)
XLA Modules:
  0.0 111.2 jit_solution(1666598311235823291)
XLA Ops:
  0.0 2.1 %copy_bitcast_fusion = (bf16[1,24,4,8,640]{4,1,3,2,0:T(8,128)(2,1)S(1)}, bf16[1,24,4,8,640]{4,1,3,2,0:T(8,128)(2,1)S(1)}) fusion(bf16[24,4,8,640]{3,2,1,0:T(8,128)(2,1)} %param.18, bf16[24,4,8,640]{3,2,1,0:T(8,128)(2,1)} %param.17), kind=kLoop, calls=%fused_computation.73 | loop fusion | bytes 3932160 | tf_op jit(solution)/shard_map/stack | solution.py:129
  2.2 0.9 pad_maximum_fusion.3
  3.1 4.6 %collective-permute-start = (bf16[2,24,1,8,640]{4,1,3,2,0:T(8,128)(2,1)}, bf16[2,24,1,8,640]{4,1,3,2,0:T(8,128)(2,1)S(1)}, u32[]{:S(2)}, u32[]{:S(2)}) collective-permute-start(bf16[2,24,1,8,640]{4,1,3,2,0:T(8,128)(2,1)} %get-tuple-element.15), channel_id=1, source_target_pairs={{0,4},{4,8},{8,12},{1,5},{5,9},{9,13},{2,6},{6,10},{10,14},{3,7},{... | collective-permute-start | bytes 1474568 | tf_op jit(solution)/shard_map/ppermute | solution.py:14
  7.7 1.9 %collective-permute-start.1 = (bf16[2,24,1,8,640]{4,1,3,2,0:T(8,128)(2,1)S(1)}, bf16[2,24,1,8,640]{4,1,3,2,0:T(8,128)(2,1)S(1)}, u32[]{:S(2)}, u32[]{:S(2)}) collective-permute-start(bf16[2,24,1,8,640]{4,1,3,2,0:T(8,128)(2,1)S(1)} %get-tuple-element.16), channel_id=1, source_target_pairs={{4,0},{8,4},{12,8},{5,1},{9,5},{13,9},{6,2},{10,6},{14,10},{7,3},{... | collective-permute-start | bytes 1474568 | tf_op jit(solution)/shard_map/ppermute | solution.py:17
  9.7 2.2 %dynamic-slice_bitcast_fusion.1 = bf16[3,3,80,640]{3,2,1,0:T(8,128)(2,1)} fusion(bf16[3,3,2,80,640]{4,3,2,1,0:T(8,128)(2,1)} %bitcast.6, s32[]{:T(128)S(6)} %select_n.125), kind=kLoop, calls=%fused_computation.76 | loop fusion | bytes 1843204 | tf_op jit(solution)/shard_map/jit(dynamic_index_in_dim)/squeeze | solution.py:33
  11.9 1.8 %collective-permute-start.5 = (bf16[3,3,80,640]{3,2,1,0:T(8,128)(2,1)}, bf16[3,3,80,640]{3,2,1,0:T(8,128)(2,1)}, u32[]{:S(2)}, u32[]{:S(2)}) collective-permute-start(bf16[3,3,80,640]{3,2,1,0:T(8,128)(2,1)} %dynamic-slice_bitcast_fusion.1), channel_id=1, source_target_pairs={{8,0},{12,4},{0,8},{4,12},{9,1},{13,5},{1,9},{5,13},{10,2},{14,6},... | collective-permute-start | bytes 2764808 | tf_op jit(solution)/shard_map/ppermute | solution.py:39
  13.7 0.3 collective-permute-start.9
  14.1 0.5 compare_and_fusion.1
  14.6 0.6 fusion.83
  15.2 0.7 compare_reduce_fusion
  16.0 4.7 %collective-permute-done.1 = bf16[2,24,1,8,640]{4,1,3,2,0:T(8,128)(2,1)S(1)} collective-permute-done((bf16[2,24,1,8,640]{4,1,3,2,0:T(8,128)(2,1)S(1)}, bf16[2,24,1,8,640]{4,1,3,2,0:T(8,128)(2,1)S(1)}, u32[]{:S(2)}, u32[]{:S(2)}) %collective-permute-start.1) | collective-permute-done | bytes 491552 | tf_op jit(solution)/shard_map/ppermute | solution.py:17
  20.7 1.0 pad_maximum_fusion.7
  21.8 3.9 %collective-permute-start.2 = (bf16[2,24,6,1,640]{4,1,3,2,0:T(8,128)(2,1)}, bf16[2,24,6,1,640]{4,1,3,2,0:T(8,128)(2,1)}, u32[]{:S(2)}, u32[]{:S(2)}) collective-permute-start(bf16[2,24,6,1,640]{4,1,3,2,0:T(8,128)(2,1)} %get-tuple-element.11), channel_id=1, source_target_pairs={{0,1},{1,2},{2,3},{4,5},{5,6},{6,7},{8,9},{9,10},{10,11},{12,13},{... | collective-permute-start | bytes 1105928 | tf_op jit(solution)/shard_map/ppermute | solution.py:14
  25.7 1.3 %collective-permute-start.3 = (bf16[2,24,6,1,640]{4,1,3,2,0:T(8,128)(2,1)}, bf16[2,24,6,1,640]{4,1,3,2,0:T(8,128)(2,1)}, u32[]{:S(2)}, u32[]{:S(2)}) collective-permute-start(bf16[2,24,6,1,640]{4,1,3,2,0:T(8,128)(2,1)} %get-tuple-element.12), channel_id=1, source_target_pairs={{1,0},{2,1},{3,2},{5,4},{6,5},{7,6},{9,8},{10,9},{11,10},{13,12},{... | collective-permute-start | bytes 1105928 | tf_op jit(solution)/shard_map/ppermute | solution.py:17
  27.0 0.6 compare_and_fusion
  27.7 0.2 mul.115
  28.1 0.8 sub.59
  29.2 0.2 mul.128
  29.4 0.2 broadcast_in_dim.79
  29.5 0.2 sub.69
  29.8 1.3 %dynamic-slice_bitcast_fusion = bf16[3,3,80,640]{3,2,1,0:T(8,128)(2,1)S(1)} fusion(bf16[3,3,2,80,640]{4,3,2,1,0:T(8,128)(2,1)} %bitcast.38, s32[]{:T(128)S(6)} %select_n.125), kind=kLoop, calls=%fused_computation.75 | loop fusion | bytes 1843204 | tf_op jit(solution)/shard_map/jit(dynamic_index_in_dim)/squeeze | solution.py:33
  31.1 0.7 and_convert_fusion
  31.7 3.0 %collective-permute-done.3 = bf16[2,24,6,1,640]{4,1,3,2,0:T(8,128)(2,1)} collective-permute-done((bf16[2,24,6,1,640]{4,1,3,2,0:T(8,128)(2,1)}, bf16[2,24,6,1,640]{4,1,3,2,0:T(8,128)(2,1)}, u32[]{:S(2)}, u32[]{:S(2)}) %collective-permute-start.3) | collective-permute-done | bytes 368672 | tf_op jit(solution)/shard_map/ppermute | solution.py:17
  34.7 3.0 %pad_maximum_fusion = bf16[2,24,6,10,640]{4,1,3,2,0:T(8,128)(2,1)S(1)} fusion(bf16[2,24,6,1,640]{4,1,3,2,0:T(8,128)(2,1)} %collective-permute-done.3, bf16[2,24,1,8,640]{4,1,3,2,0:T(8,128)(2,1)S(1)} %collective-permute-done.1, bf16[1,24,4,8,640]{4,1,3,2,0:T(8,128)(2,1)S(1)} %get-tuple-element.17, bf16[1,24,4,8,640]{4,1,3,2,0:T(8,128)(2,1)S(1)} %get-tuple-element.18, ...), kind=kLoop, calls=%fused_computation.1 | loop fusion | flops 9216000 | bytes 7372800 | tf_op jit(solution)/shard_map/concatenate | solution.py:18
  37.7 3.3 %fusion.35 = bf16[24,6,10,640]{3,0,2,1:T(8,128)(2,1)S(1)} fusion(bf16[2,24,6,10,640]{4,1,3,2,0:T(8,128)(2,1)S(1)} %pad_maximum_fusion, f32[640]{0:T(1024)S(1)} %copy-done.15, f32[640]{0:T(1024)S(1)} %copy-done.16, f32[24,640]{1,0:T(8,128)S(1)} %mul.128, f32[24,640]{1,0:T(8,128)S(1)} %sub.69, f32[6,10]{1,0:T(8,128)S(1)} %and_convert_fusion, ...), kind=kOutput, calls=%fused_computation.46 | convolution fusion | flops 1190195200 | bytes 3825664 | tf_op jit(solution)/shard_map/dot_general | solution.py:72
  41.1 1.3 %collective-permute-start.6 = (bf16[3,3,80,640]{3,2,1,0:T(8,128)(2,1)}, bf16[3,3,80,640]{3,2,1,0:T(8,128)(2,1)S(1)}, u32[]{:S(2)}, u32[]{:S(2)}) collective-permute-start(bf16[3,3,80,640]{3,2,1,0:T(8,128)(2,1)} %collective-permute-done.5), channel_id=1, source_target_pairs={{0,16},{16,0},{1,17},{17,1},{2,18},{18,2},{3,19},{19,3},{4,20},{20... | collective-permute-start | bytes 2764808 | tf_op jit(solution)/shard_map/ppermute | solution.py:41
  42.4 0.2 fusion.37
  42.7 0.4 copy.63
  43.1 0.3 copy-done.2
  43.5 3.3 %fusion.45 = bf16[24,6,10,640]{3,0,2,1:T(8,128)(2,1)S(1)} fusion(f32[6,10]{1,0:T(8,128)S(1)} %and_convert_fusion, f32[640]{0:T(1024)S(1)} %copy-done.13, f32[640]{0:T(1024)S(1)} %copy-done.14, f32[24,640]{1,0:T(8,128)S(1)} %mul.115, f32[24,640]{1,0:T(8,128)S(1)} %copy-done.2, s32[640]{0:T(1024)S(1)} %copy-done.8, ...), kind=kOutput, calls=%fused_computation.57 | convolution fusion | flops 1191116800 | bytes 3825664 | tf_op jit(solution)/shard_map/dot_general | solution.py:72
  46.8 1.5 %collective-permute-start.7 = (bf16[3,3,80,640]{3,2,1,0:T(8,128)(2,1)}, bf16[3,3,80,640]{3,2,1,0:T(8,128)(2,1)S(1)}, u32[]{:S(2)}, u32[]{:S(2)}) collective-permute-start(bf16[3,3,80,640]{3,2,1,0:T(8,128)(2,1)} %collective-permute-done.5), channel_id=1, source_target_pairs={{0,4},{4,0},{8,12},{12,8},{1,5},{5,1},{9,13},{13,9},{2,6},{6,2},{1... | collective-permute-start | bytes 2764808 | tf_op jit(solution)/shard_map/ppermute | solution.py:42
  48.3 14.9 %collective-permute-done.10 = bf16[3,3,80,640]{3,2,1,0:T(8,128)(2,1)S(1)} collective-permute-done((bf16[3,3,80,640]{3,2,1,0:T(8,128)(2,1)S(1)}, bf16[3,3,80,640]{3,2,1,0:T(8,128)(2,1)S(1)}, u32[]{:S(2)}, u32[]{:S(2)}) %collective-permute-start.10) | collective-permute-done | bytes 921632 | tf_op jit(solution)/shard_map/ppermute | solution.py:39
  63.2 1.2 %collective-permute-start.11 = (bf16[3,3,80,640]{3,2,1,0:T(8,128)(2,1)S(1)}, bf16[3,3,80,640]{3,2,1,0:T(8,128)(2,1)S(1)}, u32[]{:S(2)}, u32[]{:S(2)}) collective-permute-start(bf16[3,3,80,640]{3,2,1,0:T(8,128)(2,1)S(1)} %collective-permute-done.10), channel_id=1, source_target_pairs={{0,16},{16,0},{1,17},{17,1},{2,18},{18,2},{3,19},{19,3},{4,20},{20... | collective-permute-start | bytes 2764808 | tf_op jit(solution)/shard_map/ppermute | solution.py:41
  64.4 0.3 collective-permute-start.12
  64.8 0.2 collective-permute-start.8
  65.0 6.0 %fusion = f32[24,4,8,640]{3,0,2,1:T(8,128)S(1)} fusion(bf16[3,3,160,640]{3,2,1,0:T(8,128)(2,1)} %collective-permute-done.4, bf16[3,3,160,640]{3,2,1,0:T(8,128)(2,1)} %param.25, bf16[24,6,10,640]{3,0,2,1:T(8,128)(2,1)S(1)} %fusion.45), kind=kOutput, calls=%fused_computation.2 | convolution fusion | flops 2838528000 | bytes 6758400 | tf_op jit(solution)/shard_map/conv_general_dilated | solution.py:81
  70.9 14.3 %collective-permute-done.11 = bf16[3,3,80,640]{3,2,1,0:T(8,128)(2,1)S(1)} collective-permute-done((bf16[3,3,80,640]{3,2,1,0:T(8,128)(2,1)S(1)}, bf16[3,3,80,640]{3,2,1,0:T(8,128)(2,1)S(1)}, u32[]{:S(2)}, u32[]{:S(2)}) %collective-permute-start.11) | collective-permute-done | bytes 921632 | tf_op jit(solution)/shard_map/ppermute | solution.py:41
  85.2 0.8 collective-permute-start.13
  86.1 6.0 %multiply_convert_fusion.1 = bf16[24,4,8,640]{3,0,2,1:T(8,128)(2,1)S(1)} fusion(f32[24,4,8,640]{3,0,2,1:T(8,128)S(1)} %fusion, bf16[3,3,80,640]{3,2,1,0:T(8,128)(2,1)S(1)} %collective-permute-done.8, bf16[3,3,80,640]{3,2,1,0:T(8,128)(2,1)S(1)} %collective-permute-done.7, bf16[3,3,80,640]{3,2,1,0:T(8,128)(2,1)S(1)} %collective-permute-done.6, ...), kind=kOutput, calls=%fused_computation.45 | convolution fusion | flops 2851799040 | bytes 7938048 | tf_op jit(solution)/shard_map/conv_general_dilated | solution.py:81
  92.1 1.1 fusion.59
  93.2 1.2 %fusion.58 = (bf16[24,6,6,640]{3,2,1,0:T(8,128)(2,1)S(1)}, bf16[24,6,6,640]{3,2,1,0:T(8,128)(2,1)S(1)}) fusion(bf16[24,4,8,640]{3,2,1,0:T(8,128)(2,1)S(1)} %fusion.59, bf16[24,6,10,640]{3,2,1,0:T(8,128)(2,1)S(1)} %copy.63, pred[6,6]{1,0:T(8,128)(4,1)S(1)} %broadcast_and_fusion), kind=kLoop, calls=%fused_computation.65 | loop fusion | flops 1105920 | bytes 5406756 | tf_op jit(solution)/shard_map/jit(_where)/select_n | solution.py:175
  94.4 2.1 %pad_maximum_fusion.1 = (bf16[24,6,12,320]{3,2,1,0:T(8,128)(2,1)S(1)}, bf16[24,6,12,320]{3,2,1,0:T(8,128)(2,1)S(1)}) fusion(bf16[24,6,6,640]{3,2,1,0:T(8,128)(2,1)S(1)} %get-tuple-element.7, bf16[24,6,6,640]{3,2,1,0:T(8,128)(2,1)S(1)} %get-tuple-element.8), kind=kLoop, calls=%fused_computation.59 | loop fusion | flops 4423680 | bytes 4423680 | tf_op jit(solution)/shard_map/concatenate | solution.py:176
  96.5 6.5 %fusion.12 = f32[24,4,10,640]{3,0,2,1:T(8,128)S(1)} fusion(bf16[3,3,160,640]{3,2,1,0:T(8,128)(2,1)} %collective-permute-done.9, bf16[3,3,160,640]{3,2,1,0:T(8,128)(2,1)S(1)} %copy-done.1, bf16[24,6,12,320]{3,2,1,0:T(8,128)(2,1)S(1)} %get-tuple-element.10), kind=kOutput, calls=%fused_computation.14 | convolution fusion | flops 3546316800 | bytes 7249920 | tf_op jit(solution)/shard_map/conv_general_dilated | solution.py:81
  103.0 5.3 %fusion.47 = f32[24,4,10,640]{3,0,2,1:T(8,128)S(1)} fusion(f32[24,4,10,640]{3,0,2,1:T(8,128)S(1)} %fusion.12, bf16[3,3,80,640]{3,2,1,0:T(8,128)(2,1)S(1)} %collective-permute-done.13, bf16[3,3,80,640]{3,2,1,0:T(8,128)(2,1)S(1)} %collective-permute-done.12, bf16[3,3,80,640]{3,2,1,0:T(8,128)(2,1)S(1)} %collective-permute-done.11, ...), kind=kOutput, calls=%fused_computation.60 | convolution fusion | flops 3554304000 | bytes 9707520 | tf_op jit(solution)/shard_map/conv_general_dilated | solution.py:81
  108.6 0.5 copy-done.10
  109.1 0.5 copy-done
  109.6 0.6 fusion.66
  110.2 1.1 copy.49
  (53 shorter events, 1.0 us)
Async XLA Ops:
  2.2 13.1 %copy-start.7 = (s32[24,16]{0,1:T(8,128)S(1)}, s32[24,16]{0,1:T(8,128)}, u32[]{:S(2)}) copy-start(s32[24,16]{0,1:T(8,128)} %param.20) | copy-start | bytes 4612
  3.1 24.5 %copy-start.3 = (f32[24,32]{1,0:T(8,128)S(1)}, f32[24,32]{1,0:T(8,128)}, u32[]{:S(2)}) copy-start(f32[24,32]{1,0:T(8,128)} %param.22) | copy-start | bytes 9220
  3.1 12.9 %collective-permute-start = (bf16[2,24,1,8,640]{4,1,3,2,0:T(8,128)(2,1)}, bf16[2,24,1,8,640]{4,1,3,2,0:T(8,128)(2,1)S(1)}, u32[]{:S(2)}, u32[]{:S(2)}) collective-permute-start(bf16[2,24,1,8,640]{4,1,3,2,0:T(8,128)(2,1)} %get-tuple-element.15), channel_id=1, source_target_pairs={{0,4},{4,8},{8,12},{1,5},{5,9},{9,13},{2,6},{6,10},{10,14},{3,7},{... | collective-permute-start | bytes 1474568 | tf_op jit(solution)/shard_map/ppermute | solution.py:14
  7.7 13.0 %collective-permute-start.1 = (bf16[2,24,1,8,640]{4,1,3,2,0:T(8,128)(2,1)S(1)}, bf16[2,24,1,8,640]{4,1,3,2,0:T(8,128)(2,1)S(1)}, u32[]{:S(2)}, u32[]{:S(2)}) collective-permute-start(bf16[2,24,1,8,640]{4,1,3,2,0:T(8,128)(2,1)S(1)} %get-tuple-element.16), channel_id=1, source_target_pairs={{4,0},{8,4},{12,8},{5,1},{9,5},{13,9},{6,2},{10,6},{14,10},{7,3},{... | collective-permute-start | bytes 1474568 | tf_op jit(solution)/shard_map/ppermute | solution.py:17
  9.6 54.8 %collective-permute-start.4 = (bf16[3,3,160,640]{3,2,1,0:T(8,128)(2,1)}, bf16[3,3,160,640]{3,2,1,0:T(8,128)(2,1)}, u32[]{:S(2)}, u32[]{:S(2)}) collective-permute-start(bf16[3,3,160,640]{3,2,1,0:T(8,128)(2,1)} %param.25), channel_id=1, source_target_pairs={{0,4},{4,0},{8,12},{12,8},{1,5},{5,1},{9,13},{13,9},{2,6},{6,2},{1... | collective-permute-start | bytes 5529608 | tf_op jit(solution)/shard_map/ppermute | solution.py:34
  9.7 18.2 %copy-start.4 = (f32[24,32]{1,0:T(8,128)S(1)}, f32[24,32]{1,0:T(8,128)}, u32[]{:S(2)}) copy-start(f32[24,32]{1,0:T(8,128)} %param.21) | copy-start | bytes 9220
  11.9 17.1 %copy-start.5 = (f32[24,32]{1,0:T(8,128)S(1)}, f32[24,32]{1,0:T(8,128)}, u32[]{:S(2)}) copy-start(f32[24,32]{1,0:T(8,128)} %param.29) | copy-start | bytes 9220
  11.9 29.1 %collective-permute-start.5 = (bf16[3,3,80,640]{3,2,1,0:T(8,128)(2,1)}, bf16[3,3,80,640]{3,2,1,0:T(8,128)(2,1)}, u32[]{:S(2)}, u32[]{:S(2)}) collective-permute-start(bf16[3,3,80,640]{3,2,1,0:T(8,128)(2,1)} %dynamic-slice_bitcast_fusion.1), channel_id=1, source_target_pairs={{8,0},{12,4},{0,8},{4,12},{9,1},{13,5},{1,9},{5,13},{10,2},{14,6},... | collective-permute-start | bytes 2764808 | tf_op jit(solution)/shard_map/ppermute | solution.py:39
  13.7 82.7 %collective-permute-start.9 = (bf16[3,3,160,640]{3,2,1,0:T(8,128)(2,1)}, bf16[3,3,160,640]{3,2,1,0:T(8,128)(2,1)}, u32[]{:S(2)}, u32[]{:S(2)}) collective-permute-start(bf16[3,3,160,640]{3,2,1,0:T(8,128)(2,1)} %param.32), channel_id=1, source_target_pairs={{0,4},{4,0},{8,12},{12,8},{1,5},{5,1},{9,13},{13,9},{2,6},{6,2},{1... | collective-permute-start | bytes 5529608 | tf_op jit(solution)/shard_map/ppermute | solution.py:34
  16.0 13.4 %copy-start.6 = (f32[24,32]{1,0:T(8,128)S(1)}, f32[24,32]{1,0:T(8,128)}, u32[]{:S(2)}) copy-start(f32[24,32]{1,0:T(8,128)} %param.28) | copy-start | bytes 9220
  21.8 10.0 %collective-permute-start.2 = (bf16[2,24,6,1,640]{4,1,3,2,0:T(8,128)(2,1)}, bf16[2,24,6,1,640]{4,1,3,2,0:T(8,128)(2,1)}, u32[]{:S(2)}, u32[]{:S(2)}) collective-permute-start(bf16[2,24,6,1,640]{4,1,3,2,0:T(8,128)(2,1)} %get-tuple-element.11), channel_id=1, source_target_pairs={{0,1},{1,2},{2,3},{4,5},{5,6},{6,7},{8,9},{9,10},{10,11},{12,13},{... | collective-permute-start | bytes 1105928 | tf_op jit(solution)/shard_map/ppermute | solution.py:14
  25.7 9.0 %collective-permute-start.3 = (bf16[2,24,6,1,640]{4,1,3,2,0:T(8,128)(2,1)}, bf16[2,24,6,1,640]{4,1,3,2,0:T(8,128)(2,1)}, u32[]{:S(2)}, u32[]{:S(2)}) collective-permute-start(bf16[2,24,6,1,640]{4,1,3,2,0:T(8,128)(2,1)} %get-tuple-element.12), channel_id=1, source_target_pairs={{1,0},{2,1},{3,2},{5,4},{6,5},{7,6},{9,8},{10,9},{11,10},{13,12},{... | collective-permute-start | bytes 1105928 | tf_op jit(solution)/shard_map/ppermute | solution.py:17
  29.1 1.9 %copy-start.11 = (pred[10]{0:T(512)(128)(4,1)S(1)}, pred[10]{0:T(512)(128)(4,1)}, u32[]{:S(2)}) copy-start(pred[10]{0:T(512)(128)(4,1)} %compare_and_fusion) | copy-start | bytes 34
  31.7 5.9 %copy-start.8 = (s32[640]{0:T(1024)S(1)}, s32[640]{0:T(1024)}, u32[]{:S(2)}) copy-start(s32[640]{0:T(1024)} %fusion.83) | copy-start | bytes 7684
  31.7 5.9 %copy-start.15 = (f32[640]{0:T(1024)S(1)}, f32[640]{0:T(1024)}, u32[]{:S(2)}) copy-start(f32[640]{0:T(1024)} %param.31) | copy-start | bytes 7684
  31.7 6.0 %copy-start.16 = (f32[640]{0:T(1024)S(1)}, f32[640]{0:T(1024)}, u32[]{:S(2)}) copy-start(f32[640]{0:T(1024)} %param.30) | copy-start | bytes 7684
  41.0 22.2 %collective-permute-start.10 = (bf16[3,3,80,640]{3,2,1,0:T(8,128)(2,1)S(1)}, bf16[3,3,80,640]{3,2,1,0:T(8,128)(2,1)S(1)}, u32[]{:S(2)}, u32[]{:S(2)}) collective-permute-start(bf16[3,3,80,640]{3,2,1,0:T(8,128)(2,1)S(1)} %dynamic-slice_bitcast_fusion), channel_id=1, source_target_pairs={{8,0},{12,4},{0,8},{4,12},{9,1},{13,5},{1,9},{5,13},{10,2},{14,6},... | collective-permute-start | bytes 2764808 | tf_op jit(solution)/shard_map/ppermute | solution.py:39
  41.1 23.7 %collective-permute-start.6 = (bf16[3,3,80,640]{3,2,1,0:T(8,128)(2,1)}, bf16[3,3,80,640]{3,2,1,0:T(8,128)(2,1)S(1)}, u32[]{:S(2)}, u32[]{:S(2)}) collective-permute-start(bf16[3,3,80,640]{3,2,1,0:T(8,128)(2,1)} %collective-permute-done.5), channel_id=1, source_target_pairs={{0,16},{16,0},{1,17},{17,1},{2,18},{18,2},{3,19},{19,3},{4,20},{20... | collective-permute-start | bytes 2764808 | tf_op jit(solution)/shard_map/ppermute | solution.py:41
  42.6 0.8 copy-start.2
  42.6 0.8 copy-start.13
  42.7 0.8 copy-start.14
  46.8 39.3 %copy-start.12 = (f32[24,640]{1,0:T(8,128)S(1)}, f32[24,640]{1,0:T(8,128)}, u32[]{:S(2)}) copy-start(f32[24,640]{1,0:T(8,128)} %param.27) | copy-start | bytes 184324
  46.8 39.3 %copy-start.17 = (f32[640]{0:T(1024)S(1)}, f32[640]{0:T(1024)}, u32[]{:S(2)}) copy-start(f32[640]{0:T(1024)} %param.26) | copy-start | bytes 7684
  46.8 39.3 %collective-permute-start.7 = (bf16[3,3,80,640]{3,2,1,0:T(8,128)(2,1)}, bf16[3,3,80,640]{3,2,1,0:T(8,128)(2,1)S(1)}, u32[]{:S(2)}, u32[]{:S(2)}) collective-permute-start(bf16[3,3,80,640]{3,2,1,0:T(8,128)(2,1)} %collective-permute-done.5), channel_id=1, source_target_pairs={{0,4},{4,0},{8,12},{12,8},{1,5},{5,1},{9,13},{13,9},{2,6},{6,2},{1... | collective-permute-start | bytes 2764808 | tf_op jit(solution)/shard_map/ppermute | solution.py:42
  63.2 22.0 %collective-permute-start.11 = (bf16[3,3,80,640]{3,2,1,0:T(8,128)(2,1)S(1)}, bf16[3,3,80,640]{3,2,1,0:T(8,128)(2,1)S(1)}, u32[]{:S(2)}, u32[]{:S(2)}) collective-permute-start(bf16[3,3,80,640]{3,2,1,0:T(8,128)(2,1)S(1)} %collective-permute-done.10), channel_id=1, source_target_pairs={{0,16},{16,0},{1,17},{17,1},{2,18},{18,2},{3,19},{19,3},{4,20},{20... | collective-permute-start | bytes 2764808 | tf_op jit(solution)/shard_map/ppermute | solution.py:41
  64.4 38.6 %collective-permute-start.12 = (bf16[3,3,80,640]{3,2,1,0:T(8,128)(2,1)S(1)}, bf16[3,3,80,640]{3,2,1,0:T(8,128)(2,1)S(1)}, u32[]{:S(2)}, u32[]{:S(2)}) collective-permute-start(bf16[3,3,80,640]{3,2,1,0:T(8,128)(2,1)S(1)} %collective-permute-done.10), channel_id=1, source_target_pairs={{0,4},{4,0},{8,12},{12,8},{1,5},{5,1},{9,13},{13,9},{2,6},{6,2},{1... | collective-permute-start | bytes 2764808 | tf_op jit(solution)/shard_map/ppermute | solution.py:42
  64.8 21.3 %collective-permute-start.8 = (bf16[3,3,80,640]{3,2,1,0:T(8,128)(2,1)S(1)}, bf16[3,3,80,640]{3,2,1,0:T(8,128)(2,1)S(1)}, u32[]{:S(2)}, u32[]{:S(2)}) collective-permute-start(bf16[3,3,80,640]{3,2,1,0:T(8,128)(2,1)S(1)} %collective-permute-done.6), channel_id=1, source_target_pairs={{0,4},{4,0},{8,12},{12,8},{1,5},{5,1},{9,13},{13,9},{2,6},{6,2},{1... | collective-permute-start | bytes 2764808 | tf_op jit(solution)/shard_map/ppermute | solution.py:43
  85.2 17.8 %collective-permute-start.13 = (bf16[3,3,80,640]{3,2,1,0:T(8,128)(2,1)S(1)}, bf16[3,3,80,640]{3,2,1,0:T(8,128)(2,1)S(1)}, u32[]{:S(2)}, u32[]{:S(2)}) collective-permute-start(bf16[3,3,80,640]{3,2,1,0:T(8,128)(2,1)S(1)} %collective-permute-done.11), channel_id=1, source_target_pairs={{0,4},{4,0},{8,12},{12,8},{1,5},{5,1},{9,13},{13,9},{2,6},{6,2},{1... | collective-permute-start | bytes 2764808 | tf_op jit(solution)/shard_map/ppermute | solution.py:43
  94.4 2.1 %copy-start.1 = (bf16[3,3,160,640]{3,2,1,0:T(8,128)(2,1)S(1)}, bf16[3,3,160,640]{3,2,1,0:T(8,128)(2,1)}, u32[]{:S(2)}) copy-start(bf16[3,3,160,640]{3,2,1,0:T(8,128)(2,1)} %param.32) | copy-start | bytes 5529604
  108.4 0.7 copy-start.10
  108.4 1.2 %copy-start = (bf16[24,4,8,640]{3,2,1,0:T(8,128)(2,1)S(1)}, bf16[24,4,8,640]{3,2,1,0:T(8,128)(2,1)}, u32[]{:S(2)}) copy-start(bf16[24,4,8,640]{3,2,1,0:T(8,128)(2,1)} %param.19) | copy-start | bytes 2949124
  108.4 1.2 %copy-start.9 = (f32[640]{0:T(1024)S(1)}, f32[640]{0:T(1024)}, u32[]{:S(2)}) copy-start(f32[640]{0:T(1024)} %param.33) | copy-start | bytes 7684

commit v16 on v13

--- a/solution.py
+++ b/solution.py
@@ -45,7 +45,7 @@
                 jnp.concatenate([fetched, other], axis=2),
                 jnp.concatenate([relayed, other_relayed], axis=2),
             ]
-        wholes.append(jnp.concatenate(held, axis=2))
+        wholes.append(held)
     return wholes
 
 
@@ -75,6 +75,17 @@
 
 def conv_relative(activation, kernel, order):
     return conv_valid(to_relative(activation, order), kernel)
+
+
+def conv_parts(activation, kernels):
+    total = None
+    start = 0
+    for kernel in kernels:
+        depth = kernel.shape[2]
+        part = conv_valid(activation[..., start : start + depth], kernel)
+        total = part if total is None else total + part
+        start += depth
+    return total
 
 
 def conv_valid(activation, kernel):
@@ -116,7 +127,9 @@
     groups_total = norm1_mean.shape[1]
     per_group = channels // groups_total
 
-    first_whole, second_whole = gather_weights([conv1_weight, conv2_weight])
+    first_held, second_held = gather_weights([conv1_weight, conv2_weight])
+    first_parts = [jnp.concatenate(first_held[:2], axis=2)] + first_held[2:]
+    second_parts = [jnp.concatenate(second_held[:2], axis=2)] + second_held[2:]
     order = relative_order(channels)
 
     def expand(values):
@@ -142,8 +155,11 @@
         )
         * inside
     ).astype(jnp.bfloat16)
+    first_moved = to_relative(first_act, order)
     fresh_mid = (
-        conv_relative(first_act, first_whole, order) + conv1_bias + step_embed[:, None, None, :]
+        conv_parts(first_moved, first_parts)
+        + conv1_bias
+        + step_embed[:, None, None, :]
     )
 
     if tiles_down != 1:
@@ -164,7 +180,8 @@
     for tile_across in range(tiles_across):
         cut = slice(tile_across * TILE, tile_across * TILE + TILE + 2)
         windows.append(jnp.where(interior, fresh_pad[:, :, cut], cached_act[:, :, cut]))
-    wide_sum = conv_valid(jnp.concatenate(windows, axis=2), second_whole)
+    wide = jnp.concatenate(windows, axis=2)
+    wide_sum = conv_parts(wide, second_parts)
     stride = TILE + 2
     second_sum = jnp.concatenate(
         [wide_sum[:, :, t * stride : t * stride + TILE] for t in range(tiles_across)], axis=2

time: 123 us -> 112 us (0.911)
  local copies, waits for them, and re-layouts: 33.6 us -> 10.8 us
  waiting for transfers between devices: 26.7 us -> 34.3 us
  matrix products: 28.8 us -> 33.6 us
    ppermute x2, waiting for transfers between devices: 0.38 us -> 25 us  [gather_weights(): other = lax.ppermute(fetched, 'groups', y_pairs)]
    unnamed x50 -> x30, local copies, waits for them, and re-layouts: 23.1 us -> 1.43 us
    ppermute x2, waiting for transfers between devices: 13.7 us -> 0.01 us  [padded_2(): lax.ppermute(lax.slice_in_dim(block, block.shape[dim] - width, None, axis...]
    ppermute x2, waiting for transfers between devices: 10.6 us -> 0.01 us  [gather_weights(): fetched = lax.ppermute(mine, 'row', pairs)]
    ppermute x2, waiting for transfers between devices: 1.99 us -> 9.3 us  [padded_2(): lax.ppermute(lax.slice_in_dim(block, 0, width, axis=dim), axis, backward)]
    ppermute x2, starting transfers between devices: 6.45 us -> 1.59 us  [gather_weights(): relayed = lax.ppermute(fetched, 'row', mate_pairs)]
    dot_general x2 -> x3, matrix products: 4.33 us -> 7.62 us  [to_relative(): moved = jnp.dot(activation, chooser, preferred_element_type=jnp.float32)]
    ppermute x2, starting transfers between devices: 5.73 us -> 8.97 us  [padded_2(): lax.ppermute(lax.slice_in_dim(block, block.shape[dim] - width, None, axis...]
  transfers between devices with their start and end apart: 14 -> 14, of which waited for: 5 -> 4; matrix products, arithmetic and copies ran while one was open for 50% -> 41% of each run, Pallas kernels for 0% -> 0%
where the time goes in v16:
time: 112 us; the launch traced here: 111 us
  waiting for transfers between devices  34.3 us (31%)
  matrix products  33.6 us (30%)
  starting transfers between devices  21.1 us (19%)
  local copies, waits for them, and re-layouts  10.8 us (10%)
  other arithmetic  10.7 us (10%)
    conv_general_dilated x6, matrix products, conv_valid(): lax.conv_general_dilated(activation, kernel, window_strides=(1, 1), paddi...  26 us
    ppermute x2, waiting for transfers between devices, gather_weights(): other = lax.ppermute(fetched, 'groups', y_pairs)  25 us
    ppermute x2, waiting for transfers between devices, padded_2(): lax.ppermute(lax.slice_in_dim(block, 0, width, axis=dim), axis, backward)  9.3 us
    ppermute x2, starting transfers between devices, padded_2(): lax.ppermute(lax.slice_in_dim(block, block.shape[dim] - width, None, axis...  8.97 us
    dot_general x3, matrix products, to_relative(): moved = jnp.dot(activation, chooser, preferred_element_type=jnp.float32)  7.62 us
    squeeze x2, local copies, waits for them, and re-layouts, gather_weights(): mine = lax.dynamic_index_in_dim(halves, parity, axis=2, keepdims=False)  3.46 us
    ppermute x2, starting transfers between devices, padded_2(): lax.ppermute(lax.slice_in_dim(block, 0, width, axis=dim), axis, backward)  3.2 us
    concatenate x1, other arithmetic, padded_2(): block = jnp.concatenate([low, block, high], axis=dim)  2.97 us
  transfers between devices with their start and end apart: 14, of which 4 were waited for; matrix products, arithmetic and copies ran while one was open for 41% of the time, Pallas kernels for 0%

profile of v16, /device:TPU:1, one launch (start us, length us, event | category | flops | bytes accessed | tf_op | source)
XLA Modules:
  0.0 111.1 jit_solution(2099923270569889977)
XLA Ops:
  0.0 2.1 %copy_bitcast_fusion = (bf16[1,24,4,8,640]{4,1,3,2,0:T(8,128)(2,1)S(1)}, bf16[1,24,4,8,640]{4,1,3,2,0:T(8,128)(2,1)S(1)}) fusion(bf16[24,4,8,640]{3,2,1,0:T(8,128)(2,1)} %param.18, bf16[24,4,8,640]{3,2,1,0:T(8,128)(2,1)} %param.17), kind=kLoop, calls=%fused_computation.74 | loop fusion | bytes 3932160 | tf_op jit(solution)/shard_map/stack | solution.py:138
  2.2 0.9 pad_maximum_fusion.3
  3.1 4.5 %collective-permute-start = (bf16[2,24,1,8,640]{4,1,3,2,0:T(8,128)(2,1)}, bf16[2,24,1,8,640]{4,1,3,2,0:T(8,128)(2,1)S(1)}, u32[]{:S(2)}, u32[]{:S(2)}) collective-permute-start(bf16[2,24,1,8,640]{4,1,3,2,0:T(8,128)(2,1)} %get-tuple-element.15), channel_id=1, source_target_pairs={{0,4},{4,8},{8,12},{1,5},{5,9},{9,13},{2,6},{6,10},{10,14},{3,7},{... | collective-permute-start | bytes 1474568 | tf_op jit(solution)/shard_map/ppermute | solution.py:14
  7.6 1.9 %collective-permute-start.1 = (bf16[2,24,1,8,640]{4,1,3,2,0:T(8,128)(2,1)S(1)}, bf16[2,24,1,8,640]{4,1,3,2,0:T(8,128)(2,1)S(1)}, u32[]{:S(2)}, u32[]{:S(2)}) collective-permute-start(bf16[2,24,1,8,640]{4,1,3,2,0:T(8,128)(2,1)S(1)} %get-tuple-element.16), channel_id=1, source_target_pairs={{4,0},{8,4},{12,8},{5,1},{9,5},{13,9},{6,2},{10,6},{14,10},{7,3},{... | collective-permute-start | bytes 1474568 | tf_op jit(solution)/shard_map/ppermute | solution.py:17
  9.6 2.2 %dynamic-slice_bitcast_fusion.1 = bf16[3,3,80,640]{3,2,1,0:T(8,128)(2,1)} fusion(bf16[3,3,2,80,640]{4,3,2,1,0:T(8,128)(2,1)} %bitcast.6, s32[]{:T(128)S(6)} %select_n.125), kind=kLoop, calls=%fused_computation.77 | loop fusion | bytes 1843204 | tf_op jit(solution)/shard_map/jit(dynamic_index_in_dim)/squeeze | solution.py:33
  11.8 1.8 %collective-permute-start.5 = (bf16[3,3,80,640]{3,2,1,0:T(8,128)(2,1)}, bf16[3,3,80,640]{3,2,1,0:T(8,128)(2,1)}, u32[]{:S(2)}, u32[]{:S(2)}) collective-permute-start(bf16[3,3,80,640]{3,2,1,0:T(8,128)(2,1)} %dynamic-slice_bitcast_fusion.1), channel_id=1, source_target_pairs={{8,0},{12,4},{0,8},{4,12},{9,1},{13,5},{1,9},{5,13},{10,2},{14,6},... | collective-permute-start | bytes 2764808 | tf_op jit(solution)/shard_map/ppermute | solution.py:39
  13.6 0.3 collective-permute-start.9
  14.2 6.4 %collective-permute-done.1 = bf16[2,24,1,8,640]{4,1,3,2,0:T(8,128)(2,1)S(1)} collective-permute-done((bf16[2,24,1,8,640]{4,1,3,2,0:T(8,128)(2,1)S(1)}, bf16[2,24,1,8,640]{4,1,3,2,0:T(8,128)(2,1)S(1)}, u32[]{:S(2)}, u32[]{:S(2)}) %collective-permute-start.1) | collective-permute-done | bytes 491552 | tf_op jit(solution)/shard_map/ppermute | solution.py:17
  20.6 1.0 pad_maximum_fusion.7
  21.6 4.5 %collective-permute-start.2 = (bf16[2,24,6,1,640]{4,1,3,2,0:T(8,128)(2,1)}, bf16[2,24,6,1,640]{4,1,3,2,0:T(8,128)(2,1)}, u32[]{:S(2)}, u32[]{:S(2)}) collective-permute-start(bf16[2,24,6,1,640]{4,1,3,2,0:T(8,128)(2,1)} %get-tuple-element.11), channel_id=1, source_target_pairs={{0,1},{1,2},{2,3},{4,5},{5,6},{6,7},{8,9},{9,10},{10,11},{12,13},{... | collective-permute-start | bytes 1105928 | tf_op jit(solution)/shard_map/ppermute | solution.py:14
  26.1 1.3 %collective-permute-start.3 = (bf16[2,24,6,1,640]{4,1,3,2,0:T(8,128)(2,1)}, bf16[2,24,6,1,640]{4,1,3,2,0:T(8,128)(2,1)}, u32[]{:S(2)}, u32[]{:S(2)}) collective-permute-start(bf16[2,24,6,1,640]{4,1,3,2,0:T(8,128)(2,1)} %get-tuple-element.12), channel_id=1, source_target_pairs={{1,0},{2,1},{3,2},{5,4},{6,5},{7,6},{9,8},{10,9},{11,10},{13,12},{... | collective-permute-start | bytes 1105928 | tf_op jit(solution)/shard_map/ppermute | solution.py:17
  27.4 0.5 compare_and_fusion
  28.1 0.2 mul.115
  28.3 0.2 broadcast_in_dim.42
  28.5 0.8 sub.59
  29.5 0.2 mul.128
  29.7 0.2 broadcast_in_dim.79
  29.9 0.2 sub.69
  30.1 1.3 %dynamic-slice_bitcast_fusion = bf16[3,3,80,640]{3,2,1,0:T(8,128)(2,1)S(1)} fusion(bf16[3,3,2,80,640]{4,3,2,1,0:T(8,128)(2,1)} %bitcast.38, s32[]{:T(128)S(6)} %select_n.125), kind=kLoop, calls=%fused_computation.76 | loop fusion | bytes 1843204 | tf_op jit(solution)/shard_map/jit(dynamic_index_in_dim)/squeeze | solution.py:33
  31.4 0.7 and_convert_fusion
  32.1 2.9 %collective-permute-done.3 = bf16[2,24,6,1,640]{4,1,3,2,0:T(8,128)(2,1)} collective-permute-done((bf16[2,24,6,1,640]{4,1,3,2,0:T(8,128)(2,1)}, bf16[2,24,6,1,640]{4,1,3,2,0:T(8,128)(2,1)}, u32[]{:S(2)}, u32[]{:S(2)}) %collective-permute-start.3) | collective-permute-done | bytes 368672 | tf_op jit(solution)/shard_map/ppermute | solution.py:17
  35.0 3.0 %pad_maximum_fusion = bf16[2,24,6,10,640]{4,1,3,2,0:T(8,128)(2,1)S(1)} fusion(bf16[2,24,6,1,640]{4,1,3,2,0:T(8,128)(2,1)} %collective-permute-done.3, bf16[2,24,1,8,640]{4,1,3,2,0:T(8,128)(2,1)S(1)} %collective-permute-done.1, bf16[1,24,4,8,640]{4,1,3,2,0:T(8,128)(2,1)S(1)} %get-tuple-element.17, bf16[1,24,4,8,640]{4,1,3,2,0:T(8,128)(2,1)S(1)} %get-tuple-element.18, ...), kind=kLoop, calls=%fused_computation.1 | loop fusion | flops 9216000 | bytes 7372800 | tf_op jit(solution)/shard_map/concatenate | solution.py:18
  38.0 3.3 %fusion.19 = bf16[24,6,10,640]{3,0,2,1:T(8,128)(2,1)S(1)} fusion(bf16[2,24,6,10,640]{4,1,3,2,0:T(8,128)(2,1)S(1)} %pad_maximum_fusion, f32[640]{0:T(1024)S(1)} %copy-done.12, f32[640]{0:T(1024)S(1)} %copy-done.13, f32[24,640]{1,0:T(8,128)S(1)} %mul.128, f32[24,640]{1,0:T(8,128)S(1)} %sub.69, f32[6,10]{1,0:T(8,128)S(1)} %and_convert_fusion, s32[640]{0:T(1024)S(1)} %fusion.85), kind=kOutput, calls=%fused_computation.33 | convolution fusion | flops 1190195200 | bytes 3825664 | tf_op jit(solution)/shard_map/dot_general | solution.py:72
  41.3 1.3 %collective-permute-start.6 = (bf16[3,3,80,640]{3,2,1,0:T(8,128)(2,1)}, bf16[3,3,80,640]{3,2,1,0:T(8,128)(2,1)S(1)}, u32[]{:S(2)}, u32[]{:S(2)}) collective-permute-start(bf16[3,3,80,640]{3,2,1,0:T(8,128)(2,1)} %collective-permute-done.5), channel_id=1, source_target_pairs={{0,16},{16,0},{1,17},{17,1},{2,18},{18,2},{3,19},{19,3},{4,20},{20... | collective-permute-start | bytes 2764808 | tf_op jit(solution)/shard_map/ppermute | solution.py:41
  42.6 0.2 fusion.21
  42.9 0.4 copy.68
  43.4 0.3 copy-done.2
  43.7 3.3 %fusion.45 = bf16[24,6,10,640]{3,0,2,1:T(8,128)(2,1)S(1)} fusion(f32[6,10]{1,0:T(8,128)S(1)} %and_convert_fusion, f32[640]{0:T(1024)S(1)} %copy-done.10, f32[640]{0:T(1024)S(1)} %copy-done.11, f32[24,640]{1,0:T(8,128)S(1)} %mul.115, f32[24,640]{1,0:T(8,128)S(1)} %copy-done.2, s32[640]{0:T(1024)S(1)} %fusion.85, ...), kind=kOutput, calls=%fused_computation.60 | convolution fusion | flops 1191116800 | bytes 3825664 | tf_op jit(solution)/shard_map/dot_general | solution.py:72
  47.0 1.2 %collective-permute-start.7 = (bf16[3,3,80,640]{3,2,1,0:T(8,128)(2,1)}, bf16[3,3,80,640]{3,2,1,0:T(8,128)(2,1)S(1)}, u32[]{:S(2)}, u32[]{:S(2)}) collective-permute-start(bf16[3,3,80,640]{3,2,1,0:T(8,128)(2,1)} %collective-permute-done.5), channel_id=1, source_target_pairs={{0,4},{4,0},{8,12},{12,8},{1,5},{5,1},{9,13},{13,9},{2,6},{6,2},{1... | collective-permute-start | bytes 2764808 | tf_op jit(solution)/shard_map/ppermute | solution.py:42
  48.2 14.4 %collective-permute-done.6 = bf16[3,3,80,640]{3,2,1,0:T(8,128)(2,1)S(1)} collective-permute-done((bf16[3,3,80,640]{3,2,1,0:T(8,128)(2,1)}, bf16[3,3,80,640]{3,2,1,0:T(8,128)(2,1)S(1)}, u32[]{:S(2)}, u32[]{:S(2)}) %collective-permute-start.6) | collective-permute-done | bytes 921632 | tf_op jit(solution)/shard_map/ppermute | solution.py:41
  62.7 1.8 %collective-permute-start.8 = (bf16[3,3,80,640]{3,2,1,0:T(8,128)(2,1)S(1)}, bf16[3,3,80,640]{3,2,1,0:T(8,128)(2,1)S(1)}, u32[]{:S(2)}, u32[]{:S(2)}) collective-permute-start(bf16[3,3,80,640]{3,2,1,0:T(8,128)(2,1)S(1)} %collective-permute-done.6), channel_id=1, source_target_pairs={{0,4},{4,0},{8,12},{12,8},{1,5},{5,1},{9,13},{13,9},{2,6},{6,2},{1... | collective-permute-start | bytes 2764808 | tf_op jit(solution)/shard_map/ppermute | solution.py:43
  64.5 1.2 %collective-permute-start.11 = (bf16[3,3,80,640]{3,2,1,0:T(8,128)(2,1)S(1)}, bf16[3,3,80,640]{3,2,1,0:T(8,128)(2,1)S(1)}, u32[]{:S(2)}, u32[]{:S(2)}) collective-permute-start(bf16[3,3,80,640]{3,2,1,0:T(8,128)(2,1)S(1)} %collective-permute-done.10), channel_id=1, source_target_pairs={{0,16},{16,0},{1,17},{17,1},{2,18},{18,2},{3,19},{19,3},{4,20},{20... | collective-permute-start | bytes 2764808 | tf_op jit(solution)/shard_map/ppermute | solution.py:41
  65.7 3.7 %fusion.22 = f32[24,4,8,640]{3,0,2,1:T(8,128)S(1)} fusion(bf16[3,3,80,640]{3,2,1,0:T(8,128)(2,1)S(1)} %collective-permute-done.6, bf16[3,3,80,640]{3,2,1,0:T(8,128)(2,1)} %collective-permute-done.5, bf16[24,6,10,640]{3,0,2,1:T(8,128)(2,1)S(1)} %fusion.45), kind=kOutput, calls=%fused_computation.37 | convolution fusion | flops 1419264000 | bytes 4546560 | tf_op jit(solution)/shard_map/conv_general_dilated | solution.py:92
  69.5 0.3 collective-permute-start.12
  69.8 6.2 %fusion = f32[24,4,8,640]{3,0,2,1:T(8,128)S(1)} fusion(bf16[3,3,160,640]{3,2,1,0:T(8,128)(2,1)} %collective-permute-done.4, bf16[3,3,160,640]{3,2,1,0:T(8,128)(2,1)} %param.25, bf16[24,6,10,640]{3,0,2,1:T(8,128)(2,1)S(1)} %fusion.45), kind=kOutput, calls=%fused_computation.2 | convolution fusion | flops 2838528000 | bytes 6758400 | tf_op jit(solution)/shard_map/conv_general_dilated | solution.py:92
  76.0 10.5 %collective-permute-done.11 = bf16[3,3,80,640]{3,2,1,0:T(8,128)(2,1)S(1)} collective-permute-done((bf16[3,3,80,640]{3,2,1,0:T(8,128)(2,1)S(1)}, bf16[3,3,80,640]{3,2,1,0:T(8,128)(2,1)S(1)}, u32[]{:S(2)}, u32[]{:S(2)}) %collective-permute-start.11) | collective-permute-done | bytes 921632 | tf_op jit(solution)/shard_map/ppermute | solution.py:41
  86.5 0.8 collective-permute-start.13
  87.3 3.1 %multiply_convert_fusion.1 = bf16[24,4,8,640]{3,0,2,1:T(8,128)(2,1)S(1)} fusion(f32[24,4,8,640]{3,0,2,1:T(8,128)S(1)} %fusion, f32[24,4,8,640]{3,0,2,1:T(8,128)S(1)} %fusion.22, bf16[3,3,80,640]{3,2,1,0:T(8,128)(2,1)S(1)} %collective-permute-done.8, bf16[3,3,80,640]{3,2,1,0:T(8,128)(2,1)S(1)} %collective-permute-done.7, f32[640]{0:T(1024)S(1)} %copy-done.12, ...), kind=kOutput, calls=%fused_computation.32 | convolution fusion | flops 1425653760 | bytes 7692288 | tf_op jit(solution)/shard_map/conv_general_dilated | solution.py:92
  90.4 1.1 fusion.54
  91.5 1.2 %fusion.53 = (bf16[24,6,6,640]{3,2,1,0:T(8,128)(2,1)S(1)}, bf16[24,6,6,640]{3,2,1,0:T(8,128)(2,1)S(1)}) fusion(bf16[24,4,8,640]{3,2,1,0:T(8,128)(2,1)S(1)} %fusion.54, bf16[24,6,10,640]{3,2,1,0:T(8,128)(2,1)S(1)} %copy.68, pred[6,6]{1,0:T(8,128)(4,1)S(1)} %broadcast_and_fusion), kind=kLoop, calls=%fused_computation.66 | loop fusion | flops 1105920 | bytes 5406756 | tf_op jit(solution)/shard_map/jit(_where)/select_n | solution.py:182
  92.7 0.7 fusion.46
  93.3 1.8 %pad_maximum_fusion.1 = (bf16[24,6,12,160]{3,2,1,0:T(8,128)(2,1)S(1)}, bf16[24,6,12,160]{3,2,1,0:T(8,128)(2,1)S(1)}) fusion(bf16[24,6,6,640]{3,2,1,0:T(8,128)(2,1)S(1)} %get-tuple-element.7, bf16[24,6,6,640]{3,2,1,0:T(8,128)(2,1)S(1)} %get-tuple-element.8), kind=kLoop, calls=%fused_computation.70 | loop fusion | flops 2211840 | bytes 3317760 | tf_op jit(solution)/shard_map/concatenate | solution.py:183
  95.1 3.1 %fusion.30 = f32[24,4,10,640]{3,0,2,1:T(8,128)S(1)} fusion(bf16[3,3,80,640]{3,2,1,0:T(8,128)(2,1)S(1)} %collective-permute-done.11, bf16[3,3,80,640]{3,2,1,0:T(8,128)(2,1)S(1)} %collective-permute-done.10, bf16[24,6,12,160]{3,2,1,0:T(8,128)(2,1)S(1)} %get-tuple-element.10), kind=kOutput, calls=%fused_computation.45 | convolution fusion | flops 1773158400 | bytes 4853760 | tf_op jit(solution)/shard_map/conv_general_dilated | solution.py:92
  98.3 6.8 %fusion.4 = f32[24,4,10,640]{3,0,2,1:T(8,128)S(1)} fusion(bf16[3,3,160,640]{3,2,1,0:T(8,128)(2,1)} %collective-permute-done.9, bf16[3,3,160,640]{3,2,1,0:T(8,128)(2,1)S(1)} %copy-done.1, bf16[24,6,12,320]{3,2,1,0:T(8,128)(2,1)S(1)} %fusion.46), kind=kOutput, calls=%fused_computation.6 | convolution fusion | flops 3546316800 | bytes 7249920 | tf_op jit(solution)/shard_map/conv_general_dilated | solution.py:92
  105.1 3.1 %add_add_fusion = f32[24,4,10,640]{3,0,2,1:T(8,128)S(1)} fusion(f32[24,4,10,640]{3,0,2,1:T(8,128)S(1)} %fusion.4, f32[24,4,10,640]{3,0,2,1:T(8,128)S(1)} %fusion.30, bf16[3,3,80,640]{3,2,1,0:T(8,128)(2,1)S(1)} %collective-permute-done.13, bf16[3,3,80,640]{3,2,1,0:T(8,128)(2,1)S(1)} %collective-permute-done.12, bf16[24,6,12,160]{3,2,1,0:T(8,128)(2,1)S(1)} %get-tuple-element.9), kind=kOutput, calls=%fused_computation.28 | convolution fusion | flops 1774387200 | bytes 9768960 | tf_op jit(solution)/shard_map/conv_general_dilated | solution.py:92
  108.4 1.0 copy-done
  109.4 0.6 fusion.64
  110.0 1.1 copy.52
  (50 shorter events, 0.9 us)
Async XLA Ops:
  2.2 11.9 %copy-start.7 = (s32[24,16]{0,1:T(8,128)S(1)}, s32[24,16]{0,1:T(8,128)}, u32[]{:S(2)}) copy-start(s32[24,16]{0,1:T(8,128)} %param.20) | copy-start | bytes 4612
  3.1 11.1 %collective-permute-start = (bf16[2,24,1,8,640]{4,1,3,2,0:T(8,128)(2,1)}, bf16[2,24,1,8,640]{4,1,3,2,0:T(8,128)(2,1)S(1)}, u32[]{:S(2)}, u32[]{:S(2)}) collective-permute-start(bf16[2,24,1,8,640]{4,1,3,2,0:T(8,128)(2,1)} %get-tuple-element.15), channel_id=1, source_target_pairs={{0,4},{4,8},{8,12},{1,5},{5,9},{9,13},{2,6},{6,10},{10,14},{3,7},{... | collective-permute-start | bytes 1474568 | tf_op jit(solution)/shard_map/ppermute | solution.py:14
  7.6 13.0 %collective-permute-start.1 = (bf16[2,24,1,8,640]{4,1,3,2,0:T(8,128)(2,1)S(1)}, bf16[2,24,1,8,640]{4,1,3,2,0:T(8,128)(2,1)S(1)}, u32[]{:S(2)}, u32[]{:S(2)}) collective-permute-start(bf16[2,24,1,8,640]{4,1,3,2,0:T(8,128)(2,1)S(1)} %get-tuple-element.16), channel_id=1, source_target_pairs={{4,0},{8,4},{12,8},{5,1},{9,5},{13,9},{6,2},{10,6},{14,10},{7,3},{... | collective-permute-start | bytes 1474568 | tf_op jit(solution)/shard_map/ppermute | solution.py:17
  9.5 60.0 %collective-permute-start.4 = (bf16[3,3,160,640]{3,2,1,0:T(8,128)(2,1)}, bf16[3,3,160,640]{3,2,1,0:T(8,128)(2,1)}, u32[]{:S(2)}, u32[]{:S(2)}) collective-permute-start(bf16[3,3,160,640]{3,2,1,0:T(8,128)(2,1)} %param.25), channel_id=1, source_target_pairs={{0,4},{4,0},{8,12},{12,8},{1,5},{5,1},{9,13},{13,9},{2,6},{6,2},{1... | collective-permute-start | bytes 5529608 | tf_op jit(solution)/shard_map/ppermute | solution.py:34
  11.8 16.1 %copy-start.3 = (f32[24,32]{1,0:T(8,128)S(1)}, f32[24,32]{1,0:T(8,128)}, u32[]{:S(2)}) copy-start(f32[24,32]{1,0:T(8,128)} %param.22) | copy-start | bytes 9220
  11.8 29.5 %collective-permute-start.5 = (bf16[3,3,80,640]{3,2,1,0:T(8,128)(2,1)}, bf16[3,3,80,640]{3,2,1,0:T(8,128)(2,1)}, u32[]{:S(2)}, u32[]{:S(2)}) collective-permute-start(bf16[3,3,80,640]{3,2,1,0:T(8,128)(2,1)} %dynamic-slice_bitcast_fusion.1), channel_id=1, source_target_pairs={{8,0},{12,4},{0,8},{4,12},{9,1},{13,5},{1,9},{5,13},{10,2},{14,6},... | collective-permute-start | bytes 2764808 | tf_op jit(solution)/shard_map/ppermute | solution.py:39
  13.6 84.7 %collective-permute-start.9 = (bf16[3,3,160,640]{3,2,1,0:T(8,128)(2,1)}, bf16[3,3,160,640]{3,2,1,0:T(8,128)(2,1)}, u32[]{:S(2)}, u32[]{:S(2)}) collective-permute-start(bf16[3,3,160,640]{3,2,1,0:T(8,128)(2,1)} %param.32), channel_id=1, source_target_pairs={{0,4},{4,0},{8,12},{12,8},{1,5},{5,1},{9,13},{13,9},{2,6},{6,2},{1... | collective-permute-start | bytes 5529608 | tf_op jit(solution)/shard_map/ppermute | solution.py:34
  14.2 14.1 %copy-start.4 = (f32[24,32]{1,0:T(8,128)S(1)}, f32[24,32]{1,0:T(8,128)}, u32[]{:S(2)}) copy-start(f32[24,32]{1,0:T(8,128)} %param.21) | copy-start | bytes 9220
  14.2 15.1 %copy-start.5 = (f32[24,32]{1,0:T(8,128)S(1)}, f32[24,32]{1,0:T(8,128)}, u32[]{:S(2)}) copy-start(f32[24,32]{1,0:T(8,128)} %param.29) | copy-start | bytes 9220
  21.6 8.1 %copy-start.6 = (f32[24,32]{1,0:T(8,128)S(1)}, f32[24,32]{1,0:T(8,128)}, u32[]{:S(2)}) copy-start(f32[24,32]{1,0:T(8,128)} %param.28) | copy-start | bytes 9220
  21.6 10.4 %collective-permute-start.2 = (bf16[2,24,6,1,640]{4,1,3,2,0:T(8,128)(2,1)}, bf16[2,24,6,1,640]{4,1,3,2,0:T(8,128)(2,1)}, u32[]{:S(2)}, u32[]{:S(2)}) collective-permute-start(bf16[2,24,6,1,640]{4,1,3,2,0:T(8,128)(2,1)} %get-tuple-element.11), channel_id=1, source_target_pairs={{0,1},{1,2},{2,3},{4,5},{5,6},{6,7},{8,9},{9,10},{10,11},{12,13},{... | collective-permute-start | bytes 1105928 | tf_op jit(solution)/shard_map/ppermute | solution.py:14
  26.1 8.9 %collective-permute-start.3 = (bf16[2,24,6,1,640]{4,1,3,2,0:T(8,128)(2,1)}, bf16[2,24,6,1,640]{4,1,3,2,0:T(8,128)(2,1)}, u32[]{:S(2)}, u32[]{:S(2)}) collective-permute-start(bf16[2,24,6,1,640]{4,1,3,2,0:T(8,128)(2,1)} %get-tuple-element.12), channel_id=1, source_target_pairs={{1,0},{2,1},{3,2},{5,4},{6,5},{7,6},{9,8},{10,9},{11,10},{13,12},{... | collective-permute-start | bytes 1105928 | tf_op jit(solution)/shard_map/ppermute | solution.py:17
  32.1 5.9 %copy-start.12 = (f32[640]{0:T(1024)S(1)}, f32[640]{0:T(1024)}, u32[]{:S(2)}) copy-start(f32[640]{0:T(1024)} %param.31) | copy-start | bytes 7684
  32.1 5.9 %copy-start.13 = (f32[640]{0:T(1024)S(1)}, f32[640]{0:T(1024)}, u32[]{:S(2)}) copy-start(f32[640]{0:T(1024)} %param.30) | copy-start | bytes 7684
  41.3 23.2 %collective-permute-start.10 = (bf16[3,3,80,640]{3,2,1,0:T(8,128)(2,1)S(1)}, bf16[3,3,80,640]{3,2,1,0:T(8,128)(2,1)S(1)}, u32[]{:S(2)}, u32[]{:S(2)}) collective-permute-start(bf16[3,3,80,640]{3,2,1,0:T(8,128)(2,1)S(1)} %dynamic-slice_bitcast_fusion), channel_id=1, source_target_pairs={{8,0},{12,4},{0,8},{4,12},{9,1},{13,5},{1,9},{5,13},{10,2},{14,6},... | collective-permute-start | bytes 2764808 | tf_op jit(solution)/shard_map/ppermute | solution.py:39
  41.3 21.3 %collective-permute-start.6 = (bf16[3,3,80,640]{3,2,1,0:T(8,128)(2,1)}, bf16[3,3,80,640]{3,2,1,0:T(8,128)(2,1)S(1)}, u32[]{:S(2)}, u32[]{:S(2)}) collective-permute-start(bf16[3,3,80,640]{3,2,1,0:T(8,128)(2,1)} %collective-permute-done.5), channel_id=1, source_target_pairs={{0,16},{16,0},{1,17},{17,1},{2,18},{18,2},{3,19},{19,3},{4,20},{20... | collective-permute-start | bytes 2764808 | tf_op jit(solution)/shard_map/ppermute | solution.py:41
  42.9 0.8 copy-start.2
  42.9 0.8 copy-start.10
  42.9 0.8 copy-start.11
  47.0 40.3 %collective-permute-start.7 = (bf16[3,3,80,640]{3,2,1,0:T(8,128)(2,1)}, bf16[3,3,80,640]{3,2,1,0:T(8,128)(2,1)S(1)}, u32[]{:S(2)}, u32[]{:S(2)}) collective-permute-start(bf16[3,3,80,640]{3,2,1,0:T(8,128)(2,1)} %collective-permute-done.5), channel_id=1, source_target_pairs={{0,4},{4,0},{8,12},{12,8},{1,5},{5,1},{9,13},{13,9},{2,6},{6,2},{1... | collective-permute-start | bytes 2764808 | tf_op jit(solution)/shard_map/ppermute | solution.py:42
  62.7 24.7 %collective-permute-start.8 = (bf16[3,3,80,640]{3,2,1,0:T(8,128)(2,1)S(1)}, bf16[3,3,80,640]{3,2,1,0:T(8,128)(2,1)S(1)}, u32[]{:S(2)}, u32[]{:S(2)}) collective-permute-start(bf16[3,3,80,640]{3,2,1,0:T(8,128)(2,1)S(1)} %collective-permute-done.6), channel_id=1, source_target_pairs={{0,4},{4,0},{8,12},{12,8},{1,5},{5,1},{9,13},{13,9},{2,6},{6,2},{1... | collective-permute-start | bytes 2764808 | tf_op jit(solution)/shard_map/ppermute | solution.py:43
  64.5 22.1 %collective-permute-start.11 = (bf16[3,3,80,640]{3,2,1,0:T(8,128)(2,1)S(1)}, bf16[3,3,80,640]{3,2,1,0:T(8,128)(2,1)S(1)}, u32[]{:S(2)}, u32[]{:S(2)}) collective-permute-start(bf16[3,3,80,640]{3,2,1,0:T(8,128)(2,1)S(1)} %collective-permute-done.10), channel_id=1, source_target_pairs={{0,16},{16,0},{1,17},{17,1},{2,18},{18,2},{3,19},{19,3},{4,20},{20... | collective-permute-start | bytes 2764808 | tf_op jit(solution)/shard_map/ppermute | solution.py:41
  69.4 17.9 %copy-start.9 = (f32[24,640]{1,0:T(8,128)S(1)}, f32[24,640]{1,0:T(8,128)}, u32[]{:S(2)}) copy-start(f32[24,640]{1,0:T(8,128)} %param.27) | copy-start | bytes 184324
  69.5 17.9 %copy-start.14 = (f32[640]{0:T(1024)S(1)}, f32[640]{0:T(1024)}, u32[]{:S(2)}) copy-start(f32[640]{0:T(1024)} %param.26) | copy-start | bytes 7684
  69.5 35.6 %collective-permute-start.12 = (bf16[3,3,80,640]{3,2,1,0:T(8,128)(2,1)S(1)}, bf16[3,3,80,640]{3,2,1,0:T(8,128)(2,1)S(1)}, u32[]{:S(2)}, u32[]{:S(2)}) collective-permute-start(bf16[3,3,80,640]{3,2,1,0:T(8,128)(2,1)S(1)} %collective-permute-done.10), channel_id=1, source_target_pairs={{0,4},{4,0},{8,12},{12,8},{1,5},{5,1},{9,13},{13,9},{2,6},{6,2},{1... | collective-permute-start | bytes 2764808 | tf_op jit(solution)/shard_map/ppermute | solution.py:42
  86.5 18.6 %collective-permute-start.13 = (bf16[3,3,80,640]{3,2,1,0:T(8,128)(2,1)S(1)}, bf16[3,3,80,640]{3,2,1,0:T(8,128)(2,1)S(1)}, u32[]{:S(2)}, u32[]{:S(2)}) collective-permute-start(bf16[3,3,80,640]{3,2,1,0:T(8,128)(2,1)S(1)} %collective-permute-done.11), channel_id=1, source_target_pairs={{0,4},{4,0},{8,12},{12,8},{1,5},{5,1},{9,13},{13,9},{2,6},{6,2},{1... | collective-permute-start | bytes 2764808 | tf_op jit(solution)/shard_map/ppermute | solution.py:43
  95.1 3.2 %copy-start.1 = (bf16[3,3,160,640]{3,2,1,0:T(8,128)(2,1)S(1)}, bf16[3,3,160,640]{3,2,1,0:T(8,128)(2,1)}, u32[]{:S(2)}) copy-start(bf16[3,3,160,640]{3,2,1,0:T(8,128)(2,1)} %param.32) | copy-start | bytes 5529604
  108.2 1.2 %copy-start = (bf16[24,4,8,640]{3,2,1,0:T(8,128)(2,1)S(1)}, bf16[24,4,8,640]{3,2,1,0:T(8,128)(2,1)}, u32[]{:S(2)}) copy-start(bf16[24,4,8,640]{3,2,1,0:T(8,128)(2,1)} %param.19) | copy-start | bytes 2949124
  108.2 1.2 %copy-start.8 = (f32[640]{0:T(1024)S(1)}, f32[640]{0:T(1024)}, u32[]{:S(2)}) copy-start(f32[640]{0:T(1024)} %param.33) | copy-start | bytes 7684

commit v17 on v15

--- a/solution.py
+++ b/solution.py
@@ -69,8 +69,7 @@
 def to_relative(activation, order):
     natural = jnp.arange(activation.shape[-1], dtype=jnp.int32)[:, None]
     chooser = (natural == order[None, :]).astype(activation.dtype)
-    moved = jnp.dot(activation, chooser, preferred_element_type=jnp.float32)
-    return moved.astype(activation.dtype)
+    return jnp.dot(activation, chooser, preferred_element_type=activation.dtype)
 
 
 def conv_relative(activation, kernel, order):

time: 112 us -> 112 us (level)
  transfers between devices with their start and end apart: 14 -> 14, of which waited for: 4 -> 4; matrix products, arithmetic and copies ran while one was open for 39% -> 38% of each run, Pallas kernels for 0% -> 0%
where the time goes in v17:
time: 112 us
  waiting for transfers between devices  37.8 us (34%)
  matrix products  31.5 us (28%)
  starting transfers between devices  19.3 us (17%)
  other arithmetic  12.1 us (11%)
  local copies, waits for them, and re-layouts  10.7 us (10%)
    conv_general_dilated x4, matrix products, conv_valid(): lax.conv_general_dilated(activation, kernel, window_strides=(1, 1), paddi...  23.8 us
    ppermute x2, waiting for transfers between devices, gather_weights(): fetched = lax.ppermute(mine, 'row', pairs)  15.8 us
    ppermute x2, waiting for transfers between devices, gather_weights(): other = lax.ppermute(fetched, 'groups', y_pairs)  14.3 us
    ppermute x2, starting transfers between devices, padded_2(): lax.ppermute(lax.slice_in_dim(block, block.shape[dim] - width, None, axis...  8.44 us
    ppermute x2, waiting for transfers between devices, padded_2(): lax.ppermute(lax.slice_in_dim(block, 0, width, axis=dim), axis, backward)  7.67 us
    dot_general x3, matrix products, to_relative(): return jnp.dot(activation, chooser, preferred_element_type=activation.dtype)  7.61 us
    squeeze x2, local copies, waits for them, and re-layouts, gather_weights(): mine = lax.dynamic_index_in_dim(halves, parity, axis=2, keepdims=False)  3.46 us
    ppermute x2, starting transfers between devices, padded_2(): lax.ppermute(lax.slice_in_dim(block, 0, width, axis=dim), axis, backward)  3.2 us
  transfers between devices with their start and end apart: 14, of which 4 were waited for; matrix products, arithmetic and copies ran while one was open for 38% of the time, Pallas kernels for 0%

profile of v17, /device:TPU:1, one launch (start us, length us, event | category | flops | bytes accessed | tf_op | source)
XLA Modules:
  0.0 111.7 jit_solution(10736419697649732078)
XLA Ops:
  0.0 2.1 %copy_bitcast_fusion = (bf16[1,24,4,8,640]{4,1,3,2,0:T(8,128)(2,1)S(1)}, bf16[1,24,4,8,640]{4,1,3,2,0:T(8,128)(2,1)S(1)}) fusion(bf16[24,4,8,640]{3,2,1,0:T(8,128)(2,1)} %param.18, bf16[24,4,8,640]{3,2,1,0:T(8,128)(2,1)} %param.17), kind=kLoop, calls=%fused_computation.64 | loop fusion | bytes 3932160 | tf_op jit(solution)/shard_map/stack | solution.py:128
  2.2 0.9 pad_maximum_fusion.3
  3.1 4.5 %collective-permute-start = (bf16[2,24,1,8,640]{4,1,3,2,0:T(8,128)(2,1)}, bf16[2,24,1,8,640]{4,1,3,2,0:T(8,128)(2,1)S(1)}, u32[]{:S(2)}, u32[]{:S(2)}) collective-permute-start(bf16[2,24,1,8,640]{4,1,3,2,0:T(8,128)(2,1)} %get-tuple-element.13), channel_id=1, source_target_pairs={{0,4},{4,8},{8,12},{1,5},{5,9},{9,13},{2,6},{6,10},{10,14},{3,7},{... | collective-permute-start | bytes 1474568 | tf_op jit(solution)/shard_map/ppermute | solution.py:14
  7.6 1.9 %collective-permute-start.1 = (bf16[2,24,1,8,640]{4,1,3,2,0:T(8,128)(2,1)S(1)}, bf16[2,24,1,8,640]{4,1,3,2,0:T(8,128)(2,1)S(1)}, u32[]{:S(2)}, u32[]{:S(2)}) collective-permute-start(bf16[2,24,1,8,640]{4,1,3,2,0:T(8,128)(2,1)S(1)} %get-tuple-element.14), channel_id=1, source_target_pairs={{4,0},{8,4},{12,8},{5,1},{9,5},{13,9},{6,2},{10,6},{14,10},{7,3},{... | collective-permute-start | bytes 1474568 | tf_op jit(solution)/shard_map/ppermute | solution.py:17
  9.6 2.2 %dynamic-slice_bitcast_fusion.1 = bf16[3,3,80,640]{3,2,1,0:T(8,128)(2,1)} fusion(bf16[3,3,2,80,640]{4,3,2,1,0:T(8,128)(2,1)} %bitcast.6, s32[]{:T(128)S(6)} %select_n.125), kind=kLoop, calls=%fused_computation.67 | loop fusion | bytes 1843204 | tf_op jit(solution)/shard_map/jit(dynamic_index_in_dim)/squeeze | solution.py:33
  11.8 1.8 %collective-permute-start.5 = (bf16[3,3,80,640]{3,2,1,0:T(8,128)(2,1)}, bf16[3,3,80,640]{3,2,1,0:T(8,128)(2,1)}, u32[]{:S(2)}, u32[]{:S(2)}) collective-permute-start(bf16[3,3,80,640]{3,2,1,0:T(8,128)(2,1)} %dynamic-slice_bitcast_fusion.1), channel_id=1, source_target_pairs={{8,0},{12,4},{0,8},{4,12},{9,1},{13,5},{1,9},{5,13},{10,2},{14,6},... | collective-permute-start | bytes 2764808 | tf_op jit(solution)/shard_map/ppermute | solution.py:39
  13.6 0.3 collective-permute-start.9
  13.9 0.5 compare_and_fusion.1
  14.5 0.6 fusion.73
  15.1 0.7 compare_reduce_fusion
  15.8 4.7 %collective-permute-done.1 = bf16[2,24,1,8,640]{4,1,3,2,0:T(8,128)(2,1)S(1)} collective-permute-done((bf16[2,24,1,8,640]{4,1,3,2,0:T(8,128)(2,1)S(1)}, bf16[2,24,1,8,640]{4,1,3,2,0:T(8,128)(2,1)S(1)}, u32[]{:S(2)}, u32[]{:S(2)}) %collective-permute-start.1) | collective-permute-done | bytes 491552 | tf_op jit(solution)/shard_map/ppermute | solution.py:17
  20.6 1.0 pad_maximum_fusion.7
  21.6 3.9 %collective-permute-start.2 = (bf16[2,24,6,1,640]{4,1,3,2,0:T(8,128)(2,1)}, bf16[2,24,6,1,640]{4,1,3,2,0:T(8,128)(2,1)}, u32[]{:S(2)}, u32[]{:S(2)}) collective-permute-start(bf16[2,24,6,1,640]{4,1,3,2,0:T(8,128)(2,1)} %get-tuple-element.9), channel_id=1, source_target_pairs={{0,1},{1,2},{2,3},{4,5},{5,6},{6,7},{8,9},{9,10},{10,11},{12,13},{... | collective-permute-start | bytes 1105928 | tf_op jit(solution)/shard_map/ppermute | solution.py:14
  25.6 1.3 %collective-permute-start.3 = (bf16[2,24,6,1,640]{4,1,3,2,0:T(8,128)(2,1)}, bf16[2,24,6,1,640]{4,1,3,2,0:T(8,128)(2,1)}, u32[]{:S(2)}, u32[]{:S(2)}) collective-permute-start(bf16[2,24,6,1,640]{4,1,3,2,0:T(8,128)(2,1)} %get-tuple-element.10), channel_id=1, source_target_pairs={{1,0},{2,1},{3,2},{5,4},{6,5},{7,6},{9,8},{10,9},{11,10},{13,12},{... | collective-permute-start | bytes 1105928 | tf_op jit(solution)/shard_map/ppermute | solution.py:17
  26.9 0.6 compare_and_fusion
  27.6 0.2 mul.115
  27.8 0.2 broadcast_in_dim.42
  28.0 0.8 sub.59
  29.0 0.2 mul.128
  29.4 0.2 sub.69
  29.6 1.3 %dynamic-slice_bitcast_fusion = bf16[3,3,80,640]{3,2,1,0:T(8,128)(2,1)S(1)} fusion(bf16[3,3,2,80,640]{4,3,2,1,0:T(8,128)(2,1)} %bitcast.36, s32[]{:T(128)S(6)} %select_n.125), kind=kLoop, calls=%fused_computation.66 | loop fusion | bytes 1843204 | tf_op jit(solution)/shard_map/jit(dynamic_index_in_dim)/squeeze | solution.py:33
  30.9 0.7 and_convert_fusion
  31.6 2.9 %collective-permute-done.3 = bf16[2,24,6,1,640]{4,1,3,2,0:T(8,128)(2,1)} collective-permute-done((bf16[2,24,6,1,640]{4,1,3,2,0:T(8,128)(2,1)}, bf16[2,24,6,1,640]{4,1,3,2,0:T(8,128)(2,1)}, u32[]{:S(2)}, u32[]{:S(2)}) %collective-permute-start.3) | collective-permute-done | bytes 368672 | tf_op jit(solution)/shard_map/ppermute | solution.py:17
  34.6 3.0 %pad_maximum_fusion = bf16[2,24,6,10,640]{4,1,3,2,0:T(8,128)(2,1)S(1)} fusion(bf16[2,24,6,1,640]{4,1,3,2,0:T(8,128)(2,1)} %collective-permute-done.3, bf16[2,24,1,8,640]{4,1,3,2,0:T(8,128)(2,1)S(1)} %collective-permute-done.1, bf16[1,24,4,8,640]{4,1,3,2,0:T(8,128)(2,1)S(1)} %get-tuple-element.19, bf16[1,24,4,8,640]{4,1,3,2,0:T(8,128)(2,1)S(1)} %get-tuple-element.20, ...), kind=kLoop, calls=%fused_computation | loop fusion | flops 9216000 | bytes 7372800 | tf_op jit(solution)/shard_map/concatenate | solution.py:18
  37.6 0.2 fusion.35
  37.8 0.4 copy-done.8
  38.3 3.3 %fusion.36 = bf16[24,6,10,640]{3,0,2,1:T(8,128)(2,1)S(1)} fusion(bf16[2,24,6,10,640]{4,1,3,2,0:T(8,128)(2,1)S(1)} %pad_maximum_fusion, f32[640]{0:T(1024)S(1)} %copy-done.14, f32[640]{0:T(1024)S(1)} %copy-done.15, f32[24,640]{1,0:T(8,128)S(1)} %mul.128, f32[24,640]{1,0:T(8,128)S(1)} %sub.69, f32[6,10]{1,0:T(8,128)S(1)} %and_convert_fusion, ...), kind=kOutput, calls=%fused_computation.48 | convolution fusion | flops 1190195200 | bytes 3825664 | tf_op jit(solution)/shard_map/dot_general | solution.py:72
  41.7 1.3 %collective-permute-start.6 = (bf16[3,3,80,640]{3,2,1,0:T(8,128)(2,1)}, bf16[3,3,80,640]{3,2,1,0:T(8,128)(2,1)S(1)}, u32[]{:S(2)}, u32[]{:S(2)}) collective-permute-start(bf16[3,3,80,640]{3,2,1,0:T(8,128)(2,1)} %collective-permute-done.5), channel_id=1, source_target_pairs={{0,16},{16,0},{1,17},{17,1},{2,18},{18,2},{3,19},{19,3},{4,20},{20... | collective-permute-start | bytes 2764808 | tf_op jit(solution)/shard_map/ppermute | solution.py:41
  43.0 0.2 fusion.97
  43.2 3.3 %fusion.38 = bf16[24,6,10,640]{3,0,2,1:T(8,128)(2,1)S(1)} fusion(f32[6,10]{1,0:T(8,128)S(1)} %and_convert_fusion, f32[640]{0:T(1024)S(1)} %copy-done.12, f32[640]{0:T(1024)S(1)} %copy-done.13, f32[24,640]{1,0:T(8,128)S(1)} %mul.115, f32[24,640]{1,0:T(8,128)S(1)} %copy-done.2, s32[640]{0:T(1024)S(1)} %copy-done.8, ...), kind=kOutput, calls=%fused_computation.49 | convolution fusion | flops 1190195200 | bytes 3825664 | tf_op jit(solution)/shard_map/dot_general | solution.py:72
  46.5 1.5 %collective-permute-start.7 = (bf16[3,3,80,640]{3,2,1,0:T(8,128)(2,1)}, bf16[3,3,80,640]{3,2,1,0:T(8,128)(2,1)S(1)}, u32[]{:S(2)}, u32[]{:S(2)}) collective-permute-start(bf16[3,3,80,640]{3,2,1,0:T(8,128)(2,1)} %collective-permute-done.5), channel_id=1, source_target_pairs={{0,4},{4,0},{8,12},{12,8},{1,5},{5,1},{9,13},{13,9},{2,6},{6,2},{1... | collective-permute-start | bytes 2764808 | tf_op jit(solution)/shard_map/ppermute | solution.py:42
  48.0 15.8 %collective-permute-done.10 = bf16[3,3,80,640]{3,2,1,0:T(8,128)(2,1)S(1)} collective-permute-done((bf16[3,3,80,640]{3,2,1,0:T(8,128)(2,1)S(1)}, bf16[3,3,80,640]{3,2,1,0:T(8,128)(2,1)S(1)}, u32[]{:S(2)}, u32[]{:S(2)}) %collective-permute-start.10) | collective-permute-done | bytes 921632 | tf_op jit(solution)/shard_map/ppermute | solution.py:39
  63.8 1.2 %collective-permute-start.11 = (bf16[3,3,80,640]{3,2,1,0:T(8,128)(2,1)S(1)}, bf16[3,3,80,640]{3,2,1,0:T(8,128)(2,1)S(1)}, u32[]{:S(2)}, u32[]{:S(2)}) collective-permute-start(bf16[3,3,80,640]{3,2,1,0:T(8,128)(2,1)S(1)} %collective-permute-done.10), channel_id=1, source_target_pairs={{0,16},{16,0},{1,17},{17,1},{2,18},{18,2},{3,19},{19,3},{4,20},{20... | collective-permute-start | bytes 2764808 | tf_op jit(solution)/shard_map/ppermute | solution.py:41
  65.0 0.3 collective-permute-start.12
  65.4 0.2 collective-permute-start.8
  65.5 6.0 %fusion = f32[24,4,8,640]{3,0,2,1:T(8,128)S(1)} fusion(bf16[3,3,160,640]{3,2,1,0:T(8,128)(2,1)} %collective-permute-done.4, bf16[3,3,160,640]{3,2,1,0:T(8,128)(2,1)} %param.25, bf16[24,6,10,640]{3,0,2,1:T(8,128)(2,1)S(1)} %fusion.38), kind=kOutput, calls=%fused_computation.1 | convolution fusion | flops 2838528000 | bytes 6758400 | tf_op jit(solution)/shard_map/conv_general_dilated | solution.py:80
  71.5 14.3 %collective-permute-done.11 = bf16[3,3,80,640]{3,2,1,0:T(8,128)(2,1)S(1)} collective-permute-done((bf16[3,3,80,640]{3,2,1,0:T(8,128)(2,1)S(1)}, bf16[3,3,80,640]{3,2,1,0:T(8,128)(2,1)S(1)}, u32[]{:S(2)}, u32[]{:S(2)}) %collective-permute-start.11) | collective-permute-done | bytes 921632 | tf_op jit(solution)/shard_map/ppermute | solution.py:41
  85.8 0.8 collective-permute-start.13
  86.7 6.0 %multiply_convert_fusion.1 = bf16[24,4,8,640]{3,0,2,1:T(8,128)(2,1)S(1)} fusion(f32[24,4,8,640]{3,0,2,1:T(8,128)S(1)} %fusion, bf16[3,3,80,640]{3,2,1,0:T(8,128)(2,1)S(1)} %collective-permute-done.8, bf16[3,3,80,640]{3,2,1,0:T(8,128)(2,1)S(1)} %collective-permute-done.7, bf16[3,3,80,640]{3,2,1,0:T(8,128)(2,1)S(1)} %collective-permute-done.6, ...), kind=kOutput, calls=%fused_computation.44 | convolution fusion | flops 2851799040 | bytes 7938048 | tf_op jit(solution)/shard_map/conv_general_dilated | solution.py:80
  92.7 1.0 fusion.45
  93.8 1.0 fusion.51
  94.8 2.1 %pad_maximum_fusion.1 = (bf16[24,6,12,320]{3,2,1,0:T(8,128)(2,1)S(1)}, bf16[24,6,12,320]{3,2,1,0:T(8,128)(2,1)S(1)}) fusion(bf16[24,6,6,640]{3,2,1,0:T(8,128)(2,1)S(1)} %get-tuple-element.17, bf16[24,6,6,640]{3,2,1,0:T(8,128)(2,1)S(1)} %get-tuple-element.18), kind=kLoop, calls=%fused_computation.51 | loop fusion | flops 4423680 | bytes 4423680 | tf_op jit(solution)/shard_map/concatenate | solution.py:175
  96.9 6.5 %fusion.12 = f32[24,4,10,640]{3,0,2,1:T(8,128)S(1)} fusion(bf16[3,3,160,640]{3,2,1,0:T(8,128)(2,1)} %collective-permute-done.9, bf16[3,3,160,640]{3,2,1,0:T(8,128)(2,1)S(1)} %copy-done.1, bf16[24,6,12,320]{3,2,1,0:T(8,128)(2,1)S(1)} %get-tuple-element.8), kind=kOutput, calls=%fused_computation.13 | convolution fusion | flops 3546316800 | bytes 7249920 | tf_op jit(solution)/shard_map/conv_general_dilated | solution.py:80
  103.5 5.3 %fusion.40 = f32[24,4,10,640]{3,0,2,1:T(8,128)S(1)} fusion(f32[24,4,10,640]{3,0,2,1:T(8,128)S(1)} %fusion.12, bf16[3,3,80,640]{3,2,1,0:T(8,128)(2,1)S(1)} %collective-permute-done.13, bf16[3,3,80,640]{3,2,1,0:T(8,128)(2,1)S(1)} %collective-permute-done.12, bf16[3,3,80,640]{3,2,1,0:T(8,128)(2,1)S(1)} %collective-permute-done.11, ...), kind=kOutput, calls=%fused_computation.52 | convolution fusion | flops 3554304000 | bytes 9707520 | tf_op jit(solution)/shard_map/conv_general_dilated | solution.py:80
  109.0 0.5 copy-done.10
  109.5 0.5 copy-done
  110.0 0.7 fusion.56
  110.7 1.1 copy.52
  (51 shorter events, 1.0 us)
Async XLA Ops:
  2.2 12.9 %copy-start.7 = (s32[24,16]{0,1:T(8,128)S(1)}, s32[24,16]{0,1:T(8,128)}, u32[]{:S(2)}) copy-start(s32[24,16]{0,1:T(8,128)} %param.20) | copy-start | bytes 4612
  3.1 12.8 %collective-permute-start = (bf16[2,24,1,8,640]{4,1,3,2,0:T(8,128)(2,1)}, bf16[2,24,1,8,640]{4,1,3,2,0:T(8,128)(2,1)S(1)}, u32[]{:S(2)}, u32[]{:S(2)}) collective-permute-start(bf16[2,24,1,8,640]{4,1,3,2,0:T(8,128)(2,1)} %get-tuple-element.13), channel_id=1, source_target_pairs={{0,4},{4,8},{8,12},{1,5},{5,9},{9,13},{2,6},{6,10},{10,14},{3,7},{... | collective-permute-start | bytes 1474568 | tf_op jit(solution)/shard_map/ppermute | solution.py:14
  7.6 13.0 %collective-permute-start.1 = (bf16[2,24,1,8,640]{4,1,3,2,0:T(8,128)(2,1)S(1)}, bf16[2,24,1,8,640]{4,1,3,2,0:T(8,128)(2,1)S(1)}, u32[]{:S(2)}, u32[]{:S(2)}) collective-permute-start(bf16[2,24,1,8,640]{4,1,3,2,0:T(8,128)(2,1)S(1)} %get-tuple-element.14), channel_id=1, source_target_pairs={{4,0},{8,4},{12,8},{5,1},{9,5},{13,9},{6,2},{10,6},{14,10},{7,3},{... | collective-permute-start | bytes 1474568 | tf_op jit(solution)/shard_map/ppermute | solution.py:17
  9.5 55.5 %collective-permute-start.4 = (bf16[3,3,160,640]{3,2,1,0:T(8,128)(2,1)}, bf16[3,3,160,640]{3,2,1,0:T(8,128)(2,1)}, u32[]{:S(2)}, u32[]{:S(2)}) collective-permute-start(bf16[3,3,160,640]{3,2,1,0:T(8,128)(2,1)} %param.25), channel_id=1, source_target_pairs={{0,4},{4,0},{8,12},{12,8},{1,5},{5,1},{9,13},{13,9},{2,6},{6,2},{1... | collective-permute-start | bytes 5529608 | tf_op jit(solution)/shard_map/ppermute | solution.py:34
  9.6 17.8 %copy-start.3 = (f32[24,32]{1,0:T(8,128)S(1)}, f32[24,32]{1,0:T(8,128)}, u32[]{:S(2)}) copy-start(f32[24,32]{1,0:T(8,128)} %param.22) | copy-start | bytes 9220
  11.8 16.0 %copy-start.4 = (f32[24,32]{1,0:T(8,128)S(1)}, f32[24,32]{1,0:T(8,128)}, u32[]{:S(2)}) copy-start(f32[24,32]{1,0:T(8,128)} %param.21) | copy-start | bytes 9220
  11.8 29.8 %collective-permute-start.5 = (bf16[3,3,80,640]{3,2,1,0:T(8,128)(2,1)}, bf16[3,3,80,640]{3,2,1,0:T(8,128)(2,1)}, u32[]{:S(2)}, u32[]{:S(2)}) collective-permute-start(bf16[3,3,80,640]{3,2,1,0:T(8,128)(2,1)} %dynamic-slice_bitcast_fusion.1), channel_id=1, source_target_pairs={{8,0},{12,4},{0,8},{4,12},{9,1},{13,5},{1,9},{5,13},{10,2},{14,6},... | collective-permute-start | bytes 2764808 | tf_op jit(solution)/shard_map/ppermute | solution.py:39
  13.6 83.3 %collective-permute-start.9 = (bf16[3,3,160,640]{3,2,1,0:T(8,128)(2,1)}, bf16[3,3,160,640]{3,2,1,0:T(8,128)(2,1)}, u32[]{:S(2)}, u32[]{:S(2)}) collective-permute-start(bf16[3,3,160,640]{3,2,1,0:T(8,128)(2,1)} %param.32), channel_id=1, source_target_pairs={{0,4},{4,0},{8,12},{12,8},{1,5},{5,1},{9,13},{13,9},{2,6},{6,2},{1... | collective-permute-start | bytes 5529608 | tf_op jit(solution)/shard_map/ppermute | solution.py:34
  15.8 13.0 %copy-start.5 = (f32[24,32]{1,0:T(8,128)S(1)}, f32[24,32]{1,0:T(8,128)}, u32[]{:S(2)}) copy-start(f32[24,32]{1,0:T(8,128)} %param.29) | copy-start | bytes 9220
  15.8 13.4 %copy-start.6 = (f32[24,32]{1,0:T(8,128)S(1)}, f32[24,32]{1,0:T(8,128)}, u32[]{:S(2)}) copy-start(f32[24,32]{1,0:T(8,128)} %param.28) | copy-start | bytes 9220
  21.6 10.0 %collective-permute-start.2 = (bf16[2,24,6,1,640]{4,1,3,2,0:T(8,128)(2,1)}, bf16[2,24,6,1,640]{4,1,3,2,0:T(8,128)(2,1)}, u32[]{:S(2)}, u32[]{:S(2)}) collective-permute-start(bf16[2,24,6,1,640]{4,1,3,2,0:T(8,128)(2,1)} %get-tuple-element.9), channel_id=1, source_target_pairs={{0,1},{1,2},{2,3},{4,5},{5,6},{6,7},{8,9},{9,10},{10,11},{12,13},{... | collective-permute-start | bytes 1105928 | tf_op jit(solution)/shard_map/ppermute | solution.py:14
  25.6 9.0 %collective-permute-start.3 = (bf16[2,24,6,1,640]{4,1,3,2,0:T(8,128)(2,1)}, bf16[2,24,6,1,640]{4,1,3,2,0:T(8,128)(2,1)}, u32[]{:S(2)}, u32[]{:S(2)}) collective-permute-start(bf16[2,24,6,1,640]{4,1,3,2,0:T(8,128)(2,1)} %get-tuple-element.10), channel_id=1, source_target_pairs={{1,0},{2,1},{3,2},{5,4},{6,5},{7,6},{9,8},{10,9},{11,10},{13,12},{... | collective-permute-start | bytes 1105928 | tf_op jit(solution)/shard_map/ppermute | solution.py:17
  37.5 0.7 copy-start.8
  37.6 0.7 copy-start.14
  37.6 0.7 copy-start.15
  41.6 1.6 %copy-start.2 = (f32[24,640]{1,0:T(8,128)S(1)}, f32[24,640]{1,0:T(8,128)}, u32[]{:S(2)}) copy-start(f32[24,640]{1,0:T(8,128)} %sub.59) | copy-start | bytes 184324
  41.6 1.6 %copy-start.12 = (f32[640]{0:T(1024)S(1)}, f32[640]{0:T(1024)}, u32[]{:S(2)}) copy-start(f32[640]{0:T(1024)} %param.24) | copy-start | bytes 7684
  41.6 1.6 %copy-start.13 = (f32[640]{0:T(1024)S(1)}, f32[640]{0:T(1024)}, u32[]{:S(2)}) copy-start(f32[640]{0:T(1024)} %param.23) | copy-start | bytes 7684
  41.6 22.2 %collective-permute-start.10 = (bf16[3,3,80,640]{3,2,1,0:T(8,128)(2,1)S(1)}, bf16[3,3,80,640]{3,2,1,0:T(8,128)(2,1)S(1)}, u32[]{:S(2)}, u32[]{:S(2)}) collective-permute-start(bf16[3,3,80,640]{3,2,1,0:T(8,128)(2,1)S(1)} %dynamic-slice_bitcast_fusion), channel_id=1, source_target_pairs={{8,0},{12,4},{0,8},{4,12},{9,1},{13,5},{1,9},{5,13},{10,2},{14,6},... | collective-permute-start | bytes 2764808 | tf_op jit(solution)/shard_map/ppermute | solution.py:39
  41.7 23.7 %collective-permute-start.6 = (bf16[3,3,80,640]{3,2,1,0:T(8,128)(2,1)}, bf16[3,3,80,640]{3,2,1,0:T(8,128)(2,1)S(1)}, u32[]{:S(2)}, u32[]{:S(2)}) collective-permute-start(bf16[3,3,80,640]{3,2,1,0:T(8,128)(2,1)} %collective-permute-done.5), channel_id=1, source_target_pairs={{0,16},{16,0},{1,17},{17,1},{2,18},{18,2},{3,19},{19,3},{4,20},{20... | collective-permute-start | bytes 2764808 | tf_op jit(solution)/shard_map/ppermute | solution.py:41
  46.5 40.2 %copy-start.11 = (f32[24,640]{1,0:T(8,128)S(1)}, f32[24,640]{1,0:T(8,128)}, u32[]{:S(2)}) copy-start(f32[24,640]{1,0:T(8,128)} %param.27) | copy-start | bytes 184324
  46.5 40.2 %copy-start.16 = (f32[640]{0:T(1024)S(1)}, f32[640]{0:T(1024)}, u32[]{:S(2)}) copy-start(f32[640]{0:T(1024)} %param.26) | copy-start | bytes 7684
  46.5 40.1 %collective-permute-start.7 = (bf16[3,3,80,640]{3,2,1,0:T(8,128)(2,1)}, bf16[3,3,80,640]{3,2,1,0:T(8,128)(2,1)S(1)}, u32[]{:S(2)}, u32[]{:S(2)}) collective-permute-start(bf16[3,3,80,640]{3,2,1,0:T(8,128)(2,1)} %collective-permute-done.5), channel_id=1, source_target_pairs={{0,4},{4,0},{8,12},{12,8},{1,5},{5,1},{9,13},{13,9},{2,6},{6,2},{1... | collective-permute-start | bytes 2764808 | tf_op jit(solution)/shard_map/ppermute | solution.py:42
  63.8 22.0 %collective-permute-start.11 = (bf16[3,3,80,640]{3,2,1,0:T(8,128)(2,1)S(1)}, bf16[3,3,80,640]{3,2,1,0:T(8,128)(2,1)S(1)}, u32[]{:S(2)}, u32[]{:S(2)}) collective-permute-start(bf16[3,3,80,640]{3,2,1,0:T(8,128)(2,1)S(1)} %collective-permute-done.10), channel_id=1, source_target_pairs={{0,16},{16,0},{1,17},{17,1},{2,18},{18,2},{3,19},{19,3},{4,20},{20... | collective-permute-start | bytes 2764808 | tf_op jit(solution)/shard_map/ppermute | solution.py:41
  65.0 38.4 %collective-permute-start.12 = (bf16[3,3,80,640]{3,2,1,0:T(8,128)(2,1)S(1)}, bf16[3,3,80,640]{3,2,1,0:T(8,128)(2,1)S(1)}, u32[]{:S(2)}, u32[]{:S(2)}) collective-permute-start(bf16[3,3,80,640]{3,2,1,0:T(8,128)(2,1)S(1)} %collective-permute-done.10), channel_id=1, source_target_pairs={{0,4},{4,0},{8,12},{12,8},{1,5},{5,1},{9,13},{13,9},{2,6},{6,2},{1... | collective-permute-start | bytes 2764808 | tf_op jit(solution)/shard_map/ppermute | solution.py:42
  65.4 21.3 %collective-permute-start.8 = (bf16[3,3,80,640]{3,2,1,0:T(8,128)(2,1)S(1)}, bf16[3,3,80,640]{3,2,1,0:T(8,128)(2,1)S(1)}, u32[]{:S(2)}, u32[]{:S(2)}) collective-permute-start(bf16[3,3,80,640]{3,2,1,0:T(8,128)(2,1)S(1)} %collective-permute-done.6), channel_id=1, source_target_pairs={{0,4},{4,0},{8,12},{12,8},{1,5},{5,1},{9,13},{13,9},{2,6},{6,2},{1... | collective-permute-start | bytes 2764808 | tf_op jit(solution)/shard_map/ppermute | solution.py:43
  85.8 17.7 %collective-permute-start.13 = (bf16[3,3,80,640]{3,2,1,0:T(8,128)(2,1)S(1)}, bf16[3,3,80,640]{3,2,1,0:T(8,128)(2,1)S(1)}, u32[]{:S(2)}, u32[]{:S(2)}) collective-permute-start(bf16[3,3,80,640]{3,2,1,0:T(8,128)(2,1)S(1)} %collective-permute-done.11), channel_id=1, source_target_pairs={{0,4},{4,0},{8,12},{12,8},{1,5},{5,1},{9,13},{13,9},{2,6},{6,2},{1... | collective-permute-start | bytes 2764808 | tf_op jit(solution)/shard_map/ppermute | solution.py:43
  94.8 2.1 %copy-start.1 = (bf16[3,3,160,640]{3,2,1,0:T(8,128)(2,1)S(1)}, bf16[3,3,160,640]{3,2,1,0:T(8,128)(2,1)}, u32[]{:S(2)}) copy-start(bf16[3,3,160,640]{3,2,1,0:T(8,128)(2,1)} %param.32) | copy-start | bytes 5529604
  108.8 0.7 copy-start.10
  108.8 1.2 %copy-start = (bf16[24,4,8,640]{3,2,1,0:T(8,128)(2,1)S(1)}, bf16[24,4,8,640]{3,2,1,0:T(8,128)(2,1)}, u32[]{:S(2)}) copy-start(bf16[24,4,8,640]{3,2,1,0:T(8,128)(2,1)} %param.19) | copy-start | bytes 2949124
  108.8 1.2 %copy-start.9 = (f32[640]{0:T(1024)S(1)}, f32[640]{0:T(1024)}, u32[]{:S(2)}) copy-start(f32[640]{0:T(1024)} %param.33) | copy-start | bytes 7684

commit v18 on v15

--- a/solution.py
+++ b/solution.py
@@ -163,21 +163,22 @@
     def second_norm(values):
         return jax.nn.silu((values - second_mean) * second_rstd * norm2_gain + norm2_shift)
 
-    cached_act = to_relative((second_norm(margins_pad) * inside).astype(jnp.bfloat16), order)
-    fresh_act = to_relative(second_norm(fresh_mid).astype(jnp.bfloat16), order)
-    fresh_pad = jnp.pad(fresh_act, ((0, 0), (1, 1), (1, 1), (0, 0)))
+    cached_norm = (second_norm(margins_pad) * inside).astype(jnp.bfloat16)
+    fresh_norm = second_norm(fresh_mid).astype(jnp.bfloat16)
     edge = jnp.arange(TILE + 2, dtype=jnp.int32)
     interior = ((edge >= 1) & (edge <= TILE))[:, None] & ((edge >= 1) & (edge <= TILE))[None, :]
     interior = interior[None, :, :, None]
-    windows = []
-    for tile_across in range(tiles_across):
-        cut = slice(tile_across * TILE, tile_across * TILE + TILE + 2)
-        windows.append(jnp.where(interior, fresh_pad[:, :, cut], cached_act[:, :, cut]))
-    wide = jnp.concatenate(windows, axis=2)
     split = second_local.shape[2]
-    wide_sum = conv_valid(wide[..., :split], second_local) + conv_valid(
-        wide[..., split:], second_remote
-    )
+    wide_sum = None
+    for kernel, picks in ((second_local, order[:split]), (second_remote, order[split:])):
+        cached_act = to_relative(cached_norm, picks)
+        fresh_pad = jnp.pad(to_relative(fresh_norm, picks), ((0, 0), (1, 1), (1, 1), (0, 0)))
+        windows = []
+        for tile_across in range(tiles_across):
+            cut = slice(tile_across * TILE, tile_across * TILE + TILE + 2)
+            windows.append(jnp.where(interior, fresh_pad[:, :, cut], cached_act[:, :, cut]))
+        part = conv_valid(jnp.concatenate(windows, axis=2), kernel)
+        wide_sum = part if wide_sum is None else wide_sum + part
     stride = TILE + 2
     second_sum = jnp.concatenate(
         [wide_sum[:, :, t * stride : t * stride + TILE] for t in range(tiles_across)], axis=2

time: 112 us -> 113 us (level)
  other arithmetic: 12.2 us -> 10.6 us
  local copies, waits for them, and re-layouts: 10.9 us -> 12.4 us
    ppermute x2, waiting for transfers between devices: 7.7 us -> 9.63 us  [padded_2(): lax.ppermute(lax.slice_in_dim(block, 0, width, axis=dim), axis, backward)]
    convert_element_type x0 -> x1, other arithmetic: none -> 1.49 us  [body(): cached_norm = (second_norm(margins_pad) * inside).astype(jnp.bfloat16)]
    ppermute x2, waiting for transfers between devices: 14.9 us -> 13.7 us  [gather_weights(): fetched = lax.ppermute(mine, 'row', pairs)]
    dot_general x3 -> x5, matrix products: 7.62 us -> 7.74 us  [to_relative(): moved = jnp.dot(activation, chooser, preferred_element_type=jnp.float32)]
  transfers between devices with their start and end apart: 14 -> 14, of which waited for: 4 -> 4; matrix products, arithmetic and copies ran while one was open for 39% -> 38% of each run, Pallas kernels for 0% -> 0%
where the time goes in v18:
time: 113 us; the launch traced here: 112 us
  waiting for transfers between devices  37.8 us (33%)
  matrix products  31.4 us (28%)
  starting transfers between devices  19.3 us (17%)
  local copies, waits for them, and re-layouts  12.4 us (11%)
  other arithmetic  10.6 us (9%)
    conv_general_dilated x4, matrix products, conv_valid(): lax.conv_general_dilated(activation, kernel, window_strides=(1, 1), paddi...  23.7 us
    ppermute x2, waiting for transfers between devices, gather_weights(): other = lax.ppermute(fetched, 'groups', y_pairs)  14.4 us
    ppermute x2, waiting for transfers between devices, gather_weights(): fetched = lax.ppermute(mine, 'row', pairs)  13.7 us
    ppermute x2, waiting for transfers between devices, padded_2(): lax.ppermute(lax.slice_in_dim(block, 0, width, axis=dim), axis, backward)  9.63 us
    ppermute x2, starting transfers between devices, padded_2(): lax.ppermute(lax.slice_in_dim(block, block.shape[dim] - width, None, axis...  8.85 us
    dot_general x5, matrix products, to_relative(): moved = jnp.dot(activation, chooser, preferred_element_type=jnp.float32)  7.74 us
    squeeze x2, local copies, waits for them, and re-layouts, gather_weights(): mine = lax.dynamic_index_in_dim(halves, parity, axis=2, keepdims=False)  3.46 us
    ppermute x2, starting transfers between devices, padded_2(): lax.ppermute(lax.slice_in_dim(block, 0, width, axis=dim), axis, backward)  3.2 us
  transfers between devices with their start and end apart: 14, of which 4 were waited for; matrix products, arithmetic and copies ran while one was open for 38% of the time, Pallas kernels for 0%

profile of v18, /device:TPU:1, one launch (start us, length us, event | category | flops | bytes accessed | tf_op | source)
XLA Modules:
  0.0 112.0 jit_solution(15533275650296706600)
XLA Ops:
  0.0 2.1 %copy_bitcast_fusion = (bf16[1,24,4,8,640]{4,1,3,2,0:T(8,128)(2,1)S(1)}, bf16[1,24,4,8,640]{4,1,3,2,0:T(8,128)(2,1)S(1)}) fusion(bf16[24,4,8,640]{3,2,1,0:T(8,128)(2,1)} %param.18, bf16[24,4,8,640]{3,2,1,0:T(8,128)(2,1)} %param.17), kind=kLoop, calls=%fused_computation.64 | loop fusion | bytes 3932160 | tf_op jit(solution)/shard_map/stack | solution.py:129
  2.2 0.9 pad_maximum_fusion.4
  3.1 4.5 %collective-permute-start = (bf16[2,24,1,8,640]{4,1,3,2,0:T(8,128)(2,1)}, bf16[2,24,1,8,640]{4,1,3,2,0:T(8,128)(2,1)S(1)}, u32[]{:S(2)}, u32[]{:S(2)}) collective-permute-start(bf16[2,24,1,8,640]{4,1,3,2,0:T(8,128)(2,1)} %get-tuple-element.15), channel_id=1, source_target_pairs={{0,4},{4,8},{8,12},{1,5},{5,9},{9,13},{2,6},{6,10},{10,14},{3,7},{... | collective-permute-start | bytes 1474568 | tf_op jit(solution)/shard_map/ppermute | solution.py:14
  7.6 1.9 %collective-permute-start.1 = (bf16[2,24,1,8,640]{4,1,3,2,0:T(8,128)(2,1)S(1)}, bf16[2,24,1,8,640]{4,1,3,2,0:T(8,128)(2,1)S(1)}, u32[]{:S(2)}, u32[]{:S(2)}) collective-permute-start(bf16[2,24,1,8,640]{4,1,3,2,0:T(8,128)(2,1)S(1)} %get-tuple-element.16), channel_id=1, source_target_pairs={{4,0},{8,4},{12,8},{5,1},{9,5},{13,9},{6,2},{10,6},{14,10},{7,3},{... | collective-permute-start | bytes 1474568 | tf_op jit(solution)/shard_map/ppermute | solution.py:17
  9.6 2.2 %dynamic-slice_bitcast_fusion.1 = bf16[3,3,80,640]{3,2,1,0:T(8,128)(2,1)} fusion(bf16[3,3,2,80,640]{4,3,2,1,0:T(8,128)(2,1)} %bitcast.6, s32[]{:T(128)S(6)} %select_n.131), kind=kLoop, calls=%fused_computation.67 | loop fusion | bytes 1843204 | tf_op jit(solution)/shard_map/jit(dynamic_index_in_dim)/squeeze | solution.py:33
  11.8 1.8 %collective-permute-start.5 = (bf16[3,3,80,640]{3,2,1,0:T(8,128)(2,1)}, bf16[3,3,80,640]{3,2,1,0:T(8,128)(2,1)}, u32[]{:S(2)}, u32[]{:S(2)}) collective-permute-start(bf16[3,3,80,640]{3,2,1,0:T(8,128)(2,1)} %dynamic-slice_bitcast_fusion.1), channel_id=1, source_target_pairs={{8,0},{12,4},{0,8},{4,12},{9,1},{13,5},{1,9},{5,13},{10,2},{14,6},... | collective-permute-start | bytes 2764808 | tf_op jit(solution)/shard_map/ppermute | solution.py:39
  13.6 0.3 collective-permute-start.9
  14.2 6.3 %collective-permute-done.1 = bf16[2,24,1,8,640]{4,1,3,2,0:T(8,128)(2,1)S(1)} collective-permute-done((bf16[2,24,1,8,640]{4,1,3,2,0:T(8,128)(2,1)S(1)}, bf16[2,24,1,8,640]{4,1,3,2,0:T(8,128)(2,1)S(1)}, u32[]{:S(2)}, u32[]{:S(2)}) %collective-permute-start.1) | collective-permute-done | bytes 491552 | tf_op jit(solution)/shard_map/ppermute | solution.py:17
  20.6 1.0 pad_maximum_fusion.8
  21.6 4.4 %collective-permute-start.2 = (bf16[2,24,6,1,640]{4,1,3,2,0:T(8,128)(2,1)}, bf16[2,24,6,1,640]{4,1,3,2,0:T(8,128)(2,1)}, u32[]{:S(2)}, u32[]{:S(2)}) collective-permute-start(bf16[2,24,6,1,640]{4,1,3,2,0:T(8,128)(2,1)} %get-tuple-element.7), channel_id=1, source_target_pairs={{0,1},{1,2},{2,3},{4,5},{5,6},{6,7},{8,9},{9,10},{10,11},{12,13},{... | collective-permute-start | bytes 1105928 | tf_op jit(solution)/shard_map/ppermute | solution.py:14
  26.0 1.3 %collective-permute-start.3 = (bf16[2,24,6,1,640]{4,1,3,2,0:T(8,128)(2,1)}, bf16[2,24,6,1,640]{4,1,3,2,0:T(8,128)(2,1)}, u32[]{:S(2)}, u32[]{:S(2)}) collective-permute-start(bf16[2,24,6,1,640]{4,1,3,2,0:T(8,128)(2,1)} %get-tuple-element.8), channel_id=1, source_target_pairs={{1,0},{2,1},{3,2},{5,4},{6,5},{7,6},{9,8},{10,9},{11,10},{13,12},{... | collective-permute-start | bytes 1105928 | tf_op jit(solution)/shard_map/ppermute | solution.py:17
  27.3 0.2 broadcast_in_dim.90
  27.5 0.2 mul.115
  27.9 0.8 sub.59
  28.9 0.2 mul.128
  29.1 0.9 broadcast_in_dim.93
  30.0 0.2 sub.69
  30.2 1.3 %dynamic-slice_bitcast_fusion = bf16[3,3,80,640]{3,2,1,0:T(8,128)(2,1)S(1)} fusion(bf16[3,3,2,80,640]{4,3,2,1,0:T(8,128)(2,1)} %bitcast.47, s32[]{:T(128)S(6)} %select_n.131), kind=kLoop, calls=%fused_computation.66 | loop fusion | bytes 1843204 | tf_op jit(solution)/shard_map/jit(dynamic_index_in_dim)/squeeze | solution.py:33
  31.5 3.3 %collective-permute-done.3 = bf16[2,24,6,1,640]{4,1,3,2,0:T(8,128)(2,1)} collective-permute-done((bf16[2,24,6,1,640]{4,1,3,2,0:T(8,128)(2,1)}, bf16[2,24,6,1,640]{4,1,3,2,0:T(8,128)(2,1)}, u32[]{:S(2)}, u32[]{:S(2)}) %collective-permute-start.3) | collective-permute-done | bytes 368672 | tf_op jit(solution)/shard_map/ppermute | solution.py:17
  34.8 3.0 %pad_maximum_fusion = bf16[2,24,6,10,640]{4,1,3,2,0:T(8,128)(2,1)S(1)} fusion(bf16[2,24,6,1,640]{4,1,3,2,0:T(8,128)(2,1)} %collective-permute-done.3, bf16[2,24,1,8,640]{4,1,3,2,0:T(8,128)(2,1)S(1)} %collective-permute-done.1, bf16[1,24,4,8,640]{4,1,3,2,0:T(8,128)(2,1)S(1)} %get-tuple-element.21, bf16[1,24,4,8,640]{4,1,3,2,0:T(8,128)(2,1)S(1)} %get-tuple-element.22, ...), kind=kLoop, calls=%fused_computation | loop fusion | flops 9216000 | bytes 7372800 | tf_op jit(solution)/shard_map/concatenate | solution.py:18
  37.8 1.5 %fusion.33 = bf16[24,6,10,640]{3,0,2,1:T(8,128)(2,1)S(1)} fusion(bf16[2,24,6,10,640]{4,1,3,2,0:T(8,128)(2,1)S(1)} %pad_maximum_fusion, f32[640]{0:T(1024)S(1)} %copy-done.7, f32[640]{0:T(1024)S(1)} %copy-done.8, f32[24,640]{1,0:T(8,128)S(1)} %mul.128, f32[24,640]{1,0:T(8,128)S(1)} %sub.69, f32[6,10]{1,0:T(8,128)S(1)} %and_convert_fusion), kind=kLoop, calls=%fused_computation.35 | loop fusion | flops 10137600 | bytes 3814640 | tf_op jit(solution)/shard_map/convert_element_type | solution.py:166
  39.3 1.4 %fusion.62 = bf16[24,6,10,320]{3,0,2,1:T(8,128)(2,1)S(1)} fusion(bf16[24,6,10,640]{3,0,2,1:T(8,128)(2,1)S(1)} %fusion.33, s32[320]{0:T(512)S(1)} %get-tuple-element.17), kind=kOutput, calls=%fused_computation.80 | convolution fusion | flops 590028800 | bytes 2766080 | tf_op jit(solution)/shard_map/dot_general | solution.py:72
  40.7 0.2 fusion.35
  41.1 1.3 %collective-permute-start.6 = (bf16[3,3,80,640]{3,2,1,0:T(8,128)(2,1)}, bf16[3,3,80,640]{3,2,1,0:T(8,128)(2,1)S(1)}, u32[]{:S(2)}, u32[]{:S(2)}) collective-permute-start(bf16[3,3,80,640]{3,2,1,0:T(8,128)(2,1)} %collective-permute-done.5), channel_id=1, source_target_pairs={{0,16},{16,0},{1,17},{17,1},{2,18},{18,2},{3,19},{19,3},{4,20},{20... | collective-permute-start | bytes 2764808 | tf_op jit(solution)/shard_map/ppermute | solution.py:41
  42.4 1.4 %fusion.58 = bf16[24,6,10,320]{3,0,2,1:T(8,128)(2,1)S(1)} fusion(bf16[24,6,10,640]{3,0,2,1:T(8,128)(2,1)S(1)} %fusion.33, s32[320]{0:T(512)S(1)} %get-tuple-element.18), kind=kOutput, calls=%fused_computation.78 | convolution fusion | flops 590028800 | bytes 2766080 | tf_op jit(solution)/shard_map/dot_general | solution.py:72
  43.8 0.3 copy.74
  44.1 0.3 copy.75
  44.4 0.2 copy-done.2
  44.6 3.3 %fusion.37 = bf16[24,6,10,640]{3,0,2,1:T(8,128)(2,1)S(1)} fusion(f32[6,10]{1,0:T(8,128)S(1)} %and_convert_fusion, f32[640]{0:T(1024)S(1)} %copy-done.11, f32[640]{0:T(1024)S(1)} %copy-done.12, f32[24,640]{1,0:T(8,128)S(1)} %mul.115, f32[24,640]{1,0:T(8,128)S(1)} %copy-done.2, s32[640]{0:T(1024)S(1)} %fusion.81, ...), kind=kOutput, calls=%fused_computation.51 | convolution fusion | flops 1191116800 | bytes 3825664 | tf_op jit(solution)/shard_map/dot_general | solution.py:72
  47.9 1.2 %collective-permute-start.7 = (bf16[3,3,80,640]{3,2,1,0:T(8,128)(2,1)}, bf16[3,3,80,640]{3,2,1,0:T(8,128)(2,1)S(1)}, u32[]{:S(2)}, u32[]{:S(2)}) collective-permute-start(bf16[3,3,80,640]{3,2,1,0:T(8,128)(2,1)} %collective-permute-done.5), channel_id=1, source_target_pairs={{0,4},{4,0},{8,12},{12,8},{1,5},{5,1},{9,13},{13,9},{2,6},{6,2},{1... | collective-permute-start | bytes 2764808 | tf_op jit(solution)/shard_map/ppermute | solution.py:42
  49.2 13.7 %collective-permute-done.10 = bf16[3,3,80,640]{3,2,1,0:T(8,128)(2,1)S(1)} collective-permute-done((bf16[3,3,80,640]{3,2,1,0:T(8,128)(2,1)S(1)}, bf16[3,3,80,640]{3,2,1,0:T(8,128)(2,1)S(1)}, u32[]{:S(2)}, u32[]{:S(2)}) %collective-permute-start.10) | collective-permute-done | bytes 921632 | tf_op jit(solution)/shard_map/ppermute | solution.py:39
  62.9 1.2 %collective-permute-start.11 = (bf16[3,3,80,640]{3,2,1,0:T(8,128)(2,1)S(1)}, bf16[3,3,80,640]{3,2,1,0:T(8,128)(2,1)S(1)}, u32[]{:S(2)}, u32[]{:S(2)}) collective-permute-start(bf16[3,3,80,640]{3,2,1,0:T(8,128)(2,1)S(1)} %collective-permute-done.10), channel_id=1, source_target_pairs={{0,16},{16,0},{1,17},{17,1},{2,18},{18,2},{3,19},{19,3},{4,20},{20... | collective-permute-start | bytes 2764808 | tf_op jit(solution)/shard_map/ppermute | solution.py:41
  64.3 0.4 collective-permute-start.8
  64.7 6.0 %fusion = f32[24,4,8,640]{3,0,2,1:T(8,128)S(1)} fusion(bf16[3,3,160,640]{3,2,1,0:T(8,128)(2,1)} %collective-permute-done.4, bf16[3,3,160,640]{3,2,1,0:T(8,128)(2,1)} %param.25, bf16[24,6,10,640]{3,0,2,1:T(8,128)(2,1)S(1)} %fusion.37), kind=kOutput, calls=%fused_computation.1 | convolution fusion | flops 2838528000 | bytes 6758400 | tf_op jit(solution)/shard_map/conv_general_dilated | solution.py:81
  70.6 14.4 %collective-permute-done.11 = bf16[3,3,80,640]{3,2,1,0:T(8,128)(2,1)S(1)} collective-permute-done((bf16[3,3,80,640]{3,2,1,0:T(8,128)(2,1)S(1)}, bf16[3,3,80,640]{3,2,1,0:T(8,128)(2,1)S(1)}, u32[]{:S(2)}, u32[]{:S(2)}) %collective-permute-start.11) | collective-permute-done | bytes 921632 | tf_op jit(solution)/shard_map/ppermute | solution.py:41
  85.1 0.7 collective-permute-start.13
  85.8 6.0 %multiply_convert_fusion.1 = bf16[24,4,8,640]{3,0,2,1:T(8,128)(2,1)S(1)} fusion(f32[24,4,8,640]{3,0,2,1:T(8,128)S(1)} %fusion, bf16[3,3,80,640]{3,2,1,0:T(8,128)(2,1)S(1)} %collective-permute-done.8, bf16[3,3,80,640]{3,2,1,0:T(8,128)(2,1)S(1)} %collective-permute-done.7, bf16[3,3,80,640]{3,2,1,0:T(8,128)(2,1)S(1)} %collective-permute-done.6, ...), kind=kOutput, calls=%fused_computation.46 | convolution fusion | flops 2851799040 | bytes 7938048 | tf_op jit(solution)/shard_map/conv_general_dilated | solution.py:81
  91.8 0.8 convolution_convert_fusion.1
  92.6 0.8 convolution_convert_fusion
  93.4 1.7 %fusion.52 = (bf16[24,6,6,320]{3,2,1,0:T(8,128)(2,1)S(1)}, bf16[24,6,6,320]{3,2,1,0:T(8,128)(2,1)S(1)}, bf16[24,6,6,320]{3,2,1,0:T(8,128)(2,1)S(1)}, bf16[24,6,6,320]{3,2,1,0:T(8,128)(2,1)S(1)}) fusion(bf16[24,4,8,320]{3,2,1,0:T(8,128)(2,1)S(1)} %convolution_convert_fusion, bf16[24,6,10,320]{3,2,1,0:T(8,128)(2,1)S(1)} %copy.74, ...), kind=kLoop, calls=%fused_computation.70 | loop fusion | flops 1105920 | bytes 5406756 | tf_op jit(solution)/shard_map/jit(_where)/select_n | solution.py:179
  95.1 0.7 pad_maximum_fusion.2
  95.8 0.7 pad_maximum_fusion.1
  96.5 0.8 copy-done.1
  97.3 6.7 %fusion.12 = f32[24,4,10,640]{3,0,2,1:T(8,128)S(1)} fusion(bf16[3,3,160,640]{3,2,1,0:T(8,128)(2,1)} %collective-permute-done.9, bf16[3,3,160,640]{3,2,1,0:T(8,128)(2,1)S(1)} %copy-done.1, bf16[24,6,12,320]{3,2,1,0:T(8,128)(2,1)S(1)} %pad_maximum_fusion.1), kind=kOutput, calls=%fused_computation.13 | convolution fusion | flops 3546316800 | bytes 7249920 | tf_op jit(solution)/shard_map/conv_general_dilated | solution.py:81
  104.0 5.1 %fusion.38 = f32[24,4,10,640]{3,0,2,1:T(8,128)S(1)} fusion(f32[24,4,10,640]{3,0,2,1:T(8,128)S(1)} %fusion.12, bf16[3,3,80,640]{3,2,1,0:T(8,128)(2,1)S(1)} %collective-permute-done.13, bf16[3,3,80,640]{3,2,1,0:T(8,128)(2,1)S(1)} %collective-permute-done.12, bf16[3,3,80,640]{3,2,1,0:T(8,128)(2,1)S(1)} %collective-permute-done.11, ...), kind=kOutput, calls=%fused_computation.54 | convolution fusion | flops 3554304000 | bytes 9707520 | tf_op jit(solution)/shard_map/conv_general_dilated | solution.py:81
  109.3 1.0 copy-done
  110.3 0.7 fusion.49
  111.0 1.1 copy.55
  (51 shorter events, 1.2 us)
Async XLA Ops:
  2.2 11.8 %copy-start.6 = (s32[24,16]{0,1:T(8,128)S(1)}, s32[24,16]{0,1:T(8,128)}, u32[]{:S(2)}) copy-start(s32[24,16]{0,1:T(8,128)} %param.20) | copy-start | bytes 4612
  3.1 11.2 %collective-permute-start = (bf16[2,24,1,8,640]{4,1,3,2,0:T(8,128)(2,1)}, bf16[2,24,1,8,640]{4,1,3,2,0:T(8,128)(2,1)S(1)}, u32[]{:S(2)}, u32[]{:S(2)}) collective-permute-start(bf16[2,24,1,8,640]{4,1,3,2,0:T(8,128)(2,1)} %get-tuple-element.15), channel_id=1, source_target_pairs={{0,4},{4,8},{8,12},{1,5},{5,9},{9,13},{2,6},{6,10},{10,14},{3,7},{... | collective-permute-start | bytes 1474568 | tf_op jit(solution)/shard_map/ppermute | solution.py:14
  7.6 13.0 %collective-permute-start.1 = (bf16[2,24,1,8,640]{4,1,3,2,0:T(8,128)(2,1)S(1)}, bf16[2,24,1,8,640]{4,1,3,2,0:T(8,128)(2,1)S(1)}, u32[]{:S(2)}, u32[]{:S(2)}) collective-permute-start(bf16[2,24,1,8,640]{4,1,3,2,0:T(8,128)(2,1)S(1)} %get-tuple-element.16), channel_id=1, source_target_pairs={{4,0},{8,4},{12,8},{5,1},{9,5},{13,9},{6,2},{10,6},{14,10},{7,3},{... | collective-permute-start | bytes 1474568 | tf_op jit(solution)/shard_map/ppermute | solution.py:17
  9.5 54.7 %collective-permute-start.4 = (bf16[3,3,160,640]{3,2,1,0:T(8,128)(2,1)}, bf16[3,3,160,640]{3,2,1,0:T(8,128)(2,1)}, u32[]{:S(2)}, u32[]{:S(2)}) collective-permute-start(bf16[3,3,160,640]{3,2,1,0:T(8,128)(2,1)} %param.25), channel_id=1, source_target_pairs={{0,4},{4,0},{8,12},{12,8},{1,5},{5,1},{9,13},{13,9},{2,6},{6,2},{1... | collective-permute-start | bytes 5529608 | tf_op jit(solution)/shard_map/ppermute | solution.py:34
  9.6 17.7 %copy-start.3 = (f32[24,32]{1,0:T(8,128)S(1)}, f32[24,32]{1,0:T(8,128)}, u32[]{:S(2)}) copy-start(f32[24,32]{1,0:T(8,128)} %param.22) | copy-start | bytes 9220
  11.8 15.9 %copy-start.4 = (f32[24,32]{1,0:T(8,128)S(1)}, f32[24,32]{1,0:T(8,128)}, u32[]{:S(2)}) copy-start(f32[24,32]{1,0:T(8,128)} %param.21) | copy-start | bytes 9220
  11.8 29.2 %collective-permute-start.5 = (bf16[3,3,80,640]{3,2,1,0:T(8,128)(2,1)}, bf16[3,3,80,640]{3,2,1,0:T(8,128)(2,1)}, u32[]{:S(2)}, u32[]{:S(2)}) collective-permute-start(bf16[3,3,80,640]{3,2,1,0:T(8,128)(2,1)} %dynamic-slice_bitcast_fusion.1), channel_id=1, source_target_pairs={{8,0},{12,4},{0,8},{4,12},{9,1},{13,5},{1,9},{5,13},{10,2},{14,6},... | collective-permute-start | bytes 2764808 | tf_op jit(solution)/shard_map/ppermute | solution.py:39
  13.6 82.9 %collective-permute-start.9 = (bf16[3,3,160,640]{3,2,1,0:T(8,128)(2,1)}, bf16[3,3,160,640]{3,2,1,0:T(8,128)(2,1)}, u32[]{:S(2)}, u32[]{:S(2)}) collective-permute-start(bf16[3,3,160,640]{3,2,1,0:T(8,128)(2,1)} %param.32), channel_id=1, source_target_pairs={{0,4},{4,0},{8,12},{12,8},{1,5},{5,1},{9,13},{13,9},{2,6},{6,2},{1... | collective-permute-start | bytes 5529608 | tf_op jit(solution)/shard_map/ppermute | solution.py:34
  14.2 14.5 %copy-start.5 = (f32[24,32]{1,0:T(8,128)S(1)}, f32[24,32]{1,0:T(8,128)}, u32[]{:S(2)}) copy-start(f32[24,32]{1,0:T(8,128)} %param.29) | copy-start | bytes 9220
  21.6 9.9 %collective-permute-start.2 = (bf16[2,24,6,1,640]{4,1,3,2,0:T(8,128)(2,1)}, bf16[2,24,6,1,640]{4,1,3,2,0:T(8,128)(2,1)}, u32[]{:S(2)}, u32[]{:S(2)}) collective-permute-start(bf16[2,24,6,1,640]{4,1,3,2,0:T(8,128)(2,1)} %get-tuple-element.7), channel_id=1, source_target_pairs={{0,1},{1,2},{2,3},{4,5},{5,6},{6,7},{8,9},{9,10},{10,11},{12,13},{... | collective-permute-start | bytes 1105928 | tf_op jit(solution)/shard_map/ppermute | solution.py:14
  26.0 8.9 %collective-permute-start.3 = (bf16[2,24,6,1,640]{4,1,3,2,0:T(8,128)(2,1)}, bf16[2,24,6,1,640]{4,1,3,2,0:T(8,128)(2,1)}, u32[]{:S(2)}, u32[]{:S(2)}) collective-permute-start(bf16[2,24,6,1,640]{4,1,3,2,0:T(8,128)(2,1)} %get-tuple-element.8), channel_id=1, source_target_pairs={{1,0},{2,1},{3,2},{5,4},{6,5},{7,6},{9,8},{10,9},{11,10},{13,12},{... | collective-permute-start | bytes 1105928 | tf_op jit(solution)/shard_map/ppermute | solution.py:17
  31.5 6.3 %copy-start.7 = (f32[640]{0:T(1024)S(1)}, f32[640]{0:T(1024)}, u32[]{:S(2)}) copy-start(f32[640]{0:T(1024)} %param.31) | copy-start | bytes 7684
  31.5 6.3 %copy-start.8 = (f32[640]{0:T(1024)S(1)}, f32[640]{0:T(1024)}, u32[]{:S(2)}) copy-start(f32[640]{0:T(1024)} %param.30) | copy-start | bytes 7684
  41.0 21.9 %collective-permute-start.10 = (bf16[3,3,80,640]{3,2,1,0:T(8,128)(2,1)S(1)}, bf16[3,3,80,640]{3,2,1,0:T(8,128)(2,1)S(1)}, u32[]{:S(2)}, u32[]{:S(2)}) collective-permute-start(bf16[3,3,80,640]{3,2,1,0:T(8,128)(2,1)S(1)} %dynamic-slice_bitcast_fusion), channel_id=1, source_target_pairs={{8,0},{12,4},{0,8},{4,12},{9,1},{13,5},{1,9},{5,13},{10,2},{14,6},... | collective-permute-start | bytes 2764808 | tf_op jit(solution)/shard_map/ppermute | solution.py:39
  41.1 23.2 %collective-permute-start.6 = (bf16[3,3,80,640]{3,2,1,0:T(8,128)(2,1)}, bf16[3,3,80,640]{3,2,1,0:T(8,128)(2,1)S(1)}, u32[]{:S(2)}, u32[]{:S(2)}) collective-permute-start(bf16[3,3,80,640]{3,2,1,0:T(8,128)(2,1)} %collective-permute-done.5), channel_id=1, source_target_pairs={{0,16},{16,0},{1,17},{17,1},{2,18},{18,2},{3,19},{19,3},{4,20},{20... | collective-permute-start | bytes 2764808 | tf_op jit(solution)/shard_map/ppermute | solution.py:41
  43.8 0.8 copy-start.2
  43.8 0.8 copy-start.11
  43.8 0.8 copy-start.12
  47.9 37.9 %copy-start.10 = (f32[24,640]{1,0:T(8,128)S(1)}, f32[24,640]{1,0:T(8,128)}, u32[]{:S(2)}) copy-start(f32[24,640]{1,0:T(8,128)} %param.27) | copy-start | bytes 184324
  47.9 37.9 %copy-start.13 = (f32[640]{0:T(1024)S(1)}, f32[640]{0:T(1024)}, u32[]{:S(2)}) copy-start(f32[640]{0:T(1024)} %param.26) | copy-start | bytes 7684
  47.9 37.8 %collective-permute-start.7 = (bf16[3,3,80,640]{3,2,1,0:T(8,128)(2,1)}, bf16[3,3,80,640]{3,2,1,0:T(8,128)(2,1)S(1)}, u32[]{:S(2)}, u32[]{:S(2)}) collective-permute-start(bf16[3,3,80,640]{3,2,1,0:T(8,128)(2,1)} %collective-permute-done.5), channel_id=1, source_target_pairs={{0,4},{4,0},{8,12},{12,8},{1,5},{5,1},{9,13},{13,9},{2,6},{6,2},{1... | collective-permute-start | bytes 2764808 | tf_op jit(solution)/shard_map/ppermute | solution.py:42
  62.9 22.1 %collective-permute-start.11 = (bf16[3,3,80,640]{3,2,1,0:T(8,128)(2,1)S(1)}, bf16[3,3,80,640]{3,2,1,0:T(8,128)(2,1)S(1)}, u32[]{:S(2)}, u32[]{:S(2)}) collective-permute-start(bf16[3,3,80,640]{3,2,1,0:T(8,128)(2,1)S(1)} %collective-permute-done.10), channel_id=1, source_target_pairs={{0,16},{16,0},{1,17},{17,1},{2,18},{18,2},{3,19},{19,3},{4,20},{20... | collective-permute-start | bytes 2764808 | tf_op jit(solution)/shard_map/ppermute | solution.py:41
  64.2 39.8 %collective-permute-start.12 = (bf16[3,3,80,640]{3,2,1,0:T(8,128)(2,1)S(1)}, bf16[3,3,80,640]{3,2,1,0:T(8,128)(2,1)S(1)}, u32[]{:S(2)}, u32[]{:S(2)}) collective-permute-start(bf16[3,3,80,640]{3,2,1,0:T(8,128)(2,1)S(1)} %collective-permute-done.10), channel_id=1, source_target_pairs={{0,4},{4,0},{8,12},{12,8},{1,5},{5,1},{9,13},{13,9},{2,6},{6,2},{1... | collective-permute-start | bytes 2764808 | tf_op jit(solution)/shard_map/ppermute | solution.py:42
  64.3 21.5 %collective-permute-start.8 = (bf16[3,3,80,640]{3,2,1,0:T(8,128)(2,1)S(1)}, bf16[3,3,80,640]{3,2,1,0:T(8,128)(2,1)S(1)}, u32[]{:S(2)}, u32[]{:S(2)}) collective-permute-start(bf16[3,3,80,640]{3,2,1,0:T(8,128)(2,1)S(1)} %collective-permute-done.6), channel_id=1, source_target_pairs={{0,4},{4,0},{8,12},{12,8},{1,5},{5,1},{9,13},{13,9},{2,6},{6,2},{1... | collective-permute-start | bytes 2764808 | tf_op jit(solution)/shard_map/ppermute | solution.py:43
  85.1 18.9 %collective-permute-start.13 = (bf16[3,3,80,640]{3,2,1,0:T(8,128)(2,1)S(1)}, bf16[3,3,80,640]{3,2,1,0:T(8,128)(2,1)S(1)}, u32[]{:S(2)}, u32[]{:S(2)}) collective-permute-start(bf16[3,3,80,640]{3,2,1,0:T(8,128)(2,1)S(1)} %collective-permute-done.11), channel_id=1, source_target_pairs={{0,4},{4,0},{8,12},{12,8},{1,5},{5,1},{9,13},{13,9},{2,6},{6,2},{1... | collective-permute-start | bytes 2764808 | tf_op jit(solution)/shard_map/ppermute | solution.py:43
  95.8 1.5 %copy-start.1 = (bf16[3,3,160,640]{3,2,1,0:T(8,128)(2,1)S(1)}, bf16[3,3,160,640]{3,2,1,0:T(8,128)(2,1)}, u32[]{:S(2)}) copy-start(bf16[3,3,160,640]{3,2,1,0:T(8,128)(2,1)} %param.32) | copy-start | bytes 5529604
  109.1 1.2 %copy-start = (bf16[24,4,8,640]{3,2,1,0:T(8,128)(2,1)S(1)}, bf16[24,4,8,640]{3,2,1,0:T(8,128)(2,1)}, u32[]{:S(2)}) copy-start(bf16[24,4,8,640]{3,2,1,0:T(8,128)(2,1)} %param.19) | copy-start | bytes 2949124
  109.1 1.2 %copy-start.9 = (f32[640]{0:T(1024)S(1)}, f32[640]{0:T(1024)}, u32[]{:S(2)}) copy-start(f32[640]{0:T(1024)} %param.33) | copy-start | bytes 7684

commit v19 on v15

--- a/solution.py
+++ b/solution.py
@@ -26,18 +26,14 @@
     mate_pairs = [(i, i ^ 1) for i in range(count)]
     parity = lax.axis_index("groups") % 2
     wholes = []
-    previous = None
     for shard in kernels:
         depth = shard.shape[2]
         halves = shard.reshape(shard.shape[:2] + (2, depth // 2) + shard.shape[3:])
         mine = lax.dynamic_index_in_dim(halves, parity, axis=2, keepdims=False)
         held = [shard, lax.ppermute(shard, "row", mate_pairs)]
         for step in range(1, chips):
-            if previous is not None:
-                mine, _ = lax.optimization_barrier((mine, previous))
             pairs = [(((i // 2 + step) % chips) * 2 + i % 2, i) for i in range(count)]
             fetched = lax.ppermute(mine, "row", pairs)
-            previous = fetched
             other = lax.ppermute(fetched, "groups", y_pairs)
             relayed = lax.ppermute(fetched, "row", mate_pairs)
             other_relayed = lax.ppermute(other, "row", mate_pairs)

time: 112 us -> 116 us (1.036)
  starting transfers between devices: 19.4 us -> 21.9 us
  waiting for transfers between devices: 36.9 us -> 38.2 us
    ppermute x2, waiting for transfers between devices: 14.3 us -> 18.1 us  [gather_weights(): other = lax.ppermute(fetched, 'groups', y_pairs)]
    ppermute x2, waiting for transfers between devices: 14.9 us -> 12.5 us  [gather_weights(): fetched = lax.ppermute(mine, 'row', pairs)]
    ppermute x2, starting transfers between devices: 1.84 us -> 3.71 us  [gather_weights(): relayed = lax.ppermute(fetched, 'row', mate_pairs)]
  transfers between devices with their start and end apart: 14 -> 14, of which waited for: 4 -> 4; matrix products, arithmetic and copies ran while one was open for 39% -> 37% of each run, Pallas kernels for 0% -> 0%
where the time goes in v19:
time: 116 us; the launch traced here: 115 us
  waiting for transfers between devices  38.2 us (33%)
  matrix products  31.4 us (27%)
  starting transfers between devices  21.9 us (19%)
  other arithmetic  12.2 us (11%)
  local copies, waits for them, and re-layouts  10.9 us (9%)
    conv_general_dilated x4, matrix products, conv_valid(): lax.conv_general_dilated(activation, kernel, window_strides=(1, 1), paddi...  23.8 us
    ppermute x2, waiting for transfers between devices, gather_weights(): other = lax.ppermute(fetched, 'groups', y_pairs)  18.1 us
    ppermute x2, waiting for transfers between devices, gather_weights(): fetched = lax.ppermute(mine, 'row', pairs)  12.5 us
    ppermute x2, starting transfers between devices, padded_2(): lax.ppermute(lax.slice_in_dim(block, block.shape[dim] - width, None, axis...  8.57 us
    ppermute x2, waiting for transfers between devices, padded_2(): lax.ppermute(lax.slice_in_dim(block, 0, width, axis=dim), axis, backward)  7.62 us
    dot_general x3, matrix products, to_relative(): moved = jnp.dot(activation, chooser, preferred_element_type=jnp.float32)  7.61 us
    ppermute x2, starting transfers between devices, gather_weights(): relayed = lax.ppermute(fetched, 'row', mate_pairs)  3.71 us
    squeeze x2, local copies, waits for them, and re-layouts, gather_weights(): mine = lax.dynamic_index_in_dim(halves, parity, axis=2, keepdims=False)  3.46 us
  transfers between devices with their start and end apart: 14, of which 4 were waited for; matrix products, arithmetic and copies ran while one was open for 37% of the time, Pallas kernels for 0%

profile of v19, /device:TPU:1, one launch (start us, length us, event | category | flops | bytes accessed | tf_op | source)
XLA Modules:
  0.0 115.0 jit_solution(4878221824937272406)
XLA Ops:
  0.0 2.1 %copy_bitcast_fusion = (bf16[1,24,4,8,640]{4,1,3,2,0:T(8,128)(2,1)S(1)}, bf16[1,24,4,8,640]{4,1,3,2,0:T(8,128)(2,1)S(1)}) fusion(bf16[24,4,8,640]{3,2,1,0:T(8,128)(2,1)} %param.18, bf16[24,4,8,640]{3,2,1,0:T(8,128)(2,1)} %param.17), kind=kLoop, calls=%fused_computation.73 | loop fusion | bytes 3932160 | tf_op jit(solution)/shard_map/stack | solution.py:125
  2.2 0.9 pad_maximum_fusion.3
  3.1 4.6 %collective-permute-start = (bf16[2,24,1,8,640]{4,1,3,2,0:T(8,128)(2,1)}, bf16[2,24,1,8,640]{4,1,3,2,0:T(8,128)(2,1)S(1)}, u32[]{:S(2)}, u32[]{:S(2)}) collective-permute-start(bf16[2,24,1,8,640]{4,1,3,2,0:T(8,128)(2,1)} %get-tuple-element.13), channel_id=1, source_target_pairs={{0,4},{4,8},{8,12},{1,5},{5,9},{9,13},{2,6},{6,10},{10,14},{3,7},{... | collective-permute-start | bytes 1474568 | tf_op jit(solution)/shard_map/ppermute | solution.py:14
  7.7 1.9 %collective-permute-start.1 = (bf16[2,24,1,8,640]{4,1,3,2,0:T(8,128)(2,1)S(1)}, bf16[2,24,1,8,640]{4,1,3,2,0:T(8,128)(2,1)S(1)}, u32[]{:S(2)}, u32[]{:S(2)}) collective-permute-start(bf16[2,24,1,8,640]{4,1,3,2,0:T(8,128)(2,1)S(1)} %get-tuple-element.14), channel_id=1, source_target_pairs={{4,0},{8,4},{12,8},{5,1},{9,5},{13,9},{6,2},{10,6},{14,10},{7,3},{... | collective-permute-start | bytes 1474568 | tf_op jit(solution)/shard_map/ppermute | solution.py:17
  9.7 2.2 %dynamic-slice_bitcast_fusion.1 = bf16[3,3,80,640]{3,2,1,0:T(8,128)(2,1)} fusion(bf16[3,3,2,80,640]{4,3,2,1,0:T(8,128)(2,1)} %bitcast.6, s32[]{:T(128)S(6)} %select_n.125), kind=kLoop, calls=%fused_computation.76 | loop fusion | bytes 1843204 | tf_op jit(solution)/shard_map/jit(dynamic_index_in_dim)/squeeze | solution.py:32
  11.9 1.8 %collective-permute-start.5 = (bf16[3,3,80,640]{3,2,1,0:T(8,128)(2,1)}, bf16[3,3,80,640]{3,2,1,0:T(8,128)(2,1)}, u32[]{:S(2)}, u32[]{:S(2)}) collective-permute-start(bf16[3,3,80,640]{3,2,1,0:T(8,128)(2,1)} %dynamic-slice_bitcast_fusion.1), channel_id=1, source_target_pairs={{8,0},{12,4},{0,8},{4,12},{9,1},{13,5},{1,9},{5,13},{10,2},{14,6},... | collective-permute-start | bytes 2764808 | tf_op jit(solution)/shard_map/ppermute | solution.py:36
  13.7 0.3 collective-permute-start.9
  14.1 0.5 compare_and_fusion.1
  14.6 0.6 fusion.83
  15.2 0.7 compare_reduce_fusion
  16.0 4.7 %collective-permute-done.1 = bf16[2,24,1,8,640]{4,1,3,2,0:T(8,128)(2,1)S(1)} collective-permute-done((bf16[2,24,1,8,640]{4,1,3,2,0:T(8,128)(2,1)S(1)}, bf16[2,24,1,8,640]{4,1,3,2,0:T(8,128)(2,1)S(1)}, u32[]{:S(2)}, u32[]{:S(2)}) %collective-permute-start.1) | collective-permute-done | bytes 491552 | tf_op jit(solution)/shard_map/ppermute | solution.py:17
  20.7 1.0 pad_maximum_fusion.7
  21.8 3.9 %collective-permute-start.2 = (bf16[2,24,6,1,640]{4,1,3,2,0:T(8,128)(2,1)}, bf16[2,24,6,1,640]{4,1,3,2,0:T(8,128)(2,1)}, u32[]{:S(2)}, u32[]{:S(2)}) collective-permute-start(bf16[2,24,6,1,640]{4,1,3,2,0:T(8,128)(2,1)} %get-tuple-element.9), channel_id=1, source_target_pairs={{0,1},{1,2},{2,3},{4,5},{5,6},{6,7},{8,9},{9,10},{10,11},{12,13},{... | collective-permute-start | bytes 1105928 | tf_op jit(solution)/shard_map/ppermute | solution.py:14
  25.7 1.3 %collective-permute-start.3 = (bf16[2,24,6,1,640]{4,1,3,2,0:T(8,128)(2,1)}, bf16[2,24,6,1,640]{4,1,3,2,0:T(8,128)(2,1)}, u32[]{:S(2)}, u32[]{:S(2)}) collective-permute-start(bf16[2,24,6,1,640]{4,1,3,2,0:T(8,128)(2,1)} %get-tuple-element.10), channel_id=1, source_target_pairs={{1,0},{2,1},{3,2},{5,4},{6,5},{7,6},{9,8},{10,9},{11,10},{13,12},{... | collective-permute-start | bytes 1105928 | tf_op jit(solution)/shard_map/ppermute | solution.py:17
  27.0 0.6 compare_and_fusion
  27.7 0.2 mul.115
  28.0 0.2 broadcast_in_dim.42
  28.1 0.8 sub.59
  29.2 0.2 mul.128
  29.4 0.2 broadcast_in_dim.79
  29.5 0.2 sub.69
  29.8 1.3 %dynamic-slice_bitcast_fusion = bf16[3,3,80,640]{3,2,1,0:T(8,128)(2,1)S(1)} fusion(bf16[3,3,2,80,640]{4,3,2,1,0:T(8,128)(2,1)} %bitcast.38, s32[]{:T(128)S(6)} %select_n.125), kind=kLoop, calls=%fused_computation.75 | loop fusion | bytes 1843204 | tf_op jit(solution)/shard_map/jit(dynamic_index_in_dim)/squeeze | solution.py:32
  31.1 0.7 and_convert_fusion
  31.8 2.9 %collective-permute-done.3 = bf16[2,24,6,1,640]{4,1,3,2,0:T(8,128)(2,1)} collective-permute-done((bf16[2,24,6,1,640]{4,1,3,2,0:T(8,128)(2,1)}, bf16[2,24,6,1,640]{4,1,3,2,0:T(8,128)(2,1)}, u32[]{:S(2)}, u32[]{:S(2)}) %collective-permute-start.3) | collective-permute-done | bytes 368672 | tf_op jit(solution)/shard_map/ppermute | solution.py:17
  34.7 3.0 %pad_maximum_fusion = bf16[2,24,6,10,640]{4,1,3,2,0:T(8,128)(2,1)S(1)} fusion(bf16[2,24,6,1,640]{4,1,3,2,0:T(8,128)(2,1)} %collective-permute-done.3, bf16[2,24,1,8,640]{4,1,3,2,0:T(8,128)(2,1)S(1)} %collective-permute-done.1, bf16[1,24,4,8,640]{4,1,3,2,0:T(8,128)(2,1)S(1)} %get-tuple-element.15, bf16[1,24,4,8,640]{4,1,3,2,0:T(8,128)(2,1)S(1)} %get-tuple-element.16, ...), kind=kLoop, calls=%fused_computation.1 | loop fusion | flops 9216000 | bytes 7372800 | tf_op jit(solution)/shard_map/concatenate | solution.py:18
  37.7 3.3 %fusion.35 = bf16[24,6,10,640]{3,0,2,1:T(8,128)(2,1)S(1)} fusion(bf16[2,24,6,10,640]{4,1,3,2,0:T(8,128)(2,1)S(1)} %pad_maximum_fusion, f32[640]{0:T(1024)S(1)} %copy-done.15, f32[640]{0:T(1024)S(1)} %copy-done.16, f32[24,640]{1,0:T(8,128)S(1)} %mul.128, f32[24,640]{1,0:T(8,128)S(1)} %sub.69, f32[6,10]{1,0:T(8,128)S(1)} %and_convert_fusion, ...), kind=kOutput, calls=%fused_computation.46 | convolution fusion | flops 1190195200 | bytes 3825664 | tf_op jit(solution)/shard_map/dot_general | solution.py:68
  41.0 1.3 %collective-permute-start.6 = (bf16[3,3,80,640]{3,2,1,0:T(8,128)(2,1)}, bf16[3,3,80,640]{3,2,1,0:T(8,128)(2,1)S(1)}, u32[]{:S(2)}, u32[]{:S(2)}) collective-permute-start(bf16[3,3,80,640]{3,2,1,0:T(8,128)(2,1)} %collective-permute-done.5), channel_id=1, source_target_pairs={{0,16},{16,0},{1,17},{17,1},{2,18},{18,2},{3,19},{19,3},{4,20},{20... | collective-permute-start | bytes 2764808 | tf_op jit(solution)/shard_map/ppermute | solution.py:37
  42.3 12.5 %collective-permute-done.10 = bf16[3,3,80,640]{3,2,1,0:T(8,128)(2,1)S(1)} collective-permute-done((bf16[3,3,80,640]{3,2,1,0:T(8,128)(2,1)S(1)}, bf16[3,3,80,640]{3,2,1,0:T(8,128)(2,1)S(1)}, u32[]{:S(2)}, u32[]{:S(2)}) %collective-permute-start.10) | collective-permute-done | bytes 921632 | tf_op jit(solution)/shard_map/ppermute | solution.py:36
  54.8 1.2 %collective-permute-start.11 = (bf16[3,3,80,640]{3,2,1,0:T(8,128)(2,1)S(1)}, bf16[3,3,80,640]{3,2,1,0:T(8,128)(2,1)S(1)}, u32[]{:S(2)}, u32[]{:S(2)}) collective-permute-start(bf16[3,3,80,640]{3,2,1,0:T(8,128)(2,1)S(1)} %collective-permute-done.10), channel_id=1, source_target_pairs={{0,16},{16,0},{1,17},{17,1},{2,18},{18,2},{3,19},{19,3},{4,20},{20... | collective-permute-start | bytes 2764808 | tf_op jit(solution)/shard_map/ppermute | solution.py:37
  56.0 0.2 fusion.37
  56.3 0.4 copy.63
  56.7 0.3 copy-done.2
  57.1 3.3 %fusion.45 = bf16[24,6,10,640]{3,0,2,1:T(8,128)(2,1)S(1)} fusion(f32[6,10]{1,0:T(8,128)S(1)} %and_convert_fusion, f32[640]{0:T(1024)S(1)} %copy-done.13, f32[640]{0:T(1024)S(1)} %copy-done.14, f32[24,640]{1,0:T(8,128)S(1)} %mul.115, f32[24,640]{1,0:T(8,128)S(1)} %copy-done.2, s32[640]{0:T(1024)S(1)} %copy-done.8, ...), kind=kOutput, calls=%fused_computation.57 | convolution fusion | flops 1191116800 | bytes 3825664 | tf_op jit(solution)/shard_map/dot_general | solution.py:68
  60.4 3.6 %collective-permute-start.7 = (bf16[3,3,80,640]{3,2,1,0:T(8,128)(2,1)}, bf16[3,3,80,640]{3,2,1,0:T(8,128)(2,1)S(1)}, u32[]{:S(2)}, u32[]{:S(2)}) collective-permute-start(bf16[3,3,80,640]{3,2,1,0:T(8,128)(2,1)} %collective-permute-done.5), channel_id=1, source_target_pairs={{0,4},{4,0},{8,12},{12,8},{1,5},{5,1},{9,13},{13,9},{2,6},{6,2},{1... | collective-permute-start | bytes 2764808 | tf_op jit(solution)/shard_map/ppermute | solution.py:38
  64.1 0.6 collective-permute-start.8
  64.7 18.1 %collective-permute-done.11 = bf16[3,3,80,640]{3,2,1,0:T(8,128)(2,1)S(1)} collective-permute-done((bf16[3,3,80,640]{3,2,1,0:T(8,128)(2,1)S(1)}, bf16[3,3,80,640]{3,2,1,0:T(8,128)(2,1)S(1)}, u32[]{:S(2)}, u32[]{:S(2)}) %collective-permute-start.11) | collective-permute-done | bytes 921632 | tf_op jit(solution)/shard_map/ppermute | solution.py:37
  82.9 1.0 collective-permute-start.13
  83.9 6.0 %fusion = f32[24,4,8,640]{3,0,2,1:T(8,128)S(1)} fusion(bf16[3,3,160,640]{3,2,1,0:T(8,128)(2,1)} %collective-permute-done.4, bf16[3,3,160,640]{3,2,1,0:T(8,128)(2,1)} %param.25, bf16[24,6,10,640]{3,0,2,1:T(8,128)(2,1)S(1)} %fusion.45), kind=kOutput, calls=%fused_computation.2 | convolution fusion | flops 2838528000 | bytes 6758400 | tf_op jit(solution)/shard_map/conv_general_dilated | solution.py:77
  89.9 6.0 %multiply_convert_fusion.1 = bf16[24,4,8,640]{3,0,2,1:T(8,128)(2,1)S(1)} fusion(f32[24,4,8,640]{3,0,2,1:T(8,128)S(1)} %fusion, bf16[3,3,80,640]{3,2,1,0:T(8,128)(2,1)S(1)} %collective-permute-done.8, bf16[3,3,80,640]{3,2,1,0:T(8,128)(2,1)S(1)} %collective-permute-done.7, bf16[3,3,80,640]{3,2,1,0:T(8,128)(2,1)S(1)} %collective-permute-done.6, ...), kind=kOutput, calls=%fused_computation.45 | convolution fusion | flops 2851799040 | bytes 7938048 | tf_op jit(solution)/shard_map/conv_general_dilated | solution.py:77
  95.9 1.0 fusion.59
  97.0 1.2 %fusion.58 = (bf16[24,6,6,640]{3,2,1,0:T(8,128)(2,1)S(1)}, bf16[24,6,6,640]{3,2,1,0:T(8,128)(2,1)S(1)}) fusion(bf16[24,4,8,640]{3,2,1,0:T(8,128)(2,1)S(1)} %fusion.59, bf16[24,6,10,640]{3,2,1,0:T(8,128)(2,1)S(1)} %copy.63, pred[6,6]{1,0:T(8,128)(4,1)S(1)} %broadcast_and_fusion), kind=kLoop, calls=%fused_computation.65 | loop fusion | flops 1105920 | bytes 5406756 | tf_op jit(solution)/shard_map/jit(_where)/select_n | solution.py:171
  98.2 2.1 %pad_maximum_fusion.1 = (bf16[24,6,12,320]{3,2,1,0:T(8,128)(2,1)S(1)}, bf16[24,6,12,320]{3,2,1,0:T(8,128)(2,1)S(1)}) fusion(bf16[24,6,6,640]{3,2,1,0:T(8,128)(2,1)S(1)} %get-tuple-element.5, bf16[24,6,6,640]{3,2,1,0:T(8,128)(2,1)S(1)} %get-tuple-element.6), kind=kLoop, calls=%fused_computation.59 | loop fusion | flops 4423680 | bytes 4423680 | tf_op jit(solution)/shard_map/concatenate | solution.py:172
  100.3 6.5 %fusion.12 = f32[24,4,10,640]{3,0,2,1:T(8,128)S(1)} fusion(bf16[3,3,160,640]{3,2,1,0:T(8,128)(2,1)} %collective-permute-done.9, bf16[3,3,160,640]{3,2,1,0:T(8,128)(2,1)S(1)} %copy-done.1, bf16[24,6,12,320]{3,2,1,0:T(8,128)(2,1)S(1)} %get-tuple-element.8), kind=kOutput, calls=%fused_computation.14 | convolution fusion | flops 3546316800 | bytes 7249920 | tf_op jit(solution)/shard_map/conv_general_dilated | solution.py:77
  106.8 5.3 %fusion.47 = f32[24,4,10,640]{3,0,2,1:T(8,128)S(1)} fusion(f32[24,4,10,640]{3,0,2,1:T(8,128)S(1)} %fusion.12, bf16[3,3,80,640]{3,2,1,0:T(8,128)(2,1)S(1)} %collective-permute-done.13, bf16[3,3,80,640]{3,2,1,0:T(8,128)(2,1)S(1)} %collective-permute-done.12, bf16[3,3,80,640]{3,2,1,0:T(8,128)(2,1)S(1)} %collective-permute-done.11, ...), kind=kOutput, calls=%fused_computation.60 | convolution fusion | flops 3554304000 | bytes 9707520 | tf_op jit(solution)/shard_map/conv_general_dilated | solution.py:77
  112.4 0.5 copy-done.10
  112.9 0.5 copy-done
  113.4 0.6 fusion.66
  114.0 1.1 copy.49
  (53 shorter events, 0.9 us)
Async XLA Ops:
  2.2 13.1 %copy-start.7 = (s32[24,16]{0,1:T(8,128)S(1)}, s32[24,16]{0,1:T(8,128)}, u32[]{:S(2)}) copy-start(s32[24,16]{0,1:T(8,128)} %param.20) | copy-start | bytes 4612
  3.1 24.5 %copy-start.3 = (f32[24,32]{1,0:T(8,128)S(1)}, f32[24,32]{1,0:T(8,128)}, u32[]{:S(2)}) copy-start(f32[24,32]{1,0:T(8,128)} %param.22) | copy-start | bytes 9220
  3.1 12.9 %collective-permute-start = (bf16[2,24,1,8,640]{4,1,3,2,0:T(8,128)(2,1)}, bf16[2,24,1,8,640]{4,1,3,2,0:T(8,128)(2,1)S(1)}, u32[]{:S(2)}, u32[]{:S(2)}) collective-permute-start(bf16[2,24,1,8,640]{4,1,3,2,0:T(8,128)(2,1)} %get-tuple-element.13), channel_id=1, source_target_pairs={{0,4},{4,8},{8,12},{1,5},{5,9},{9,13},{2,6},{6,10},{10,14},{3,7},{... | collective-permute-start | bytes 1474568 | tf_op jit(solution)/shard_map/ppermute | solution.py:14
  7.7 13.0 %collective-permute-start.1 = (bf16[2,24,1,8,640]{4,1,3,2,0:T(8,128)(2,1)S(1)}, bf16[2,24,1,8,640]{4,1,3,2,0:T(8,128)(2,1)S(1)}, u32[]{:S(2)}, u32[]{:S(2)}) collective-permute-start(bf16[2,24,1,8,640]{4,1,3,2,0:T(8,128)(2,1)S(1)} %get-tuple-element.14), channel_id=1, source_target_pairs={{4,0},{8,4},{12,8},{5,1},{9,5},{13,9},{6,2},{10,6},{14,10},{7,3},{... | collective-permute-start | bytes 1474568 | tf_op jit(solution)/shard_map/ppermute | solution.py:17
  9.6 54.4 %collective-permute-start.4 = (bf16[3,3,160,640]{3,2,1,0:T(8,128)(2,1)}, bf16[3,3,160,640]{3,2,1,0:T(8,128)(2,1)}, u32[]{:S(2)}, u32[]{:S(2)}) collective-permute-start(bf16[3,3,160,640]{3,2,1,0:T(8,128)(2,1)} %param.25), channel_id=1, source_target_pairs={{0,4},{4,0},{8,12},{12,8},{1,5},{5,1},{9,13},{13,9},{2,6},{6,2},{1... | collective-permute-start | bytes 5529608 | tf_op jit(solution)/shard_map/ppermute | solution.py:33
  9.7 18.2 %copy-start.4 = (f32[24,32]{1,0:T(8,128)S(1)}, f32[24,32]{1,0:T(8,128)}, u32[]{:S(2)}) copy-start(f32[24,32]{1,0:T(8,128)} %param.21) | copy-start | bytes 9220
  11.9 17.1 %copy-start.5 = (f32[24,32]{1,0:T(8,128)S(1)}, f32[24,32]{1,0:T(8,128)}, u32[]{:S(2)}) copy-start(f32[24,32]{1,0:T(8,128)} %param.29) | copy-start | bytes 9220
  11.9 29.1 %collective-permute-start.5 = (bf16[3,3,80,640]{3,2,1,0:T(8,128)(2,1)}, bf16[3,3,80,640]{3,2,1,0:T(8,128)(2,1)}, u32[]{:S(2)}, u32[]{:S(2)}) collective-permute-start(bf16[3,3,80,640]{3,2,1,0:T(8,128)(2,1)} %dynamic-slice_bitcast_fusion.1), channel_id=1, source_target_pairs={{8,0},{12,4},{0,8},{4,12},{9,1},{13,5},{1,9},{5,13},{10,2},{14,6},... | collective-permute-start | bytes 2764808 | tf_op jit(solution)/shard_map/ppermute | solution.py:36
  13.7 86.5 %collective-permute-start.9 = (bf16[3,3,160,640]{3,2,1,0:T(8,128)(2,1)}, bf16[3,3,160,640]{3,2,1,0:T(8,128)(2,1)}, u32[]{:S(2)}, u32[]{:S(2)}) collective-permute-start(bf16[3,3,160,640]{3,2,1,0:T(8,128)(2,1)} %param.32), channel_id=1, source_target_pairs={{0,4},{4,0},{8,12},{12,8},{1,5},{5,1},{9,13},{13,9},{2,6},{6,2},{1... | collective-permute-start | bytes 5529608 | tf_op jit(solution)/shard_map/ppermute | solution.py:33
  16.0 13.4 %copy-start.6 = (f32[24,32]{1,0:T(8,128)S(1)}, f32[24,32]{1,0:T(8,128)}, u32[]{:S(2)}) copy-start(f32[24,32]{1,0:T(8,128)} %param.28) | copy-start | bytes 9220
  21.8 10.0 %collective-permute-start.2 = (bf16[2,24,6,1,640]{4,1,3,2,0:T(8,128)(2,1)}, bf16[2,24,6,1,640]{4,1,3,2,0:T(8,128)(2,1)}, u32[]{:S(2)}, u32[]{:S(2)}) collective-permute-start(bf16[2,24,6,1,640]{4,1,3,2,0:T(8,128)(2,1)} %get-tuple-element.9), channel_id=1, source_target_pairs={{0,1},{1,2},{2,3},{4,5},{5,6},{6,7},{8,9},{9,10},{10,11},{12,13},{... | collective-permute-start | bytes 1105928 | tf_op jit(solution)/shard_map/ppermute | solution.py:14
  25.7 9.0 %collective-permute-start.3 = (bf16[2,24,6,1,640]{4,1,3,2,0:T(8,128)(2,1)}, bf16[2,24,6,1,640]{4,1,3,2,0:T(8,128)(2,1)}, u32[]{:S(2)}, u32[]{:S(2)}) collective-permute-start(bf16[2,24,6,1,640]{4,1,3,2,0:T(8,128)(2,1)} %get-tuple-element.10), channel_id=1, source_target_pairs={{1,0},{2,1},{3,2},{5,4},{6,5},{7,6},{9,8},{10,9},{11,10},{13,12},{... | collective-permute-start | bytes 1105928 | tf_op jit(solution)/shard_map/ppermute | solution.py:17
  29.1 1.9 %copy-start.11 = (pred[10]{0:T(512)(128)(4,1)S(1)}, pred[10]{0:T(512)(128)(4,1)}, u32[]{:S(2)}) copy-start(pred[10]{0:T(512)(128)(4,1)} %compare_and_fusion) | copy-start | bytes 34
  31.7 5.9 %copy-start.8 = (s32[640]{0:T(1024)S(1)}, s32[640]{0:T(1024)}, u32[]{:S(2)}) copy-start(s32[640]{0:T(1024)} %fusion.83) | copy-start | bytes 7684
  31.7 5.9 %copy-start.15 = (f32[640]{0:T(1024)S(1)}, f32[640]{0:T(1024)}, u32[]{:S(2)}) copy-start(f32[640]{0:T(1024)} %param.31) | copy-start | bytes 7684
  31.7 6.0 %copy-start.16 = (f32[640]{0:T(1024)S(1)}, f32[640]{0:T(1024)}, u32[]{:S(2)}) copy-start(f32[640]{0:T(1024)} %param.30) | copy-start | bytes 7684
  31.7 23.0 %collective-permute-start.10 = (bf16[3,3,80,640]{3,2,1,0:T(8,128)(2,1)S(1)}, bf16[3,3,80,640]{3,2,1,0:T(8,128)(2,1)S(1)}, u32[]{:S(2)}, u32[]{:S(2)}) collective-permute-start(bf16[3,3,80,640]{3,2,1,0:T(8,128)(2,1)S(1)} %dynamic-slice_bitcast_fusion), channel_id=1, source_target_pairs={{8,0},{12,4},{0,8},{4,12},{9,1},{13,5},{1,9},{5,13},{10,2},{14,6},... | collective-permute-start | bytes 2764808 | tf_op jit(solution)/shard_map/ppermute | solution.py:36
  41.0 23.1 %collective-permute-start.6 = (bf16[3,3,80,640]{3,2,1,0:T(8,128)(2,1)}, bf16[3,3,80,640]{3,2,1,0:T(8,128)(2,1)S(1)}, u32[]{:S(2)}, u32[]{:S(2)}) collective-permute-start(bf16[3,3,80,640]{3,2,1,0:T(8,128)(2,1)} %collective-permute-done.5), channel_id=1, source_target_pairs={{0,16},{16,0},{1,17},{17,1},{2,18},{18,2},{3,19},{19,3},{4,20},{20... | collective-permute-start | bytes 2764808 | tf_op jit(solution)/shard_map/ppermute | solution.py:37
  54.8 28.1 %collective-permute-start.11 = (bf16[3,3,80,640]{3,2,1,0:T(8,128)(2,1)S(1)}, bf16[3,3,80,640]{3,2,1,0:T(8,128)(2,1)S(1)}, u32[]{:S(2)}, u32[]{:S(2)}) collective-permute-start(bf16[3,3,80,640]{3,2,1,0:T(8,128)(2,1)S(1)} %collective-permute-done.10), channel_id=1, source_target_pairs={{0,16},{16,0},{1,17},{17,1},{2,18},{18,2},{3,19},{19,3},{4,20},{20... | collective-permute-start | bytes 2764808 | tf_op jit(solution)/shard_map/ppermute | solution.py:37
  56.2 0.8 copy-start.2
  56.3 0.8 copy-start.13
  56.3 0.8 copy-start.14
  60.4 29.5 %copy-start.12 = (f32[24,640]{1,0:T(8,128)S(1)}, f32[24,640]{1,0:T(8,128)}, u32[]{:S(2)}) copy-start(f32[24,640]{1,0:T(8,128)} %param.27) | copy-start | bytes 184324
  60.4 29.5 %copy-start.17 = (f32[640]{0:T(1024)S(1)}, f32[640]{0:T(1024)}, u32[]{:S(2)}) copy-start(f32[640]{0:T(1024)} %param.26) | copy-start | bytes 7684
  60.4 29.5 %collective-permute-start.7 = (bf16[3,3,80,640]{3,2,1,0:T(8,128)(2,1)}, bf16[3,3,80,640]{3,2,1,0:T(8,128)(2,1)S(1)}, u32[]{:S(2)}, u32[]{:S(2)}) collective-permute-start(bf16[3,3,80,640]{3,2,1,0:T(8,128)(2,1)} %collective-permute-done.5), channel_id=1, source_target_pairs={{0,4},{4,0},{8,12},{12,8},{1,5},{5,1},{9,13},{13,9},{2,6},{6,2},{1... | collective-permute-start | bytes 2764808 | tf_op jit(solution)/shard_map/ppermute | solution.py:38
  64.0 42.8 %collective-permute-start.12 = (bf16[3,3,80,640]{3,2,1,0:T(8,128)(2,1)S(1)}, bf16[3,3,80,640]{3,2,1,0:T(8,128)(2,1)S(1)}, u32[]{:S(2)}, u32[]{:S(2)}) collective-permute-start(bf16[3,3,80,640]{3,2,1,0:T(8,128)(2,1)S(1)} %collective-permute-done.10), channel_id=1, source_target_pairs={{0,4},{4,0},{8,12},{12,8},{1,5},{5,1},{9,13},{13,9},{2,6},{6,2},{1... | collective-permute-start | bytes 2764808 | tf_op jit(solution)/shard_map/ppermute | solution.py:38
  64.1 25.8 %collective-permute-start.8 = (bf16[3,3,80,640]{3,2,1,0:T(8,128)(2,1)S(1)}, bf16[3,3,80,640]{3,2,1,0:T(8,128)(2,1)S(1)}, u32[]{:S(2)}, u32[]{:S(2)}) collective-permute-start(bf16[3,3,80,640]{3,2,1,0:T(8,128)(2,1)S(1)} %collective-permute-done.6), channel_id=1, source_target_pairs={{0,4},{4,0},{8,12},{12,8},{1,5},{5,1},{9,13},{13,9},{2,6},{6,2},{1... | collective-permute-start | bytes 2764808 | tf_op jit(solution)/shard_map/ppermute | solution.py:39
  82.9 24.0 %collective-permute-start.13 = (bf16[3,3,80,640]{3,2,1,0:T(8,128)(2,1)S(1)}, bf16[3,3,80,640]{3,2,1,0:T(8,128)(2,1)S(1)}, u32[]{:S(2)}, u32[]{:S(2)}) collective-permute-start(bf16[3,3,80,640]{3,2,1,0:T(8,128)(2,1)S(1)} %collective-permute-done.11), channel_id=1, source_target_pairs={{0,4},{4,0},{8,12},{12,8},{1,5},{5,1},{9,13},{13,9},{2,6},{6,2},{1... | collective-permute-start | bytes 2764808 | tf_op jit(solution)/shard_map/ppermute | solution.py:39
  98.2 2.1 %copy-start.1 = (bf16[3,3,160,640]{3,2,1,0:T(8,128)(2,1)S(1)}, bf16[3,3,160,640]{3,2,1,0:T(8,128)(2,1)}, u32[]{:S(2)}) copy-start(bf16[3,3,160,640]{3,2,1,0:T(8,128)(2,1)} %param.32) | copy-start | bytes 5529604
  112.2 0.7 copy-start.10
  112.2 1.2 %copy-start = (bf16[24,4,8,640]{3,2,1,0:T(8,128)(2,1)S(1)}, bf16[24,4,8,640]{3,2,1,0:T(8,128)(2,1)}, u32[]{:S(2)}) copy-start(bf16[24,4,8,640]{3,2,1,0:T(8,128)(2,1)} %param.19) | copy-start | bytes 2949124
  112.2 1.2 %copy-start.9 = (f32[640]{0:T(1024)S(1)}, f32[640]{0:T(1024)}, u32[]{:S(2)}) copy-start(f32[640]{0:T(1024)} %param.33) | copy-start | bytes 7684
